TPU v7x, 32 devices: a whole 2x2x4 slice. The times are simulated.
32 devices in a mesh: dp: 4 (over y, x), fsdp: 8 (over z, core).
Axes of the slice: x: 2, y: 2, z: 4, core: 2. Of those that a mesh axis runs over, the one named last changes fastest.
Arguments:
- token_ids: int32 [32, 128], P(('dp', 'fsdp')), may hold values from 0 to 8191
- target_ids: int32 [32, 128], P(('dp', 'fsdp')), may hold values from 0 to 8191
- domain_ids: int32 [32, 1], P(('dp', 'fsdp')), may hold values from 0 to 21
- in_embed: bfloat16 [8192, 128], P('fsdp'), may hold values from -6 to 6
- out_embed: bfloat16 [8192, 128], P('fsdp'), may hold values from -42.426407 to 42.426407
- ref_norm1: bfloat16 [128], P('fsdp'), may hold values from 0.5 to 1.5
- ref_gate: bfloat16 [512, 128], P('fsdp'), may hold values from -0.5 to 0.5
- ref_up: bfloat16 [512, 128], P('fsdp'), may hold values from -0.5 to 0.5
- ref_down: bfloat16 [512, 128], P('fsdp'), may hold values from -0.25 to 0.25
- ref_norm2: bfloat16 [128], P('fsdp'), may hold values from 0.5 to 1.5
- prx_norm1: bfloat16 [128], P('fsdp'), may hold values from 0.5 to 1.5
- prx_gate: bfloat16 [512, 128], P('fsdp'), may hold values from -0.5 to 0.5
- prx_up: bfloat16 [512, 128], P('fsdp'), may hold values from -0.5 to 0.5
- prx_down: bfloat16 [512, 128], P('fsdp'), may hold values from -0.25 to 0.25
- prx_norm2: bfloat16 [128], P('fsdp'), may hold values from 0.5 to 1.5
- alpha_prev: float32 [22], replicated, may hold values from 0.01 to 0.1
Outputs:
- alpha_new: float32 [22], replicated
- grad_gate: float32 [512, 128], P('fsdp')
- grad_up: float32 [512, 128], P('fsdp')
- grad_down: float32 [512, 128], P('fsdp')
Inputs may be any that keep to these rules, and one draw needn't show every extreme that they name: `domain_ids`: every one of the 22 domains is the domain of at least one row.
All inputs are finite; a program needn't handle non-finite values.
Results may differ from a plain program's by a relative error of at most 0.0075.
The roundings to bfloat16 on the way count: a program that leaves them out, or rounds other values in their place, can miss the bound.
Values may be sent and summed in bfloat16 or wider, within the bound.
No kernel may reach another device: no remote copies, remote signals or barrier semaphores. Data moves between devices by JAX's collectives and lax.ppermute only.
A program may use at most 64 MiB of HBM per device.

v0:
```python
import math

import jax
import jax.numpy as jnp
from jax import lax
from jax.sharding import PartitionSpec as P

EPSILON = 1e-05
SMOOTHING = 0.001


def combined_all(value, axis, join):
    pieces = jax.tree.map(lambda part: lax.all_gather(part, axis), value)
    head = jax.tree.map(lambda part: part[0], pieces)
    tail = jax.tree.map(lambda part: part[1:], pieces)
    running, _ = lax.scan(lambda running, piece: (join(running, piece), None), head, tail)
    return running


def rms_scale(values):
    return lax.rsqrt(jnp.mean(values * values, axis=1, keepdims=True) + EPSILON)


def contract_last(left_side, right_side):
    return lax.dot_general(
        left_side, right_side, (((1,), (1,)), ((), ())), preferred_element_type=jnp.float32
    )


def contract_first(left_side, right_side):
    return lax.dot_general(
        left_side, right_side, (((0,), (0,)), ((), ())), preferred_element_type=jnp.float32
    )


def feed_forward(embedded, normed, weights):
    gate_weight, up_weight, down_weight, norm_first, norm_second = weights
    first_in = (normed * norm_first.astype(jnp.float32)).astype(jnp.bfloat16)
    gate_act = contract_last(first_in, gate_weight)
    up_act = contract_last(first_in, up_weight)
    hidden = (gate_act * jax.nn.sigmoid(gate_act) * up_act).astype(jnp.bfloat16)
    stream = embedded + jnp.dot(hidden, down_weight, preferred_element_type=jnp.float32)
    second_scale = rms_scale(stream)
    unit_stream = stream * second_scale
    second_in = (unit_stream * norm_second.astype(jnp.float32)).astype(jnp.bfloat16)
    return (second_in, (first_in, gate_act, up_act, hidden, second_scale, unit_stream))


def gather_layer(gate_shard, up_shard, down_shard, norm_first, norm_second):
    return (
        lax.all_gather(gate_shard, "fsdp", axis=0, tiled=True),
        lax.all_gather(up_shard, "fsdp", axis=0, tiled=True),
        lax.all_gather(down_shard, "fsdp", axis=0, tiled=True),
        lax.all_gather(norm_first, "fsdp", axis=0, tiled=True),
        lax.all_gather(norm_second, "fsdp", axis=0, tiled=True),
    )


def shard_stats(second_in, table, local_target):
    row_total = second_in.shape[0]
    block_rows = math.gcd(row_total, 512)
    block_count = row_total // block_rows
    column_range = jnp.arange(table.shape[0], dtype=jnp.int32)

    def shard_one_block(block):
        inputs, targets = block
        logits = contract_last(inputs, table)
        top_logit = jnp.max(logits, axis=1)
        exp_total = jnp.sum(jnp.exp(logits - top_logit[:, None]), axis=1)
        picked = jnp.sum(jnp.where(targets[:, None] == column_range[None, :], logits, 0.0), axis=1)
        return (top_logit, exp_total, picked)

    results = lax.map(
        shard_one_block,
        (
            second_in.reshape(block_count, block_rows, -1),
            local_target.reshape(block_count, block_rows),
        ),
    )
    return tuple((item.reshape(row_total) for item in results))


def combine_stats(first, second):
    merged = []
    for offset in range(0, len(first), 3):
        top_first, total_first, pick_first = (first[offset], first[offset + 1], first[offset + 2])
        top_second, total_second, pick_second = (
            second[offset],
            second[offset + 1],
            second[offset + 2],
        )
        top_logit = jnp.maximum(top_first, top_second)
        exp_total = total_first * jnp.exp(top_first - top_logit) + total_second * jnp.exp(
            top_second - top_logit
        )
        merged = merged + [top_logit, exp_total, pick_first + pick_second]
    return tuple(merged)


def body(
    token_ids,
    target_ids,
    domain_ids,
    in_embed,
    out_embed,
    ref_norm1,
    ref_gate,
    ref_up,
    ref_down,
    ref_norm2,
    prx_norm1,
    prx_gate,
    prx_up,
    prx_down,
    prx_norm2,
    alpha_prev,
):
    domain_total = alpha_prev.shape[0]
    rows_here, seq_len = token_ids.shape
    per_device = rows_here * seq_len
    vocab_here = in_embed.shape[0]
    width = in_embed.shape[1]
    fsdp_size = lax.axis_size("fsdp")
    vocab_start = lax.axis_index("fsdp") * vocab_here
    all_tokens, all_targets, all_domains = (
        lax.all_gather(token_ids, "fsdp", axis=0, tiled=True),
        lax.all_gather(target_ids, "fsdp", axis=0, tiled=True),
        lax.all_gather(domain_ids, "fsdp", axis=0, tiled=True),
    )
    token_local = all_tokens.reshape(-1) - vocab_start
    target_local = all_targets.reshape(-1) - vocab_start
    domain_flat = jnp.repeat(all_domains[:, 0], seq_len)
    domain_range = jnp.arange(domain_total, dtype=jnp.int32)
    dom_hits = (domain_flat[:, None] == domain_range[None, :]).astype(jnp.float32)
    inside = ((token_local >= 0) & (token_local < vocab_here)).astype(jnp.float32)
    picked_rows = (
        jnp.take(in_embed, jnp.clip(token_local, 0, vocab_here - 1), axis=0).astype(jnp.float32)
        * inside[:, None]
    )
    ref_weights = gather_layer(ref_gate, ref_up, ref_down, ref_norm1, ref_norm2)
    prx_weights = gather_layer(prx_gate, prx_up, prx_down, prx_norm1, prx_norm2)
    embedded = lax.psum_scatter(
        picked_rows.astype(jnp.bfloat16), "fsdp", scatter_dimension=0, tiled=True
    ).astype(jnp.float32)
    normed = embedded * rms_scale(embedded)
    ref_own = feed_forward(embedded, normed, ref_weights)[0]
    prx_own, saved_state = feed_forward(embedded, normed, prx_weights)
    ref_group, prx_group = (
        lax.all_gather(ref_own, "fsdp", axis=0, tiled=True),
        lax.all_gather(prx_own, "fsdp", axis=0, tiled=True),
    )
    ref_top, ref_sum, ref_pick = shard_stats(ref_group, out_embed, target_local)
    prx_top, prx_sum, prx_pick = shard_stats(prx_group, out_embed, target_local)
    merged = combined_all(
        (ref_top, ref_sum, ref_pick, prx_top, prx_sum, prx_pick), "fsdp", combine_stats
    )
    ref_loss = merged[0] + jnp.log(merged[1]) - merged[2]
    prx_total = merged[3] + jnp.log(merged[4])
    excess = jnp.maximum(prx_total - merged[5] - ref_loss, 0.0)
    total_sums, domain_counts = lax.psum(
        (jnp.sum(dom_hits * excess[:, None], axis=0), jnp.sum(dom_hits, axis=0)), "dp"
    )
    softmax_mix = jax.nn.softmax(jnp.log(alpha_prev) + total_sums / domain_counts)
    alpha_new = (1.0 - SMOOTHING) * softmax_mix + SMOOTHING / domain_total
    device_total = per_device * lax.axis_size("dp") * fsdp_size
    token_ratio = math.sqrt(device_total) * alpha_new / domain_counts
    token_weight = jnp.sum(dom_hits * token_ratio[None, :], axis=1)
    column_range = jnp.arange(vocab_here, dtype=jnp.int32)
    block_rows = math.gcd(per_device * lax.axis_size("fsdp"), 512)
    block_count = per_device * lax.axis_size("fsdp") // block_rows
    inputs = prx_group.reshape(block_count, block_rows, -1)
    totals = prx_total.reshape(block_count, block_rows)
    weights = token_weight.reshape(block_count, block_rows)
    targets = target_local.reshape(block_count, block_rows)

    def head_one_block(block):
        block_in, block_total, block_weight, block_target = block
        logits = contract_last(block_in, out_embed)
        probs = jnp.exp(logits - block_total[:, None])
        hits = (block_target[:, None] == column_range[None, :]).astype(jnp.float32)
        d_logits = (block_weight[:, None] * (probs - hits)).astype(jnp.bfloat16)
        return jnp.dot(d_logits, out_embed, preferred_element_type=jnp.float32)

    d_second = lax.psum_scatter(
        lax.map(head_one_block, (inputs, totals, weights, targets)).reshape(
            per_device * lax.axis_size("fsdp"), -1
        ),
        "fsdp",
        scatter_dimension=0,
        tiled=True,
    )
    first_in, gate_act, up_act, hidden, second_scale, unit_stream = saved_state
    d_unit = d_second * prx_weights[4].astype(jnp.float32)
    d_branch = (
        second_scale
        * (d_unit - unit_stream * jnp.mean(d_unit * unit_stream, axis=1, keepdims=True))
    ).astype(jnp.bfloat16)
    d_hidden = contract_last(d_branch, prx_weights[2])
    sigmoid_gate = jax.nn.sigmoid(gate_act)
    d_gate = (d_hidden * up_act * sigmoid_gate * (1.0 + gate_act * (1.0 - sigmoid_gate))).astype(
        jnp.bfloat16
    )
    d_up = (d_hidden * gate_act * sigmoid_gate).astype(jnp.bfloat16)
    partial_grad = jnp.concatenate(
        [
            contract_first(d_gate, first_in),
            contract_first(d_up, first_in),
            contract_first(hidden, d_branch),
        ],
        axis=1,
    )
    rounded = lax.optimization_barrier(partial_grad.astype(jnp.bfloat16))
    local_grad = lax.psum_scatter(
        rounded.astype(jnp.float32).astype(jnp.bfloat16), "fsdp", scatter_dimension=0, tiled=True
    ).astype(jnp.float32)
    grad_shard = lax.psum(local_grad, "dp")
    return (
        alpha_new,
        grad_shard[:, :width],
        grad_shard[:, width : 2 * width],
        grad_shard[:, 2 * width :],
    )


def solution(mesh):
    placed = (
        P(("dp", "fsdp"), None),
        P(("dp", "fsdp"), None),
        P(("dp", "fsdp"), None),
        P("fsdp", None),
        P("fsdp", None),
        P("fsdp"),
        P("fsdp", None),
        P("fsdp", None),
        P("fsdp", None),
        P("fsdp"),
        P("fsdp"),
        P("fsdp", None),
        P("fsdp", None),
        P("fsdp", None),
        P("fsdp"),
        P(),
    )
    return jax.shard_map(
        body,
        mesh=mesh,
        in_specs=placed,
        out_specs=(P(), P("fsdp", None), P("fsdp", None), P("fsdp", None)),
        check_vma=False,
    )
```

profile of v0, /device:TPU:0, one launch (start us, length us, event | category | flops | bytes accessed | tf_op | source)
XLA Modules:
  0.0 369.3 jit_solution(6620996398305857346)
XLA Ops:
  7.4 13.7 %all-gather = s32[8,1,128]{2,1,0:T(1,128)S(1)} all-gather(s32[1,1,128]{2,1,0:T(1,128)} %bitcast.177), channel_id=1, replica_groups=mesh['dp'=4,'fsdp'=8] {'fsdp'}, dimensions={0}, use_global_device_ids=true | all-gather | bytes 4608 | tf_op jit(solution)/shard_map/all_gather | solution.py:126
  21.1 3.2 gather_fusion
  24.3 1.0 multiply_convert_fusion.1
  26.1 8.6 %all-gather.1 = s32[8,1,128]{2,1,0:T(1,128)S(1)} all-gather(s32[1,1,128]{2,1,0:T(1,128)S(1)} %bitcast.178), channel_id=1, replica_groups=mesh['dp'=4,'fsdp'=8] {'fsdp'}, dimensions={0}, use_global_device_ids=true | all-gather | bytes 4608 | tf_op jit(solution)/shard_map/all_gather | solution.py:127
  36.1 14.1 %all_gather.78 = bf16[512,128]{1,0:T(8,128)(2,1)S(1)} all-gather(bf16[64,128]{1,0:T(8,128)(2,1)S(1)} %copy-done.2), channel_id=1, replica_groups=mesh['dp'=4,'fsdp'=8] {'fsdp'}, dimensions={0}, use_global_device_ids=true | all-gather | bytes 147456 | tf_op jit(solution)/shard_map/all_gather | solution.py:53
  50.1 7.2 %all-reduce = s32[8]{0:T(128)S(1)} all-reduce(s32[8]{0:T(128)S(1)} %bitcast_dynamic-update-slice_fusion), channel_id=1, replica_groups=mesh['dp'=4,'fsdp'=8] {'fsdp'}, use_global_device_ids=true, to_apply=%add | all-reduce | flops 8 | bytes 64
  59.0 13.9 %all-reduce.6 = (bf16[128]{0:T(256)(128)(2,1)S(1)}, bf16[128]{0:T(256)(128)(2,1)S(1)}, bf16[128]{0:T(256)(128)(2,1)S(1)}, bf16[128]{0:T(256)(128)(2,1)S(1)}) all-reduce(bf16[128]{0:T(256)(128)(2,1)S(1)} %dynamic-update-slice.1, bf16[128]{0:T(256)(128)(2,1)S(1)} %dynamic-update-slice.2, ...), channel_id=1, replica_groups=mesh['dp'=4,'fsdp'=8] {'fsdp'}, use_global_device_ids=true, to_apply=%add.1 | all-reduce | flops 512 | bytes 2048
  73.0 14.0 %all_gather.66 = bf16[512,128]{1,0:T(8,128)(2,1)S(1)} all-gather(bf16[64,128]{1,0:T(8,128)(2,1)S(1)} %copy-done.3), channel_id=1, replica_groups=mesh['dp'=4,'fsdp'=8] {'fsdp'}, dimensions={0}, use_global_device_ids=true | all-gather | bytes 147456 | tf_op jit(solution)/shard_map/all_gather | solution.py:51
  87.0 14.0 %all_gather.67 = bf16[512,128]{1,0:T(8,128)(2,1)S(1)} all-gather(bf16[64,128]{1,0:T(8,128)(2,1)S(1)} %copy-done.4), channel_id=1, replica_groups=mesh['dp'=4,'fsdp'=8] {'fsdp'}, dimensions={0}, use_global_device_ids=true | all-gather | bytes 147456 | tf_op jit(solution)/shard_map/all_gather | solution.py:52
  101.0 14.0 %all_gather.68 = bf16[512,128]{1,0:T(8,128)(2,1)S(1)} all-gather(bf16[64,128]{1,0:T(8,128)(2,1)S(1)} %copy-done.5), channel_id=1, replica_groups=mesh['dp'=4,'fsdp'=8] {'fsdp'}, dimensions={0}, use_global_device_ids=true | all-gather | bytes 147456 | tf_op jit(solution)/shard_map/all_gather | solution.py:53
  114.9 14.0 %all_gather.76 = bf16[512,128]{1,0:T(8,128)(2,1)S(1)} all-gather(bf16[64,128]{1,0:T(8,128)(2,1)S(1)} %copy-done.6), channel_id=1, replica_groups=mesh['dp'=4,'fsdp'=8] {'fsdp'}, dimensions={0}, use_global_device_ids=true | all-gather | bytes 147456 | tf_op jit(solution)/shard_map/all_gather | solution.py:51
  128.9 14.0 %all_gather.77 = bf16[512,128]{1,0:T(8,128)(2,1)S(1)} all-gather(bf16[64,128]{1,0:T(8,128)(2,1)S(1)} %copy-done.7), channel_id=1, replica_groups=mesh['dp'=4,'fsdp'=8] {'fsdp'}, dimensions={0}, use_global_device_ids=true | all-gather | bytes 147456 | tf_op jit(solution)/shard_map/all_gather | solution.py:52
  144.7 13.1 %all_gather.70 = bf16[1024,128]{0,1:T(8,128)(2,1)S(1)} all-gather(bf16[128,128]{0,1:T(8,128)(2,1)S(1)} %multiply_convert_fusion.9), channel_id=1, replica_groups=mesh['dp'=4,'fsdp'=8] {'fsdp'}, dimensions={0}, use_global_device_ids=true | all-gather | bytes 294912 | tf_op jit(solution)/shard_map/all_gather | solution.py:149
  158.0 3.0 while.62
  161.0 14.0 %all-gather.3 = f32[8,1,1024]{2,1,0:T(1,128)S(1)} all-gather(f32[1,1,1024]{2,1,0:T(1,128)S(1)} %reshape.171), channel_id=1, replica_groups=mesh['dp'=4,'fsdp'=8] {'fsdp'}, dimensions={0}, use_global_device_ids=true | all-gather | bytes 36864 | tf_op jit(solution)/shard_map/all_gather | solution.py:13
  175.1 14.0 %all-gather.2 = f32[8,1,1024]{2,1,0:T(1,128)S(1)} all-gather(f32[1,1,1024]{2,1,0:T(1,128)S(1)} %reshape.169), channel_id=1, replica_groups=mesh['dp'=4,'fsdp'=8] {'fsdp'}, dimensions={0}, use_global_device_ids=true | all-gather | bytes 36864 | tf_op jit(solution)/shard_map/all_gather | solution.py:13
  189.1 14.0 %all-gather.4 = f32[8,1,1024]{2,1,0:T(1,128)S(1)} all-gather(f32[1,1,1024]{2,1,0:T(1,128)S(1)} %reshape.173), channel_id=1, replica_groups=mesh['dp'=4,'fsdp'=8] {'fsdp'}, dimensions={0}, use_global_device_ids=true | all-gather | bytes 36864 | tf_op jit(solution)/shard_map/all_gather | solution.py:13
  204.0 13.3 %all_gather.80 = bf16[1024,128]{0,1:T(8,128)(2,1)S(1)} all-gather(bf16[128,128]{0,1:T(8,128)(2,1)S(1)} %multiply_convert_fusion.8), channel_id=1, replica_groups=mesh['dp'=4,'fsdp'=8] {'fsdp'}, dimensions={0}, use_global_device_ids=true | all-gather | bytes 294912 | tf_op jit(solution)/shard_map/all_gather | solution.py:150
  217.5 3.0 while.63
  220.5 14.0 %all-gather.6 = f32[8,1,1024]{2,1,0:T(1,128)S(1)} all-gather(f32[1,1,1024]{2,1,0:T(1,128)S(1)} %reshape.177), channel_id=1, replica_groups=mesh['dp'=4,'fsdp'=8] {'fsdp'}, dimensions={0}, use_global_device_ids=true | all-gather | bytes 36864 | tf_op jit(solution)/shard_map/all_gather | solution.py:13
  234.5 14.0 %all-gather.5 = f32[8,1,1024]{2,1,0:T(1,128)S(1)} all-gather(f32[1,1,1024]{2,1,0:T(1,128)S(1)} %reshape.175), channel_id=1, replica_groups=mesh['dp'=4,'fsdp'=8] {'fsdp'}, dimensions={0}, use_global_device_ids=true | all-gather | bytes 36864 | tf_op jit(solution)/shard_map/all_gather | solution.py:13
  248.6 14.0 %all-gather.7 = f32[8,1,1024]{2,1,0:T(1,128)S(1)} all-gather(f32[1,1,1024]{2,1,0:T(1,128)S(1)} %reshape.179), channel_id=1, replica_groups=mesh['dp'=4,'fsdp'=8] {'fsdp'}, dimensions={0}, use_global_device_ids=true | all-gather | bytes 36864 | tf_op jit(solution)/shard_map/all_gather | solution.py:13
  262.7 1.1 while.61
  263.9 9.9 %all-reduce.5 = (f32[22]{0:T(128)S(1)}, f32[22]{0:T(128)S(1)}) all-reduce(f32[22]{0:T(128)S(1)} %get-tuple-element.346, f32[22]{0:T(128)S(1)} %get-tuple-element.347), channel_id=1, replica_groups=mesh['dp'=4,'fsdp'=8] {'dp'}, use_global_device_ids=true, to_apply=%region_19.20 | all-reduce | flops 44 | bytes 352 | tf_op jit(solution)/shard_map/psum | solution.py:160
  274.5 1.2 fusion.53
  275.7 1.8 multiply_divide_fusion
  277.7 1.8 while.64
  279.5 1.0 copy.51
  280.5 27.4 %reduce-scatter.8.cloned.1.call-done = f32[128,128]{0,1:T(8,128)} async-done(((f32[1024,128]{0,1:T(8,128)}), f32[128,128]{0,1:T(8,128)}) %reduce-scatter.8.cloned.1.call-update) | async-done | bytes 65552 | tf_op jit(solution)/shard_map/reduce_scatter | solution.py:184
  307.9 0.9 multiply_reduce_fusion
  311.7 29.0 %reduce-scatter.12.cloned.1.call-done = bf16[64,384]{1,0:T(8,128)(2,1)} async-done(((bf16[512,384]{1,0:T(8,128)(2,1)}), bf16[64,384]{1,0:T(8,128)(2,1)}) %reduce-scatter.12.cloned.1.call-update) | async-done | bytes 49168
  341.6 19.0 %all-reduce.8 = f32[64,384]{0,1:T(8,128)S(1)} all-reduce(bf16[64,384]{0,1:T(8,128)(2,1)S(1)} %copy.55), channel_id=1, replica_groups=mesh['dp'=4,'fsdp'=8] {'dp'}, use_global_device_ids=true, to_apply=%region_28.29 | all-reduce | flops 24576 | bytes 147456 | tf_op jit(solution)/shard_map/psum | solution.py:216
  (209 shorter events, 20.6 us)
Async XLA Ops:
  7.2 13.9 %copy-start = (bf16[1024,128]{1,0:T(8,128)(2,1)S(1)}, bf16[1024,128]{1,0:T(8,128)(2,1)}, u32[]{:S(2)}) copy-start(bf16[1024,128]{1,0:T(8,128)(2,1)} %param.27) | copy-start | bytes 786436
  7.2 27.6 %copy-start.14 = (u32[32]{0:T(128)S(1)}, u32[32]{0:T(128)}, u32[]{:S(2)}) copy-start(u32[32]{0:T(128)} %constant.110) | copy-start | bytes 388
  7.2 18.9 %copy-start.8 = (s32[1,128]{1,0:T(1,128)S(1)}, s32[1,128]{1,0:T(1,128)}, u32[]{:S(2)}) copy-start(s32[1,128]{1,0:T(1,128)} %param.25) | copy-start | bytes 1540
  7.2 28.9 %copy-start.2 = (bf16[64,128]{1,0:T(8,128)(2,1)S(1)}, bf16[64,128]{1,0:T(8,128)(2,1)}, u32[]{:S(2)}) copy-start(bf16[64,128]{1,0:T(8,128)(2,1)} %param.37) | copy-start | bytes 49156
  7.2 50.8 %copy-start.10 = (bf16[16]{0:T(256)(128)(2,1)S(1)}, bf16[16]{0:T(256)(128)(2,1)}, u32[]{:S(2)}) copy-start(bf16[16]{0:T(256)(128)(2,1)} %param.34) | copy-start | bytes 100
  7.2 51.1 %copy-start.11 = (bf16[16]{0:T(256)(128)(2,1)S(1)}, bf16[16]{0:T(256)(128)(2,1)}, u32[]{:S(2)}) copy-start(bf16[16]{0:T(256)(128)(2,1)} %param.33) | copy-start | bytes 100
  7.2 51.3 %copy-start.12 = (bf16[16]{0:T(256)(128)(2,1)S(1)}, bf16[16]{0:T(256)(128)(2,1)}, u32[]{:S(2)}) copy-start(bf16[16]{0:T(256)(128)(2,1)} %param.29) | copy-start | bytes 100
  7.2 51.5 %copy-start.13 = (bf16[16]{0:T(256)(128)(2,1)S(1)}, bf16[16]{0:T(256)(128)(2,1)}, u32[]{:S(2)}) copy-start(bf16[16]{0:T(256)(128)(2,1)} %param.38) | copy-start | bytes 100
  7.3 65.8 %copy-start.3 = (bf16[64,128]{1,0:T(8,128)(2,1)S(1)}, bf16[64,128]{1,0:T(8,128)(2,1)}, u32[]{:S(2)}) copy-start(bf16[64,128]{1,0:T(8,128)(2,1)} %param.30) | copy-start | bytes 49156
  7.3 79.7 %copy-start.4 = (bf16[64,128]{1,0:T(8,128)(2,1)S(1)}, bf16[64,128]{1,0:T(8,128)(2,1)}, u32[]{:S(2)}) copy-start(bf16[64,128]{1,0:T(8,128)(2,1)} %param.31) | copy-start | bytes 49156
  7.3 93.7 %copy-start.5 = (bf16[64,128]{1,0:T(8,128)(2,1)S(1)}, bf16[64,128]{1,0:T(8,128)(2,1)}, u32[]{:S(2)}) copy-start(bf16[64,128]{1,0:T(8,128)(2,1)} %param.32) | copy-start | bytes 49156
  7.3 107.6 %copy-start.6 = (bf16[64,128]{1,0:T(8,128)(2,1)S(1)}, bf16[64,128]{1,0:T(8,128)(2,1)}, u32[]{:S(2)}) copy-start(bf16[64,128]{1,0:T(8,128)(2,1)} %param.35) | copy-start | bytes 49156
  7.3 121.6 %copy-start.7 = (bf16[64,128]{1,0:T(8,128)(2,1)S(1)}, bf16[64,128]{1,0:T(8,128)(2,1)}, u32[]{:S(2)}) copy-start(bf16[64,128]{1,0:T(8,128)(2,1)} %param.36) | copy-start | bytes 49156
  7.3 135.6 %reduce-scatter.10.cloned.1.call-start = ((), (), s32[]{:S(2)}) async-start(), calls=%async_computation.4 | async-start | bytes 294912
  25.4 132.7 %copy-start.1 = (bf16[1024,128]{1,0:T(8,128)(2,1)S(1)}, bf16[1024,128]{1,0:T(8,128)(2,1)}, u32[]{:S(2)}) copy-start(bf16[1024,128]{1,0:T(8,128)(2,1)} %param.28) | copy-start | bytes 786436
  25.4 282.5 %reduce-scatter.8.cloned.1.call-start = ((), (), s32[]{:S(2)}) async-start(), calls=%async_computation.3 | async-start | bytes 589824 | tf_op jit(solution)/shard_map/reduce_scatter | solution.py:184
  217.5 56.4 %copy-start.9 = (f32[22]{0:T(128)S(1)}, f32[22]{0:T(128)}, u32[]{:S(2)}) copy-start(f32[22]{0:T(128)} %param.39) | copy-start | bytes 268
  280.5 60.2 %reduce-scatter.12.cloned.1.call-start = ((), (), s32[]{:S(2)}) async-start(), calls=%async_computation.5 | async-start | bytes 442368
Sparse Core Ops, SparseCore 0:
  25.5 28.6 reduce-scatter.9
  280.6 27.2 reduce-scatter.7
  311.8 28.8 reduce-scatter.11
where the time goes:
time: 370 us; the launch traced here: 369 us
  blocking collectives  267 us (72%)
  waiting for transfers between devices  56.4 us (15%)
  between operations  15.6 us (4%)
  local copies, waits for them, and re-layouts  12.9 us (3%)
  other arithmetic  10.5 us (3%)
  matrix products  6.23 us (2%)
    all_gather x6, blocking collectives, combined_all(): pieces = jax.tree.map(lambda part: lax.all_gather(part, axis), value)  84 us
    unnamed x5, waiting for transfers between devices  29.1 us
    all_gather x2, blocking collectives, gather_layer(): lax.all_gather(down_shard, 'fsdp', axis=0, tiled=True)  28 us
    all_gather x2, blocking collectives, gather_layer(): lax.all_gather(gate_shard, 'fsdp', axis=0, tiled=True)  27.9 us
    all_gather x2, blocking collectives, gather_layer(): lax.all_gather(up_shard, 'fsdp', axis=0, tiled=True)  27.9 us
    reduce_scatter x1, waiting for transfers between devices, body(): lax.psum_scatter(lax.map(head_one_block, (inputs, totals, weights, target...  27.4 us
    unnamed x2, blocking collectives  21.2 us
    psum x1, blocking collectives, body(): grad_shard = lax.psum(local_grad, 'dp')  19 us
  transfers between devices with their start and end apart: 3, of which 2 were waited for; matrix products, arithmetic and copies ran while one was open for 1% of the time, Pallas kernels for 0%

commit v1 on v0

v1 whole, which is shorter than its diff:
```python
import math

import jax
import jax.numpy as jnp
from jax import lax
from jax.sharding import PartitionSpec as P

EPSILON = 1e-05
SMOOTHING = 0.001
FAN_OUT_MAX = 8
ID_BASE = 128


def rms_scale(values):
    return lax.rsqrt(jnp.mean(values * values, axis=1, keepdims=True) + EPSILON)


def contract_last(left_side, right_side):
    return lax.dot_general(
        left_side, right_side, (((1,), (1,)), ((), ())), preferred_element_type=jnp.float32
    )


def contract_first(left_side, right_side):
    return lax.dot_general(
        left_side, right_side, (((0,), (0,)), ((), ())), preferred_element_type=jnp.float32
    )


def shift_pairs(size, shift):
    return [(source, (source + shift) % size) for source in range(size)]


def gather_relative(value, axis):
    size = lax.axis_size(axis)
    if size <= FAN_OUT_MAX:
        pieces = [value] + [
            lax.ppermute(value, axis, shift_pairs(size, shift)) for shift in range(1, size)
        ]
        return jnp.stack(pieces)
    here = lax.axis_index(axis)
    stacked = lax.all_gather(value, axis)
    return jnp.take(stacked, (here - jnp.arange(size)) % size, axis=0)


def to_absolute(stack, axis):
    return jnp.roll(stack[::-1], lax.axis_index(axis) + 1, axis=0)


def exchange_relative(blocks, axis):
    size = lax.axis_size(axis)
    if size <= FAN_OUT_MAX:
        pieces = [blocks[0]] + [
            lax.ppermute(blocks[(-shift) % size], axis, shift_pairs(size, shift))
            for shift in range(1, size)
        ]
        return jnp.stack(pieces)
    here = lax.axis_index(axis)
    ordered = jnp.take(blocks, (here - jnp.arange(size)) % size, axis=0)
    return lax.all_to_all(ordered, axis, 0, 0, tiled=True)


def feed_forward(embedded, normed, weights):
    gate_weight, up_weight, down_weight, norm_first, norm_second = weights
    first_in = (normed * norm_first.astype(jnp.float32)).astype(jnp.bfloat16)
    gate_act = contract_last(first_in, gate_weight)
    up_act = contract_last(first_in, up_weight)
    hidden = (gate_act * jax.nn.sigmoid(gate_act) * up_act).astype(jnp.bfloat16)
    stream = embedded + jnp.dot(hidden, down_weight, preferred_element_type=jnp.float32)
    second_scale = rms_scale(stream)
    unit_stream = stream * second_scale
    second_in = (unit_stream * norm_second.astype(jnp.float32)).astype(jnp.bfloat16)
    return (second_in, (first_in, gate_act, up_act, hidden, second_scale, unit_stream))


def block_rows_of(total):
    return math.gcd(total, 1024)


def vocab_stats(inputs, table, targets):
    total = inputs.shape[0]
    rows = block_rows_of(total)
    columns = jnp.arange(table.shape[0], dtype=jnp.int32)

    def one_block(block):
        block_in, block_target = block
        logits = contract_last(block_in, table)
        top_logit = jnp.max(logits, axis=1)
        exp_total = jnp.sum(jnp.exp(logits - top_logit[:, None]), axis=1)
        picked = jnp.sum(jnp.where(block_target[:, None] == columns[None, :], logits, 0.0), axis=1)
        return jnp.stack([top_logit, exp_total, picked])

    if rows == total:
        return one_block((inputs, targets))
    result = lax.map(
        one_block, (inputs.reshape(total // rows, rows, -1), targets.reshape(total // rows, rows))
    )
    return jnp.moveaxis(result, 1, 0).reshape(3, total)


def head_gradient(inputs, table, log_total, weight, targets):
    total = inputs.shape[0]
    rows = block_rows_of(total)
    columns = jnp.arange(table.shape[0], dtype=jnp.int32)

    def one_block(block):
        block_in, block_total, block_weight, block_target = block
        logits = contract_last(block_in, table)
        probs = jnp.exp(logits - block_total[:, None])
        hits = (block_target[:, None] == columns[None, :]).astype(jnp.float32)
        d_logits = (block_weight[:, None] * (probs - hits)).astype(jnp.bfloat16)
        return jnp.dot(d_logits, table, preferred_element_type=jnp.float32)

    if rows == total:
        return one_block((inputs, log_total, weight, targets))
    count = total // rows
    result = lax.map(
        one_block,
        (
            inputs.reshape(count, rows, -1),
            log_total.reshape(count, rows),
            weight.reshape(count, rows),
            targets.reshape(count, rows),
        ),
    )
    return result.reshape(total, -1)


def body(
    token_ids,
    target_ids,
    domain_ids,
    in_embed,
    out_embed,
    ref_norm1,
    ref_gate,
    ref_up,
    ref_down,
    ref_norm2,
    prx_norm1,
    prx_gate,
    prx_up,
    prx_down,
    prx_norm2,
    alpha_prev,
):
    domain_total = alpha_prev.shape[0]
    rows_here, seq_len = token_ids.shape
    per_device = rows_here * seq_len
    vocab_here, width = in_embed.shape
    fsdp_size = lax.axis_size("fsdp")
    group_total = per_device * fsdp_size
    vocab_start = lax.axis_index("fsdp") * vocab_here
    unit_rows = ref_gate.shape[0]
    gain_here = ref_norm1.shape[0]

    tokens = token_ids.reshape(-1)
    targets = target_ids.reshape(-1)
    id_parts = jnp.stack(
        [tokens // ID_BASE, tokens % ID_BASE, targets // ID_BASE, targets % ID_BASE]
    ).astype(jnp.bfloat16)
    matrices = (ref_gate, ref_up, ref_down, prx_gate, prx_up, prx_down)
    gains = (ref_norm1, ref_norm2, prx_norm1, prx_norm2)
    packed = jnp.concatenate(
        [id_parts.reshape(-1), domain_ids.reshape(-1).astype(jnp.bfloat16)]
        + [item.reshape(-1) for item in matrices]
        + [item.reshape(-1) for item in gains]
    )
    gathered = gather_relative(packed, "fsdp")
    offset = 4 * per_device
    group_ids = gathered[:, :offset].astype(jnp.int32).reshape(fsdp_size, 4, per_device)
    group_tokens = (group_ids[:, 0] * ID_BASE + group_ids[:, 1]).reshape(-1)
    group_targets = (group_ids[:, 2] * ID_BASE + group_ids[:, 3]).reshape(-1)
    group_domains = gathered[:, offset : offset + rows_here].astype(jnp.int32)
    offset += rows_here
    matrix_size = unit_rows * width
    full_matrices = []
    for _ in matrices:
        full_matrices.append(
            gathered[:, offset : offset + matrix_size].reshape(fsdp_size * unit_rows, width)
        )
        offset += matrix_size
    full_gains = []
    for _ in gains:
        piece = gathered[:, offset : offset + gain_here]
        full_gains.append(to_absolute(piece, "fsdp").reshape(-1))
        offset += gain_here
    ref_weights = (*full_matrices[:3], full_gains[0], full_gains[1])
    prx_weights = (*full_matrices[3:], full_gains[2], full_gains[3])

    token_local = group_tokens - vocab_start
    inside = (token_local >= 0) & (token_local < vocab_here)
    picked_rows = jnp.where(
        inside[:, None], jnp.take(in_embed, jnp.clip(token_local, 0, vocab_here - 1), axis=0), 0
    ).astype(jnp.bfloat16)
    arrived = exchange_relative(picked_rows.reshape(fsdp_size, per_device, width), "fsdp")
    embedded = jnp.sum(arrived.astype(jnp.float32), axis=0)

    normed = embedded * rms_scale(embedded)
    ref_own = feed_forward(embedded, normed, ref_weights)[0]
    prx_own, saved_state = feed_forward(embedded, normed, prx_weights)

    group_features = gather_relative(jnp.concatenate([ref_own, prx_own], axis=1), "fsdp")
    group_features = group_features.reshape(group_total, 2 * width)
    ref_group = group_features[:, :width]
    prx_group = group_features[:, width:]

    target_local = group_targets - vocab_start
    ref_stats = vocab_stats(ref_group, out_embed, target_local)
    prx_stats = vocab_stats(prx_group, out_embed, target_local)

    local_stats = jnp.concatenate([ref_stats, prx_stats]).reshape(6, fsdp_size, per_device)
    local_stats = to_absolute(jnp.swapaxes(local_stats, 0, 1), "fsdp")
    all_stats = to_absolute(gather_relative(local_stats, "fsdp"), "fsdp")
    tops = all_stats[:, :, 0::3]
    exp_totals = all_stats[:, :, 1::3]
    picks = all_stats[:, :, 2::3]
    top_logit = jnp.max(tops, axis=0)
    exp_total = jnp.sum(exp_totals * jnp.exp(tops - top_logit[None]), axis=0)
    pick_total = jnp.sum(picks, axis=0)
    log_total = top_logit + jnp.log(exp_total)
    losses = log_total - pick_total
    excess = jnp.maximum(losses[:, 1] - losses[:, 0], 0.0)
    relative_order = (lax.axis_index("fsdp") - jnp.arange(fsdp_size)) % fsdp_size
    prx_log_total = jnp.take(log_total[:, 1], relative_order, axis=0).reshape(-1)

    row_excess = jnp.sum(excess.reshape(fsdp_size * rows_here, seq_len), axis=1)
    row_domains = to_absolute(group_domains, "fsdp").reshape(-1)
    domain_range = jnp.arange(domain_total, dtype=jnp.int32)
    row_hits = (row_domains[:, None] == domain_range[None, :]).astype(jnp.float32)
    group_sums = jnp.sum(row_hits * row_excess[:, None], axis=0)
    group_counts = jnp.sum(row_hits, axis=0) * seq_len

    summed = jnp.sum(
        to_absolute(gather_relative(jnp.stack([group_sums, group_counts]), "dp"), "dp"), axis=0
    )
    total_sums = summed[0]
    domain_counts = summed[1]
    softmax_mix = jax.nn.softmax(jnp.log(alpha_prev) + total_sums / domain_counts)
    alpha_new = (1.0 - SMOOTHING) * softmax_mix + SMOOTHING / domain_total
    device_total = group_total * lax.axis_size("dp")
    token_ratio = math.sqrt(device_total) * alpha_new / domain_counts
    group_rows = group_domains.reshape(-1)
    row_weight = jnp.take(token_ratio, group_rows)
    token_weight = jnp.repeat(row_weight, seq_len)

    d_second_part = head_gradient(prx_group, out_embed, prx_log_total, token_weight, target_local)

    d_second = jnp.sum(
        exchange_relative(d_second_part.reshape(fsdp_size, per_device, width), "fsdp"), axis=0
    )
    first_in, gate_act, up_act, hidden, second_scale, unit_stream = saved_state
    d_unit = d_second * prx_weights[4].astype(jnp.float32)
    d_branch = (
        second_scale
        * (d_unit - unit_stream * jnp.mean(d_unit * unit_stream, axis=1, keepdims=True))
    ).astype(jnp.bfloat16)
    d_hidden = contract_last(d_branch, prx_weights[2])
    sigmoid_gate = jax.nn.sigmoid(gate_act)
    d_gate = (d_hidden * up_act * sigmoid_gate * (1.0 + gate_act * (1.0 - sigmoid_gate))).astype(
        jnp.bfloat16
    )
    d_up = (d_hidden * gate_act * sigmoid_gate).astype(jnp.bfloat16)
    partial_grad = jnp.concatenate(
        [
            contract_first(d_gate, first_in),
            contract_first(d_up, first_in),
            contract_first(hidden, d_branch),
        ],
        axis=1,
    ).astype(jnp.bfloat16)

    arrived_grad = exchange_relative(
        partial_grad.reshape(fsdp_size, unit_rows, 3 * width), "fsdp"
    )
    local_grad = jnp.sum(arrived_grad.astype(jnp.float32), axis=0)

    grad_shard = jnp.sum(to_absolute(gather_relative(local_grad, "dp"), "dp"), axis=0)
    return (
        alpha_new,
        grad_shard[:, :width],
        grad_shard[:, width : 2 * width],
        grad_shard[:, 2 * width :],
    )


def solution(mesh):
    placed = (
        P(("dp", "fsdp"), None),
        P(("dp", "fsdp"), None),
        P(("dp", "fsdp"), None),
        P("fsdp", None),
        P("fsdp", None),
        P("fsdp"),
        P("fsdp", None),
        P("fsdp", None),
        P("fsdp", None),
        P("fsdp"),
        P("fsdp"),
        P("fsdp", None),
        P("fsdp", None),
        P("fsdp", None),
        P("fsdp"),
        P(),
    )
    return jax.shard_map(
        body,
        mesh=mesh,
        in_specs=placed,
        out_specs=(P(), P("fsdp", None), P("fsdp", None), P("fsdp", None)),
        check_vma=False,
    )
```

time: 370 us -> 169 us (0.46)
  blocking collectives: 267 us -> 0 us
  starting transfers between devices: 0.12 us -> 50.6 us
  waiting for transfers between devices: 56.4 us -> 75 us
  between operations: 15.6 us -> 2.31 us
  local copies, waits for them, and re-layouts: 12.9 us -> 23.6 us
    all_gather x16 -> x0, blocking collectives: 217 us -> none  [the longest x6 84 us: combined_all(): pieces = jax.tree.map(lambda part: lax.all_gather(part, axis), value)]
    ppermute x0 -> x48, waiting for transfers between devices: none -> 75 us  [the longest x27 43.4 us: gather_relative(): lax.ppermute(value, axis, shift_pairs(size, shift))]
    ppermute x0 -> x48, starting transfers between devices: none -> 50.6 us  [the longest x27 27.8 us: gather_relative(): lax.ppermute(value, axis, shift_pairs(size, shift))]
    unnamed x5 -> x0, waiting for transfers between devices: 29.1 us -> none
    psum x2 -> x0, blocking collectives: 29 us -> none  [the longest x1 19 us: body(): grad_shard = lax.psum(local_grad, 'dp')]
    reduce_scatter x1 -> x0, waiting for transfers between devices: 27.4 us -> none  [body(): lax.psum_scatter(lax.map(head_one_block, (inputs, totals, weights, target...]
    unnamed x2 -> x0, blocking collectives: 21.2 us -> none
    another operation x6 -> x14, local copies, waits for them, and re-layouts: 0.02 us -> 7.79 us  [the longest x12 7.76 us: gather_relative(): return jnp.stack(pieces)]
  transfers between devices with their start and end apart: 3 -> 48, of which waited for: 2 -> 22; matrix products, arithmetic and copies ran while one was open for 1% -> 2% of each run, Pallas kernels for 0% -> 0%
where the time goes in v1:
time: 169 us; the launch traced here: 168 us
  waiting for transfers between devices  75 us (44%)
  starting transfers between devices  50.6 us (30%)
  local copies, waits for them, and re-layouts  23.6 us (14%)
  other arithmetic  9.3 us (6%)
  matrix products  7.08 us (4%)
  between operations  2.31 us (1%)
    ppermute x27, waiting for transfers between devices, gather_relative(): lax.ppermute(value, axis, shift_pairs(size, shift))  43.4 us
    ppermute x21, waiting for transfers between devices, exchange_relative(): lax.ppermute(blocks[-shift % size], axis, shift_pairs(size, shift))  31.7 us
    ppermute x27, starting transfers between devices, gather_relative(): lax.ppermute(value, axis, shift_pairs(size, shift))  27.8 us
    ppermute x21, starting transfers between devices, exchange_relative(): lax.ppermute(blocks[-shift % size], axis, shift_pairs(size, shift))  22.7 us
    another operation x12, local copies, waits for them, and re-layouts, gather_relative(): return jnp.stack(pieces)  7.76 us
    concatenate x1, local copies, waits for them, and re-layouts, body(): jnp.concatenate([id_parts.reshape(-1), domain_ids.reshape(-1).astype(jnp....  7.18 us
    dot_general x1, matrix products, one_block(): return jnp.dot(d_logits, table, preferred_element_type=jnp.float32)  3.51 us
  transfers between devices with their start and end apart: 48, of which 22 were waited for; matrix products, arithmetic and copies ran while one was open for 2% of the time, Pallas kernels for 0%

profile of v1, /device:TPU:0, one launch (start us, length us, event | category | flops | bytes accessed | tf_op | source)
XLA Modules:
  0.0 167.9 jit_solution(2190926012333749813)
XLA Ops:
  2.7 7.2 %concatenate.49 = bf16[49729]{0:T(1024)(128)(2,1)S(1)} concatenate(bf16[512]{0:T(512)(128)(2,1)S(1)} %maximum_bitcast_fusion, bf16[1]{0:T(256)(128)(2,1)} %bitcast.1, bf16[8192]{0:T(1024)(128)(2,1)} %bitcast.160, bf16[8192]{0:T(1024)(128)(2,1)} %bitcast.161, bf16[8192]{0:T(1024)(128)(2,1)} %bitcast.162, bf16[8192]{0:T(1024)(128)(2,1)} %bitcast.163, bf16[8192]{0:T(1024)(128)(2,1)} %bitcast.164, ...), dimensions={0} | concatenate | bytes 198916 | tf_op jit(solution)/shard_map/concatenate | solution.py:164
  9.9 4.5 %collective-permute-start.6 = (bf16[49729]{0:T(1024)(128)(2,1)S(1)}, bf16[49729]{0:T(1024)(128)(2,1)S(1)}, u32[]{:S(2)}, u32[]{:S(2)}) collective-permute-start(bf16[49729]{0:T(1024)(128)(2,1)S(1)} %concatenate.49), channel_id=1, source_target_pairs={{0,7},{1,0},{2,1},{3,2},{4,3},{5,4},{6,5},{7,6},{8,15},{9,8},{10,9... | collective-permute-start | bytes 298382 | tf_op jit(solution)/shard_map/ppermute | solution.py:38
  15.1 2.7 %collective-permute-start.3 = (bf16[49729]{0:T(1024)(128)(2,1)S(1)}, bf16[49729]{0:T(1024)(128)(2,1)S(1)}, u32[]{:S(2)}, u32[]{:S(2)}) collective-permute-start(bf16[49729]{0:T(1024)(128)(2,1)S(1)} %concatenate.49), channel_id=1, source_target_pairs={{0,4},{1,5},{2,6},{3,7},{4,0},{5,1},{6,2},{7,3},{8,12},{9,13},{10,... | collective-permute-start | bytes 298382 | tf_op jit(solution)/shard_map/ppermute | solution.py:38
  18.7 2.4 %collective-permute-done.5 = bf16[49729]{0:T(1024)(128)(2,1)S(1)} collective-permute-done((bf16[49729]{0:T(1024)(128)(2,1)S(1)}, bf16[49729]{0:T(1024)(128)(2,1)S(1)}, u32[]{:S(2)}, u32[]{:S(2)}) %collective-permute-start.5) | collective-permute-done | bytes 99490 | tf_op jit(solution)/shard_map/ppermute | solution.py:38
  22.0 10.1 %collective-permute-done.3 = bf16[49729]{0:T(1024)(128)(2,1)S(1)} collective-permute-done((bf16[49729]{0:T(1024)(128)(2,1)S(1)}, bf16[49729]{0:T(1024)(128)(2,1)S(1)}, u32[]{:S(2)}, u32[]{:S(2)}) %collective-permute-start.3) | collective-permute-done | bytes 99490 | tf_op jit(solution)/shard_map/ppermute | solution.py:38
  33.2 6.7 %stack.197 = bf16[8,49729]{1,0:T(8,128)(2,1)S(1)} concatenate(bf16[1,49729]{1,0:T(2,128)(2,1)S(1)} %stack.189, bf16[1,49729]{1,0:T(2,128)(2,1)S(1)} %stack.190, bf16[1,49729]{1,0:T(2,128)(2,1)S(1)} %stack.191, bf16[1,49729]{1,0:T(2,128)(2,1)S(1)} %stack.192, bf16[1,49729]{1,0:T(2,128)(2,1)S(1)} %stack.193, bf16[1,49729]{1,0:T(2,128)(2,1)S(1)} %stack.194, ...), dimensions={0} | concatenate | bytes 1591328 | tf_op jit(solution)/shard_map/stack | solution.py:40
  40.7 3.2 %gather_fusion = bf16[1024,128]{1,0:T(8,128)(2,1)S(1)} fusion(bf16[1024,128]{1,0:T(8,128)(2,1)S(1)} %copy-done.1, s32[1024]{0:T(1024)S(1)} %broadcast_clamp_fusion), kind=kCustom, calls=%fused_computation | custom fusion | bytes 528384 | tf_op jit(solution)/shard_map/jit(_take)/gather | solution.py:194
  45.4 3.6 %collective-permute-start.13 = (bf16[128,128]{1,0:T(8,128)(2,1)S(1)}, bf16[128,128]{1,0:T(8,128)(2,1)S(1)}, u32[]{:S(2)}, u32[]{:S(2)}) collective-permute-start(bf16[128,128]{1,0:T(8,128)(2,1)S(1)} %get-tuple-element.59), channel_id=1, source_target_pairs={{0,7},{1,0},{2,1},{3,2},{4,3},{5,4},{6,5},{7,6},{8,15},{9,8},{10,9... | collective-permute-start | bytes 98312 | tf_op jit(solution)/shard_map/ppermute | solution.py:54
  50.1 1.6 collective-permute-start.10
  52.4 5.1 %collective-permute-done.8 = bf16[128,128]{1,0:T(8,128)(2,1)S(1)} collective-permute-done((bf16[128,128]{1,0:T(8,128)(2,1)S(1)}, bf16[128,128]{1,0:T(8,128)(2,1)S(1)}, u32[]{:S(2)}, u32[]{:S(2)}) %collective-permute-start.8) | collective-permute-done | bytes 32800 | tf_op jit(solution)/shard_map/ppermute | solution.py:54
  57.4 4.2 %collective-permute-done.9 = bf16[128,128]{1,0:T(8,128)(2,1)S(1)} collective-permute-done((bf16[128,128]{1,0:T(8,128)(2,1)S(1)}, bf16[128,128]{1,0:T(8,128)(2,1)S(1)}, u32[]{:S(2)}, u32[]{:S(2)}) %collective-permute-start.9) | collective-permute-done | bytes 32800 | tf_op jit(solution)/shard_map/ppermute | solution.py:54
  64.5 2.2 %collective-permute-start.17 = (bf16[128,256]{0,1:T(8,128)(2,1)S(1)}, bf16[128,256]{0,1:T(8,128)(2,1)S(1)}, u32[]{:S(2)}, u32[]{:S(2)}) collective-permute-start(bf16[128,256]{0,1:T(8,128)(2,1)S(1)} %pad_maximum_fusion.2), channel_id=1, source_target_pairs={{0,4},{1,5},{2,6},{3,7},{4,0},{5,1},{6,2},{7,3},{8,12},{9,13},{10,... | collective-permute-start | bytes 196616 | tf_op jit(solution)/shard_map/ppermute | solution.py:38
  67.5 6.2 %collective-permute-done.14 = bf16[128,256]{0,1:T(8,128)(2,1)S(1)} collective-permute-done((bf16[128,256]{0,1:T(8,128)(2,1)S(1)}, bf16[128,256]{0,1:T(8,128)(2,1)S(1)}, u32[]{:S(2)}, u32[]{:S(2)}) %collective-permute-start.14) | collective-permute-done | bytes 65568 | tf_op jit(solution)/shard_map/ppermute | solution.py:38
  73.8 6.0 %collective-permute-done.15 = bf16[128,256]{0,1:T(8,128)(2,1)S(1)} collective-permute-done((bf16[128,256]{0,1:T(8,128)(2,1)S(1)}, bf16[128,256]{0,1:T(8,128)(2,1)S(1)}, u32[]{:S(2)}, u32[]{:S(2)}) %collective-permute-start.15) | collective-permute-done | bytes 65568 | tf_op jit(solution)/shard_map/ppermute | solution.py:38
  79.9 1.8 %collective-permute-done.20 = bf16[128,256]{0,1:T(8,128)(2,1)S(1)} collective-permute-done((bf16[128,256]{0,1:T(8,128)(2,1)S(1)}, bf16[128,256]{0,1:T(8,128)(2,1)S(1)}, u32[]{:S(2)}, u32[]{:S(2)}) %collective-permute-start.20) | collective-permute-done | bytes 65568 | tf_op jit(solution)/shard_map/ppermute | solution.py:38
  83.4 2.0 %select_reduce_fusion = (f32[1024]{0:T(1024)S(1)}, f32[1024]{0:T(1024)S(1)}, f32[1024]{0:T(1024)S(1)}, f32[1024]{0:T(1024)S(1)}) fusion(f32[1024,1024]{0,1:T(8,128)S(1)} %get-tuple-element.84, s32[1024]{0:T(1024)S(1)} %fusion.33, f32[1024]{0:T(1024)S(1)} %get-tuple-element.83, f32[1024,1024]{0,1:T(8,128)S(1)} %get-tuple-element.82, f32[1024]{0:T(1024)S(1)} %get-tuple-element.81), kind=kLoop, calls=%fused_computation.4 | loop fusion | flops 9433088 | bytes 8417280 | tf_op jit(solution)/shard_map/reduce_sum | solution.py:90
  89.6 3.0 %collective-permute-start.22 = (f32[8,6,128]{2,0,1:T(8,128)S(1)}, f32[8,6,128]{2,0,1:T(8,128)S(1)}, u32[]{:S(2)}, u32[]{:S(2)}) collective-permute-start(f32[8,6,128]{2,0,1:T(8,128)S(1)} %get-tuple-element.32), channel_id=1, source_target_pairs={{0,2},{1,3},{2,4},{3,5},{4,6},{5,7},{6,0},{7,1},{8,10},{9,11},{10,... | collective-permute-start | bytes 73736 | tf_op jit(solution)/shard_map/ppermute | solution.py:38
  93.5 1.9 %collective-permute-done.22 = f32[8,6,128]{2,0,1:T(8,128)S(1)} collective-permute-done((f32[8,6,128]{2,0,1:T(8,128)S(1)}, f32[8,6,128]{2,0,1:T(8,128)S(1)}, u32[]{:S(2)}, u32[]{:S(2)}) %collective-permute-start.22) | collective-permute-done | bytes 24608 | tf_op jit(solution)/shard_map/ppermute | solution.py:38
  97.2 1.6 collective-permute-start.29
  105.8 1.8 %bitcast_divide_fusion = (f32[22]{0:T(128)S(1)}, f32[22]{0:T(128)}) fusion(f32[2,22]{1,0:T(2,128)S(1)} %fusion.38, f32[]{:T(128)} %fusion.58, f32[22]{0:T(128)S(1)} %get-tuple-element.28, f32[]{:T(128)} %get-tuple-element.27), kind=kLoop, calls=%fused_computation.192 | loop fusion | flops 132 | bytes 360 | tf_op jit(solution)/shard_map/div | solution.py:242
  108.3 3.5 %fusion = f32[1024,128]{0,1:T(8,128)S(1)} fusion(bf16[1024,128]{1,0:T(8,128)(2,1)S(1)} %copy-done, f32[1024,1024]{0,1:T(8,128)} %copy-done.2, f32[1024]{0:T(1024)S(1)} %select_bitcast_fusion, f32[1024]{0:T(1024)S(1)} %broadcast_bitcast_fusion, s32[1024]{0:T(1024)S(1)} %fusion.33), kind=kOutput, calls=%fused_computation.9 | convolution fusion | flops 274726912 | bytes 4993024 | tf_op jit(solution)/shard_map/dot_general | solution.py:112
  112.0 3.5 %collective-permute-start.37 = (f32[128,128]{0,1:T(8,128)S(1)}, f32[128,128]{0,1:T(8,128)S(1)}, u32[]{:S(2)}, u32[]{:S(2)}) collective-permute-start(f32[128,128]{0,1:T(8,128)S(1)} %get-tuple-element.46), channel_id=1, source_target_pairs={{0,7},{1,0},{2,1},{3,2},{4,3},{5,4},{6,5},{7,6},{8,15},{9,8},{10,9... | collective-permute-start | bytes 196616 | tf_op jit(solution)/shard_map/ppermute | solution.py:54
  116.0 2.2 %collective-permute-start.34 = (f32[128,128]{0,1:T(8,128)S(1)}, f32[128,128]{0,1:T(8,128)S(1)}, u32[]{:S(2)}, u32[]{:S(2)}) collective-permute-start(f32[128,128]{0,1:T(8,128)S(1)} %get-tuple-element.49), channel_id=1, source_target_pairs={{0,4},{1,5},{2,6},{3,7},{4,0},{5,1},{6,2},{7,3},{8,12},{9,13},{10,... | collective-permute-start | bytes 196616 | tf_op jit(solution)/shard_map/ppermute | solution.py:54
  120.8 6.4 %collective-permute-done.34 = f32[128,128]{0,1:T(8,128)S(1)} collective-permute-done((f32[128,128]{0,1:T(8,128)S(1)}, f32[128,128]{0,1:T(8,128)S(1)}, u32[]{:S(2)}, u32[]{:S(2)}) %collective-permute-start.34) | collective-permute-done | bytes 65568 | tf_op jit(solution)/shard_map/ppermute | solution.py:54
  129.5 3.6 %collective-permute-start.44 = (bf16[64,384]{0,1:T(8,128)(2,1)S(1)}, bf16[64,384]{0,1:T(8,128)(2,1)S(1)}, u32[]{:S(2)}, u32[]{:S(2)}) collective-permute-start(bf16[64,384]{0,1:T(8,128)(2,1)S(1)} %get-tuple-element.52), channel_id=1, source_target_pairs={{0,7},{1,0},{2,1},{3,2},{4,3},{5,4},{6,5},{7,6},{8,15},{9,8},{10,9... | collective-permute-start | bytes 147464 | tf_op jit(solution)/shard_map/ppermute | solution.py:54
  133.1 2.7 %collective-permute-start.41 = (bf16[64,384]{0,1:T(8,128)(2,1)S(1)}, bf16[64,384]{0,1:T(8,128)(2,1)S(1)}, u32[]{:S(2)}, u32[]{:S(2)}) collective-permute-start(bf16[64,384]{0,1:T(8,128)(2,1)S(1)} %get-tuple-element.55), channel_id=1, source_target_pairs={{0,4},{1,5},{2,6},{3,7},{4,0},{5,1},{6,2},{7,3},{8,12},{9,13},{10,... | collective-permute-start | bytes 147464 | tf_op jit(solution)/shard_map/ppermute | solution.py:54
  136.0 8.5 %collective-permute-done.39 = bf16[64,384]{0,1:T(8,128)(2,1)S(1)} collective-permute-done((bf16[64,384]{0,1:T(8,128)(2,1)S(1)}, bf16[64,384]{0,1:T(8,128)(2,1)S(1)}, u32[]{:S(2)}, u32[]{:S(2)}) %collective-permute-start.39) | collective-permute-done | bytes 49184 | tf_op jit(solution)/shard_map/ppermute | solution.py:54
  144.5 1.9 %collective-permute-start.40 = (bf16[64,384]{0,1:T(8,128)(2,1)S(1)}, bf16[64,384]{0,1:T(8,128)(2,1)S(1)}, u32[]{:S(2)}, u32[]{:S(2)}) collective-permute-start(bf16[64,384]{0,1:T(8,128)(2,1)S(1)} %get-tuple-element.56), channel_id=1, source_target_pairs={{0,3},{1,4},{2,5},{3,6},{4,7},{5,0},{6,1},{7,2},{8,11},{9,12},{10,... | collective-permute-start | bytes 147464 | tf_op jit(solution)/shard_map/ppermute | solution.py:54
  146.4 4.9 %collective-permute-done.40 = bf16[64,384]{0,1:T(8,128)(2,1)S(1)} collective-permute-done((bf16[64,384]{0,1:T(8,128)(2,1)S(1)}, bf16[64,384]{0,1:T(8,128)(2,1)S(1)}, u32[]{:S(2)}, u32[]{:S(2)}) %collective-permute-start.40) | collective-permute-done | bytes 49184 | tf_op jit(solution)/shard_map/ppermute | solution.py:54
  151.7 2.4 %collective-permute-start.47 = (f32[64,384]{0,1:T(8,128)S(1)}, f32[64,384]{0,1:T(8,128)S(1)}, u32[]{:S(2)}, u32[]{:S(2)}) collective-permute-start(f32[64,384]{0,1:T(8,128)S(1)} %convert_reduce_fusion), channel_id=1, source_target_pairs={{0,24},{8,0},{16,8},{24,16},{1,25},{9,1},{17,9},{25,17},{2,26},{10... | collective-permute-start | bytes 294920 | tf_op jit(solution)/shard_map/ppermute | solution.py:38
  154.7 4.8 %collective-permute-done.47 = f32[64,384]{0,1:T(8,128)S(1)} collective-permute-done((f32[64,384]{0,1:T(8,128)S(1)}, f32[64,384]{0,1:T(8,128)S(1)}, u32[]{:S(2)}, u32[]{:S(2)}) %collective-permute-start.47) | collective-permute-done | bytes 98336 | tf_op jit(solution)/shard_map/ppermute | solution.py:38
  159.5 5.9 %collective-permute-done.46 = f32[64,384]{0,1:T(8,128)S(1)} collective-permute-done((f32[64,384]{0,1:T(8,128)S(1)}, f32[64,384]{0,1:T(8,128)S(1)}, u32[]{:S(2)}, u32[]{:S(2)}) %collective-permute-start.46) | collective-permute-done | bytes 98336 | tf_op jit(solution)/shard_map/ppermute | solution.py:38
  (220 shorter events, 37.4 us)
Async XLA Ops:
  9.9 8.0 %collective-permute-start.6 = (bf16[49729]{0:T(1024)(128)(2,1)S(1)}, bf16[49729]{0:T(1024)(128)(2,1)S(1)}, u32[]{:S(2)}, u32[]{:S(2)}) collective-permute-start(bf16[49729]{0:T(1024)(128)(2,1)S(1)} %concatenate.49), channel_id=1, source_target_pairs={{0,7},{1,0},{2,1},{3,2},{4,3},{5,4},{6,5},{7,6},{8,15},{9,8},{10,9... | collective-permute-start | bytes 298382 | tf_op jit(solution)/shard_map/ppermute | solution.py:38
  15.1 6.9 %collective-permute-start.4 = (bf16[49729]{0:T(1024)(128)(2,1)S(1)}, bf16[49729]{0:T(1024)(128)(2,1)S(1)}, u32[]{:S(2)}, u32[]{:S(2)}) collective-permute-start(bf16[49729]{0:T(1024)(128)(2,1)S(1)} %concatenate.49), channel_id=1, source_target_pairs={{0,5},{1,6},{2,7},{3,0},{4,1},{5,2},{6,3},{7,4},{8,13},{9,14},{10,... | collective-permute-start | bytes 298382 | tf_op jit(solution)/shard_map/ppermute | solution.py:38
  15.1 17.0 %collective-permute-start.3 = (bf16[49729]{0:T(1024)(128)(2,1)S(1)}, bf16[49729]{0:T(1024)(128)(2,1)S(1)}, u32[]{:S(2)}, u32[]{:S(2)}) collective-permute-start(bf16[49729]{0:T(1024)(128)(2,1)S(1)} %concatenate.49), channel_id=1, source_target_pairs={{0,4},{1,5},{2,6},{3,7},{4,0},{5,1},{6,2},{7,3},{8,12},{9,13},{10,... | collective-permute-start | bytes 298382 | tf_op jit(solution)/shard_map/ppermute | solution.py:38
  17.8 15.1 %collective-permute-start.2 = (bf16[49729]{0:T(1024)(128)(2,1)S(1)}, bf16[49729]{0:T(1024)(128)(2,1)S(1)}, u32[]{:S(2)}, u32[]{:S(2)}) collective-permute-start(bf16[49729]{0:T(1024)(128)(2,1)S(1)} %concatenate.49), channel_id=1, source_target_pairs={{0,3},{1,4},{2,5},{3,6},{4,7},{5,0},{6,1},{7,2},{8,11},{9,12},{10,... | collective-permute-start | bytes 298382 | tf_op jit(solution)/shard_map/ppermute | solution.py:38
  17.9 15.1 %collective-permute-start.1 = (bf16[49729]{0:T(1024)(128)(2,1)S(1)}, bf16[49729]{0:T(1024)(128)(2,1)S(1)}, u32[]{:S(2)}, u32[]{:S(2)}) collective-permute-start(bf16[49729]{0:T(1024)(128)(2,1)S(1)} %concatenate.49), channel_id=1, source_target_pairs={{0,2},{1,3},{2,4},{3,5},{4,6},{5,7},{6,0},{7,1},{8,10},{9,11},{10,... | collective-permute-start | bytes 298382 | tf_op jit(solution)/shard_map/ppermute | solution.py:38
  21.1 12.0 %collective-permute-start = (bf16[49729]{0:T(1024)(128)(2,1)S(1)}, bf16[49729]{0:T(1024)(128)(2,1)S(1)}, u32[]{:S(2)}, u32[]{:S(2)}) collective-permute-start(bf16[49729]{0:T(1024)(128)(2,1)S(1)} %concatenate.49), channel_id=1, source_target_pairs={{0,1},{1,2},{2,3},{3,4},{4,5},{5,6},{6,7},{7,0},{8,9},{9,10},{10,1... | collective-permute-start | bytes 298382 | tf_op jit(solution)/shard_map/ppermute | solution.py:38
  44.5 7.2 %collective-permute-start.7 = (bf16[128,128]{1,0:T(8,128)(2,1)S(1)}, bf16[128,128]{1,0:T(8,128)(2,1)S(1)}, u32[]{:S(2)}, u32[]{:S(2)}) collective-permute-start(bf16[128,128]{1,0:T(8,128)(2,1)S(1)} %get-tuple-element.65), channel_id=1, source_target_pairs={{0,1},{1,2},{2,3},{3,4},{4,5},{5,6},{6,7},{7,0},{8,9},{9,10},{10,1... | collective-permute-start | bytes 98312 | tf_op jit(solution)/shard_map/ppermute | solution.py:54
  45.4 16.3 %collective-permute-start.13 = (bf16[128,128]{1,0:T(8,128)(2,1)S(1)}, bf16[128,128]{1,0:T(8,128)(2,1)S(1)}, u32[]{:S(2)}, u32[]{:S(2)}) collective-permute-start(bf16[128,128]{1,0:T(8,128)(2,1)S(1)} %get-tuple-element.59), channel_id=1, source_target_pairs={{0,7},{1,0},{2,1},{3,2},{4,3},{5,4},{6,5},{7,6},{8,15},{9,8},{10,9... | collective-permute-start | bytes 98312 | tf_op jit(solution)/shard_map/ppermute | solution.py:54
  49.0 12.7 %collective-permute-start.12 = (bf16[128,128]{1,0:T(8,128)(2,1)S(1)}, bf16[128,128]{1,0:T(8,128)(2,1)S(1)}, u32[]{:S(2)}, u32[]{:S(2)}) collective-permute-start(bf16[128,128]{1,0:T(8,128)(2,1)S(1)} %get-tuple-element.60), channel_id=1, source_target_pairs={{0,6},{1,7},{2,0},{3,1},{4,2},{5,3},{6,4},{7,5},{8,14},{9,15},{10,... | collective-permute-start | bytes 98312 | tf_op jit(solution)/shard_map/ppermute | solution.py:54
  49.0 12.7 %collective-permute-start.11 = (bf16[128,128]{1,0:T(8,128)(2,1)S(1)}, bf16[128,128]{1,0:T(8,128)(2,1)S(1)}, u32[]{:S(2)}, u32[]{:S(2)}) collective-permute-start(bf16[128,128]{1,0:T(8,128)(2,1)S(1)} %get-tuple-element.61), channel_id=1, source_target_pairs={{0,5},{1,6},{2,7},{3,0},{4,1},{5,2},{6,3},{7,4},{8,13},{9,14},{10,... | collective-permute-start | bytes 98312 | tf_op jit(solution)/shard_map/ppermute | solution.py:54
  50.1 11.6 %collective-permute-start.10 = (bf16[128,128]{1,0:T(8,128)(2,1)S(1)}, bf16[128,128]{1,0:T(8,128)(2,1)S(1)}, u32[]{:S(2)}, u32[]{:S(2)}) collective-permute-start(bf16[128,128]{1,0:T(8,128)(2,1)S(1)} %get-tuple-element.62), channel_id=1, source_target_pairs={{0,4},{1,5},{2,6},{3,7},{4,0},{5,1},{6,2},{7,3},{8,12},{9,13},{10,... | collective-permute-start | bytes 98312 | tf_op jit(solution)/shard_map/ppermute | solution.py:54
  63.6 16.3 %collective-permute-start.19 = (bf16[128,256]{0,1:T(8,128)(2,1)S(1)}, bf16[128,256]{0,1:T(8,128)(2,1)S(1)}, u32[]{:S(2)}, u32[]{:S(2)}) collective-permute-start(bf16[128,256]{0,1:T(8,128)(2,1)S(1)} %pad_maximum_fusion.2), channel_id=1, source_target_pairs={{0,6},{1,7},{2,0},{3,1},{4,2},{5,3},{6,4},{7,5},{8,14},{9,15},{10,... | collective-permute-start | bytes 196616 | tf_op jit(solution)/shard_map/ppermute | solution.py:38
  64.5 15.4 %collective-permute-start.18 = (bf16[128,256]{0,1:T(8,128)(2,1)S(1)}, bf16[128,256]{0,1:T(8,128)(2,1)S(1)}, u32[]{:S(2)}, u32[]{:S(2)}) collective-permute-start(bf16[128,256]{0,1:T(8,128)(2,1)S(1)} %pad_maximum_fusion.2), channel_id=1, source_target_pairs={{0,5},{1,6},{2,7},{3,0},{4,1},{5,2},{6,3},{7,4},{8,13},{9,14},{10,... | collective-permute-start | bytes 196616 | tf_op jit(solution)/shard_map/ppermute | solution.py:38
  64.5 15.4 %collective-permute-start.17 = (bf16[128,256]{0,1:T(8,128)(2,1)S(1)}, bf16[128,256]{0,1:T(8,128)(2,1)S(1)}, u32[]{:S(2)}, u32[]{:S(2)}) collective-permute-start(bf16[128,256]{0,1:T(8,128)(2,1)S(1)} %pad_maximum_fusion.2), channel_id=1, source_target_pairs={{0,4},{1,5},{2,6},{3,7},{4,0},{5,1},{6,2},{7,3},{8,12},{9,13},{10,... | collective-permute-start | bytes 196616 | tf_op jit(solution)/shard_map/ppermute | solution.py:38
  66.6 13.2 %collective-permute-start.16 = (bf16[128,256]{0,1:T(8,128)(2,1)S(1)}, bf16[128,256]{0,1:T(8,128)(2,1)S(1)}, u32[]{:S(2)}, u32[]{:S(2)}) collective-permute-start(bf16[128,256]{0,1:T(8,128)(2,1)S(1)} %pad_maximum_fusion.2), channel_id=1, source_target_pairs={{0,3},{1,4},{2,5},{3,6},{4,7},{5,0},{6,1},{7,2},{8,11},{9,12},{10,... | collective-permute-start | bytes 196616 | tf_op jit(solution)/shard_map/ppermute | solution.py:38
  66.6 7.1 %collective-permute-start.14 = (bf16[128,256]{0,1:T(8,128)(2,1)S(1)}, bf16[128,256]{0,1:T(8,128)(2,1)S(1)}, u32[]{:S(2)}, u32[]{:S(2)}) collective-permute-start(bf16[128,256]{0,1:T(8,128)(2,1)S(1)} %pad_maximum_fusion.2), channel_id=1, source_target_pairs={{0,1},{1,2},{2,3},{3,4},{4,5},{5,6},{6,7},{7,0},{8,9},{9,10},{10,1... | collective-permute-start | bytes 196616 | tf_op jit(solution)/shard_map/ppermute | solution.py:38
  85.6 7.0 %collective-permute-start.21 = (f32[8,6,128]{2,0,1:T(8,128)S(1)}, f32[8,6,128]{2,0,1:T(8,128)S(1)}, u32[]{:S(2)}, u32[]{:S(2)}) collective-permute-start(f32[8,6,128]{2,0,1:T(8,128)S(1)} %get-tuple-element.32), channel_id=1, source_target_pairs={{0,1},{1,2},{2,3},{3,4},{4,5},{5,6},{6,7},{7,0},{8,9},{9,10},{10,1... | collective-permute-start | bytes 73736 | tf_op jit(solution)/shard_map/ppermute | solution.py:38
  85.7 9.7 %collective-permute-start.25 = (f32[8,6,128]{2,0,1:T(8,128)S(1)}, f32[8,6,128]{2,0,1:T(8,128)S(1)}, u32[]{:S(2)}, u32[]{:S(2)}) collective-permute-start(f32[8,6,128]{2,0,1:T(8,128)S(1)} %get-tuple-element.32), channel_id=1, source_target_pairs={{0,5},{1,6},{2,7},{3,0},{4,1},{5,2},{6,3},{7,4},{8,13},{9,14},{10,... | collective-permute-start | bytes 73736 | tf_op jit(solution)/shard_map/ppermute | solution.py:38
  87.1 8.3 %collective-permute-start.24 = (f32[8,6,128]{2,0,1:T(8,128)S(1)}, f32[8,6,128]{2,0,1:T(8,128)S(1)}, u32[]{:S(2)}, u32[]{:S(2)}) collective-permute-start(f32[8,6,128]{2,0,1:T(8,128)S(1)} %get-tuple-element.32), channel_id=1, source_target_pairs={{0,4},{1,5},{2,6},{3,7},{4,0},{5,1},{6,2},{7,3},{8,12},{9,13},{10,... | collective-permute-start | bytes 73736 | tf_op jit(solution)/shard_map/ppermute | solution.py:38
  88.2 7.1 %collective-permute-start.23 = (f32[8,6,128]{2,0,1:T(8,128)S(1)}, f32[8,6,128]{2,0,1:T(8,128)S(1)}, u32[]{:S(2)}, u32[]{:S(2)}) collective-permute-start(f32[8,6,128]{2,0,1:T(8,128)S(1)} %get-tuple-element.32), channel_id=1, source_target_pairs={{0,3},{1,4},{2,5},{3,6},{4,7},{5,0},{6,1},{7,2},{8,11},{9,12},{10,... | collective-permute-start | bytes 73736 | tf_op jit(solution)/shard_map/ppermute | solution.py:38
  116.0 11.2 %collective-permute-start.34 = (f32[128,128]{0,1:T(8,128)S(1)}, f32[128,128]{0,1:T(8,128)S(1)}, u32[]{:S(2)}, u32[]{:S(2)}) collective-permute-start(f32[128,128]{0,1:T(8,128)S(1)} %get-tuple-element.49), channel_id=1, source_target_pairs={{0,4},{1,5},{2,6},{3,7},{4,0},{5,1},{6,2},{7,3},{8,12},{9,13},{10,... | collective-permute-start | bytes 196616 | tf_op jit(solution)/shard_map/ppermute | solution.py:54
  118.2 10.0 %collective-permute-start.33 = (f32[128,128]{0,1:T(8,128)S(1)}, f32[128,128]{0,1:T(8,128)S(1)}, u32[]{:S(2)}, u32[]{:S(2)}) collective-permute-start(f32[128,128]{0,1:T(8,128)S(1)} %get-tuple-element.50), channel_id=1, source_target_pairs={{0,3},{1,4},{2,5},{3,6},{4,7},{5,0},{6,1},{7,2},{8,11},{9,12},{10,... | collective-permute-start | bytes 196616 | tf_op jit(solution)/shard_map/ppermute | solution.py:54
  118.2 10.0 %collective-permute-start.32 = (f32[128,128]{0,1:T(8,128)S(1)}, f32[128,128]{0,1:T(8,128)S(1)}, u32[]{:S(2)}, u32[]{:S(2)}) collective-permute-start(f32[128,128]{0,1:T(8,128)S(1)} %get-tuple-element.51), channel_id=1, source_target_pairs={{0,2},{1,3},{2,4},{3,5},{4,6},{5,7},{6,0},{7,1},{8,10},{9,11},{10,... | collective-permute-start | bytes 196616 | tf_op jit(solution)/shard_map/ppermute | solution.py:54
  129.5 22.0 %collective-permute-start.44 = (bf16[64,384]{0,1:T(8,128)(2,1)S(1)}, bf16[64,384]{0,1:T(8,128)(2,1)S(1)}, u32[]{:S(2)}, u32[]{:S(2)}) collective-permute-start(bf16[64,384]{0,1:T(8,128)(2,1)S(1)} %get-tuple-element.52), channel_id=1, source_target_pairs={{0,7},{1,0},{2,1},{3,2},{4,3},{5,4},{6,5},{7,6},{8,15},{9,8},{10,9... | collective-permute-start | bytes 147464 | tf_op jit(solution)/shard_map/ppermute | solution.py:54
  133.1 18.4 %collective-permute-start.43 = (bf16[64,384]{0,1:T(8,128)(2,1)S(1)}, bf16[64,384]{0,1:T(8,128)(2,1)S(1)}, u32[]{:S(2)}, u32[]{:S(2)}) collective-permute-start(bf16[64,384]{0,1:T(8,128)(2,1)S(1)} %get-tuple-element.53), channel_id=1, source_target_pairs={{0,6},{1,7},{2,0},{3,1},{4,2},{5,3},{6,4},{7,5},{8,14},{9,15},{10,... | collective-permute-start | bytes 147464 | tf_op jit(solution)/shard_map/ppermute | solution.py:54
  133.1 18.3 %collective-permute-start.42 = (bf16[64,384]{0,1:T(8,128)(2,1)S(1)}, bf16[64,384]{0,1:T(8,128)(2,1)S(1)}, u32[]{:S(2)}, u32[]{:S(2)}) collective-permute-start(bf16[64,384]{0,1:T(8,128)(2,1)S(1)} %get-tuple-element.54), channel_id=1, source_target_pairs={{0,5},{1,6},{2,7},{3,0},{4,1},{5,2},{6,3},{7,4},{8,13},{9,14},{10,... | collective-permute-start | bytes 147464 | tf_op jit(solution)/shard_map/ppermute | solution.py:54
  133.1 18.3 %collective-permute-start.41 = (bf16[64,384]{0,1:T(8,128)(2,1)S(1)}, bf16[64,384]{0,1:T(8,128)(2,1)S(1)}, u32[]{:S(2)}, u32[]{:S(2)}) collective-permute-start(bf16[64,384]{0,1:T(8,128)(2,1)S(1)} %get-tuple-element.55), channel_id=1, source_target_pairs={{0,4},{1,5},{2,6},{3,7},{4,0},{5,1},{6,2},{7,3},{8,12},{9,13},{10,... | collective-permute-start | bytes 147464 | tf_op jit(solution)/shard_map/ppermute | solution.py:54
  136.0 8.5 %collective-permute-start.39 = (bf16[64,384]{0,1:T(8,128)(2,1)S(1)}, bf16[64,384]{0,1:T(8,128)(2,1)S(1)}, u32[]{:S(2)}, u32[]{:S(2)}) collective-permute-start(bf16[64,384]{0,1:T(8,128)(2,1)S(1)} %get-tuple-element.57), channel_id=1, source_target_pairs={{0,2},{1,3},{2,4},{3,5},{4,6},{5,7},{6,0},{7,1},{8,10},{9,11},{10,... | collective-permute-start | bytes 147464 | tf_op jit(solution)/shard_map/ppermute | solution.py:54
  144.5 6.9 %collective-permute-start.40 = (bf16[64,384]{0,1:T(8,128)(2,1)S(1)}, bf16[64,384]{0,1:T(8,128)(2,1)S(1)}, u32[]{:S(2)}, u32[]{:S(2)}) collective-permute-start(bf16[64,384]{0,1:T(8,128)(2,1)S(1)} %get-tuple-element.56), channel_id=1, source_target_pairs={{0,3},{1,4},{2,5},{3,6},{4,7},{5,0},{6,1},{7,2},{8,11},{9,12},{10,... | collective-permute-start | bytes 147464 | tf_op jit(solution)/shard_map/ppermute | solution.py:54
  151.7 7.8 %collective-permute-start.47 = (f32[64,384]{0,1:T(8,128)S(1)}, f32[64,384]{0,1:T(8,128)S(1)}, u32[]{:S(2)}, u32[]{:S(2)}) collective-permute-start(f32[64,384]{0,1:T(8,128)S(1)} %convert_reduce_fusion), channel_id=1, source_target_pairs={{0,24},{8,0},{16,8},{24,16},{1,25},{9,1},{17,9},{25,17},{2,26},{10... | collective-permute-start | bytes 294920 | tf_op jit(solution)/shard_map/ppermute | solution.py:38
  154.1 11.4 %collective-permute-start.46 = (f32[64,384]{0,1:T(8,128)S(1)}, f32[64,384]{0,1:T(8,128)S(1)}, u32[]{:S(2)}, u32[]{:S(2)}) collective-permute-start(f32[64,384]{0,1:T(8,128)S(1)} %convert_reduce_fusion), channel_id=1, source_target_pairs={{0,16},{8,24},{16,0},{24,8},{1,17},{9,25},{17,1},{25,9},{2,18},{10... | collective-permute-start | bytes 294920 | tf_op jit(solution)/shard_map/ppermute | solution.py:38
  154.6 10.9 %collective-permute-start.45 = (f32[64,384]{0,1:T(8,128)S(1)}, f32[64,384]{0,1:T(8,128)S(1)}, u32[]{:S(2)}, u32[]{:S(2)}) collective-permute-start(f32[64,384]{0,1:T(8,128)S(1)} %convert_reduce_fusion), channel_id=1, source_target_pairs={{0,8},{8,16},{16,24},{24,0},{1,9},{9,17},{17,25},{25,1},{2,10},{10... | collective-permute-start | bytes 294920 | tf_op jit(solution)/shard_map/ppermute | solution.py:38
  (20 other events, 222.6 us)

commit v2 on v1

--- a/solution.py
+++ b/solution.py
@@ -163,36 +163,34 @@
     gains = (ref_norm1, ref_norm2, prx_norm1, prx_norm2)
     packed = jnp.concatenate(
         [id_parts.reshape(-1), domain_ids.reshape(-1).astype(jnp.bfloat16)]
-        + [item.reshape(-1) for item in matrices]
         + [item.reshape(-1) for item in gains]
     )
     gathered = gather_relative(packed, "fsdp")
+    gathered_matrices = gather_relative(jnp.concatenate(matrices, axis=0), "fsdp")
     offset = 4 * per_device
     group_ids = gathered[:, :offset].astype(jnp.int32).reshape(fsdp_size, 4, per_device)
     group_tokens = (group_ids[:, 0] * ID_BASE + group_ids[:, 1]).reshape(-1)
     group_targets = (group_ids[:, 2] * ID_BASE + group_ids[:, 3]).reshape(-1)
     group_domains = gathered[:, offset : offset + rows_here].astype(jnp.int32)
     offset += rows_here
-    matrix_size = unit_rows * width
-    full_matrices = []
-    for _ in matrices:
-        full_matrices.append(
-            gathered[:, offset : offset + matrix_size].reshape(fsdp_size * unit_rows, width)
-        )
-        offset += matrix_size
     full_gains = []
     for _ in gains:
         piece = gathered[:, offset : offset + gain_here]
         full_gains.append(to_absolute(piece, "fsdp").reshape(-1))
         offset += gain_here
+    full_matrices = [
+        gathered_matrices[:, index * unit_rows : (index + 1) * unit_rows].reshape(-1, width)
+        for index in range(len(matrices))
+    ]
     ref_weights = (*full_matrices[:3], full_gains[0], full_gains[1])
     prx_weights = (*full_matrices[3:], full_gains[2], full_gains[3])
 
     token_local = group_tokens - vocab_start
-    inside = (token_local >= 0) & (token_local < vocab_here)
-    picked_rows = jnp.where(
-        inside[:, None], jnp.take(in_embed, jnp.clip(token_local, 0, vocab_here - 1), axis=0), 0
-    ).astype(jnp.bfloat16)
+    vocab_range = jnp.arange(vocab_here, dtype=jnp.int32)
+    token_hits = (token_local[:, None] == vocab_range[None, :]).astype(jnp.bfloat16)
+    picked_rows = jnp.dot(token_hits, in_embed, preferred_element_type=jnp.float32).astype(
+        jnp.bfloat16
+    )
     arrived = exchange_relative(picked_rows.reshape(fsdp_size, per_device, width), "fsdp")
     embedded = jnp.sum(arrived.astype(jnp.float32), axis=0)
 

time: 169 us -> 181 us (1.071)
  waiting for transfers between devices: 75 us -> 91 us
  local copies, waits for them, and re-layouts: 23.6 us -> 12.3 us
  starting transfers between devices: 50.6 us -> 57.2 us
    ppermute x21, waiting for transfers between devices: 31.7 us -> 45.5 us  [exchange_relative(): lax.ppermute(blocks[-shift % size], axis, shift_pairs(size, shift))]
    another operation x12 -> x13, local copies, waits for them, and re-layouts: 7.76 us -> 0.33 us  [gather_relative(): return jnp.stack(pieces)]
    ppermute x27 -> x34, starting transfers between devices: 27.8 us -> 34.8 us  [gather_relative(): lax.ppermute(value, axis, shift_pairs(size, shift))]
    concatenate x1, local copies, waits for them, and re-layouts: 7.18 us -> 2.76 us  [body(): jnp.concatenate([id_parts.reshape(-1), domain_ids.reshape(-1).astype(jnp....]
    unnamed x42 -> x52, local copies, waits for them, and re-layouts: 2.4 us -> 6.11 us
    gather x1 -> x0, local copies, waits for them, and re-layouts: 3.21 us -> none  [body(): jnp.take(in_embed, jnp.clip(token_local, 0, vocab_here - 1), axis=0)]
    ppermute x27 -> x34, waiting for transfers between devices: 43.4 us -> 45.5 us  [gather_relative(): lax.ppermute(value, axis, shift_pairs(size, shift))]
  transfers between devices with their start and end apart: 48 -> 55, of which waited for: 22 -> 26; matrix products, arithmetic and copies ran while one was open for 2% -> 5% of each run, Pallas kernels for 0% -> 0%
where the time goes in v2:
time: 181 us; the launch traced here: 180 us
  waiting for transfers between devices  91 us (50%)
  starting transfers between devices  57.2 us (32%)
  local copies, waits for them, and re-layouts  12.3 us (7%)
  other arithmetic  8.92 us (5%)
  matrix products  8.85 us (5%)
  between operations  2.17 us (1%)
    ppermute x21, waiting for transfers between devices, exchange_relative(): lax.ppermute(blocks[-shift % size], axis, shift_pairs(size, shift))  45.5 us
    ppermute x34, waiting for transfers between devices, gather_relative(): lax.ppermute(value, axis, shift_pairs(size, shift))  45.5 us
    ppermute x34, starting transfers between devices, gather_relative(): lax.ppermute(value, axis, shift_pairs(size, shift))  34.8 us
    ppermute x21, starting transfers between devices, exchange_relative(): lax.ppermute(blocks[-shift % size], axis, shift_pairs(size, shift))  22.4 us
    unnamed x52, local copies, waits for them, and re-layouts  6.11 us
  transfers between devices with their start and end apart: 55, of which 26 were waited for; matrix products, arithmetic and copies ran while one was open for 5% of the time, Pallas kernels for 0%

profile of v2, /device:TPU:0, one launch (start us, length us, event | category | flops | bytes accessed | tf_op | source)
XLA Modules:
  0.0 180.5 jit_solution(4980386546848687981)
XLA Ops:
  2.7 2.8 %concatenate.52 = bf16[577]{0:T(1024)(128)(2,1)S(1)} concatenate(bf16[512]{0:T(512)(128)(2,1)S(1)} %maximum_bitcast_fusion, bf16[1]{0:T(256)(128)(2,1)} %bitcast.1, bf16[16]{0:T(256)(128)(2,1)} %param.23, bf16[16]{0:T(256)(128)(2,1)} %param.27, bf16[16]{0:T(256)(128)(2,1)} %param.28, bf16[16]{0:T(256)(128)(2,1)} %param.32), dimensions={0} | concatenate | bytes 2308 | tf_op jit(solution)/shard_map/concatenate | solution.py:164
  5.4 4.5 %collective-permute-start.6 = (bf16[577]{0:T(1024)(128)(2,1)S(1)}, bf16[577]{0:T(1024)(128)(2,1)S(1)}, u32[]{:S(2)}, u32[]{:S(2)}) collective-permute-start(bf16[577]{0:T(1024)(128)(2,1)S(1)} %concatenate.52), channel_id=1, source_target_pairs={{0,7},{1,0},{2,1},{3,2},{4,3},{5,4},{6,5},{7,6},{8,15},{9,8},{10,9... | collective-permute-start | bytes 3470 | tf_op jit(solution)/shard_map/ppermute | solution.py:38
  10.5 2.7 %collective-permute-start.3 = (bf16[577]{0:T(1024)(128)(2,1)S(1)}, bf16[577]{0:T(1024)(128)(2,1)S(1)}, u32[]{:S(2)}, u32[]{:S(2)}) collective-permute-start(bf16[577]{0:T(1024)(128)(2,1)S(1)} %concatenate.52), channel_id=1, source_target_pairs={{0,4},{1,5},{2,6},{3,7},{4,0},{5,1},{6,2},{7,3},{8,12},{9,13},{10,... | collective-permute-start | bytes 3470 | tf_op jit(solution)/shard_map/ppermute | solution.py:38
  19.2 2.8 %collective-permute-start.20 = (bf16[384,128]{1,0:T(8,128)(2,1)S(1)}, bf16[384,128]{1,0:T(8,128)(2,1)S(1)}, u32[]{:S(2)}, u32[]{:S(2)}) collective-permute-start(bf16[384,128]{1,0:T(8,128)(2,1)S(1)} %constant_dynamic-update-slice_fusion.8), channel_id=1, source_target_pairs={{0,7},{1,0},{2,1},{3,2},{4,3},{5,4},{6,5},{7,6},{8,15},{9,8},{10,9... | collective-permute-start | bytes 294920 | tf_op jit(solution)/shard_map/ppermute | solution.py:38
  28.5 4.0 %collective-permute-done.7 = bf16[128,128]{1,0:T(8,128)(2,1)S(1)} collective-permute-done((bf16[128,128]{1,0:T(8,128)(2,1)S(1)}, bf16[128,128]{1,0:T(8,128)(2,1)S(1)}, u32[]{:S(2)}, u32[]{:S(2)}) %collective-permute-start.7) | collective-permute-done | bytes 32800 | tf_op jit(solution)/shard_map/ppermute | solution.py:54
  32.9 5.4 %collective-permute-done.8 = bf16[128,128]{1,0:T(8,128)(2,1)S(1)} collective-permute-done((bf16[128,128]{1,0:T(8,128)(2,1)S(1)}, bf16[128,128]{1,0:T(8,128)(2,1)S(1)}, u32[]{:S(2)}, u32[]{:S(2)}) %collective-permute-start.8) | collective-permute-done | bytes 32800 | tf_op jit(solution)/shard_map/ppermute | solution.py:54
  38.3 4.2 %collective-permute-done.9 = bf16[128,128]{1,0:T(8,128)(2,1)S(1)} collective-permute-done((bf16[128,128]{1,0:T(8,128)(2,1)S(1)}, bf16[128,128]{1,0:T(8,128)(2,1)S(1)}, u32[]{:S(2)}, u32[]{:S(2)}) %collective-permute-start.9) | collective-permute-done | bytes 32800 | tf_op jit(solution)/shard_map/ppermute | solution.py:54
  42.5 1.9 %collective-permute-start.10 = (bf16[128,128]{1,0:T(8,128)(2,1)S(1)}, bf16[128,128]{1,0:T(8,128)(2,1)S(1)}, u32[]{:S(2)}, u32[]{:S(2)}) collective-permute-start(bf16[128,128]{1,0:T(8,128)(2,1)S(1)} %get-tuple-element.56), channel_id=1, source_target_pairs={{0,4},{1,5},{2,6},{3,7},{4,0},{5,1},{6,2},{7,3},{8,12},{9,13},{10,... | collective-permute-start | bytes 98312 | tf_op jit(solution)/shard_map/ppermute | solution.py:54
  44.4 2.9 %collective-permute-done.10 = bf16[128,128]{1,0:T(8,128)(2,1)S(1)} collective-permute-done((bf16[128,128]{1,0:T(8,128)(2,1)S(1)}, bf16[128,128]{1,0:T(8,128)(2,1)S(1)}, u32[]{:S(2)}, u32[]{:S(2)}) %collective-permute-start.10) | collective-permute-done | bytes 32800 | tf_op jit(solution)/shard_map/ppermute | solution.py:54
  47.3 3.3 %collective-permute-done.11 = bf16[128,128]{1,0:T(8,128)(2,1)S(1)} collective-permute-done((bf16[128,128]{1,0:T(8,128)(2,1)S(1)}, bf16[128,128]{1,0:T(8,128)(2,1)S(1)}, u32[]{:S(2)}, u32[]{:S(2)}) %collective-permute-start.11) | collective-permute-done | bytes 32800 | tf_op jit(solution)/shard_map/ppermute | solution.py:54
  50.6 3.2 %collective-permute-start.12 = (bf16[128,128]{1,0:T(8,128)(2,1)S(1)}, bf16[128,128]{1,0:T(8,128)(2,1)S(1)}, u32[]{:S(2)}, u32[]{:S(2)}) collective-permute-start(bf16[128,128]{1,0:T(8,128)(2,1)S(1)} %get-tuple-element.54), channel_id=1, source_target_pairs={{0,6},{1,7},{2,0},{3,1},{4,2},{5,3},{6,4},{7,5},{8,14},{9,15},{10,... | collective-permute-start | bytes 98312 | tf_op jit(solution)/shard_map/ppermute | solution.py:54
  58.0 5.5 %collective-permute-done.14 = bf16[384,128]{1,0:T(8,128)(2,1)S(1)} collective-permute-done((bf16[384,128]{1,0:T(8,128)(2,1)S(1)}, bf16[384,128]{1,0:T(8,128)(2,1)S(1)}, u32[]{:S(2)}, u32[]{:S(2)}) %collective-permute-start.14) | collective-permute-done | bytes 98336 | tf_op jit(solution)/shard_map/ppermute | solution.py:38
  63.5 6.4 %collective-permute-done.15 = bf16[384,128]{1,0:T(8,128)(2,1)S(1)} collective-permute-done((bf16[384,128]{1,0:T(8,128)(2,1)S(1)}, bf16[384,128]{1,0:T(8,128)(2,1)S(1)}, u32[]{:S(2)}, u32[]{:S(2)}) %collective-permute-start.15) | collective-permute-done | bytes 98336 | tf_op jit(solution)/shard_map/ppermute | solution.py:38
  69.9 4.9 %collective-permute-done.16 = bf16[384,128]{1,0:T(8,128)(2,1)S(1)} collective-permute-done((bf16[384,128]{1,0:T(8,128)(2,1)S(1)}, bf16[384,128]{1,0:T(8,128)(2,1)S(1)}, u32[]{:S(2)}, u32[]{:S(2)}) %collective-permute-start.16) | collective-permute-done | bytes 98336 | tf_op jit(solution)/shard_map/ppermute | solution.py:38
  80.4 5.2 %collective-permute-done.21 = bf16[128,256]{0,1:T(8,128)(2,1)S(1)} collective-permute-done((bf16[128,256]{0,1:T(8,128)(2,1)S(1)}, bf16[128,256]{0,1:T(8,128)(2,1)S(1)}, u32[]{:S(2)}, u32[]{:S(2)}) %collective-permute-start.21) | collective-permute-done | bytes 65568 | tf_op jit(solution)/shard_map/ppermute | solution.py:38
  86.0 5.6 %collective-permute-done.22 = bf16[128,256]{0,1:T(8,128)(2,1)S(1)} collective-permute-done((bf16[128,256]{0,1:T(8,128)(2,1)S(1)}, bf16[128,256]{0,1:T(8,128)(2,1)S(1)}, u32[]{:S(2)}, u32[]{:S(2)}) %collective-permute-start.22) | collective-permute-done | bytes 65568 | tf_op jit(solution)/shard_map/ppermute | solution.py:38
  95.3 2.0 %select_reduce_fusion = (f32[1024]{0:T(1024)S(1)}, f32[1024]{0:T(1024)S(1)}, f32[1024]{0:T(1024)S(1)}, f32[1024]{0:T(1024)S(1)}) fusion(f32[1024,1024]{0,1:T(8,128)S(1)} %get-tuple-element.84, s32[1024]{0:T(1024)S(1)} %get-tuple-element.63, f32[1024]{0:T(1024)S(1)} %get-tuple-element.83, f32[1024,1024]{0,1:T(8,128)S(1)} %get-tuple-element.82, ...), kind=kLoop, calls=%fused_computation.3 | loop fusion | flops 9433088 | bytes 8417280 | tf_op jit(solution)/shard_map/reduce_sum | solution.py:90
  101.6 2.8 %collective-permute-start.29 = (f32[8,6,128]{2,0,1:T(8,128)S(1)}, f32[8,6,128]{2,0,1:T(8,128)S(1)}, u32[]{:S(2)}, u32[]{:S(2)}) collective-permute-start(f32[8,6,128]{2,0,1:T(8,128)S(1)} %get-tuple-element.32), channel_id=1, source_target_pairs={{0,2},{1,3},{2,4},{3,5},{4,6},{5,7},{6,0},{7,1},{8,10},{9,11},{10,... | collective-permute-start | bytes 73736 | tf_op jit(solution)/shard_map/ppermute | solution.py:38
  105.5 2.3 %collective-permute-done.29 = f32[8,6,128]{2,0,1:T(8,128)S(1)} collective-permute-done((f32[8,6,128]{2,0,1:T(8,128)S(1)}, f32[8,6,128]{2,0,1:T(8,128)S(1)}, u32[]{:S(2)}, u32[]{:S(2)}) %collective-permute-start.29) | collective-permute-done | bytes 24608 | tf_op jit(solution)/shard_map/ppermute | solution.py:38
  118.4 1.8 %bitcast_divide_fusion = (f32[22]{0:T(128)S(1)}, f32[22]{0:T(128)}) fusion(f32[2,22]{1,0:T(2,128)S(1)} %fusion.41, f32[]{:T(128)} %fusion.61, f32[22]{0:T(128)S(1)} %get-tuple-element.28, f32[]{:T(128)} %get-tuple-element.27), kind=kLoop, calls=%fused_computation.203 | loop fusion | flops 132 | bytes 360 | tf_op jit(solution)/shard_map/div | solution.py:240
  120.9 3.5 %fusion.2 = f32[1024,128]{0,1:T(8,128)S(1)} fusion(bf16[1024,128]{1,0:T(8,128)(2,1)S(1)} %copy-done, f32[1024,1024]{0,1:T(8,128)} %copy-done.1, f32[1024]{0:T(1024)S(1)} %select_bitcast_fusion, f32[1024]{0:T(1024)S(1)} %broadcast_bitcast_fusion, s32[1024]{0:T(1024)S(1)} %get-tuple-element.63), kind=kOutput, calls=%fused_computation.11 | convolution fusion | flops 274726912 | bytes 4993024 | tf_op jit(solution)/shard_map/dot_general | solution.py:112
  124.7 3.4 %collective-permute-start.44 = (f32[128,128]{0,1:T(8,128)S(1)}, f32[128,128]{0,1:T(8,128)S(1)}, u32[]{:S(2)}, u32[]{:S(2)}) collective-permute-start(f32[128,128]{0,1:T(8,128)S(1)} %get-tuple-element.40), channel_id=1, source_target_pairs={{0,7},{1,0},{2,1},{3,2},{4,3},{5,4},{6,5},{7,6},{8,15},{9,8},{10,9... | collective-permute-start | bytes 196616 | tf_op jit(solution)/shard_map/ppermute | solution.py:54
  128.2 2.6 %collective-permute-start.41 = (f32[128,128]{0,1:T(8,128)S(1)}, f32[128,128]{0,1:T(8,128)S(1)}, u32[]{:S(2)}, u32[]{:S(2)}) collective-permute-start(f32[128,128]{0,1:T(8,128)S(1)} %get-tuple-element.43), channel_id=1, source_target_pairs={{0,4},{1,5},{2,6},{3,7},{4,0},{5,1},{6,2},{7,3},{8,12},{9,13},{10,... | collective-permute-start | bytes 196616 | tf_op jit(solution)/shard_map/ppermute | solution.py:54
  132.8 7.1 %collective-permute-done.41 = f32[128,128]{0,1:T(8,128)S(1)} collective-permute-done((f32[128,128]{0,1:T(8,128)S(1)}, f32[128,128]{0,1:T(8,128)S(1)}, u32[]{:S(2)}, u32[]{:S(2)}) %collective-permute-start.41) | collective-permute-done | bytes 65568 | tf_op jit(solution)/shard_map/ppermute | solution.py:54
  142.1 3.6 %collective-permute-start.51 = (bf16[64,384]{0,1:T(8,128)(2,1)S(1)}, bf16[64,384]{0,1:T(8,128)(2,1)S(1)}, u32[]{:S(2)}, u32[]{:S(2)}) collective-permute-start(bf16[64,384]{0,1:T(8,128)(2,1)S(1)} %get-tuple-element.46), channel_id=1, source_target_pairs={{0,7},{1,0},{2,1},{3,2},{4,3},{5,4},{6,5},{7,6},{8,15},{9,8},{10,9... | collective-permute-start | bytes 147464 | tf_op jit(solution)/shard_map/ppermute | solution.py:54
  145.7 2.7 %collective-permute-start.48 = (bf16[64,384]{0,1:T(8,128)(2,1)S(1)}, bf16[64,384]{0,1:T(8,128)(2,1)S(1)}, u32[]{:S(2)}, u32[]{:S(2)}) collective-permute-start(bf16[64,384]{0,1:T(8,128)(2,1)S(1)} %get-tuple-element.49), channel_id=1, source_target_pairs={{0,4},{1,5},{2,6},{3,7},{4,0},{5,1},{6,2},{7,3},{8,12},{9,13},{10,... | collective-permute-start | bytes 147464 | tf_op jit(solution)/shard_map/ppermute | solution.py:54
  148.6 8.5 %collective-permute-done.46 = bf16[64,384]{0,1:T(8,128)(2,1)S(1)} collective-permute-done((bf16[64,384]{0,1:T(8,128)(2,1)S(1)}, bf16[64,384]{0,1:T(8,128)(2,1)S(1)}, u32[]{:S(2)}, u32[]{:S(2)}) %collective-permute-start.46) | collective-permute-done | bytes 49184 | tf_op jit(solution)/shard_map/ppermute | solution.py:54
  157.1 1.9 %collective-permute-start.47 = (bf16[64,384]{0,1:T(8,128)(2,1)S(1)}, bf16[64,384]{0,1:T(8,128)(2,1)S(1)}, u32[]{:S(2)}, u32[]{:S(2)}) collective-permute-start(bf16[64,384]{0,1:T(8,128)(2,1)S(1)} %get-tuple-element.50), channel_id=1, source_target_pairs={{0,3},{1,4},{2,5},{3,6},{4,7},{5,0},{6,1},{7,2},{8,11},{9,12},{10,... | collective-permute-start | bytes 147464 | tf_op jit(solution)/shard_map/ppermute | solution.py:54
  159.0 5.0 %collective-permute-done.47 = bf16[64,384]{0,1:T(8,128)(2,1)S(1)} collective-permute-done((bf16[64,384]{0,1:T(8,128)(2,1)S(1)}, bf16[64,384]{0,1:T(8,128)(2,1)S(1)}, u32[]{:S(2)}, u32[]{:S(2)}) %collective-permute-start.47) | collective-permute-done | bytes 49184 | tf_op jit(solution)/shard_map/ppermute | solution.py:54
  164.3 2.4 %collective-permute-start.54 = (f32[64,384]{0,1:T(8,128)S(1)}, f32[64,384]{0,1:T(8,128)S(1)}, u32[]{:S(2)}, u32[]{:S(2)}) collective-permute-start(f32[64,384]{0,1:T(8,128)S(1)} %convert_reduce_fusion), channel_id=1, source_target_pairs={{0,24},{8,0},{16,8},{24,16},{1,25},{9,1},{17,9},{25,17},{2,26},{10... | collective-permute-start | bytes 294920 | tf_op jit(solution)/shard_map/ppermute | solution.py:38
  167.3 4.7 %collective-permute-done.54 = f32[64,384]{0,1:T(8,128)S(1)} collective-permute-done((f32[64,384]{0,1:T(8,128)S(1)}, f32[64,384]{0,1:T(8,128)S(1)}, u32[]{:S(2)}, u32[]{:S(2)}) %collective-permute-start.54) | collective-permute-done | bytes 98336 | tf_op jit(solution)/shard_map/ppermute | solution.py:38
  172.0 6.0 %collective-permute-done.53 = f32[64,384]{0,1:T(8,128)S(1)} collective-permute-done((f32[64,384]{0,1:T(8,128)S(1)}, f32[64,384]{0,1:T(8,128)S(1)}, u32[]{:S(2)}, u32[]{:S(2)}) %collective-permute-start.53) | collective-permute-done | bytes 98336 | tf_op jit(solution)/shard_map/ppermute | solution.py:38
  (235 shorter events, 52.7 us)
Async XLA Ops:
  5.4 12.2 %collective-permute-start.6 = (bf16[577]{0:T(1024)(128)(2,1)S(1)}, bf16[577]{0:T(1024)(128)(2,1)S(1)}, u32[]{:S(2)}, u32[]{:S(2)}) collective-permute-start(bf16[577]{0:T(1024)(128)(2,1)S(1)} %concatenate.52), channel_id=1, source_target_pairs={{0,7},{1,0},{2,1},{3,2},{4,3},{5,4},{6,5},{7,6},{8,15},{9,8},{10,9... | collective-permute-start | bytes 3470 | tf_op jit(solution)/shard_map/ppermute | solution.py:38
  9.9 8.5 %collective-permute-start.5 = (bf16[577]{0:T(1024)(128)(2,1)S(1)}, bf16[577]{0:T(1024)(128)(2,1)S(1)}, u32[]{:S(2)}, u32[]{:S(2)}) collective-permute-start(bf16[577]{0:T(1024)(128)(2,1)S(1)} %concatenate.52), channel_id=1, source_target_pairs={{0,6},{1,7},{2,0},{3,1},{4,2},{5,3},{6,4},{7,5},{8,14},{9,15},{10,... | collective-permute-start | bytes 3470 | tf_op jit(solution)/shard_map/ppermute | solution.py:38
  10.5 8.7 %collective-permute-start.4 = (bf16[577]{0:T(1024)(128)(2,1)S(1)}, bf16[577]{0:T(1024)(128)(2,1)S(1)}, u32[]{:S(2)}, u32[]{:S(2)}) collective-permute-start(bf16[577]{0:T(1024)(128)(2,1)S(1)} %concatenate.52), channel_id=1, source_target_pairs={{0,5},{1,6},{2,7},{3,0},{4,1},{5,2},{6,3},{7,4},{8,13},{9,14},{10,... | collective-permute-start | bytes 3470 | tf_op jit(solution)/shard_map/ppermute | solution.py:38
  10.5 11.5 %collective-permute-start.3 = (bf16[577]{0:T(1024)(128)(2,1)S(1)}, bf16[577]{0:T(1024)(128)(2,1)S(1)}, u32[]{:S(2)}, u32[]{:S(2)}) collective-permute-start(bf16[577]{0:T(1024)(128)(2,1)S(1)} %concatenate.52), channel_id=1, source_target_pairs={{0,4},{1,5},{2,6},{3,7},{4,0},{5,1},{6,2},{7,3},{8,12},{9,13},{10,... | collective-permute-start | bytes 3470 | tf_op jit(solution)/shard_map/ppermute | solution.py:38
  13.3 10.2 %collective-permute-start.2 = (bf16[577]{0:T(1024)(128)(2,1)S(1)}, bf16[577]{0:T(1024)(128)(2,1)S(1)}, u32[]{:S(2)}, u32[]{:S(2)}) collective-permute-start(bf16[577]{0:T(1024)(128)(2,1)S(1)} %concatenate.52), channel_id=1, source_target_pairs={{0,3},{1,4},{2,5},{3,6},{4,7},{5,0},{6,1},{7,2},{8,11},{9,12},{10,... | collective-permute-start | bytes 3470 | tf_op jit(solution)/shard_map/ppermute | solution.py:38
  18.4 6.5 %collective-permute-start = (bf16[577]{0:T(1024)(128)(2,1)S(1)}, bf16[577]{0:T(1024)(128)(2,1)S(1)}, u32[]{:S(2)}, u32[]{:S(2)}) collective-permute-start(bf16[577]{0:T(1024)(128)(2,1)S(1)} %concatenate.52), channel_id=1, source_target_pairs={{0,1},{1,2},{2,3},{3,4},{4,5},{5,6},{6,7},{7,0},{8,9},{9,10},{10,1... | collective-permute-start | bytes 3470 | tf_op jit(solution)/shard_map/ppermute | solution.py:38
  19.2 55.7 %collective-permute-start.20 = (bf16[384,128]{1,0:T(8,128)(2,1)S(1)}, bf16[384,128]{1,0:T(8,128)(2,1)S(1)}, u32[]{:S(2)}, u32[]{:S(2)}) collective-permute-start(bf16[384,128]{1,0:T(8,128)(2,1)S(1)} %constant_dynamic-update-slice_fusion.8), channel_id=1, source_target_pairs={{0,7},{1,0},{2,1},{3,2},{4,3},{5,4},{6,5},{7,6},{8,15},{9,8},{10,9... | collective-permute-start | bytes 294920 | tf_op jit(solution)/shard_map/ppermute | solution.py:38
  22.0 52.9 %collective-permute-start.19 = (bf16[384,128]{1,0:T(8,128)(2,1)S(1)}, bf16[384,128]{1,0:T(8,128)(2,1)S(1)}, u32[]{:S(2)}, u32[]{:S(2)}) collective-permute-start(bf16[384,128]{1,0:T(8,128)(2,1)S(1)} %constant_dynamic-update-slice_fusion.8), channel_id=1, source_target_pairs={{0,6},{1,7},{2,0},{3,1},{4,2},{5,3},{6,4},{7,5},{8,14},{9,15},{10,... | collective-permute-start | bytes 294920 | tf_op jit(solution)/shard_map/ppermute | solution.py:38
  23.4 51.4 %collective-permute-start.18 = (bf16[384,128]{1,0:T(8,128)(2,1)S(1)}, bf16[384,128]{1,0:T(8,128)(2,1)S(1)}, u32[]{:S(2)}, u32[]{:S(2)}) collective-permute-start(bf16[384,128]{1,0:T(8,128)(2,1)S(1)} %constant_dynamic-update-slice_fusion.8), channel_id=1, source_target_pairs={{0,5},{1,6},{2,7},{3,0},{4,1},{5,2},{6,3},{7,4},{8,13},{9,14},{10,... | collective-permute-start | bytes 294920 | tf_op jit(solution)/shard_map/ppermute | solution.py:38
  23.5 51.3 %collective-permute-start.17 = (bf16[384,128]{1,0:T(8,128)(2,1)S(1)}, bf16[384,128]{1,0:T(8,128)(2,1)S(1)}, u32[]{:S(2)}, u32[]{:S(2)}) collective-permute-start(bf16[384,128]{1,0:T(8,128)(2,1)S(1)} %constant_dynamic-update-slice_fusion.8), channel_id=1, source_target_pairs={{0,4},{1,5},{2,6},{3,7},{4,0},{5,1},{6,2},{7,3},{8,12},{9,13},{10,... | collective-permute-start | bytes 294920 | tf_op jit(solution)/shard_map/ppermute | solution.py:38
  76.5 15.2 %collective-permute-start.26 = (bf16[128,256]{0,1:T(8,128)(2,1)S(1)}, bf16[128,256]{0,1:T(8,128)(2,1)S(1)}, u32[]{:S(2)}, u32[]{:S(2)}) collective-permute-start(bf16[128,256]{0,1:T(8,128)(2,1)S(1)} %pad_maximum_fusion.2), channel_id=1, source_target_pairs={{0,6},{1,7},{2,0},{3,1},{4,2},{5,3},{6,4},{7,5},{8,14},{9,15},{10,... | collective-permute-start | bytes 196616 | tf_op jit(solution)/shard_map/ppermute | solution.py:38
  77.3 14.4 %collective-permute-start.25 = (bf16[128,256]{0,1:T(8,128)(2,1)S(1)}, bf16[128,256]{0,1:T(8,128)(2,1)S(1)}, u32[]{:S(2)}, u32[]{:S(2)}) collective-permute-start(bf16[128,256]{0,1:T(8,128)(2,1)S(1)} %pad_maximum_fusion.2), channel_id=1, source_target_pairs={{0,5},{1,6},{2,7},{3,0},{4,1},{5,2},{6,3},{7,4},{8,13},{9,14},{10,... | collective-permute-start | bytes 196616 | tf_op jit(solution)/shard_map/ppermute | solution.py:38
  77.3 14.4 %collective-permute-start.24 = (bf16[128,256]{0,1:T(8,128)(2,1)S(1)}, bf16[128,256]{0,1:T(8,128)(2,1)S(1)}, u32[]{:S(2)}, u32[]{:S(2)}) collective-permute-start(bf16[128,256]{0,1:T(8,128)(2,1)S(1)} %pad_maximum_fusion.2), channel_id=1, source_target_pairs={{0,4},{1,5},{2,6},{3,7},{4,0},{5,1},{6,2},{7,3},{8,12},{9,13},{10,... | collective-permute-start | bytes 196616 | tf_op jit(solution)/shard_map/ppermute | solution.py:38
  77.7 14.0 %collective-permute-start.23 = (bf16[128,256]{0,1:T(8,128)(2,1)S(1)}, bf16[128,256]{0,1:T(8,128)(2,1)S(1)}, u32[]{:S(2)}, u32[]{:S(2)}) collective-permute-start(bf16[128,256]{0,1:T(8,128)(2,1)S(1)} %pad_maximum_fusion.2), channel_id=1, source_target_pairs={{0,3},{1,4},{2,5},{3,6},{4,7},{5,0},{6,1},{7,2},{8,11},{9,12},{10,... | collective-permute-start | bytes 196616 | tf_op jit(solution)/shard_map/ppermute | solution.py:38
  79.0 6.5 %collective-permute-start.21 = (bf16[128,256]{0,1:T(8,128)(2,1)S(1)}, bf16[128,256]{0,1:T(8,128)(2,1)S(1)}, u32[]{:S(2)}, u32[]{:S(2)}) collective-permute-start(bf16[128,256]{0,1:T(8,128)(2,1)S(1)} %pad_maximum_fusion.2), channel_id=1, source_target_pairs={{0,1},{1,2},{2,3},{3,4},{4,5},{5,6},{6,7},{7,0},{8,9},{9,10},{10,1... | collective-permute-start | bytes 196616 | tf_op jit(solution)/shard_map/ppermute | solution.py:38
  97.4 7.0 %collective-permute-start.28 = (f32[8,6,128]{2,0,1:T(8,128)S(1)}, f32[8,6,128]{2,0,1:T(8,128)S(1)}, u32[]{:S(2)}, u32[]{:S(2)}) collective-permute-start(f32[8,6,128]{2,0,1:T(8,128)S(1)} %get-tuple-element.32), channel_id=1, source_target_pairs={{0,1},{1,2},{2,3},{3,4},{4,5},{5,6},{6,7},{7,0},{8,9},{9,10},{10,1... | collective-permute-start | bytes 73736 | tf_op jit(solution)/shard_map/ppermute | solution.py:38
  98.2 9.7 %collective-permute-start.32 = (f32[8,6,128]{2,0,1:T(8,128)S(1)}, f32[8,6,128]{2,0,1:T(8,128)S(1)}, u32[]{:S(2)}, u32[]{:S(2)}) collective-permute-start(f32[8,6,128]{2,0,1:T(8,128)S(1)} %get-tuple-element.32), channel_id=1, source_target_pairs={{0,5},{1,6},{2,7},{3,0},{4,1},{5,2},{6,3},{7,4},{8,13},{9,14},{10,... | collective-permute-start | bytes 73736 | tf_op jit(solution)/shard_map/ppermute | solution.py:38
  99.8 8.1 %collective-permute-start.31 = (f32[8,6,128]{2,0,1:T(8,128)S(1)}, f32[8,6,128]{2,0,1:T(8,128)S(1)}, u32[]{:S(2)}, u32[]{:S(2)}) collective-permute-start(f32[8,6,128]{2,0,1:T(8,128)S(1)} %get-tuple-element.32), channel_id=1, source_target_pairs={{0,4},{1,5},{2,6},{3,7},{4,0},{5,1},{6,2},{7,3},{8,12},{9,13},{10,... | collective-permute-start | bytes 73736 | tf_op jit(solution)/shard_map/ppermute | solution.py:38
  100.8 7.2 %collective-permute-start.30 = (f32[8,6,128]{2,0,1:T(8,128)S(1)}, f32[8,6,128]{2,0,1:T(8,128)S(1)}, u32[]{:S(2)}, u32[]{:S(2)}) collective-permute-start(f32[8,6,128]{2,0,1:T(8,128)S(1)} %get-tuple-element.32), channel_id=1, source_target_pairs={{0,3},{1,4},{2,5},{3,6},{4,7},{5,0},{6,1},{7,2},{8,11},{9,12},{10,... | collective-permute-start | bytes 73736 | tf_op jit(solution)/shard_map/ppermute | solution.py:38
  128.2 11.7 %collective-permute-start.41 = (f32[128,128]{0,1:T(8,128)S(1)}, f32[128,128]{0,1:T(8,128)S(1)}, u32[]{:S(2)}, u32[]{:S(2)}) collective-permute-start(f32[128,128]{0,1:T(8,128)S(1)} %get-tuple-element.43), channel_id=1, source_target_pairs={{0,4},{1,5},{2,6},{3,7},{4,0},{5,1},{6,2},{7,3},{8,12},{9,13},{10,... | collective-permute-start | bytes 196616 | tf_op jit(solution)/shard_map/ppermute | solution.py:54
  130.8 10.0 %collective-permute-start.40 = (f32[128,128]{0,1:T(8,128)S(1)}, f32[128,128]{0,1:T(8,128)S(1)}, u32[]{:S(2)}, u32[]{:S(2)}) collective-permute-start(f32[128,128]{0,1:T(8,128)S(1)} %get-tuple-element.44), channel_id=1, source_target_pairs={{0,3},{1,4},{2,5},{3,6},{4,7},{5,0},{6,1},{7,2},{8,11},{9,12},{10,... | collective-permute-start | bytes 196616 | tf_op jit(solution)/shard_map/ppermute | solution.py:54
  130.8 10.0 %collective-permute-start.39 = (f32[128,128]{0,1:T(8,128)S(1)}, f32[128,128]{0,1:T(8,128)S(1)}, u32[]{:S(2)}, u32[]{:S(2)}) collective-permute-start(f32[128,128]{0,1:T(8,128)S(1)} %get-tuple-element.45), channel_id=1, source_target_pairs={{0,2},{1,3},{2,4},{3,5},{4,6},{5,7},{6,0},{7,1},{8,10},{9,11},{10,... | collective-permute-start | bytes 196616 | tf_op jit(solution)/shard_map/ppermute | solution.py:54
  142.0 6.6 %collective-permute-start.45 = (bf16[64,384]{0,1:T(8,128)(2,1)S(1)}, bf16[64,384]{0,1:T(8,128)(2,1)S(1)}, u32[]{:S(2)}, u32[]{:S(2)}) collective-permute-start(bf16[64,384]{0,1:T(8,128)(2,1)S(1)} %get-tuple-element.52), channel_id=1, source_target_pairs={{0,1},{1,2},{2,3},{3,4},{4,5},{5,6},{6,7},{7,0},{8,9},{9,10},{10,1... | collective-permute-start | bytes 147464 | tf_op jit(solution)/shard_map/ppermute | solution.py:54
  142.1 22.0 %collective-permute-start.51 = (bf16[64,384]{0,1:T(8,128)(2,1)S(1)}, bf16[64,384]{0,1:T(8,128)(2,1)S(1)}, u32[]{:S(2)}, u32[]{:S(2)}) collective-permute-start(bf16[64,384]{0,1:T(8,128)(2,1)S(1)} %get-tuple-element.46), channel_id=1, source_target_pairs={{0,7},{1,0},{2,1},{3,2},{4,3},{5,4},{6,5},{7,6},{8,15},{9,8},{10,9... | collective-permute-start | bytes 147464 | tf_op jit(solution)/shard_map/ppermute | solution.py:54
  145.7 18.4 %collective-permute-start.50 = (bf16[64,384]{0,1:T(8,128)(2,1)S(1)}, bf16[64,384]{0,1:T(8,128)(2,1)S(1)}, u32[]{:S(2)}, u32[]{:S(2)}) collective-permute-start(bf16[64,384]{0,1:T(8,128)(2,1)S(1)} %get-tuple-element.47), channel_id=1, source_target_pairs={{0,6},{1,7},{2,0},{3,1},{4,2},{5,3},{6,4},{7,5},{8,14},{9,15},{10,... | collective-permute-start | bytes 147464 | tf_op jit(solution)/shard_map/ppermute | solution.py:54
  145.7 18.4 %collective-permute-start.49 = (bf16[64,384]{0,1:T(8,128)(2,1)S(1)}, bf16[64,384]{0,1:T(8,128)(2,1)S(1)}, u32[]{:S(2)}, u32[]{:S(2)}) collective-permute-start(bf16[64,384]{0,1:T(8,128)(2,1)S(1)} %get-tuple-element.48), channel_id=1, source_target_pairs={{0,5},{1,6},{2,7},{3,0},{4,1},{5,2},{6,3},{7,4},{8,13},{9,14},{10,... | collective-permute-start | bytes 147464 | tf_op jit(solution)/shard_map/ppermute | solution.py:54
  145.7 18.3 %collective-permute-start.48 = (bf16[64,384]{0,1:T(8,128)(2,1)S(1)}, bf16[64,384]{0,1:T(8,128)(2,1)S(1)}, u32[]{:S(2)}, u32[]{:S(2)}) collective-permute-start(bf16[64,384]{0,1:T(8,128)(2,1)S(1)} %get-tuple-element.49), channel_id=1, source_target_pairs={{0,4},{1,5},{2,6},{3,7},{4,0},{5,1},{6,2},{7,3},{8,12},{9,13},{10,... | collective-permute-start | bytes 147464 | tf_op jit(solution)/shard_map/ppermute | solution.py:54
  148.6 8.5 %collective-permute-start.46 = (bf16[64,384]{0,1:T(8,128)(2,1)S(1)}, bf16[64,384]{0,1:T(8,128)(2,1)S(1)}, u32[]{:S(2)}, u32[]{:S(2)}) collective-permute-start(bf16[64,384]{0,1:T(8,128)(2,1)S(1)} %get-tuple-element.51), channel_id=1, source_target_pairs={{0,2},{1,3},{2,4},{3,5},{4,6},{5,7},{6,0},{7,1},{8,10},{9,11},{10,... | collective-permute-start | bytes 147464 | tf_op jit(solution)/shard_map/ppermute | solution.py:54
  157.1 6.9 %collective-permute-start.47 = (bf16[64,384]{0,1:T(8,128)(2,1)S(1)}, bf16[64,384]{0,1:T(8,128)(2,1)S(1)}, u32[]{:S(2)}, u32[]{:S(2)}) collective-permute-start(bf16[64,384]{0,1:T(8,128)(2,1)S(1)} %get-tuple-element.50), channel_id=1, source_target_pairs={{0,3},{1,4},{2,5},{3,6},{4,7},{5,0},{6,1},{7,2},{8,11},{9,12},{10,... | collective-permute-start | bytes 147464 | tf_op jit(solution)/shard_map/ppermute | solution.py:54
  164.3 7.7 %collective-permute-start.54 = (f32[64,384]{0,1:T(8,128)S(1)}, f32[64,384]{0,1:T(8,128)S(1)}, u32[]{:S(2)}, u32[]{:S(2)}) collective-permute-start(f32[64,384]{0,1:T(8,128)S(1)} %convert_reduce_fusion), channel_id=1, source_target_pairs={{0,24},{8,0},{16,8},{24,16},{1,25},{9,1},{17,9},{25,17},{2,26},{10... | collective-permute-start | bytes 294920 | tf_op jit(solution)/shard_map/ppermute | solution.py:38
  166.7 11.3 %collective-permute-start.53 = (f32[64,384]{0,1:T(8,128)S(1)}, f32[64,384]{0,1:T(8,128)S(1)}, u32[]{:S(2)}, u32[]{:S(2)}) collective-permute-start(f32[64,384]{0,1:T(8,128)S(1)} %convert_reduce_fusion), channel_id=1, source_target_pairs={{0,16},{8,24},{16,0},{24,8},{1,17},{9,25},{17,1},{25,9},{2,18},{10... | collective-permute-start | bytes 294920 | tf_op jit(solution)/shard_map/ppermute | solution.py:38
  167.2 10.8 %collective-permute-start.52 = (f32[64,384]{0,1:T(8,128)S(1)}, f32[64,384]{0,1:T(8,128)S(1)}, u32[]{:S(2)}, u32[]{:S(2)}) collective-permute-start(f32[64,384]{0,1:T(8,128)S(1)} %convert_reduce_fusion), channel_id=1, source_target_pairs={{0,8},{8,16},{16,24},{24,0},{1,9},{9,17},{17,25},{25,1},{2,10},{10... | collective-permute-start | bytes 294920 | tf_op jit(solution)/shard_map/ppermute | solution.py:38
  (26 other events, 225.0 us)

commit v3 on v2

--- a/solution.py
+++ b/solution.py
@@ -31,33 +31,34 @@
     return [(source, (source + shift) % size) for source in range(size)]
 
 
-def gather_relative(value, axis):
-    size = lax.axis_size(axis)
-    if size <= FAN_OUT_MAX:
-        pieces = [value] + [
-            lax.ppermute(value, axis, shift_pairs(size, shift)) for shift in range(1, size)
-        ]
-        return jnp.stack(pieces)
-    here = lax.axis_index(axis)
-    stacked = lax.all_gather(value, axis)
-    return jnp.take(stacked, (here - jnp.arange(size)) % size, axis=0)
-
-
 def to_absolute(stack, axis):
     return jnp.roll(stack[::-1], lax.axis_index(axis) + 1, axis=0)
 
 
-def exchange_relative(blocks, axis):
+def gather_ordered(value, axis, native):
     size = lax.axis_size(axis)
-    if size <= FAN_OUT_MAX:
-        pieces = [blocks[0]] + [
-            lax.ppermute(blocks[(-shift) % size], axis, shift_pairs(size, shift))
-            for shift in range(1, size)
-        ]
-        return jnp.stack(pieces)
+    if native or size > FAN_OUT_MAX:
+        return lax.all_gather(value, axis)
+    pieces = [value] + [
+        lax.ppermute(value, axis, shift_pairs(size, shift)) for shift in range(1, size)
+    ]
+    return to_absolute(jnp.stack(pieces), axis)
+
+
+def exchange_ordered(blocks, axis, native):
+    size = lax.axis_size(axis)
+    if native or size > FAN_OUT_MAX:
+        return lax.all_to_all(blocks, axis, 0, 0, tiled=True)
     here = lax.axis_index(axis)
-    ordered = jnp.take(blocks, (here - jnp.arange(size)) % size, axis=0)
-    return lax.all_to_all(ordered, axis, 0, 0, tiled=True)
+    pieces = [lax.dynamic_index_in_dim(blocks, here, keepdims=False)] + [
+        lax.ppermute(
+            lax.dynamic_index_in_dim(blocks, (here + shift) % size, keepdims=False),
+            axis,
+            shift_pairs(size, shift),
+        )
+        for shift in range(1, size)
+    ]
+    return to_absolute(jnp.stack(pieces), axis)
 
 
 def feed_forward(embedded, normed, weights):
@@ -161,27 +162,30 @@
     ).astype(jnp.bfloat16)
     matrices = (ref_gate, ref_up, ref_down, prx_gate, prx_up, prx_down)
     gains = (ref_norm1, ref_norm2, prx_norm1, prx_norm2)
-    packed = jnp.concatenate(
+    small = jnp.concatenate(
         [id_parts.reshape(-1), domain_ids.reshape(-1).astype(jnp.bfloat16)]
         + [item.reshape(-1) for item in gains]
     )
-    gathered = gather_relative(packed, "fsdp")
-    gathered_matrices = gather_relative(jnp.concatenate(matrices, axis=0), "fsdp")
+    small_rows = -(-small.shape[0] // width)
+    small = jnp.pad(small, (0, small_rows * width - small.shape[0])).reshape(small_rows, width)
+    matrix_rows = len(matrices) * unit_rows
+    packed = jnp.concatenate(list(matrices) + [small], axis=0)
+    gathered = gather_ordered(packed, "fsdp", True)
+    full_matrices = [
+        gathered[:, index * unit_rows : (index + 1) * unit_rows].reshape(-1, width)
+        for index in range(len(matrices))
+    ]
+    small_all = gathered[:, matrix_rows:].reshape(fsdp_size, -1)
     offset = 4 * per_device
-    group_ids = gathered[:, :offset].astype(jnp.int32).reshape(fsdp_size, 4, per_device)
+    group_ids = small_all[:, :offset].astype(jnp.int32).reshape(fsdp_size, 4, per_device)
     group_tokens = (group_ids[:, 0] * ID_BASE + group_ids[:, 1]).reshape(-1)
     group_targets = (group_ids[:, 2] * ID_BASE + group_ids[:, 3]).reshape(-1)
-    group_domains = gathered[:, offset : offset + rows_here].astype(jnp.int32)
+    group_domains = small_all[:, offset : offset + rows_here].astype(jnp.int32)
     offset += rows_here
     full_gains = []
     for _ in gains:
-        piece = gathered[:, offset : offset + gain_here]
-        full_gains.append(to_absolute(piece, "fsdp").reshape(-1))
+        full_gains.append(small_all[:, offset : offset + gain_here].reshape(-1))
         offset += gain_here
-    full_matrices = [
-        gathered_matrices[:, index * unit_rows : (index + 1) * unit_rows].reshape(-1, width)
-        for index in range(len(matrices))
-    ]
     ref_weights = (*full_matrices[:3], full_gains[0], full_gains[1])
     prx_weights = (*full_matrices[3:], full_gains[2], full_gains[3])
 
@@ -191,14 +195,14 @@
     picked_rows = jnp.dot(token_hits, in_embed, preferred_element_type=jnp.float32).astype(
         jnp.bfloat16
     )
-    arrived = exchange_relative(picked_rows.reshape(fsdp_size, per_device, width), "fsdp")
+    arrived = exchange_ordered(picked_rows.reshape(fsdp_size, per_device, width), "fsdp", True)
     embedded = jnp.sum(arrived.astype(jnp.float32), axis=0)
 
     normed = embedded * rms_scale(embedded)
     ref_own = feed_forward(embedded, normed, ref_weights)[0]
     prx_own, saved_state = feed_forward(embedded, normed, prx_weights)
 
-    group_features = gather_relative(jnp.concatenate([ref_own, prx_own], axis=1), "fsdp")
+    group_features = gather_ordered(jnp.concatenate([ref_own, prx_own], axis=1), "fsdp", False)
     group_features = group_features.reshape(group_total, 2 * width)
     ref_group = group_features[:, :width]
     prx_group = group_features[:, width:]
@@ -207,45 +211,39 @@
     ref_stats = vocab_stats(ref_group, out_embed, target_local)
     prx_stats = vocab_stats(prx_group, out_embed, target_local)
 
-    local_stats = jnp.concatenate([ref_stats, prx_stats]).reshape(6, fsdp_size, per_device)
-    local_stats = to_absolute(jnp.swapaxes(local_stats, 0, 1), "fsdp")
-    all_stats = to_absolute(gather_relative(local_stats, "fsdp"), "fsdp")
-    tops = all_stats[:, :, 0::3]
-    exp_totals = all_stats[:, :, 1::3]
-    picks = all_stats[:, :, 2::3]
+    all_stats = gather_ordered(jnp.concatenate([ref_stats, prx_stats]), "fsdp", False)
+    tops = all_stats[:, 0::3]
+    exp_totals = all_stats[:, 1::3]
+    picks = all_stats[:, 2::3]
     top_logit = jnp.max(tops, axis=0)
     exp_total = jnp.sum(exp_totals * jnp.exp(tops - top_logit[None]), axis=0)
     pick_total = jnp.sum(picks, axis=0)
     log_total = top_logit + jnp.log(exp_total)
     losses = log_total - pick_total
-    excess = jnp.maximum(losses[:, 1] - losses[:, 0], 0.0)
-    relative_order = (lax.axis_index("fsdp") - jnp.arange(fsdp_size)) % fsdp_size
-    prx_log_total = jnp.take(log_total[:, 1], relative_order, axis=0).reshape(-1)
+    excess = jnp.maximum(losses[1] - losses[0], 0.0)
 
     row_excess = jnp.sum(excess.reshape(fsdp_size * rows_here, seq_len), axis=1)
-    row_domains = to_absolute(group_domains, "fsdp").reshape(-1)
+    row_domains = group_domains.reshape(-1)
     domain_range = jnp.arange(domain_total, dtype=jnp.int32)
     row_hits = (row_domains[:, None] == domain_range[None, :]).astype(jnp.float32)
     group_sums = jnp.sum(row_hits * row_excess[:, None], axis=0)
     group_counts = jnp.sum(row_hits, axis=0) * seq_len
 
-    summed = jnp.sum(
-        to_absolute(gather_relative(jnp.stack([group_sums, group_counts]), "dp"), "dp"), axis=0
-    )
+    summed = jnp.sum(gather_ordered(jnp.stack([group_sums, group_counts]), "dp", False), axis=0)
     total_sums = summed[0]
     domain_counts = summed[1]
     softmax_mix = jax.nn.softmax(jnp.log(alpha_prev) + total_sums / domain_counts)
     alpha_new = (1.0 - SMOOTHING) * softmax_mix + SMOOTHING / domain_total
     device_total = group_total * lax.axis_size("dp")
     token_ratio = math.sqrt(device_total) * alpha_new / domain_counts
-    group_rows = group_domains.reshape(-1)
-    row_weight = jnp.take(token_ratio, group_rows)
+    row_weight = jnp.take(token_ratio, row_domains)
     token_weight = jnp.repeat(row_weight, seq_len)
 
-    d_second_part = head_gradient(prx_group, out_embed, prx_log_total, token_weight, target_local)
+    d_second_part = head_gradient(prx_group, out_embed, log_total[1], token_weight, target_local)
 
     d_second = jnp.sum(
-        exchange_relative(d_second_part.reshape(fsdp_size, per_device, width), "fsdp"), axis=0
+        exchange_ordered(d_second_part.reshape(fsdp_size, per_device, width), "fsdp", False),
+        axis=0,
     )
     first_in, gate_act, up_act, hidden, second_scale, unit_stream = saved_state
     d_unit = d_second * prx_weights[4].astype(jnp.float32)
@@ -268,12 +266,12 @@
         axis=1,
     ).astype(jnp.bfloat16)
 
-    arrived_grad = exchange_relative(
-        partial_grad.reshape(fsdp_size, unit_rows, 3 * width), "fsdp"
+    arrived_grad = exchange_ordered(
+        partial_grad.reshape(fsdp_size, unit_rows, 3 * width), "fsdp", True
     )
     local_grad = jnp.sum(arrived_grad.astype(jnp.float32), axis=0)
 
-    grad_shard = jnp.sum(to_absolute(gather_relative(local_grad, "dp"), "dp"), axis=0)
+    grad_shard = jnp.sum(gather_ordered(local_grad, "dp", False), axis=0)
     return (
         alpha_new,
         grad_shard[:, :width],

time: 181 us -> 142 us (0.78)
  waiting for transfers between devices: 91 us -> 44.7 us
  blocking collectives: 0 us -> 34.2 us
  starting transfers between devices: 57.2 us -> 32.3 us
  local copies, waits for them, and re-layouts: 12.3 us -> 10.4 us
    ppermute x55 -> x27, waiting for transfers between devices: 91 us -> 35.5 us  [the longest x20 24.6 us: gather_ordered(): lax.ppermute(value, axis, shift_pairs(size, shift))]
    ppermute x55 -> x27, starting transfers between devices: 57.2 us -> 27.4 us  [the longest x20 21 us: gather_ordered(): lax.ppermute(value, axis, shift_pairs(size, shift))]
    all_gather x0 -> x1, blocking collectives: none -> 17.3 us  [gather_ordered(): return lax.all_gather(value, axis)]
    all_to_all x0 -> x1, blocking collectives: none -> 16.9 us  [exchange_ordered(): return lax.all_to_all(blocks, axis, 0, 0, tiled=True)]
    all_to_all x0 -> x1, waiting for transfers between devices: none -> 9.12 us  [exchange_ordered(): return lax.all_to_all(blocks, axis, 0, 0, tiled=True)]
    all_to_all x0 -> x1, starting transfers between devices: none -> 4.81 us  [exchange_ordered(): return lax.all_to_all(blocks, axis, 0, 0, tiled=True)]
    unnamed x52 -> x25, local copies, waits for them, and re-layouts: 6.11 us -> 4.49 us
  transfers between devices with their start and end apart: 55 -> 28, of which waited for: 26 -> 13; matrix products, arithmetic and copies ran while one was open for 5% -> 1% of each run, Pallas kernels for 0% -> 0%
where the time goes in v3:
time: 142 us; the launch traced here: 141 us
  waiting for transfers between devices  44.7 us (31%)
  blocking collectives  34.2 us (24%)
  starting transfers between devices  32.3 us (23%)
  local copies, waits for them, and re-layouts  10.4 us (7%)
  matrix products  9.58 us (7%)
  other arithmetic  8.31 us (6%)
  between operations  1.91 us (1%)
    ppermute x20, waiting for transfers between devices, gather_ordered(): lax.ppermute(value, axis, shift_pairs(size, shift))  24.6 us
    ppermute x20, starting transfers between devices, gather_ordered(): lax.ppermute(value, axis, shift_pairs(size, shift))  21 us
    all_gather x1, blocking collectives, gather_ordered(): return lax.all_gather(value, axis)  17.3 us
    all_to_all x1, blocking collectives, exchange_ordered(): return lax.all_to_all(blocks, axis, 0, 0, tiled=True)  16.9 us
    ppermute x7, waiting for transfers between devices, exchange_ordered(): lax.ppermute(lax.dynamic_index_in_dim(blocks, (here + shift) % size, keep...  11 us
    all_to_all x1, waiting for transfers between devices, exchange_ordered(): return lax.all_to_all(blocks, axis, 0, 0, tiled=True)  9.12 us
    ppermute x7, starting transfers between devices, exchange_ordered(): lax.ppermute(lax.dynamic_index_in_dim(blocks, (here + shift) % size, keep...  6.44 us
    all_to_all x1, starting transfers between devices, exchange_ordered(): return lax.all_to_all(blocks, axis, 0, 0, tiled=True)  4.81 us
  transfers between devices with their start and end apart: 28, of which 13 were waited for; matrix products, arithmetic and copies ran while one was open for 1% of the time, Pallas kernels for 0%

profile of v3, /device:TPU:0, one launch (start us, length us, event | category | flops | bytes accessed | tf_op | source)
XLA Modules:
  0.0 141.2 jit_solution(566299644429229832)
XLA Ops:
  6.4 2.8 %concatenate.43 = bf16[577]{0:T(1024)(128)(2,1)S(1)} concatenate(bf16[512]{0:T(512)(128)(2,1)S(1)} %maximum_bitcast_fusion, bf16[1]{0:T(256)(128)(2,1)} %bitcast.1, bf16[16]{0:T(256)(128)(2,1)} %param.21, bf16[16]{0:T(256)(128)(2,1)} %param.25, bf16[16]{0:T(256)(128)(2,1)} %param.26, bf16[16]{0:T(256)(128)(2,1)} %param.30), dimensions={0} | concatenate | bytes 2308 | tf_op jit(solution)/shard_map/concatenate | solution.py:165
  9.2 17.3 %all-gather.1 = bf16[8,389,128]{2,1,0:T(8,128)(2,1)S(1)} all-gather(bf16[1,389,128]{2,1,0:T(8,128)(2,1)S(1)} %bitcast.140), channel_id=2, replica_groups=mesh['dp'=4,'fsdp'=8] {'fsdp'}, dimensions={0}, use_global_device_ids=true | all-gather | bytes 896256 | tf_op jit(solution)/shard_map/all_gather | solution.py:41
  26.5 2.5 %fusion.3 = bf16[1024,128]{1,0:T(8,128)(2,1)} fusion(bf16[1024,128]{1,0:T(8,128)(2,1)} %param.19, s32[1024]{0:T(1024)S(1)} %get-tuple-element.40), kind=kOutput, calls=%fused_computation.11 | convolution fusion | flops 269615104 | bytes 528384 | tf_op jit(solution)/shard_map/dot_general | solution.py:195
  28.9 4.8 %all-to-all-start = ((bf16[8,128,128]{2,1,0:T(8,128)(2,1)}), bf16[8,128,128]{2,1,0:T(8,128)(2,1)S(1)}, u32[]{:S(2)}, u32[]{:S(2)}) async-start(bf16[8,128,128]{2,1,0:T(8,128)(2,1)} %bitcast.8), calls=%async_computation | async-start | bytes 524288 | tf_op jit(solution)/shard_map/all_to_all | solution.py:51
  34.4 9.1 %all-to-all-done = bf16[8,128,128]{2,1,0:T(8,128)(2,1)S(1)} async-done(((bf16[8,128,128]{2,1,0:T(8,128)(2,1)}), bf16[8,128,128]{2,1,0:T(8,128)(2,1)S(1)}, u32[]{:S(2)}, u32[]{:S(2)}) %all-to-all-start) | async-done | bytes 262176 | tf_op jit(solution)/shard_map/all_to_all | solution.py:51
  45.3 1.3 collective-permute-start.5
  46.7 2.3 %collective-permute-start.3 = (bf16[128,256]{0,1:T(8,128)(2,1)S(1)}, bf16[128,256]{0,1:T(8,128)(2,1)S(1)}, u32[]{:S(2)}, u32[]{:S(2)}) collective-permute-start(bf16[128,256]{0,1:T(8,128)(2,1)S(1)} %pad_maximum_fusion.2), channel_id=1, source_target_pairs={{0,4},{1,5},{2,6},{3,7},{4,0},{5,1},{6,2},{7,3},{8,12},{9,13},{10,... | collective-permute-start | bytes 196616 | tf_op jit(solution)/shard_map/ppermute | solution.py:43
  49.7 5.4 %collective-permute-done = bf16[128,256]{0,1:T(8,128)(2,1)S(1)} collective-permute-done((bf16[128,256]{0,1:T(8,128)(2,1)S(1)}, bf16[128,256]{0,1:T(8,128)(2,1)S(1)}, u32[]{:S(2)}, u32[]{:S(2)}) %collective-permute-start) | collective-permute-done | bytes 65568 | tf_op jit(solution)/shard_map/ppermute | solution.py:43
  55.7 5.5 %collective-permute-done.1 = bf16[128,256]{0,1:T(8,128)(2,1)S(1)} collective-permute-done((bf16[128,256]{0,1:T(8,128)(2,1)S(1)}, bf16[128,256]{0,1:T(8,128)(2,1)S(1)}, u32[]{:S(2)}, u32[]{:S(2)}) %collective-permute-start.1) | collective-permute-done | bytes 65568 | tf_op jit(solution)/shard_map/ppermute | solution.py:43
  61.3 1.8 %collective-permute-done.6 = bf16[128,256]{0,1:T(8,128)(2,1)S(1)} collective-permute-done((bf16[128,256]{0,1:T(8,128)(2,1)S(1)}, bf16[128,256]{0,1:T(8,128)(2,1)S(1)}, u32[]{:S(2)}, u32[]{:S(2)}) %collective-permute-start.6) | collective-permute-done | bytes 65568 | tf_op jit(solution)/shard_map/ppermute | solution.py:43
  65.0 2.0 %select_reduce_fusion = (f32[1024]{0:T(1024)S(1)}, f32[1024]{0:T(1024)S(1)}, f32[1024]{0:T(1024)S(1)}, f32[1024]{0:T(1024)S(1)}) fusion(f32[1024,1024]{0,1:T(8,128)S(1)} %get-tuple-element.60, s32[1024]{0:T(1024)S(1)} %get-tuple-element.39, f32[1024]{0:T(1024)S(1)} %get-tuple-element.59, f32[1024,1024]{0,1:T(8,128)S(1)} %get-tuple-element.58, ...), kind=kLoop, calls=%fused_computation.2 | loop fusion | flops 9433088 | bytes 8417280 | tf_op jit(solution)/shard_map/reduce_sum | solution.py:91
  67.1 1.9 %collective-permute-start.12 = (f32[6,1024]{1,0:T(8,128)S(1)}, f32[6,1024]{1,0:T(8,128)S(1)}, u32[]{:S(2)}, u32[]{:S(2)}) collective-permute-start(f32[6,1024]{1,0:T(8,128)S(1)} %concatenate.47), channel_id=1, source_target_pairs={{0,6},{1,7},{2,0},{3,1},{4,2},{5,3},{6,4},{7,5},{8,14},{9,15},{10,... | collective-permute-start | bytes 73736 | tf_op jit(solution)/shard_map/ppermute | solution.py:43
  69.0 2.1 %collective-permute-start.11 = (f32[6,1024]{1,0:T(8,128)S(1)}, f32[6,1024]{1,0:T(8,128)S(1)}, u32[]{:S(2)}, u32[]{:S(2)}) collective-permute-start(f32[6,1024]{1,0:T(8,128)S(1)} %concatenate.47), channel_id=1, source_target_pairs={{0,5},{1,6},{2,7},{3,0},{4,1},{5,2},{6,3},{7,4},{8,13},{9,14},{10,... | collective-permute-start | bytes 73736 | tf_op jit(solution)/shard_map/ppermute | solution.py:43
  71.3 2.3 %collective-permute-start.10 = (f32[6,1024]{1,0:T(8,128)S(1)}, f32[6,1024]{1,0:T(8,128)S(1)}, u32[]{:S(2)}, u32[]{:S(2)}) collective-permute-start(f32[6,1024]{1,0:T(8,128)S(1)} %concatenate.47), channel_id=1, source_target_pairs={{0,4},{1,5},{2,6},{3,7},{4,0},{5,1},{6,2},{7,3},{8,12},{9,13},{10,... | collective-permute-start | bytes 73736 | tf_op jit(solution)/shard_map/ppermute | solution.py:43
  74.7 1.1 collective-permute-start.7
  76.7 1.2 collective-permute-done.9
  77.9 2.2 %collective-permute-done.8 = f32[6,1024]{1,0:T(8,128)S(1)} collective-permute-done((f32[6,1024]{1,0:T(8,128)S(1)}, f32[6,1024]{1,0:T(8,128)S(1)}, u32[]{:S(2)}, u32[]{:S(2)}) %collective-permute-start.8) | collective-permute-done | bytes 24608 | tf_op jit(solution)/shard_map/ppermute | solution.py:43
  81.2 1.6 %collective-permute-start.15 = (f32[2,22]{1,0:T(2,128)S(1)}, f32[2,22]{1,0:T(2,128)S(1)}, u32[]{:S(2)}, u32[]{:S(2)}) collective-permute-start(f32[2,22]{1,0:T(2,128)S(1)} %get-tuple-element.46), channel_id=1, source_target_pairs={{0,16},{8,24},{16,0},{24,8},{1,17},{9,25},{17,1},{25,9},{2,18},{10... | collective-permute-start | bytes 536 | tf_op jit(solution)/shard_map/ppermute | solution.py:43
  82.8 1.5 %collective-permute-start.14 = (f32[2,22]{1,0:T(2,128)S(1)}, f32[2,22]{1,0:T(2,128)S(1)}, u32[]{:S(2)}, u32[]{:S(2)}) collective-permute-start(f32[2,22]{1,0:T(2,128)S(1)} %get-tuple-element.46), channel_id=1, source_target_pairs={{0,8},{8,16},{16,24},{24,0},{1,9},{9,17},{17,25},{25,1},{2,10},{10... | collective-permute-start | bytes 536 | tf_op jit(solution)/shard_map/ppermute | solution.py:43
  84.3 1.4 %collective-permute-start.16 = (f32[2,22]{1,0:T(2,128)S(1)}, f32[2,22]{1,0:T(2,128)S(1)}, u32[]{:S(2)}, u32[]{:S(2)}) collective-permute-start(f32[2,22]{1,0:T(2,128)S(1)} %get-tuple-element.46), channel_id=1, source_target_pairs={{0,24},{8,0},{16,8},{24,16},{1,25},{9,1},{17,9},{25,17},{2,26},{10... | collective-permute-start | bytes 536 | tf_op jit(solution)/shard_map/ppermute | solution.py:43
  85.7 1.5 %collective-permute-done.14 = f32[2,22]{1,0:T(2,128)S(1)} collective-permute-done((f32[2,22]{1,0:T(2,128)S(1)}, f32[2,22]{1,0:T(2,128)S(1)}, u32[]{:S(2)}, u32[]{:S(2)}) %collective-permute-start.14) | collective-permute-done | bytes 208 | tf_op jit(solution)/shard_map/ppermute | solution.py:43
  88.5 1.2 fusion.44
  89.8 1.8 %bitcast_divide_fusion = (f32[22]{0:T(128)S(1)}, f32[22]{0:T(128)}) fusion(f32[2,22]{1,0:T(2,128)S(1)} %fusion.35, f32[]{:T(128)} %fusion.44, f32[22]{0:T(128)S(1)} %get-tuple-element.19, f32[]{:T(128)} %get-tuple-element.18), kind=kLoop, calls=%fused_computation.144 | loop fusion | flops 132 | bytes 360 | tf_op jit(solution)/shard_map/div | solution.py:238
  92.3 3.5 %fusion.2 = f32[1024,128]{1,0:T(8,128)S(1)} fusion(bf16[1024,128]{1,0:T(8,128)(2,1)S(1)} %copy-done, f32[1024,1024]{0,1:T(8,128)} %copy-done.1, f32[1024]{0:T(1024)S(1)} %bitcast.167, f32[1024]{0:T(1024)S(1)} %broadcast_bitcast_fusion, s32[1024]{0:T(1024)S(1)} %get-tuple-element.39), kind=kOutput, calls=%fused_computation.10 | convolution fusion | flops 274726912 | bytes 4993024 | tf_op jit(solution)/shard_map/dot_general | solution.py:113
  95.9 3.5 %collective-permute-start.23 = (f32[128,128]{1,0:T(8,128)S(1)}, f32[128,128]{1,0:T(8,128)S(1)}, u32[]{:S(2)}, u32[]{:S(2)}) collective-permute-start(f32[128,128]{1,0:T(8,128)S(1)} %get-tuple-element.28), channel_id=1, source_target_pairs={{0,7},{1,0},{2,1},{3,2},{4,3},{5,4},{6,5},{7,6},{8,15},{9,8},{10,9... | collective-permute-start | bytes 196616 | tf_op jit(solution)/shard_map/ppermute | solution.py:54
  99.5 2.7 %collective-permute-start.20 = (f32[128,128]{1,0:T(8,128)S(1)}, f32[128,128]{1,0:T(8,128)S(1)}, u32[]{:S(2)}, u32[]{:S(2)}) collective-permute-start(f32[128,128]{1,0:T(8,128)S(1)} %get-tuple-element.31), channel_id=1, source_target_pairs={{0,4},{1,5},{2,6},{3,7},{4,0},{5,1},{6,2},{7,3},{8,12},{9,13},{10,... | collective-permute-start | bytes 196616 | tf_op jit(solution)/shard_map/ppermute | solution.py:54
  102.2 6.5 %collective-permute-done.18 = f32[128,128]{1,0:T(8,128)S(1)} collective-permute-done((f32[128,128]{1,0:T(8,128)S(1)}, f32[128,128]{1,0:T(8,128)S(1)}, u32[]{:S(2)}, u32[]{:S(2)}) %collective-permute-start.18) | collective-permute-done | bytes 65568 | tf_op jit(solution)/shard_map/ppermute | solution.py:54
  108.9 4.4 %collective-permute-done.19 = f32[128,128]{1,0:T(8,128)S(1)} collective-permute-done((f32[128,128]{1,0:T(8,128)S(1)}, f32[128,128]{1,0:T(8,128)S(1)}, u32[]{:S(2)}, u32[]{:S(2)}) %collective-permute-start.19) | collective-permute-done | bytes 65568 | tf_op jit(solution)/shard_map/ppermute | solution.py:54
  114.9 16.9 %all_to_all.10 = bf16[8,64,384]{2,1,0:T(8,128)(2,1)S(1)} all-to-all(bf16[8,64,384]{2,1,0:T(8,128)(2,1)S(1)} %pad_maximum_fusion), channel_id=1, replica_groups=mesh['dp'=4,'fsdp'=8] {'fsdp'}, dimensions={0} | all-to-all | bytes 786432 | tf_op jit(solution)/shard_map/all_to_all | solution.py:51
  131.8 2.4 %collective-permute-start.26 = (f32[64,384]{1,0:T(8,128)S(1)}, f32[64,384]{1,0:T(8,128)S(1)}, u32[]{:S(2)}, u32[]{:S(2)}) collective-permute-start(f32[64,384]{1,0:T(8,128)S(1)} %convert_reduce_fusion), channel_id=1, source_target_pairs={{0,24},{8,0},{16,8},{24,16},{1,25},{9,1},{17,9},{25,17},{2,26},{10... | collective-permute-start | bytes 294920 | tf_op jit(solution)/shard_map/ppermute | solution.py:43
  134.8 2.3 %collective-permute-done.26 = f32[64,384]{1,0:T(8,128)S(1)} collective-permute-done((f32[64,384]{1,0:T(8,128)S(1)}, f32[64,384]{1,0:T(8,128)S(1)}, u32[]{:S(2)}, u32[]{:S(2)}) %collective-permute-start.26) | collective-permute-done | bytes 98336 | tf_op jit(solution)/shard_map/ppermute | solution.py:43
  137.2 3.3 %collective-permute-done.25 = f32[64,384]{1,0:T(8,128)S(1)} collective-permute-done((f32[64,384]{1,0:T(8,128)S(1)}, f32[64,384]{1,0:T(8,128)S(1)}, u32[]{:S(2)}, u32[]{:S(2)}) %collective-permute-start.25) | collective-permute-done | bytes 98336 | tf_op jit(solution)/shard_map/ppermute | solution.py:43
  (140 shorter events, 19.1 us)
Async XLA Ops:
  0.6 62.9 %copy-start = (bf16[1024,128]{1,0:T(8,128)(2,1)S(1)}, bf16[1024,128]{1,0:T(8,128)(2,1)}, u32[]{:S(2)}) copy-start(bf16[1024,128]{1,0:T(8,128)(2,1)} %param.20) | copy-start | bytes 786436
  28.9 14.6 %all-to-all-start = ((bf16[8,128,128]{2,1,0:T(8,128)(2,1)}), bf16[8,128,128]{2,1,0:T(8,128)(2,1)S(1)}, u32[]{:S(2)}, u32[]{:S(2)}) async-start(bf16[8,128,128]{2,1,0:T(8,128)(2,1)} %bitcast.8), calls=%async_computation | async-start | bytes 524288 | tf_op jit(solution)/shard_map/all_to_all | solution.py:51
  45.3 15.9 %collective-permute-start.5 = (bf16[128,256]{0,1:T(8,128)(2,1)S(1)}, bf16[128,256]{0,1:T(8,128)(2,1)S(1)}, u32[]{:S(2)}, u32[]{:S(2)}) collective-permute-start(bf16[128,256]{0,1:T(8,128)(2,1)S(1)} %pad_maximum_fusion.2), channel_id=1, source_target_pairs={{0,6},{1,7},{2,0},{3,1},{4,2},{5,3},{6,4},{7,5},{8,14},{9,15},{10,... | collective-permute-start | bytes 196616 | tf_op jit(solution)/shard_map/ppermute | solution.py:43
  46.7 14.6 %collective-permute-start.4 = (bf16[128,256]{0,1:T(8,128)(2,1)S(1)}, bf16[128,256]{0,1:T(8,128)(2,1)S(1)}, u32[]{:S(2)}, u32[]{:S(2)}) collective-permute-start(bf16[128,256]{0,1:T(8,128)(2,1)S(1)} %pad_maximum_fusion.2), channel_id=1, source_target_pairs={{0,5},{1,6},{2,7},{3,0},{4,1},{5,2},{6,3},{7,4},{8,13},{9,14},{10,... | collective-permute-start | bytes 196616 | tf_op jit(solution)/shard_map/ppermute | solution.py:43
  46.7 14.5 %collective-permute-start.3 = (bf16[128,256]{0,1:T(8,128)(2,1)S(1)}, bf16[128,256]{0,1:T(8,128)(2,1)S(1)}, u32[]{:S(2)}, u32[]{:S(2)}) collective-permute-start(bf16[128,256]{0,1:T(8,128)(2,1)S(1)} %pad_maximum_fusion.2), channel_id=1, source_target_pairs={{0,4},{1,5},{2,6},{3,7},{4,0},{5,1},{6,2},{7,3},{8,12},{9,13},{10,... | collective-permute-start | bytes 196616 | tf_op jit(solution)/shard_map/ppermute | solution.py:43
  49.0 12.2 %collective-permute-start.2 = (bf16[128,256]{0,1:T(8,128)(2,1)S(1)}, bf16[128,256]{0,1:T(8,128)(2,1)S(1)}, u32[]{:S(2)}, u32[]{:S(2)}) collective-permute-start(bf16[128,256]{0,1:T(8,128)(2,1)S(1)} %pad_maximum_fusion.2), channel_id=1, source_target_pairs={{0,3},{1,4},{2,5},{3,6},{4,7},{5,0},{6,1},{7,2},{8,11},{9,12},{10,... | collective-permute-start | bytes 196616 | tf_op jit(solution)/shard_map/ppermute | solution.py:43
  49.0 6.1 %collective-permute-start = (bf16[128,256]{0,1:T(8,128)(2,1)S(1)}, bf16[128,256]{0,1:T(8,128)(2,1)S(1)}, u32[]{:S(2)}, u32[]{:S(2)}) collective-permute-start(bf16[128,256]{0,1:T(8,128)(2,1)S(1)} %pad_maximum_fusion.2), channel_id=1, source_target_pairs={{0,1},{1,2},{2,3},{3,4},{4,5},{5,6},{6,7},{7,0},{8,9},{9,10},{10,1... | collective-permute-start | bytes 196616 | tf_op jit(solution)/shard_map/ppermute | solution.py:43
  55.1 6.1 %collective-permute-start.1 = (bf16[128,256]{0,1:T(8,128)(2,1)S(1)}, bf16[128,256]{0,1:T(8,128)(2,1)S(1)}, u32[]{:S(2)}, u32[]{:S(2)}) collective-permute-start(bf16[128,256]{0,1:T(8,128)(2,1)S(1)} %pad_maximum_fusion.2), channel_id=1, source_target_pairs={{0,2},{1,3},{2,4},{3,5},{4,6},{5,7},{6,0},{7,1},{8,10},{9,11},{10,... | collective-permute-start | bytes 196616 | tf_op jit(solution)/shard_map/ppermute | solution.py:43
  61.2 1.9 %collective-permute-start.6 = (bf16[128,256]{0,1:T(8,128)(2,1)S(1)}, bf16[128,256]{0,1:T(8,128)(2,1)S(1)}, u32[]{:S(2)}, u32[]{:S(2)}) collective-permute-start(bf16[128,256]{0,1:T(8,128)(2,1)S(1)} %pad_maximum_fusion.2), channel_id=1, source_target_pairs={{0,7},{1,0},{2,1},{3,2},{4,3},{5,4},{6,5},{7,6},{8,15},{9,8},{10,9... | collective-permute-start | bytes 196616 | tf_op jit(solution)/shard_map/ppermute | solution.py:43
  64.3 2.8 %copy-start.1 = (f32[1024,1024]{0,1:T(8,128)}, f32[1024,1024]{0,1:T(8,128)S(1)}, u32[]{:S(2)}) copy-start(f32[1024,1024]{0,1:T(8,128)S(1)} %get-tuple-element.60) | copy-start | bytes 12582916
  65.0 22.9 %copy-start.2 = (f32[22]{0:T(128)S(1)}, f32[22]{0:T(128)}, u32[]{:S(2)}) copy-start(f32[22]{0:T(128)} %param.31) | copy-start | bytes 268
  67.1 6.6 %collective-permute-start.12 = (f32[6,1024]{1,0:T(8,128)S(1)}, f32[6,1024]{1,0:T(8,128)S(1)}, u32[]{:S(2)}, u32[]{:S(2)}) collective-permute-start(f32[6,1024]{1,0:T(8,128)S(1)} %concatenate.47), channel_id=1, source_target_pairs={{0,6},{1,7},{2,0},{3,1},{4,2},{5,3},{6,4},{7,5},{8,14},{9,15},{10,... | collective-permute-start | bytes 73736 | tf_op jit(solution)/shard_map/ppermute | solution.py:43
  69.0 5.6 %collective-permute-start.11 = (f32[6,1024]{1,0:T(8,128)S(1)}, f32[6,1024]{1,0:T(8,128)S(1)}, u32[]{:S(2)}, u32[]{:S(2)}) collective-permute-start(f32[6,1024]{1,0:T(8,128)S(1)} %concatenate.47), channel_id=1, source_target_pairs={{0,5},{1,6},{2,7},{3,0},{4,1},{5,2},{6,3},{7,4},{8,13},{9,14},{10,... | collective-permute-start | bytes 73736 | tf_op jit(solution)/shard_map/ppermute | solution.py:43
  71.3 9.0 %collective-permute-start.13 = (f32[6,1024]{1,0:T(8,128)S(1)}, f32[6,1024]{1,0:T(8,128)S(1)}, u32[]{:S(2)}, u32[]{:S(2)}) collective-permute-start(f32[6,1024]{1,0:T(8,128)S(1)} %concatenate.47), channel_id=1, source_target_pairs={{0,7},{1,0},{2,1},{3,2},{4,3},{5,4},{6,5},{7,6},{8,15},{9,8},{10,9... | collective-permute-start | bytes 73736 | tf_op jit(solution)/shard_map/ppermute | solution.py:43
  71.3 5.4 %collective-permute-start.10 = (f32[6,1024]{1,0:T(8,128)S(1)}, f32[6,1024]{1,0:T(8,128)S(1)}, u32[]{:S(2)}, u32[]{:S(2)}) collective-permute-start(f32[6,1024]{1,0:T(8,128)S(1)} %concatenate.47), channel_id=1, source_target_pairs={{0,4},{1,5},{2,6},{3,7},{4,0},{5,1},{6,2},{7,3},{8,12},{9,13},{10,... | collective-permute-start | bytes 73736 | tf_op jit(solution)/shard_map/ppermute | solution.py:43
  73.7 4.2 %collective-permute-start.9 = (f32[6,1024]{1,0:T(8,128)S(1)}, f32[6,1024]{1,0:T(8,128)S(1)}, u32[]{:S(2)}, u32[]{:S(2)}) collective-permute-start(f32[6,1024]{1,0:T(8,128)S(1)} %concatenate.47), channel_id=1, source_target_pairs={{0,3},{1,4},{2,5},{3,6},{4,7},{5,0},{6,1},{7,2},{8,11},{9,12},{10,... | collective-permute-start | bytes 73736 | tf_op jit(solution)/shard_map/ppermute | solution.py:43
  73.7 6.5 %collective-permute-start.8 = (f32[6,1024]{1,0:T(8,128)S(1)}, f32[6,1024]{1,0:T(8,128)S(1)}, u32[]{:S(2)}, u32[]{:S(2)}) collective-permute-start(f32[6,1024]{1,0:T(8,128)S(1)} %concatenate.47), channel_id=1, source_target_pairs={{0,2},{1,3},{2,4},{3,5},{4,6},{5,7},{6,0},{7,1},{8,10},{9,11},{10,... | collective-permute-start | bytes 73736 | tf_op jit(solution)/shard_map/ppermute | solution.py:43
  74.7 5.5 %collective-permute-start.7 = (f32[6,1024]{1,0:T(8,128)S(1)}, f32[6,1024]{1,0:T(8,128)S(1)}, u32[]{:S(2)}, u32[]{:S(2)}) collective-permute-start(f32[6,1024]{1,0:T(8,128)S(1)} %concatenate.47), channel_id=1, source_target_pairs={{0,1},{1,2},{2,3},{3,4},{4,5},{5,6},{6,7},{7,0},{8,9},{9,10},{10,1... | collective-permute-start | bytes 73736 | tf_op jit(solution)/shard_map/ppermute | solution.py:43
  81.2 4.5 %collective-permute-start.15 = (f32[2,22]{1,0:T(2,128)S(1)}, f32[2,22]{1,0:T(2,128)S(1)}, u32[]{:S(2)}, u32[]{:S(2)}) collective-permute-start(f32[2,22]{1,0:T(2,128)S(1)} %get-tuple-element.46), channel_id=1, source_target_pairs={{0,16},{8,24},{16,0},{24,8},{1,17},{9,25},{17,1},{25,9},{2,18},{10... | collective-permute-start | bytes 536 | tf_op jit(solution)/shard_map/ppermute | solution.py:43
  82.8 4.5 %collective-permute-start.14 = (f32[2,22]{1,0:T(2,128)S(1)}, f32[2,22]{1,0:T(2,128)S(1)}, u32[]{:S(2)}, u32[]{:S(2)}) collective-permute-start(f32[2,22]{1,0:T(2,128)S(1)} %get-tuple-element.46), channel_id=1, source_target_pairs={{0,8},{8,16},{16,24},{24,0},{1,9},{9,17},{17,25},{25,1},{2,10},{10... | collective-permute-start | bytes 536 | tf_op jit(solution)/shard_map/ppermute | solution.py:43
  84.3 3.6 %collective-permute-start.16 = (f32[2,22]{1,0:T(2,128)S(1)}, f32[2,22]{1,0:T(2,128)S(1)}, u32[]{:S(2)}, u32[]{:S(2)}) collective-permute-start(f32[2,22]{1,0:T(2,128)S(1)} %get-tuple-element.46), channel_id=1, source_target_pairs={{0,24},{8,0},{16,8},{24,16},{1,25},{9,1},{17,9},{25,17},{2,26},{10... | collective-permute-start | bytes 536 | tf_op jit(solution)/shard_map/ppermute | solution.py:43
  95.9 6.3 %collective-permute-start.17 = (f32[128,128]{1,0:T(8,128)S(1)}, f32[128,128]{1,0:T(8,128)S(1)}, u32[]{:S(2)}, u32[]{:S(2)}) collective-permute-start(f32[128,128]{1,0:T(8,128)S(1)} %get-tuple-element.34), channel_id=1, source_target_pairs={{0,1},{1,2},{2,3},{3,4},{4,5},{5,6},{6,7},{7,0},{8,9},{9,10},{10,1... | collective-permute-start | bytes 196616 | tf_op jit(solution)/shard_map/ppermute | solution.py:54
  95.9 17.4 %collective-permute-start.23 = (f32[128,128]{1,0:T(8,128)S(1)}, f32[128,128]{1,0:T(8,128)S(1)}, u32[]{:S(2)}, u32[]{:S(2)}) collective-permute-start(f32[128,128]{1,0:T(8,128)S(1)} %get-tuple-element.28), channel_id=1, source_target_pairs={{0,7},{1,0},{2,1},{3,2},{4,3},{5,4},{6,5},{7,6},{8,15},{9,8},{10,9... | collective-permute-start | bytes 196616 | tf_op jit(solution)/shard_map/ppermute | solution.py:54
  99.5 13.9 %collective-permute-start.22 = (f32[128,128]{1,0:T(8,128)S(1)}, f32[128,128]{1,0:T(8,128)S(1)}, u32[]{:S(2)}, u32[]{:S(2)}) collective-permute-start(f32[128,128]{1,0:T(8,128)S(1)} %get-tuple-element.29), channel_id=1, source_target_pairs={{0,6},{1,7},{2,0},{3,1},{4,2},{5,3},{6,4},{7,5},{8,14},{9,15},{10,... | collective-permute-start | bytes 196616 | tf_op jit(solution)/shard_map/ppermute | solution.py:54
  99.5 13.8 %collective-permute-start.21 = (f32[128,128]{1,0:T(8,128)S(1)}, f32[128,128]{1,0:T(8,128)S(1)}, u32[]{:S(2)}, u32[]{:S(2)}) collective-permute-start(f32[128,128]{1,0:T(8,128)S(1)} %get-tuple-element.30), channel_id=1, source_target_pairs={{0,5},{1,6},{2,7},{3,0},{4,1},{5,2},{6,3},{7,4},{8,13},{9,14},{10,... | collective-permute-start | bytes 196616 | tf_op jit(solution)/shard_map/ppermute | solution.py:54
  99.5 13.8 %collective-permute-start.20 = (f32[128,128]{1,0:T(8,128)S(1)}, f32[128,128]{1,0:T(8,128)S(1)}, u32[]{:S(2)}, u32[]{:S(2)}) collective-permute-start(f32[128,128]{1,0:T(8,128)S(1)} %get-tuple-element.31), channel_id=1, source_target_pairs={{0,4},{1,5},{2,6},{3,7},{4,0},{5,1},{6,2},{7,3},{8,12},{9,13},{10,... | collective-permute-start | bytes 196616 | tf_op jit(solution)/shard_map/ppermute | solution.py:54
  102.2 6.5 %collective-permute-start.18 = (f32[128,128]{1,0:T(8,128)S(1)}, f32[128,128]{1,0:T(8,128)S(1)}, u32[]{:S(2)}, u32[]{:S(2)}) collective-permute-start(f32[128,128]{1,0:T(8,128)S(1)} %get-tuple-element.33), channel_id=1, source_target_pairs={{0,2},{1,3},{2,4},{3,5},{4,6},{5,7},{6,0},{7,1},{8,10},{9,11},{10,... | collective-permute-start | bytes 196616 | tf_op jit(solution)/shard_map/ppermute | solution.py:54
  108.7 4.6 %collective-permute-start.19 = (f32[128,128]{1,0:T(8,128)S(1)}, f32[128,128]{1,0:T(8,128)S(1)}, u32[]{:S(2)}, u32[]{:S(2)}) collective-permute-start(f32[128,128]{1,0:T(8,128)S(1)} %get-tuple-element.32), channel_id=1, source_target_pairs={{0,3},{1,4},{2,5},{3,6},{4,7},{5,0},{6,1},{7,2},{8,11},{9,12},{10,... | collective-permute-start | bytes 196616 | tf_op jit(solution)/shard_map/ppermute | solution.py:54
  131.8 5.3 %collective-permute-start.26 = (f32[64,384]{1,0:T(8,128)S(1)}, f32[64,384]{1,0:T(8,128)S(1)}, u32[]{:S(2)}, u32[]{:S(2)}) collective-permute-start(f32[64,384]{1,0:T(8,128)S(1)} %convert_reduce_fusion), channel_id=1, source_target_pairs={{0,24},{8,0},{16,8},{24,16},{1,25},{9,1},{17,9},{25,17},{2,26},{10... | collective-permute-start | bytes 294920 | tf_op jit(solution)/shard_map/ppermute | solution.py:43
  134.2 6.2 %collective-permute-start.25 = (f32[64,384]{1,0:T(8,128)S(1)}, f32[64,384]{1,0:T(8,128)S(1)}, u32[]{:S(2)}, u32[]{:S(2)}) collective-permute-start(f32[64,384]{1,0:T(8,128)S(1)} %convert_reduce_fusion), channel_id=1, source_target_pairs={{0,16},{8,24},{16,0},{24,8},{1,17},{9,25},{17,1},{25,9},{2,18},{10... | collective-permute-start | bytes 294920 | tf_op jit(solution)/shard_map/ppermute | solution.py:43
  134.7 5.7 %collective-permute-start.24 = (f32[64,384]{1,0:T(8,128)S(1)}, f32[64,384]{1,0:T(8,128)S(1)}, u32[]{:S(2)}, u32[]{:S(2)}) collective-permute-start(f32[64,384]{1,0:T(8,128)S(1)} %convert_reduce_fusion), channel_id=1, source_target_pairs={{0,8},{8,16},{16,24},{24,0},{1,9},{9,17},{17,25},{25,1},{2,10},{10... | collective-permute-start | bytes 294920 | tf_op jit(solution)/shard_map/ppermute | solution.py:43

commit v4 on v3

--- a/solution.py
+++ b/solution.py
@@ -162,30 +162,32 @@
     ).astype(jnp.bfloat16)
     matrices = (ref_gate, ref_up, ref_down, prx_gate, prx_up, prx_down)
     gains = (ref_norm1, ref_norm2, prx_norm1, prx_norm2)
-    small = jnp.concatenate(
-        [id_parts.reshape(-1), domain_ids.reshape(-1).astype(jnp.bfloat16)]
-        + [item.reshape(-1) for item in gains]
-    )
-    small_rows = -(-small.shape[0] // width)
-    small = jnp.pad(small, (0, small_rows * width - small.shape[0])).reshape(small_rows, width)
+    id_rows = id_parts.reshape(-1, width)
+    extra = [domain_ids.reshape(-1).astype(jnp.bfloat16)] + list(gains)
+    extra_size = rows_here + len(gains) * gain_here
+    extra_rows = -(-extra_size // width)
+    extra.append(jnp.zeros((extra_rows * width - extra_size,), jnp.bfloat16))
+    extra_rows = jnp.concatenate(extra).reshape(extra_rows, width)
     matrix_rows = len(matrices) * unit_rows
-    packed = jnp.concatenate(list(matrices) + [small], axis=0)
+    packed = jnp.concatenate(list(matrices) + [id_rows, extra_rows], axis=0)
     gathered = gather_ordered(packed, "fsdp", True)
     full_matrices = [
         gathered[:, index * unit_rows : (index + 1) * unit_rows].reshape(-1, width)
         for index in range(len(matrices))
     ]
-    small_all = gathered[:, matrix_rows:].reshape(fsdp_size, -1)
-    offset = 4 * per_device
-    group_ids = small_all[:, :offset].astype(jnp.int32).reshape(fsdp_size, 4, per_device)
+    offset = matrix_rows
+    id_count = id_rows.shape[0]
+    group_ids = gathered[:, offset : offset + id_count].astype(jnp.int32)
+    group_ids = group_ids.reshape(fsdp_size, 4, per_device)
     group_tokens = (group_ids[:, 0] * ID_BASE + group_ids[:, 1]).reshape(-1)
     group_targets = (group_ids[:, 2] * ID_BASE + group_ids[:, 3]).reshape(-1)
-    group_domains = small_all[:, offset : offset + rows_here].astype(jnp.int32)
-    offset += rows_here
-    full_gains = []
-    for _ in gains:
-        full_gains.append(small_all[:, offset : offset + gain_here].reshape(-1))
-        offset += gain_here
+    offset += id_count
+    extra_all = gathered[:, offset:].reshape(fsdp_size, -1)
+    group_domains = extra_all[:, :rows_here].astype(jnp.int32)
+    full_gains = [
+        extra_all[:, rows_here + index * gain_here : rows_here + (index + 1) * gain_here].reshape(-1)
+        for index in range(len(gains))
+    ]
     ref_weights = (*full_matrices[:3], full_gains[0], full_gains[1])
     prx_weights = (*full_matrices[3:], full_gains[2], full_gains[3])
 

time: 142 us -> 130 us (0.915)
  waiting for transfers between devices: 44.7 us -> 28.2 us
  starting transfers between devices: 32.3 us -> 37.4 us
    ppermute x20, waiting for transfers between devices: 24.6 us -> 14 us  [gather_ordered(): lax.ppermute(value, axis, shift_pairs(size, shift))]
    ppermute x7, waiting for transfers between devices: 11 us -> 5.17 us  [exchange_ordered(): lax.ppermute(lax.dynamic_index_in_dim(blocks, (here + shift) % size, keep...]
    concatenate x2, local copies, waits for them, and re-layouts: 2.78 us -> 7.15 us  [the longest x1 4.37 us: body(): packed = jnp.concatenate(list(matrices) + [id_rows, extra_rows], axis=0)]
    unnamed x25 -> x19, local copies, waits for them, and re-layouts: 4.49 us -> 0.14 us
    ppermute x20, starting transfers between devices: 21 us -> 24.2 us  [gather_ordered(): lax.ppermute(value, axis, shift_pairs(size, shift))]
    ppermute x7, starting transfers between devices: 6.44 us -> 8.39 us  [exchange_ordered(): lax.ppermute(lax.dynamic_index_in_dim(blocks, (here + shift) % size, keep...]
  transfers between devices with their start and end apart: 28 -> 28, of which waited for: 13 -> 14; matrix products, arithmetic and copies ran while one was open for 1% -> 1% of each run, Pallas kernels for 0% -> 0%
where the time goes in v4:
time: 130 us; the launch traced here: 129 us
  starting transfers between devices  37.4 us (29%)
  blocking collectives  33.7 us (26%)
  waiting for transfers between devices  28.2 us (22%)
  local copies, waits for them, and re-layouts  10.4 us (8%)
  matrix products  9.58 us (7%)
  other arithmetic  8.31 us (6%)
  between operations  1.9 us (1%)
    ppermute x20, starting transfers between devices, gather_ordered(): lax.ppermute(value, axis, shift_pairs(size, shift))  24.2 us
    all_gather x1, blocking collectives, gather_ordered(): return lax.all_gather(value, axis)  17.3 us
    all_to_all x1, blocking collectives, exchange_ordered(): return lax.all_to_all(blocks, axis, 0, 0, tiled=True)  16.4 us
    ppermute x20, waiting for transfers between devices, gather_ordered(): lax.ppermute(value, axis, shift_pairs(size, shift))  14 us
    all_to_all x1, waiting for transfers between devices, exchange_ordered(): return lax.all_to_all(blocks, axis, 0, 0, tiled=True)  9.09 us
    ppermute x7, starting transfers between devices, exchange_ordered(): lax.ppermute(lax.dynamic_index_in_dim(blocks, (here + shift) % size, keep...  8.39 us
    ppermute x7, waiting for transfers between devices, exchange_ordered(): lax.ppermute(lax.dynamic_index_in_dim(blocks, (here + shift) % size, keep...  5.17 us
    all_to_all x1, starting transfers between devices, exchange_ordered(): return lax.all_to_all(blocks, axis, 0, 0, tiled=True)  4.81 us
  transfers between devices with their start and end apart: 28, of which 14 were waited for; matrix products, arithmetic and copies ran while one was open for 1% of the time, Pallas kernels for 0%

profile of v4, /device:TPU:0, one launch (start us, length us, event | category | flops | bytes accessed | tf_op | source)
XLA Modules:
  0.0 129.5 jit_solution(560180345072620045)
XLA Ops:
  2.0 2.8 %concatenate.44 = bf16[128]{0:T(256)(128)(2,1)S(1)} concatenate(bf16[1]{0:T(256)(128)(2,1)} %bitcast, bf16[16]{0:T(256)(128)(2,1)} %param.21, bf16[16]{0:T(256)(128)(2,1)} %param.25, bf16[16]{0:T(256)(128)(2,1)} %param.26, bf16[16]{0:T(256)(128)(2,1)} %param.30, bf16[63]{0:T(256)(128)(2,1)S(1)} %broadcast_in_dim.9), dimensions={0} | concatenate | bytes 512 | tf_op jit(solution)/shard_map/concatenate | solution.py:170
  4.8 4.4 %concatenate.45 = bf16[389,128]{1,0:T(8,128)(2,1)S(1)} concatenate(bf16[64,128]{1,0:T(8,128)(2,1)} %param.22, bf16[64,128]{1,0:T(8,128)(2,1)} %param.23, bf16[64,128]{1,0:T(8,128)(2,1)} %param.24, bf16[64,128]{1,0:T(8,128)(2,1)} %param.27, bf16[64,128]{1,0:T(8,128)(2,1)} %param.28, bf16[64,128]{1,0:T(8,128)(2,1)} %param.29, bf16[1,128]{1,0:T(2,128)(2,1)S(1)} %get-tuple-element.50, ...), dimensions={0} | concatenate | bytes 199168 | tf_op jit(solution)/shard_map/concatenate | solution.py:172
  9.2 17.3 %all-gather.1 = bf16[8,389,128]{2,1,0:T(8,128)(2,1)S(1)} all-gather(bf16[1,389,128]{2,1,0:T(8,128)(2,1)S(1)} %bitcast.129), channel_id=2, replica_groups=mesh['dp'=4,'fsdp'=8] {'fsdp'}, dimensions={0}, use_global_device_ids=true | all-gather | bytes 896256 | tf_op jit(solution)/shard_map/all_gather | solution.py:41
  26.5 2.5 %fusion.3 = bf16[1024,128]{1,0:T(8,128)(2,1)} fusion(bf16[1024,128]{1,0:T(8,128)(2,1)} %param.19, s32[1024]{0:T(1024)S(1)} %bitcast.158), kind=kOutput, calls=%fused_computation.11 | convolution fusion | flops 269615104 | bytes 528384 | tf_op jit(solution)/shard_map/dot_general | solution.py:197
  29.0 4.8 %all-to-all-start = ((bf16[8,128,128]{2,1,0:T(8,128)(2,1)}), bf16[8,128,128]{2,1,0:T(8,128)(2,1)S(1)}, u32[]{:S(2)}, u32[]{:S(2)}) async-start(bf16[8,128,128]{2,1,0:T(8,128)(2,1)} %bitcast.5), calls=%async_computation | async-start | bytes 524288 | tf_op jit(solution)/shard_map/all_to_all | solution.py:51
  34.4 9.1 %all-to-all-done = bf16[8,128,128]{2,1,0:T(8,128)(2,1)S(1)} async-done(((bf16[8,128,128]{2,1,0:T(8,128)(2,1)}), bf16[8,128,128]{2,1,0:T(8,128)(2,1)S(1)}, u32[]{:S(2)}, u32[]{:S(2)}) %all-to-all-start) | async-done | bytes 262176 | tf_op jit(solution)/shard_map/all_to_all | solution.py:51
  45.7 1.6 %collective-permute-start.2 = (bf16[128,256]{0,1:T(8,128)(2,1)S(1)}, bf16[128,256]{0,1:T(8,128)(2,1)S(1)}, u32[]{:S(2)}, u32[]{:S(2)}) collective-permute-start(bf16[128,256]{0,1:T(8,128)(2,1)S(1)} %pad_maximum_fusion.2), channel_id=1, source_target_pairs={{0,3},{1,4},{2,5},{3,6},{4,7},{5,0},{6,1},{7,2},{8,11},{9,12},{10,... | collective-permute-start | bytes 196616 | tf_op jit(solution)/shard_map/ppermute | solution.py:43
  47.3 2.3 %collective-permute-start.3 = (bf16[128,256]{0,1:T(8,128)(2,1)S(1)}, bf16[128,256]{0,1:T(8,128)(2,1)S(1)}, u32[]{:S(2)}, u32[]{:S(2)}) collective-permute-start(bf16[128,256]{0,1:T(8,128)(2,1)S(1)} %pad_maximum_fusion.2), channel_id=1, source_target_pairs={{0,4},{1,5},{2,6},{3,7},{4,0},{5,1},{6,2},{7,3},{8,12},{9,13},{10,... | collective-permute-start | bytes 196616 | tf_op jit(solution)/shard_map/ppermute | solution.py:43
  49.7 1.4 %collective-permute-done = bf16[128,256]{0,1:T(8,128)(2,1)S(1)} collective-permute-done((bf16[128,256]{0,1:T(8,128)(2,1)S(1)}, bf16[128,256]{0,1:T(8,128)(2,1)S(1)}, u32[]{:S(2)}, u32[]{:S(2)}) %collective-permute-start) | collective-permute-done | bytes 65568 | tf_op jit(solution)/shard_map/ppermute | solution.py:43
  52.4 4.8 %collective-permute-done.2 = bf16[128,256]{0,1:T(8,128)(2,1)S(1)} collective-permute-done((bf16[128,256]{0,1:T(8,128)(2,1)S(1)}, bf16[128,256]{0,1:T(8,128)(2,1)S(1)}, u32[]{:S(2)}, u32[]{:S(2)}) %collective-permute-start.2) | collective-permute-done | bytes 65568 | tf_op jit(solution)/shard_map/ppermute | solution.py:43
  59.5 2.0 %select_reduce_fusion = (f32[1024]{0:T(1024)S(1)}, f32[1024]{0:T(1024)S(1)}, f32[1024]{0:T(1024)S(1)}, f32[1024]{0:T(1024)S(1)}) fusion(f32[1024,1024]{0,1:T(8,128)S(1)} %get-tuple-element.60, s32[1024]{0:T(1024)S(1)} %bitcast.155, f32[1024]{0:T(1024)S(1)} %get-tuple-element.59, f32[1024,1024]{0,1:T(8,128)S(1)} %get-tuple-element.58, ...), kind=kLoop, calls=%fused_computation.2 | loop fusion | flops 9433088 | bytes 8417280 | tf_op jit(solution)/shard_map/reduce_sum | solution.py:91
  61.6 1.8 %collective-permute-start.7 = (f32[6,1024]{1,0:T(8,128)S(1)}, f32[6,1024]{1,0:T(8,128)S(1)}, u32[]{:S(2)}, u32[]{:S(2)}) collective-permute-start(f32[6,1024]{1,0:T(8,128)S(1)} %concatenate.48), channel_id=1, source_target_pairs={{0,1},{1,2},{2,3},{3,4},{4,5},{5,6},{6,7},{7,0},{8,9},{9,10},{10,1... | collective-permute-start | bytes 73736 | tf_op jit(solution)/shard_map/ppermute | solution.py:43
  63.4 2.6 %collective-permute-start.8 = (f32[6,1024]{1,0:T(8,128)S(1)}, f32[6,1024]{1,0:T(8,128)S(1)}, u32[]{:S(2)}, u32[]{:S(2)}) collective-permute-start(f32[6,1024]{1,0:T(8,128)S(1)} %concatenate.48), channel_id=1, source_target_pairs={{0,2},{1,3},{2,4},{3,5},{4,6},{5,7},{6,0},{7,1},{8,10},{9,11},{10,... | collective-permute-start | bytes 73736 | tf_op jit(solution)/shard_map/ppermute | solution.py:43
  66.2 2.7 %collective-permute-start.10 = (f32[6,1024]{1,0:T(8,128)S(1)}, f32[6,1024]{1,0:T(8,128)S(1)}, u32[]{:S(2)}, u32[]{:S(2)}) collective-permute-start(f32[6,1024]{1,0:T(8,128)S(1)} %concatenate.48), channel_id=1, source_target_pairs={{0,4},{1,5},{2,6},{3,7},{4,0},{5,1},{6,2},{7,3},{8,12},{9,13},{10,... | collective-permute-start | bytes 73736 | tf_op jit(solution)/shard_map/ppermute | solution.py:43
  69.0 2.1 %collective-permute-start.12 = (f32[6,1024]{1,0:T(8,128)S(1)}, f32[6,1024]{1,0:T(8,128)S(1)}, u32[]{:S(2)}, u32[]{:S(2)}) collective-permute-start(f32[6,1024]{1,0:T(8,128)S(1)} %concatenate.48), channel_id=1, source_target_pairs={{0,6},{1,7},{2,0},{3,1},{4,2},{5,3},{6,4},{7,5},{8,14},{9,15},{10,... | collective-permute-start | bytes 73736 | tf_op jit(solution)/shard_map/ppermute | solution.py:43
  71.1 1.3 collective-permute-start.13
  74.9 1.5 %collective-permute-start.14 = (f32[2,22]{1,0:T(2,128)S(1)}, f32[2,22]{1,0:T(2,128)S(1)}, u32[]{:S(2)}, u32[]{:S(2)}) collective-permute-start(f32[2,22]{1,0:T(2,128)S(1)} %get-tuple-element.46), channel_id=1, source_target_pairs={{0,8},{8,16},{16,24},{24,0},{1,9},{9,17},{17,25},{25,1},{2,10},{10... | collective-permute-start | bytes 536 | tf_op jit(solution)/shard_map/ppermute | solution.py:43
  76.4 1.5 %collective-permute-start.15 = (f32[2,22]{1,0:T(2,128)S(1)}, f32[2,22]{1,0:T(2,128)S(1)}, u32[]{:S(2)}, u32[]{:S(2)}) collective-permute-start(f32[2,22]{1,0:T(2,128)S(1)} %get-tuple-element.46), channel_id=1, source_target_pairs={{0,16},{8,24},{16,0},{24,8},{1,17},{9,25},{17,1},{25,9},{2,18},{10... | collective-permute-start | bytes 536 | tf_op jit(solution)/shard_map/ppermute | solution.py:43
  77.9 1.4 %collective-permute-start.16 = (f32[2,22]{1,0:T(2,128)S(1)}, f32[2,22]{1,0:T(2,128)S(1)}, u32[]{:S(2)}, u32[]{:S(2)}) collective-permute-start(f32[2,22]{1,0:T(2,128)S(1)} %get-tuple-element.46), channel_id=1, source_target_pairs={{0,24},{8,0},{16,8},{24,16},{1,25},{9,1},{17,9},{25,17},{2,26},{10... | collective-permute-start | bytes 536 | tf_op jit(solution)/shard_map/ppermute | solution.py:43
  80.0 1.5 %collective-permute-done.16 = f32[2,22]{1,0:T(2,128)S(1)} collective-permute-done((f32[2,22]{1,0:T(2,128)S(1)}, f32[2,22]{1,0:T(2,128)S(1)}, u32[]{:S(2)}, u32[]{:S(2)}) %collective-permute-start.16) | collective-permute-done | bytes 208 | tf_op jit(solution)/shard_map/ppermute | solution.py:43
  82.2 1.2 fusion.41
  83.4 1.8 %bitcast_divide_fusion = (f32[22]{0:T(128)S(1)}, f32[22]{0:T(128)}) fusion(f32[2,22]{1,0:T(2,128)S(1)} %fusion.32, f32[]{:T(128)} %fusion.41, f32[22]{0:T(128)S(1)} %get-tuple-element.19, f32[]{:T(128)} %get-tuple-element.18), kind=kLoop, calls=%fused_computation.133 | loop fusion | flops 132 | bytes 360 | tf_op jit(solution)/shard_map/div | solution.py:240
  86.0 3.5 %fusion.2 = f32[1024,128]{1,0:T(8,128)S(1)} fusion(bf16[1024,128]{1,0:T(8,128)(2,1)S(1)} %copy-done, f32[1024,1024]{0,1:T(8,128)} %copy-done.1, f32[1024]{0:T(1024)S(1)} %bitcast.159, f32[1024]{0:T(1024)S(1)} %broadcast_bitcast_fusion, s32[1024]{0:T(1024)S(1)} %bitcast.156), kind=kOutput, calls=%fused_computation.10 | convolution fusion | flops 274726912 | bytes 4993024 | tf_op jit(solution)/shard_map/dot_general | solution.py:113
  90.5 2.6 %collective-permute-start.19 = (f32[128,128]{1,0:T(8,128)S(1)}, f32[128,128]{1,0:T(8,128)S(1)}, u32[]{:S(2)}, u32[]{:S(2)}) collective-permute-start(f32[128,128]{1,0:T(8,128)S(1)} %get-tuple-element.32), channel_id=1, source_target_pairs={{0,3},{1,4},{2,5},{3,6},{4,7},{5,0},{6,1},{7,2},{8,11},{9,12},{10,... | collective-permute-start | bytes 196616 | tf_op jit(solution)/shard_map/ppermute | solution.py:54
  94.2 1.2 collective-permute-start.21
  96.5 1.5 %collective-permute-start.23 = (f32[128,128]{1,0:T(8,128)S(1)}, f32[128,128]{1,0:T(8,128)S(1)}, u32[]{:S(2)}, u32[]{:S(2)}) collective-permute-start(f32[128,128]{1,0:T(8,128)S(1)} %get-tuple-element.28), channel_id=1, source_target_pairs={{0,7},{1,0},{2,1},{3,2},{4,3},{5,4},{6,5},{7,6},{8,15},{9,8},{10,9... | collective-permute-start | bytes 196616 | tf_op jit(solution)/shard_map/ppermute | solution.py:54
  97.9 3.4 %collective-permute-done.19 = f32[128,128]{1,0:T(8,128)S(1)} collective-permute-done((f32[128,128]{1,0:T(8,128)S(1)}, f32[128,128]{1,0:T(8,128)S(1)}, u32[]{:S(2)}, u32[]{:S(2)}) %collective-permute-start.19) | collective-permute-done | bytes 65568 | tf_op jit(solution)/shard_map/ppermute | solution.py:54
  101.6 1.5 %collective-permute-done.22 = f32[128,128]{1,0:T(8,128)S(1)} collective-permute-done((f32[128,128]{1,0:T(8,128)S(1)}, f32[128,128]{1,0:T(8,128)S(1)}, u32[]{:S(2)}, u32[]{:S(2)}) %collective-permute-start.22) | collective-permute-done | bytes 65568 | tf_op jit(solution)/shard_map/ppermute | solution.py:54
  104.6 16.4 %all_to_all.10 = bf16[8,64,384]{2,1,0:T(8,128)(2,1)S(1)} all-to-all(bf16[8,64,384]{2,1,0:T(8,128)(2,1)S(1)} %pad_maximum_fusion), channel_id=1, replica_groups=mesh['dp'=4,'fsdp'=8] {'fsdp'}, dimensions={0} | all-to-all | bytes 786432 | tf_op jit(solution)/shard_map/all_to_all | solution.py:51
  121.1 1.4 %collective-permute-start.24 = (f32[64,384]{1,0:T(8,128)S(1)}, f32[64,384]{1,0:T(8,128)S(1)}, u32[]{:S(2)}, u32[]{:S(2)}) collective-permute-start(f32[64,384]{1,0:T(8,128)S(1)} %convert_reduce_fusion), channel_id=1, source_target_pairs={{0,8},{8,16},{16,24},{24,0},{1,9},{9,17},{17,25},{25,1},{2,10},{10... | collective-permute-start | bytes 294920 | tf_op jit(solution)/shard_map/ppermute | solution.py:43
  122.5 1.5 %collective-permute-start.25 = (f32[64,384]{1,0:T(8,128)S(1)}, f32[64,384]{1,0:T(8,128)S(1)}, u32[]{:S(2)}, u32[]{:S(2)}) collective-permute-start(f32[64,384]{1,0:T(8,128)S(1)} %convert_reduce_fusion), channel_id=1, source_target_pairs={{0,16},{8,24},{16,0},{24,8},{1,17},{9,25},{17,1},{25,9},{2,18},{10... | collective-permute-start | bytes 294920 | tf_op jit(solution)/shard_map/ppermute | solution.py:43
  124.6 3.1 %collective-permute-done.24 = f32[64,384]{1,0:T(8,128)S(1)} collective-permute-done((f32[64,384]{1,0:T(8,128)S(1)}, f32[64,384]{1,0:T(8,128)S(1)}, u32[]{:S(2)}, u32[]{:S(2)}) %collective-permute-start.24) | collective-permute-done | bytes 98336 | tf_op jit(solution)/shard_map/ppermute | solution.py:43
  (134 shorter events, 18.9 us)
Async XLA Ops:
  0.6 57.4 %copy-start = (bf16[1024,128]{1,0:T(8,128)(2,1)S(1)}, bf16[1024,128]{1,0:T(8,128)(2,1)}, u32[]{:S(2)}) copy-start(bf16[1024,128]{1,0:T(8,128)(2,1)} %param.20) | copy-start | bytes 786436
  29.0 14.6 %all-to-all-start = ((bf16[8,128,128]{2,1,0:T(8,128)(2,1)}), bf16[8,128,128]{2,1,0:T(8,128)(2,1)S(1)}, u32[]{:S(2)}, u32[]{:S(2)}) async-start(bf16[8,128,128]{2,1,0:T(8,128)(2,1)} %bitcast.5), calls=%async_computation | async-start | bytes 524288 | tf_op jit(solution)/shard_map/all_to_all | solution.py:51
  45.4 5.7 %collective-permute-start = (bf16[128,256]{0,1:T(8,128)(2,1)S(1)}, bf16[128,256]{0,1:T(8,128)(2,1)S(1)}, u32[]{:S(2)}, u32[]{:S(2)}) collective-permute-start(bf16[128,256]{0,1:T(8,128)(2,1)S(1)} %pad_maximum_fusion.2), channel_id=1, source_target_pairs={{0,1},{1,2},{2,3},{3,4},{4,5},{5,6},{6,7},{7,0},{8,9},{9,10},{10,1... | collective-permute-start | bytes 196616 | tf_op jit(solution)/shard_map/ppermute | solution.py:43
  45.4 6.9 %collective-permute-start.1 = (bf16[128,256]{0,1:T(8,128)(2,1)S(1)}, bf16[128,256]{0,1:T(8,128)(2,1)S(1)}, u32[]{:S(2)}, u32[]{:S(2)}) collective-permute-start(bf16[128,256]{0,1:T(8,128)(2,1)S(1)} %pad_maximum_fusion.2), channel_id=1, source_target_pairs={{0,2},{1,3},{2,4},{3,5},{4,6},{5,7},{6,0},{7,1},{8,10},{9,11},{10,... | collective-permute-start | bytes 196616 | tf_op jit(solution)/shard_map/ppermute | solution.py:43
  45.7 11.6 %collective-permute-start.2 = (bf16[128,256]{0,1:T(8,128)(2,1)S(1)}, bf16[128,256]{0,1:T(8,128)(2,1)S(1)}, u32[]{:S(2)}, u32[]{:S(2)}) collective-permute-start(bf16[128,256]{0,1:T(8,128)(2,1)S(1)} %pad_maximum_fusion.2), channel_id=1, source_target_pairs={{0,3},{1,4},{2,5},{3,6},{4,7},{5,0},{6,1},{7,2},{8,11},{9,12},{10,... | collective-permute-start | bytes 196616 | tf_op jit(solution)/shard_map/ppermute | solution.py:43
  47.3 10.2 %collective-permute-start.3 = (bf16[128,256]{0,1:T(8,128)(2,1)S(1)}, bf16[128,256]{0,1:T(8,128)(2,1)S(1)}, u32[]{:S(2)}, u32[]{:S(2)}) collective-permute-start(bf16[128,256]{0,1:T(8,128)(2,1)S(1)} %pad_maximum_fusion.2), channel_id=1, source_target_pairs={{0,4},{1,5},{2,6},{3,7},{4,0},{5,1},{6,2},{7,3},{8,12},{9,13},{10,... | collective-permute-start | bytes 196616 | tf_op jit(solution)/shard_map/ppermute | solution.py:43
  49.6 7.9 %collective-permute-start.4 = (bf16[128,256]{0,1:T(8,128)(2,1)S(1)}, bf16[128,256]{0,1:T(8,128)(2,1)S(1)}, u32[]{:S(2)}, u32[]{:S(2)}) collective-permute-start(bf16[128,256]{0,1:T(8,128)(2,1)S(1)} %pad_maximum_fusion.2), channel_id=1, source_target_pairs={{0,5},{1,6},{2,7},{3,0},{4,1},{5,2},{6,3},{7,4},{8,13},{9,14},{10,... | collective-permute-start | bytes 196616 | tf_op jit(solution)/shard_map/ppermute | solution.py:43
  51.1 6.4 %collective-permute-start.5 = (bf16[128,256]{0,1:T(8,128)(2,1)S(1)}, bf16[128,256]{0,1:T(8,128)(2,1)S(1)}, u32[]{:S(2)}, u32[]{:S(2)}) collective-permute-start(bf16[128,256]{0,1:T(8,128)(2,1)S(1)} %pad_maximum_fusion.2), channel_id=1, source_target_pairs={{0,6},{1,7},{2,0},{3,1},{4,2},{5,3},{6,4},{7,5},{8,14},{9,15},{10,... | collective-permute-start | bytes 196616 | tf_op jit(solution)/shard_map/ppermute | solution.py:43
  52.3 5.2 %collective-permute-start.6 = (bf16[128,256]{0,1:T(8,128)(2,1)S(1)}, bf16[128,256]{0,1:T(8,128)(2,1)S(1)}, u32[]{:S(2)}, u32[]{:S(2)}) collective-permute-start(bf16[128,256]{0,1:T(8,128)(2,1)S(1)} %pad_maximum_fusion.2), channel_id=1, source_target_pairs={{0,7},{1,0},{2,1},{3,2},{4,3},{5,4},{6,5},{7,6},{8,15},{9,8},{10,9... | collective-permute-start | bytes 196616 | tf_op jit(solution)/shard_map/ppermute | solution.py:43
  59.5 2.0 %copy-start.1 = (f32[1024,1024]{0,1:T(8,128)}, f32[1024,1024]{0,1:T(8,128)S(1)}, u32[]{:S(2)}) copy-start(f32[1024,1024]{0,1:T(8,128)S(1)} %get-tuple-element.60) | copy-start | bytes 12582916
  59.5 22.1 %copy-start.2 = (f32[22]{0:T(128)S(1)}, f32[22]{0:T(128)}, u32[]{:S(2)}) copy-start(f32[22]{0:T(128)} %param.31) | copy-start | bytes 268
  61.6 7.4 %collective-permute-start.7 = (f32[6,1024]{1,0:T(8,128)S(1)}, f32[6,1024]{1,0:T(8,128)S(1)}, u32[]{:S(2)}, u32[]{:S(2)}) collective-permute-start(f32[6,1024]{1,0:T(8,128)S(1)} %concatenate.48), channel_id=1, source_target_pairs={{0,1},{1,2},{2,3},{3,4},{4,5},{5,6},{6,7},{7,0},{8,9},{9,10},{10,1... | collective-permute-start | bytes 73736 | tf_op jit(solution)/shard_map/ppermute | solution.py:43
  63.4 7.7 %collective-permute-start.8 = (f32[6,1024]{1,0:T(8,128)S(1)}, f32[6,1024]{1,0:T(8,128)S(1)}, u32[]{:S(2)}, u32[]{:S(2)}) collective-permute-start(f32[6,1024]{1,0:T(8,128)S(1)} %concatenate.48), channel_id=1, source_target_pairs={{0,2},{1,3},{2,4},{3,5},{4,6},{5,7},{6,0},{7,1},{8,10},{9,11},{10,... | collective-permute-start | bytes 73736 | tf_op jit(solution)/shard_map/ppermute | solution.py:43
  66.1 6.3 %collective-permute-start.9 = (f32[6,1024]{1,0:T(8,128)S(1)}, f32[6,1024]{1,0:T(8,128)S(1)}, u32[]{:S(2)}, u32[]{:S(2)}) collective-permute-start(f32[6,1024]{1,0:T(8,128)S(1)} %concatenate.48), channel_id=1, source_target_pairs={{0,3},{1,4},{2,5},{3,6},{4,7},{5,0},{6,1},{7,2},{8,11},{9,12},{10,... | collective-permute-start | bytes 73736 | tf_op jit(solution)/shard_map/ppermute | solution.py:43
  66.2 6.3 %collective-permute-start.10 = (f32[6,1024]{1,0:T(8,128)S(1)}, f32[6,1024]{1,0:T(8,128)S(1)}, u32[]{:S(2)}, u32[]{:S(2)}) collective-permute-start(f32[6,1024]{1,0:T(8,128)S(1)} %concatenate.48), channel_id=1, source_target_pairs={{0,4},{1,5},{2,6},{3,7},{4,0},{5,1},{6,2},{7,3},{8,12},{9,13},{10,... | collective-permute-start | bytes 73736 | tf_op jit(solution)/shard_map/ppermute | solution.py:43
  68.9 3.6 %collective-permute-start.11 = (f32[6,1024]{1,0:T(8,128)S(1)}, f32[6,1024]{1,0:T(8,128)S(1)}, u32[]{:S(2)}, u32[]{:S(2)}) collective-permute-start(f32[6,1024]{1,0:T(8,128)S(1)} %concatenate.48), channel_id=1, source_target_pairs={{0,5},{1,6},{2,7},{3,0},{4,1},{5,2},{6,3},{7,4},{8,13},{9,14},{10,... | collective-permute-start | bytes 73736 | tf_op jit(solution)/shard_map/ppermute | solution.py:43
  69.0 4.1 %collective-permute-start.12 = (f32[6,1024]{1,0:T(8,128)S(1)}, f32[6,1024]{1,0:T(8,128)S(1)}, u32[]{:S(2)}, u32[]{:S(2)}) collective-permute-start(f32[6,1024]{1,0:T(8,128)S(1)} %concatenate.48), channel_id=1, source_target_pairs={{0,6},{1,7},{2,0},{3,1},{4,2},{5,3},{6,4},{7,5},{8,14},{9,15},{10,... | collective-permute-start | bytes 73736 | tf_op jit(solution)/shard_map/ppermute | solution.py:43
  71.1 2.9 %collective-permute-start.13 = (f32[6,1024]{1,0:T(8,128)S(1)}, f32[6,1024]{1,0:T(8,128)S(1)}, u32[]{:S(2)}, u32[]{:S(2)}) collective-permute-start(f32[6,1024]{1,0:T(8,128)S(1)} %concatenate.48), channel_id=1, source_target_pairs={{0,7},{1,0},{2,1},{3,2},{4,3},{5,4},{6,5},{7,6},{8,15},{9,8},{10,9... | collective-permute-start | bytes 73736 | tf_op jit(solution)/shard_map/ppermute | solution.py:43
  74.9 4.5 %collective-permute-start.14 = (f32[2,22]{1,0:T(2,128)S(1)}, f32[2,22]{1,0:T(2,128)S(1)}, u32[]{:S(2)}, u32[]{:S(2)}) collective-permute-start(f32[2,22]{1,0:T(2,128)S(1)} %get-tuple-element.46), channel_id=1, source_target_pairs={{0,8},{8,16},{16,24},{24,0},{1,9},{9,17},{17,25},{25,1},{2,10},{10... | collective-permute-start | bytes 536 | tf_op jit(solution)/shard_map/ppermute | solution.py:43
  76.4 3.6 %collective-permute-start.15 = (f32[2,22]{1,0:T(2,128)S(1)}, f32[2,22]{1,0:T(2,128)S(1)}, u32[]{:S(2)}, u32[]{:S(2)}) collective-permute-start(f32[2,22]{1,0:T(2,128)S(1)} %get-tuple-element.46), channel_id=1, source_target_pairs={{0,16},{8,24},{16,0},{24,8},{1,17},{9,25},{17,1},{25,9},{2,18},{10... | collective-permute-start | bytes 536 | tf_op jit(solution)/shard_map/ppermute | solution.py:43
  77.9 3.6 %collective-permute-start.16 = (f32[2,22]{1,0:T(2,128)S(1)}, f32[2,22]{1,0:T(2,128)S(1)}, u32[]{:S(2)}, u32[]{:S(2)}) collective-permute-start(f32[2,22]{1,0:T(2,128)S(1)} %get-tuple-element.46), channel_id=1, source_target_pairs={{0,24},{8,0},{16,8},{24,16},{1,25},{9,1},{17,9},{25,17},{2,26},{10... | collective-permute-start | bytes 536 | tf_op jit(solution)/shard_map/ppermute | solution.py:43
  89.5 5.9 %collective-permute-start.17 = (f32[128,128]{1,0:T(8,128)S(1)}, f32[128,128]{1,0:T(8,128)S(1)}, u32[]{:S(2)}, u32[]{:S(2)}) collective-permute-start(f32[128,128]{1,0:T(8,128)S(1)} %get-tuple-element.34), channel_id=1, source_target_pairs={{0,1},{1,2},{2,3},{3,4},{4,5},{5,6},{6,7},{7,0},{8,9},{9,10},{10,1... | collective-permute-start | bytes 196616 | tf_op jit(solution)/shard_map/ppermute | solution.py:54
  89.6 6.9 %collective-permute-start.18 = (f32[128,128]{1,0:T(8,128)S(1)}, f32[128,128]{1,0:T(8,128)S(1)}, u32[]{:S(2)}, u32[]{:S(2)}) collective-permute-start(f32[128,128]{1,0:T(8,128)S(1)} %get-tuple-element.33), channel_id=1, source_target_pairs={{0,2},{1,3},{2,4},{3,5},{4,6},{5,7},{6,0},{7,1},{8,10},{9,11},{10,... | collective-permute-start | bytes 196616 | tf_op jit(solution)/shard_map/ppermute | solution.py:54
  90.5 10.9 %collective-permute-start.19 = (f32[128,128]{1,0:T(8,128)S(1)}, f32[128,128]{1,0:T(8,128)S(1)}, u32[]{:S(2)}, u32[]{:S(2)}) collective-permute-start(f32[128,128]{1,0:T(8,128)S(1)} %get-tuple-element.32), channel_id=1, source_target_pairs={{0,3},{1,4},{2,5},{3,6},{4,7},{5,0},{6,1},{7,2},{8,11},{9,12},{10,... | collective-permute-start | bytes 196616 | tf_op jit(solution)/shard_map/ppermute | solution.py:54
  93.0 8.5 %collective-permute-start.20 = (f32[128,128]{1,0:T(8,128)S(1)}, f32[128,128]{1,0:T(8,128)S(1)}, u32[]{:S(2)}, u32[]{:S(2)}) collective-permute-start(f32[128,128]{1,0:T(8,128)S(1)} %get-tuple-element.31), channel_id=1, source_target_pairs={{0,4},{1,5},{2,6},{3,7},{4,0},{5,1},{6,2},{7,3},{8,12},{9,13},{10,... | collective-permute-start | bytes 196616 | tf_op jit(solution)/shard_map/ppermute | solution.py:54
  94.2 7.4 %collective-permute-start.21 = (f32[128,128]{1,0:T(8,128)S(1)}, f32[128,128]{1,0:T(8,128)S(1)}, u32[]{:S(2)}, u32[]{:S(2)}) collective-permute-start(f32[128,128]{1,0:T(8,128)S(1)} %get-tuple-element.30), channel_id=1, source_target_pairs={{0,5},{1,6},{2,7},{3,0},{4,1},{5,2},{6,3},{7,4},{8,13},{9,14},{10,... | collective-permute-start | bytes 196616 | tf_op jit(solution)/shard_map/ppermute | solution.py:54
  95.5 7.7 %collective-permute-start.22 = (f32[128,128]{1,0:T(8,128)S(1)}, f32[128,128]{1,0:T(8,128)S(1)}, u32[]{:S(2)}, u32[]{:S(2)}) collective-permute-start(f32[128,128]{1,0:T(8,128)S(1)} %get-tuple-element.29), channel_id=1, source_target_pairs={{0,6},{1,7},{2,0},{3,1},{4,2},{5,3},{6,4},{7,5},{8,14},{9,15},{10,... | collective-permute-start | bytes 196616 | tf_op jit(solution)/shard_map/ppermute | solution.py:54
  96.5 6.7 %collective-permute-start.23 = (f32[128,128]{1,0:T(8,128)S(1)}, f32[128,128]{1,0:T(8,128)S(1)}, u32[]{:S(2)}, u32[]{:S(2)}) collective-permute-start(f32[128,128]{1,0:T(8,128)S(1)} %get-tuple-element.28), channel_id=1, source_target_pairs={{0,7},{1,0},{2,1},{3,2},{4,3},{5,4},{6,5},{7,6},{8,15},{9,8},{10,9... | collective-permute-start | bytes 196616 | tf_op jit(solution)/shard_map/ppermute | solution.py:54
  121.1 6.6 %collective-permute-start.24 = (f32[64,384]{1,0:T(8,128)S(1)}, f32[64,384]{1,0:T(8,128)S(1)}, u32[]{:S(2)}, u32[]{:S(2)}) collective-permute-start(f32[64,384]{1,0:T(8,128)S(1)} %convert_reduce_fusion), channel_id=1, source_target_pairs={{0,8},{8,16},{16,24},{24,0},{1,9},{9,17},{17,25},{25,1},{2,10},{10... | collective-permute-start | bytes 294920 | tf_op jit(solution)/shard_map/ppermute | solution.py:43
  122.5 6.0 %collective-permute-start.25 = (f32[64,384]{1,0:T(8,128)S(1)}, f32[64,384]{1,0:T(8,128)S(1)}, u32[]{:S(2)}, u32[]{:S(2)}) collective-permute-start(f32[64,384]{1,0:T(8,128)S(1)} %convert_reduce_fusion), channel_id=1, source_target_pairs={{0,16},{8,24},{16,0},{24,8},{1,17},{9,25},{17,1},{25,9},{2,18},{10... | collective-permute-start | bytes 294920 | tf_op jit(solution)/shard_map/ppermute | solution.py:43
  124.1 4.6 %collective-permute-start.26 = (f32[64,384]{1,0:T(8,128)S(1)}, f32[64,384]{1,0:T(8,128)S(1)}, u32[]{:S(2)}, u32[]{:S(2)}) collective-permute-start(f32[64,384]{1,0:T(8,128)S(1)} %convert_reduce_fusion), channel_id=1, source_target_pairs={{0,24},{8,0},{16,8},{24,16},{1,25},{9,1},{17,9},{25,17},{2,26},{10... | collective-permute-start | bytes 294920 | tf_op jit(solution)/shard_map/ppermute | solution.py:43

commit v5 on v4

--- a/solution.py
+++ b/solution.py
@@ -157,26 +157,29 @@
 
     tokens = token_ids.reshape(-1)
     targets = target_ids.reshape(-1)
-    id_parts = jnp.stack(
-        [tokens // ID_BASE, tokens % ID_BASE, targets // ID_BASE, targets % ID_BASE]
-    ).astype(jnp.bfloat16)
     matrices = (ref_gate, ref_up, ref_down, prx_gate, prx_up, prx_down)
     gains = (ref_norm1, ref_norm2, prx_norm1, prx_norm2)
-    id_rows = id_parts.reshape(-1, width)
-    extra = [domain_ids.reshape(-1).astype(jnp.bfloat16)] + list(gains)
+    id_count = 4 * per_device // width
     extra_size = rows_here + len(gains) * gain_here
-    extra_rows = -(-extra_size // width)
-    extra.append(jnp.zeros((extra_rows * width - extra_size,), jnp.bfloat16))
-    extra_rows = jnp.concatenate(extra).reshape(extra_rows, width)
+    extra_count = -(-extra_size // width)
+    small_count = id_count + extra_count
+    id_pieces = (tokens // ID_BASE, tokens % ID_BASE, targets // ID_BASE, targets % ID_BASE)
+    small = jnp.zeros((small_count * width,), jnp.bfloat16)
+    start = 0
+    for piece in id_pieces + (domain_ids.reshape(-1),) + gains:
+        piece = piece.astype(jnp.bfloat16)
+        small = small + jnp.pad(piece, (start, small_count * width - start - piece.shape[0]))
+        start += piece.shape[0]
+    id_rows = small.reshape(small_count, width)[:id_count]
+    extra_rows = small.reshape(small_count, width)[id_count:]
     matrix_rows = len(matrices) * unit_rows
-    packed = jnp.concatenate(list(matrices) + [id_rows, extra_rows], axis=0)
+    packed = jnp.concatenate(list(matrices) + [small.reshape(small_count, width)], axis=0)
     gathered = gather_ordered(packed, "fsdp", True)
     full_matrices = [
         gathered[:, index * unit_rows : (index + 1) * unit_rows].reshape(-1, width)
         for index in range(len(matrices))
     ]
     offset = matrix_rows
-    id_count = id_rows.shape[0]
     group_ids = gathered[:, offset : offset + id_count].astype(jnp.int32)
     group_ids = group_ids.reshape(fsdp_size, 4, per_device)
     group_tokens = (group_ids[:, 0] * ID_BASE + group_ids[:, 1]).reshape(-1)

time: 130 us -> 128 us (0.985)
  local copies, waits for them, and re-layouts: 10.4 us -> 7.62 us
    concatenate x2 -> x0, local copies, waits for them, and re-layouts: 7.15 us -> none  [the longest x1 4.37 us: body(): packed = jnp.concatenate(list(matrices) + [id_rows, extra_rows], axis=0)]
    unnamed x19 -> x25, local copies, waits for them, and re-layouts: 0.14 us -> 4.52 us
where the time goes in v5:
time: 128 us; the launch traced here: 127 us
  starting transfers between devices  37.4 us (29%)
  blocking collectives  33.7 us (26%)
  waiting for transfers between devices  28.2 us (22%)
  matrix products  9.58 us (7%)
  other arithmetic  9.11 us (7%)
  local copies, waits for them, and re-layouts  7.62 us (6%)
  between operations  1.85 us (1%)
    ppermute x20, starting transfers between devices, gather_ordered(): lax.ppermute(value, axis, shift_pairs(size, shift))  24.2 us
    all_gather x1, blocking collectives, gather_ordered(): return lax.all_gather(value, axis)  17.3 us
    all_to_all x1, blocking collectives, exchange_ordered(): return lax.all_to_all(blocks, axis, 0, 0, tiled=True)  16.4 us
    ppermute x20, waiting for transfers between devices, gather_ordered(): lax.ppermute(value, axis, shift_pairs(size, shift))  14 us
    all_to_all x1, waiting for transfers between devices, exchange_ordered(): return lax.all_to_all(blocks, axis, 0, 0, tiled=True)  9.09 us
    ppermute x7, starting transfers between devices, exchange_ordered(): lax.ppermute(lax.dynamic_index_in_dim(blocks, (here + shift) % size, keep...  8.39 us
    ppermute x7, waiting for transfers between devices, exchange_ordered(): lax.ppermute(lax.dynamic_index_in_dim(blocks, (here + shift) % size, keep...  5.17 us
    all_to_all x1, starting transfers between devices, exchange_ordered(): return lax.all_to_all(blocks, axis, 0, 0, tiled=True)  4.81 us
  transfers between devices with their start and end apart: 28, of which 14 were waited for; matrix products, arithmetic and copies ran while one was open for 1% of the time, Pallas kernels for 0%

profile of v5, /device:TPU:0, one launch (start us, length us, event | category | flops | bytes accessed | tf_op | source)
XLA Modules:
  0.0 127.4 jit_solution(17965605318509641350)
XLA Ops:
  7.2 17.3 %all-gather.1 = bf16[8,389,128]{2,1,0:T(8,128)(2,1)S(1)} all-gather(bf16[1,389,128]{2,1,0:T(8,128)(2,1)S(1)} %bitcast.165), channel_id=2, replica_groups=mesh['dp'=4,'fsdp'=8] {'fsdp'}, dimensions={0}, use_global_device_ids=true | all-gather | bytes 896256 | tf_op jit(solution)/shard_map/all_gather | solution.py:41
  24.5 2.5 %fusion.3 = bf16[1024,128]{1,0:T(8,128)(2,1)} fusion(bf16[1024,128]{1,0:T(8,128)(2,1)} %param.19, s32[1024]{0:T(1024)S(1)} %bitcast.193), kind=kOutput, calls=%fused_computation.11 | convolution fusion | flops 269615104 | bytes 528384 | tf_op jit(solution)/shard_map/dot_general | solution.py:200
  26.9 4.8 %all-to-all-start = ((bf16[8,128,128]{2,1,0:T(8,128)(2,1)}), bf16[8,128,128]{2,1,0:T(8,128)(2,1)S(1)}, u32[]{:S(2)}, u32[]{:S(2)}) async-start(bf16[8,128,128]{2,1,0:T(8,128)(2,1)} %bitcast.7), calls=%async_computation | async-start | bytes 524288 | tf_op jit(solution)/shard_map/all_to_all | solution.py:51
  32.4 9.1 %all-to-all-done = bf16[8,128,128]{2,1,0:T(8,128)(2,1)S(1)} async-done(((bf16[8,128,128]{2,1,0:T(8,128)(2,1)}), bf16[8,128,128]{2,1,0:T(8,128)(2,1)S(1)}, u32[]{:S(2)}, u32[]{:S(2)}) %all-to-all-start) | async-done | bytes 262176 | tf_op jit(solution)/shard_map/all_to_all | solution.py:51
  43.6 1.6 %collective-permute-start.2 = (bf16[128,256]{0,1:T(8,128)(2,1)S(1)}, bf16[128,256]{0,1:T(8,128)(2,1)S(1)}, u32[]{:S(2)}, u32[]{:S(2)}) collective-permute-start(bf16[128,256]{0,1:T(8,128)(2,1)S(1)} %pad_maximum_fusion.2), channel_id=1, source_target_pairs={{0,3},{1,4},{2,5},{3,6},{4,7},{5,0},{6,1},{7,2},{8,11},{9,12},{10,... | collective-permute-start | bytes 196616 | tf_op jit(solution)/shard_map/ppermute | solution.py:43
  45.2 2.3 %collective-permute-start.3 = (bf16[128,256]{0,1:T(8,128)(2,1)S(1)}, bf16[128,256]{0,1:T(8,128)(2,1)S(1)}, u32[]{:S(2)}, u32[]{:S(2)}) collective-permute-start(bf16[128,256]{0,1:T(8,128)(2,1)S(1)} %pad_maximum_fusion.2), channel_id=1, source_target_pairs={{0,4},{1,5},{2,6},{3,7},{4,0},{5,1},{6,2},{7,3},{8,12},{9,13},{10,... | collective-permute-start | bytes 196616 | tf_op jit(solution)/shard_map/ppermute | solution.py:43
  47.7 1.4 %collective-permute-done = bf16[128,256]{0,1:T(8,128)(2,1)S(1)} collective-permute-done((bf16[128,256]{0,1:T(8,128)(2,1)S(1)}, bf16[128,256]{0,1:T(8,128)(2,1)S(1)}, u32[]{:S(2)}, u32[]{:S(2)}) %collective-permute-start) | collective-permute-done | bytes 65568 | tf_op jit(solution)/shard_map/ppermute | solution.py:43
  49.1 1.2 collective-permute-start.5
  50.4 4.8 %collective-permute-done.2 = bf16[128,256]{0,1:T(8,128)(2,1)S(1)} collective-permute-done((bf16[128,256]{0,1:T(8,128)(2,1)S(1)}, bf16[128,256]{0,1:T(8,128)(2,1)S(1)}, u32[]{:S(2)}, u32[]{:S(2)}) %collective-permute-start.2) | collective-permute-done | bytes 65568 | tf_op jit(solution)/shard_map/ppermute | solution.py:43
  57.5 2.0 %select_reduce_fusion = (f32[1024]{0:T(1024)S(1)}, f32[1024]{0:T(1024)S(1)}, f32[1024]{0:T(1024)S(1)}, f32[1024]{0:T(1024)S(1)}) fusion(f32[1024,1024]{0,1:T(8,128)S(1)} %get-tuple-element.60, s32[1024]{0:T(1024)S(1)} %bitcast.190, f32[1024]{0:T(1024)S(1)} %get-tuple-element.59, f32[1024,1024]{0,1:T(8,128)S(1)} %get-tuple-element.58, ...), kind=kLoop, calls=%fused_computation.2 | loop fusion | flops 9433088 | bytes 8417280 | tf_op jit(solution)/shard_map/reduce_sum | solution.py:91
  59.5 1.8 %collective-permute-start.7 = (f32[6,1024]{1,0:T(8,128)S(1)}, f32[6,1024]{1,0:T(8,128)S(1)}, u32[]{:S(2)}, u32[]{:S(2)}) collective-permute-start(f32[6,1024]{1,0:T(8,128)S(1)} %concatenate.43), channel_id=1, source_target_pairs={{0,1},{1,2},{2,3},{3,4},{4,5},{5,6},{6,7},{7,0},{8,9},{9,10},{10,1... | collective-permute-start | bytes 73736 | tf_op jit(solution)/shard_map/ppermute | solution.py:43
  61.4 2.6 %collective-permute-start.8 = (f32[6,1024]{1,0:T(8,128)S(1)}, f32[6,1024]{1,0:T(8,128)S(1)}, u32[]{:S(2)}, u32[]{:S(2)}) collective-permute-start(f32[6,1024]{1,0:T(8,128)S(1)} %concatenate.43), channel_id=1, source_target_pairs={{0,2},{1,3},{2,4},{3,5},{4,6},{5,7},{6,0},{7,1},{8,10},{9,11},{10,... | collective-permute-start | bytes 73736 | tf_op jit(solution)/shard_map/ppermute | solution.py:43
  64.2 2.7 %collective-permute-start.10 = (f32[6,1024]{1,0:T(8,128)S(1)}, f32[6,1024]{1,0:T(8,128)S(1)}, u32[]{:S(2)}, u32[]{:S(2)}) collective-permute-start(f32[6,1024]{1,0:T(8,128)S(1)} %concatenate.43), channel_id=1, source_target_pairs={{0,4},{1,5},{2,6},{3,7},{4,0},{5,1},{6,2},{7,3},{8,12},{9,13},{10,... | collective-permute-start | bytes 73736 | tf_op jit(solution)/shard_map/ppermute | solution.py:43
  67.0 2.1 %collective-permute-start.12 = (f32[6,1024]{1,0:T(8,128)S(1)}, f32[6,1024]{1,0:T(8,128)S(1)}, u32[]{:S(2)}, u32[]{:S(2)}) collective-permute-start(f32[6,1024]{1,0:T(8,128)S(1)} %concatenate.43), channel_id=1, source_target_pairs={{0,6},{1,7},{2,0},{3,1},{4,2},{5,3},{6,4},{7,5},{8,14},{9,15},{10,... | collective-permute-start | bytes 73736 | tf_op jit(solution)/shard_map/ppermute | solution.py:43
  69.0 1.3 collective-permute-start.13
  72.9 1.5 %collective-permute-start.14 = (f32[2,22]{1,0:T(2,128)S(1)}, f32[2,22]{1,0:T(2,128)S(1)}, u32[]{:S(2)}, u32[]{:S(2)}) collective-permute-start(f32[2,22]{1,0:T(2,128)S(1)} %get-tuple-element.46), channel_id=1, source_target_pairs={{0,8},{8,16},{16,24},{24,0},{1,9},{9,17},{17,25},{25,1},{2,10},{10... | collective-permute-start | bytes 536 | tf_op jit(solution)/shard_map/ppermute | solution.py:43
  74.4 1.5 %collective-permute-start.15 = (f32[2,22]{1,0:T(2,128)S(1)}, f32[2,22]{1,0:T(2,128)S(1)}, u32[]{:S(2)}, u32[]{:S(2)}) collective-permute-start(f32[2,22]{1,0:T(2,128)S(1)} %get-tuple-element.46), channel_id=1, source_target_pairs={{0,16},{8,24},{16,0},{24,8},{1,17},{9,25},{17,1},{25,9},{2,18},{10... | collective-permute-start | bytes 536 | tf_op jit(solution)/shard_map/ppermute | solution.py:43
  75.9 1.4 %collective-permute-start.16 = (f32[2,22]{1,0:T(2,128)S(1)}, f32[2,22]{1,0:T(2,128)S(1)}, u32[]{:S(2)}, u32[]{:S(2)}) collective-permute-start(f32[2,22]{1,0:T(2,128)S(1)} %get-tuple-element.46), channel_id=1, source_target_pairs={{0,24},{8,0},{16,8},{24,16},{1,25},{9,1},{17,9},{25,17},{2,26},{10... | collective-permute-start | bytes 536 | tf_op jit(solution)/shard_map/ppermute | solution.py:43
  78.0 1.5 %collective-permute-done.16 = f32[2,22]{1,0:T(2,128)S(1)} collective-permute-done((f32[2,22]{1,0:T(2,128)S(1)}, f32[2,22]{1,0:T(2,128)S(1)}, u32[]{:S(2)}, u32[]{:S(2)}) %collective-permute-start.16) | collective-permute-done | bytes 208 | tf_op jit(solution)/shard_map/ppermute | solution.py:43
  80.2 1.2 fusion.41
  81.4 1.8 %bitcast_divide_fusion = (f32[22]{0:T(128)S(1)}, f32[22]{0:T(128)}) fusion(f32[2,22]{1,0:T(2,128)S(1)} %fusion.32, f32[]{:T(128)} %fusion.41, f32[22]{0:T(128)S(1)} %get-tuple-element.19, f32[]{:T(128)} %get-tuple-element.18), kind=kLoop, calls=%fused_computation.140 | loop fusion | flops 132 | bytes 360 | tf_op jit(solution)/shard_map/div | solution.py:243
  83.9 3.5 %fusion.2 = f32[1024,128]{1,0:T(8,128)S(1)} fusion(bf16[1024,128]{1,0:T(8,128)(2,1)S(1)} %copy-done, f32[1024,1024]{0,1:T(8,128)} %copy-done.1, f32[1024]{0:T(1024)S(1)} %bitcast.194, f32[1024]{0:T(1024)S(1)} %broadcast_bitcast_fusion, s32[1024]{0:T(1024)S(1)} %bitcast.191), kind=kOutput, calls=%fused_computation.10 | convolution fusion | flops 274726912 | bytes 4993024 | tf_op jit(solution)/shard_map/dot_general | solution.py:113
  88.4 2.6 %collective-permute-start.19 = (f32[128,128]{1,0:T(8,128)S(1)}, f32[128,128]{1,0:T(8,128)S(1)}, u32[]{:S(2)}, u32[]{:S(2)}) collective-permute-start(f32[128,128]{1,0:T(8,128)S(1)} %get-tuple-element.32), channel_id=1, source_target_pairs={{0,3},{1,4},{2,5},{3,6},{4,7},{5,0},{6,1},{7,2},{8,11},{9,12},{10,... | collective-permute-start | bytes 196616 | tf_op jit(solution)/shard_map/ppermute | solution.py:54
  91.0 1.2 collective-permute-start.20
  92.2 1.2 collective-permute-start.21
  94.4 1.5 %collective-permute-start.23 = (f32[128,128]{1,0:T(8,128)S(1)}, f32[128,128]{1,0:T(8,128)S(1)}, u32[]{:S(2)}, u32[]{:S(2)}) collective-permute-start(f32[128,128]{1,0:T(8,128)S(1)} %get-tuple-element.28), channel_id=1, source_target_pairs={{0,7},{1,0},{2,1},{3,2},{4,3},{5,4},{6,5},{7,6},{8,15},{9,8},{10,9... | collective-permute-start | bytes 196616 | tf_op jit(solution)/shard_map/ppermute | solution.py:54
  95.9 3.4 %collective-permute-done.19 = f32[128,128]{1,0:T(8,128)S(1)} collective-permute-done((f32[128,128]{1,0:T(8,128)S(1)}, f32[128,128]{1,0:T(8,128)S(1)}, u32[]{:S(2)}, u32[]{:S(2)}) %collective-permute-start.19) | collective-permute-done | bytes 65568 | tf_op jit(solution)/shard_map/ppermute | solution.py:54
  99.6 1.5 %collective-permute-done.22 = f32[128,128]{1,0:T(8,128)S(1)} collective-permute-done((f32[128,128]{1,0:T(8,128)S(1)}, f32[128,128]{1,0:T(8,128)S(1)}, u32[]{:S(2)}, u32[]{:S(2)}) %collective-permute-start.22) | collective-permute-done | bytes 65568 | tf_op jit(solution)/shard_map/ppermute | solution.py:54
  102.6 16.4 %all_to_all.10 = bf16[8,64,384]{2,1,0:T(8,128)(2,1)S(1)} all-to-all(bf16[8,64,384]{2,1,0:T(8,128)(2,1)S(1)} %pad_maximum_fusion), channel_id=1, replica_groups=mesh['dp'=4,'fsdp'=8] {'fsdp'}, dimensions={0} | all-to-all | bytes 786432 | tf_op jit(solution)/shard_map/all_to_all | solution.py:51
  119.1 1.4 %collective-permute-start.24 = (f32[64,384]{1,0:T(8,128)S(1)}, f32[64,384]{1,0:T(8,128)S(1)}, u32[]{:S(2)}, u32[]{:S(2)}) collective-permute-start(f32[64,384]{1,0:T(8,128)S(1)} %convert_reduce_fusion), channel_id=1, source_target_pairs={{0,8},{8,16},{16,24},{24,0},{1,9},{9,17},{17,25},{25,1},{2,10},{10... | collective-permute-start | bytes 294920 | tf_op jit(solution)/shard_map/ppermute | solution.py:43
  120.5 1.5 %collective-permute-start.25 = (f32[64,384]{1,0:T(8,128)S(1)}, f32[64,384]{1,0:T(8,128)S(1)}, u32[]{:S(2)}, u32[]{:S(2)}) collective-permute-start(f32[64,384]{1,0:T(8,128)S(1)} %convert_reduce_fusion), channel_id=1, source_target_pairs={{0,16},{8,24},{16,0},{24,8},{1,17},{9,25},{17,1},{25,9},{2,18},{10... | collective-permute-start | bytes 294920 | tf_op jit(solution)/shard_map/ppermute | solution.py:43
  122.6 3.1 %collective-permute-done.24 = f32[64,384]{1,0:T(8,128)S(1)} collective-permute-done((f32[64,384]{1,0:T(8,128)S(1)}, f32[64,384]{1,0:T(8,128)S(1)}, u32[]{:S(2)}, u32[]{:S(2)}) %collective-permute-start.24) | collective-permute-done | bytes 98336 | tf_op jit(solution)/shard_map/ppermute | solution.py:43
  (138 shorter events, 21.7 us)
Async XLA Ops:
  0.6 55.4 %copy-start = (bf16[1024,128]{1,0:T(8,128)(2,1)S(1)}, bf16[1024,128]{1,0:T(8,128)(2,1)}, u32[]{:S(2)}) copy-start(bf16[1024,128]{1,0:T(8,128)(2,1)} %param.20) | copy-start | bytes 786436
  26.9 14.6 %all-to-all-start = ((bf16[8,128,128]{2,1,0:T(8,128)(2,1)}), bf16[8,128,128]{2,1,0:T(8,128)(2,1)S(1)}, u32[]{:S(2)}, u32[]{:S(2)}) async-start(bf16[8,128,128]{2,1,0:T(8,128)(2,1)} %bitcast.7), calls=%async_computation | async-start | bytes 524288 | tf_op jit(solution)/shard_map/all_to_all | solution.py:51
  43.4 5.7 %collective-permute-start = (bf16[128,256]{0,1:T(8,128)(2,1)S(1)}, bf16[128,256]{0,1:T(8,128)(2,1)S(1)}, u32[]{:S(2)}, u32[]{:S(2)}) collective-permute-start(bf16[128,256]{0,1:T(8,128)(2,1)S(1)} %pad_maximum_fusion.2), channel_id=1, source_target_pairs={{0,1},{1,2},{2,3},{3,4},{4,5},{5,6},{6,7},{7,0},{8,9},{9,10},{10,1... | collective-permute-start | bytes 196616 | tf_op jit(solution)/shard_map/ppermute | solution.py:43
  43.4 6.9 %collective-permute-start.1 = (bf16[128,256]{0,1:T(8,128)(2,1)S(1)}, bf16[128,256]{0,1:T(8,128)(2,1)S(1)}, u32[]{:S(2)}, u32[]{:S(2)}) collective-permute-start(bf16[128,256]{0,1:T(8,128)(2,1)S(1)} %pad_maximum_fusion.2), channel_id=1, source_target_pairs={{0,2},{1,3},{2,4},{3,5},{4,6},{5,7},{6,0},{7,1},{8,10},{9,11},{10,... | collective-permute-start | bytes 196616 | tf_op jit(solution)/shard_map/ppermute | solution.py:43
  43.6 11.6 %collective-permute-start.2 = (bf16[128,256]{0,1:T(8,128)(2,1)S(1)}, bf16[128,256]{0,1:T(8,128)(2,1)S(1)}, u32[]{:S(2)}, u32[]{:S(2)}) collective-permute-start(bf16[128,256]{0,1:T(8,128)(2,1)S(1)} %pad_maximum_fusion.2), channel_id=1, source_target_pairs={{0,3},{1,4},{2,5},{3,6},{4,7},{5,0},{6,1},{7,2},{8,11},{9,12},{10,... | collective-permute-start | bytes 196616 | tf_op jit(solution)/shard_map/ppermute | solution.py:43
  45.2 10.2 %collective-permute-start.3 = (bf16[128,256]{0,1:T(8,128)(2,1)S(1)}, bf16[128,256]{0,1:T(8,128)(2,1)S(1)}, u32[]{:S(2)}, u32[]{:S(2)}) collective-permute-start(bf16[128,256]{0,1:T(8,128)(2,1)S(1)} %pad_maximum_fusion.2), channel_id=1, source_target_pairs={{0,4},{1,5},{2,6},{3,7},{4,0},{5,1},{6,2},{7,3},{8,12},{9,13},{10,... | collective-permute-start | bytes 196616 | tf_op jit(solution)/shard_map/ppermute | solution.py:43
  47.5 7.9 %collective-permute-start.4 = (bf16[128,256]{0,1:T(8,128)(2,1)S(1)}, bf16[128,256]{0,1:T(8,128)(2,1)S(1)}, u32[]{:S(2)}, u32[]{:S(2)}) collective-permute-start(bf16[128,256]{0,1:T(8,128)(2,1)S(1)} %pad_maximum_fusion.2), channel_id=1, source_target_pairs={{0,5},{1,6},{2,7},{3,0},{4,1},{5,2},{6,3},{7,4},{8,13},{9,14},{10,... | collective-permute-start | bytes 196616 | tf_op jit(solution)/shard_map/ppermute | solution.py:43
  49.1 6.4 %collective-permute-start.5 = (bf16[128,256]{0,1:T(8,128)(2,1)S(1)}, bf16[128,256]{0,1:T(8,128)(2,1)S(1)}, u32[]{:S(2)}, u32[]{:S(2)}) collective-permute-start(bf16[128,256]{0,1:T(8,128)(2,1)S(1)} %pad_maximum_fusion.2), channel_id=1, source_target_pairs={{0,6},{1,7},{2,0},{3,1},{4,2},{5,3},{6,4},{7,5},{8,14},{9,15},{10,... | collective-permute-start | bytes 196616 | tf_op jit(solution)/shard_map/ppermute | solution.py:43
  50.3 5.2 %collective-permute-start.6 = (bf16[128,256]{0,1:T(8,128)(2,1)S(1)}, bf16[128,256]{0,1:T(8,128)(2,1)S(1)}, u32[]{:S(2)}, u32[]{:S(2)}) collective-permute-start(bf16[128,256]{0,1:T(8,128)(2,1)S(1)} %pad_maximum_fusion.2), channel_id=1, source_target_pairs={{0,7},{1,0},{2,1},{3,2},{4,3},{5,4},{6,5},{7,6},{8,15},{9,8},{10,9... | collective-permute-start | bytes 196616 | tf_op jit(solution)/shard_map/ppermute | solution.py:43
  57.4 2.0 %copy-start.1 = (f32[1024,1024]{0,1:T(8,128)}, f32[1024,1024]{0,1:T(8,128)S(1)}, u32[]{:S(2)}) copy-start(f32[1024,1024]{0,1:T(8,128)S(1)} %get-tuple-element.60) | copy-start | bytes 12582916
  57.5 22.1 %copy-start.2 = (f32[22]{0:T(128)S(1)}, f32[22]{0:T(128)}, u32[]{:S(2)}) copy-start(f32[22]{0:T(128)} %param.31) | copy-start | bytes 268
  59.5 7.4 %collective-permute-start.7 = (f32[6,1024]{1,0:T(8,128)S(1)}, f32[6,1024]{1,0:T(8,128)S(1)}, u32[]{:S(2)}, u32[]{:S(2)}) collective-permute-start(f32[6,1024]{1,0:T(8,128)S(1)} %concatenate.43), channel_id=1, source_target_pairs={{0,1},{1,2},{2,3},{3,4},{4,5},{5,6},{6,7},{7,0},{8,9},{9,10},{10,1... | collective-permute-start | bytes 73736 | tf_op jit(solution)/shard_map/ppermute | solution.py:43
  61.4 7.7 %collective-permute-start.8 = (f32[6,1024]{1,0:T(8,128)S(1)}, f32[6,1024]{1,0:T(8,128)S(1)}, u32[]{:S(2)}, u32[]{:S(2)}) collective-permute-start(f32[6,1024]{1,0:T(8,128)S(1)} %concatenate.43), channel_id=1, source_target_pairs={{0,2},{1,3},{2,4},{3,5},{4,6},{5,7},{6,0},{7,1},{8,10},{9,11},{10,... | collective-permute-start | bytes 73736 | tf_op jit(solution)/shard_map/ppermute | solution.py:43
  64.1 6.3 %collective-permute-start.9 = (f32[6,1024]{1,0:T(8,128)S(1)}, f32[6,1024]{1,0:T(8,128)S(1)}, u32[]{:S(2)}, u32[]{:S(2)}) collective-permute-start(f32[6,1024]{1,0:T(8,128)S(1)} %concatenate.43), channel_id=1, source_target_pairs={{0,3},{1,4},{2,5},{3,6},{4,7},{5,0},{6,1},{7,2},{8,11},{9,12},{10,... | collective-permute-start | bytes 73736 | tf_op jit(solution)/shard_map/ppermute | solution.py:43
  64.2 6.3 %collective-permute-start.10 = (f32[6,1024]{1,0:T(8,128)S(1)}, f32[6,1024]{1,0:T(8,128)S(1)}, u32[]{:S(2)}, u32[]{:S(2)}) collective-permute-start(f32[6,1024]{1,0:T(8,128)S(1)} %concatenate.43), channel_id=1, source_target_pairs={{0,4},{1,5},{2,6},{3,7},{4,0},{5,1},{6,2},{7,3},{8,12},{9,13},{10,... | collective-permute-start | bytes 73736 | tf_op jit(solution)/shard_map/ppermute | solution.py:43
  66.9 3.6 %collective-permute-start.11 = (f32[6,1024]{1,0:T(8,128)S(1)}, f32[6,1024]{1,0:T(8,128)S(1)}, u32[]{:S(2)}, u32[]{:S(2)}) collective-permute-start(f32[6,1024]{1,0:T(8,128)S(1)} %concatenate.43), channel_id=1, source_target_pairs={{0,5},{1,6},{2,7},{3,0},{4,1},{5,2},{6,3},{7,4},{8,13},{9,14},{10,... | collective-permute-start | bytes 73736 | tf_op jit(solution)/shard_map/ppermute | solution.py:43
  67.0 4.1 %collective-permute-start.12 = (f32[6,1024]{1,0:T(8,128)S(1)}, f32[6,1024]{1,0:T(8,128)S(1)}, u32[]{:S(2)}, u32[]{:S(2)}) collective-permute-start(f32[6,1024]{1,0:T(8,128)S(1)} %concatenate.43), channel_id=1, source_target_pairs={{0,6},{1,7},{2,0},{3,1},{4,2},{5,3},{6,4},{7,5},{8,14},{9,15},{10,... | collective-permute-start | bytes 73736 | tf_op jit(solution)/shard_map/ppermute | solution.py:43
  69.0 2.9 %collective-permute-start.13 = (f32[6,1024]{1,0:T(8,128)S(1)}, f32[6,1024]{1,0:T(8,128)S(1)}, u32[]{:S(2)}, u32[]{:S(2)}) collective-permute-start(f32[6,1024]{1,0:T(8,128)S(1)} %concatenate.43), channel_id=1, source_target_pairs={{0,7},{1,0},{2,1},{3,2},{4,3},{5,4},{6,5},{7,6},{8,15},{9,8},{10,9... | collective-permute-start | bytes 73736 | tf_op jit(solution)/shard_map/ppermute | solution.py:43
  72.9 4.5 %collective-permute-start.14 = (f32[2,22]{1,0:T(2,128)S(1)}, f32[2,22]{1,0:T(2,128)S(1)}, u32[]{:S(2)}, u32[]{:S(2)}) collective-permute-start(f32[2,22]{1,0:T(2,128)S(1)} %get-tuple-element.46), channel_id=1, source_target_pairs={{0,8},{8,16},{16,24},{24,0},{1,9},{9,17},{17,25},{25,1},{2,10},{10... | collective-permute-start | bytes 536 | tf_op jit(solution)/shard_map/ppermute | solution.py:43
  74.4 3.6 %collective-permute-start.15 = (f32[2,22]{1,0:T(2,128)S(1)}, f32[2,22]{1,0:T(2,128)S(1)}, u32[]{:S(2)}, u32[]{:S(2)}) collective-permute-start(f32[2,22]{1,0:T(2,128)S(1)} %get-tuple-element.46), channel_id=1, source_target_pairs={{0,16},{8,24},{16,0},{24,8},{1,17},{9,25},{17,1},{25,9},{2,18},{10... | collective-permute-start | bytes 536 | tf_op jit(solution)/shard_map/ppermute | solution.py:43
  75.9 3.6 %collective-permute-start.16 = (f32[2,22]{1,0:T(2,128)S(1)}, f32[2,22]{1,0:T(2,128)S(1)}, u32[]{:S(2)}, u32[]{:S(2)}) collective-permute-start(f32[2,22]{1,0:T(2,128)S(1)} %get-tuple-element.46), channel_id=1, source_target_pairs={{0,24},{8,0},{16,8},{24,16},{1,25},{9,1},{17,9},{25,17},{2,26},{10... | collective-permute-start | bytes 536 | tf_op jit(solution)/shard_map/ppermute | solution.py:43
  87.5 5.9 %collective-permute-start.17 = (f32[128,128]{1,0:T(8,128)S(1)}, f32[128,128]{1,0:T(8,128)S(1)}, u32[]{:S(2)}, u32[]{:S(2)}) collective-permute-start(f32[128,128]{1,0:T(8,128)S(1)} %get-tuple-element.34), channel_id=1, source_target_pairs={{0,1},{1,2},{2,3},{3,4},{4,5},{5,6},{6,7},{7,0},{8,9},{9,10},{10,1... | collective-permute-start | bytes 196616 | tf_op jit(solution)/shard_map/ppermute | solution.py:54
  87.6 6.9 %collective-permute-start.18 = (f32[128,128]{1,0:T(8,128)S(1)}, f32[128,128]{1,0:T(8,128)S(1)}, u32[]{:S(2)}, u32[]{:S(2)}) collective-permute-start(f32[128,128]{1,0:T(8,128)S(1)} %get-tuple-element.33), channel_id=1, source_target_pairs={{0,2},{1,3},{2,4},{3,5},{4,6},{5,7},{6,0},{7,1},{8,10},{9,11},{10,... | collective-permute-start | bytes 196616 | tf_op jit(solution)/shard_map/ppermute | solution.py:54
  88.4 10.9 %collective-permute-start.19 = (f32[128,128]{1,0:T(8,128)S(1)}, f32[128,128]{1,0:T(8,128)S(1)}, u32[]{:S(2)}, u32[]{:S(2)}) collective-permute-start(f32[128,128]{1,0:T(8,128)S(1)} %get-tuple-element.32), channel_id=1, source_target_pairs={{0,3},{1,4},{2,5},{3,6},{4,7},{5,0},{6,1},{7,2},{8,11},{9,12},{10,... | collective-permute-start | bytes 196616 | tf_op jit(solution)/shard_map/ppermute | solution.py:54
  91.0 8.5 %collective-permute-start.20 = (f32[128,128]{1,0:T(8,128)S(1)}, f32[128,128]{1,0:T(8,128)S(1)}, u32[]{:S(2)}, u32[]{:S(2)}) collective-permute-start(f32[128,128]{1,0:T(8,128)S(1)} %get-tuple-element.31), channel_id=1, source_target_pairs={{0,4},{1,5},{2,6},{3,7},{4,0},{5,1},{6,2},{7,3},{8,12},{9,13},{10,... | collective-permute-start | bytes 196616 | tf_op jit(solution)/shard_map/ppermute | solution.py:54
  92.2 7.4 %collective-permute-start.21 = (f32[128,128]{1,0:T(8,128)S(1)}, f32[128,128]{1,0:T(8,128)S(1)}, u32[]{:S(2)}, u32[]{:S(2)}) collective-permute-start(f32[128,128]{1,0:T(8,128)S(1)} %get-tuple-element.30), channel_id=1, source_target_pairs={{0,5},{1,6},{2,7},{3,0},{4,1},{5,2},{6,3},{7,4},{8,13},{9,14},{10,... | collective-permute-start | bytes 196616 | tf_op jit(solution)/shard_map/ppermute | solution.py:54
  93.5 7.7 %collective-permute-start.22 = (f32[128,128]{1,0:T(8,128)S(1)}, f32[128,128]{1,0:T(8,128)S(1)}, u32[]{:S(2)}, u32[]{:S(2)}) collective-permute-start(f32[128,128]{1,0:T(8,128)S(1)} %get-tuple-element.29), channel_id=1, source_target_pairs={{0,6},{1,7},{2,0},{3,1},{4,2},{5,3},{6,4},{7,5},{8,14},{9,15},{10,... | collective-permute-start | bytes 196616 | tf_op jit(solution)/shard_map/ppermute | solution.py:54
  94.4 6.7 %collective-permute-start.23 = (f32[128,128]{1,0:T(8,128)S(1)}, f32[128,128]{1,0:T(8,128)S(1)}, u32[]{:S(2)}, u32[]{:S(2)}) collective-permute-start(f32[128,128]{1,0:T(8,128)S(1)} %get-tuple-element.28), channel_id=1, source_target_pairs={{0,7},{1,0},{2,1},{3,2},{4,3},{5,4},{6,5},{7,6},{8,15},{9,8},{10,9... | collective-permute-start | bytes 196616 | tf_op jit(solution)/shard_map/ppermute | solution.py:54
  119.1 6.6 %collective-permute-start.24 = (f32[64,384]{1,0:T(8,128)S(1)}, f32[64,384]{1,0:T(8,128)S(1)}, u32[]{:S(2)}, u32[]{:S(2)}) collective-permute-start(f32[64,384]{1,0:T(8,128)S(1)} %convert_reduce_fusion), channel_id=1, source_target_pairs={{0,8},{8,16},{16,24},{24,0},{1,9},{9,17},{17,25},{25,1},{2,10},{10... | collective-permute-start | bytes 294920 | tf_op jit(solution)/shard_map/ppermute | solution.py:43
  120.5 6.0 %collective-permute-start.25 = (f32[64,384]{1,0:T(8,128)S(1)}, f32[64,384]{1,0:T(8,128)S(1)}, u32[]{:S(2)}, u32[]{:S(2)}) collective-permute-start(f32[64,384]{1,0:T(8,128)S(1)} %convert_reduce_fusion), channel_id=1, source_target_pairs={{0,16},{8,24},{16,0},{24,8},{1,17},{9,25},{17,1},{25,9},{2,18},{10... | collective-permute-start | bytes 294920 | tf_op jit(solution)/shard_map/ppermute | solution.py:43
  122.0 4.6 %collective-permute-start.26 = (f32[64,384]{1,0:T(8,128)S(1)}, f32[64,384]{1,0:T(8,128)S(1)}, u32[]{:S(2)}, u32[]{:S(2)}) collective-permute-start(f32[64,384]{1,0:T(8,128)S(1)} %convert_reduce_fusion), channel_id=1, source_target_pairs={{0,24},{8,0},{16,8},{24,16},{1,25},{9,1},{17,9},{25,17},{2,26},{10... | collective-permute-start | bytes 294920 | tf_op jit(solution)/shard_map/ppermute | solution.py:43

commit v6 on v5

--- a/solution.py
+++ b/solution.py
@@ -272,7 +272,7 @@
     ).astype(jnp.bfloat16)
 
     arrived_grad = exchange_ordered(
-        partial_grad.reshape(fsdp_size, unit_rows, 3 * width), "fsdp", True
+        partial_grad.reshape(fsdp_size, unit_rows, 3 * width), "fsdp", False
     )
     local_grad = jnp.sum(arrived_grad.astype(jnp.float32), axis=0)
 

time: 128 us -> 125 us (0.977)
  blocking collectives: 33.7 us -> 17.3 us
  starting transfers between devices: 37.4 us -> 46.5 us
  waiting for transfers between devices: 28.2 us -> 31.8 us
    all_to_all x1 -> x0, blocking collectives: 16.4 us -> none  [exchange_ordered(): return lax.all_to_all(blocks, axis, 0, 0, tiled=True)]
    ppermute x7 -> x14, starting transfers between devices: 8.39 us -> 17.5 us  [exchange_ordered(): lax.ppermute(lax.dynamic_index_in_dim(blocks, (here + shift) % size, keep...]
    ppermute x7 -> x14, waiting for transfers between devices: 5.17 us -> 8.25 us  [exchange_ordered(): lax.ppermute(lax.dynamic_index_in_dim(blocks, (here + shift) % size, keep...]
    unnamed x25 -> x31, local copies, waits for them, and re-layouts: 4.52 us -> 4.6 us
  transfers between devices with their start and end apart: 28 -> 35, of which waited for: 14 -> 16; matrix products, arithmetic and copies ran while one was open for 1% -> 1% of each run, Pallas kernels for 0% -> 0%
where the time goes in v6:
time: 125 us; the launch traced here: 124 us
  starting transfers between devices  46.5 us (37%)
  waiting for transfers between devices  31.8 us (25%)
  blocking collectives  17.3 us (14%)
  matrix products  9.58 us (8%)
  other arithmetic  9.26 us (7%)
  local copies, waits for them, and re-layouts  7.81 us (6%)
  between operations  1.92 us (2%)
    ppermute x20, starting transfers between devices, gather_ordered(): lax.ppermute(value, axis, shift_pairs(size, shift))  24.2 us
    ppermute x14, starting transfers between devices, exchange_ordered(): lax.ppermute(lax.dynamic_index_in_dim(blocks, (here + shift) % size, keep...  17.5 us
    all_gather x1, blocking collectives, gather_ordered(): return lax.all_gather(value, axis)  17.3 us
    ppermute x20, waiting for transfers between devices, gather_ordered(): lax.ppermute(value, axis, shift_pairs(size, shift))  14.5 us
    all_to_all x1, waiting for transfers between devices, exchange_ordered(): return lax.all_to_all(blocks, axis, 0, 0, tiled=True)  9.09 us
    ppermute x14, waiting for transfers between devices, exchange_ordered(): lax.ppermute(lax.dynamic_index_in_dim(blocks, (here + shift) % size, keep...  8.25 us
    all_to_all x1, starting transfers between devices, exchange_ordered(): return lax.all_to_all(blocks, axis, 0, 0, tiled=True)  4.81 us
    unnamed x31, local copies, waits for them, and re-layouts  4.6 us
  transfers between devices with their start and end apart: 35, of which 16 were waited for; matrix products, arithmetic and copies ran while one was open for 1% of the time, Pallas kernels for 0%

profile of v6, /device:TPU:0, one launch (start us, length us, event | category | flops | bytes accessed | tf_op | source)
XLA Modules:
  0.0 124.1 jit_solution(16097980497568567092)
XLA Ops:
  7.2 17.3 %all-gather.1 = bf16[8,389,128]{2,1,0:T(8,128)(2,1)S(1)} all-gather(bf16[1,389,128]{2,1,0:T(8,128)(2,1)S(1)} %bitcast.193), channel_id=2, replica_groups=mesh['dp'=4,'fsdp'=8] {'fsdp'}, dimensions={0}, use_global_device_ids=true | all-gather | bytes 896256 | tf_op jit(solution)/shard_map/all_gather | solution.py:41
  24.5 2.5 %fusion.3 = bf16[1024,128]{1,0:T(8,128)(2,1)} fusion(bf16[1024,128]{1,0:T(8,128)(2,1)} %param.19, s32[1024]{0:T(1024)S(1)} %bitcast.221), kind=kOutput, calls=%fused_computation.11 | convolution fusion | flops 269615104 | bytes 528384 | tf_op jit(solution)/shard_map/dot_general | solution.py:200
  26.9 4.8 %all-to-all-start = ((bf16[8,128,128]{2,1,0:T(8,128)(2,1)}), bf16[8,128,128]{2,1,0:T(8,128)(2,1)S(1)}, u32[]{:S(2)}, u32[]{:S(2)}) async-start(bf16[8,128,128]{2,1,0:T(8,128)(2,1)} %bitcast.7), calls=%async_computation | async-start | bytes 524288 | tf_op jit(solution)/shard_map/all_to_all | solution.py:51
  32.4 9.1 %all-to-all-done = bf16[8,128,128]{2,1,0:T(8,128)(2,1)S(1)} async-done(((bf16[8,128,128]{2,1,0:T(8,128)(2,1)}), bf16[8,128,128]{2,1,0:T(8,128)(2,1)S(1)}, u32[]{:S(2)}, u32[]{:S(2)}) %all-to-all-start) | async-done | bytes 262176 | tf_op jit(solution)/shard_map/all_to_all | solution.py:51
  43.6 1.6 %collective-permute-start.2 = (bf16[128,256]{0,1:T(8,128)(2,1)S(1)}, bf16[128,256]{0,1:T(8,128)(2,1)S(1)}, u32[]{:S(2)}, u32[]{:S(2)}) collective-permute-start(bf16[128,256]{0,1:T(8,128)(2,1)S(1)} %pad_maximum_fusion.2), channel_id=1, source_target_pairs={{0,3},{1,4},{2,5},{3,6},{4,7},{5,0},{6,1},{7,2},{8,11},{9,12},{10,... | collective-permute-start | bytes 196616 | tf_op jit(solution)/shard_map/ppermute | solution.py:43
  45.2 2.3 %collective-permute-start.3 = (bf16[128,256]{0,1:T(8,128)(2,1)S(1)}, bf16[128,256]{0,1:T(8,128)(2,1)S(1)}, u32[]{:S(2)}, u32[]{:S(2)}) collective-permute-start(bf16[128,256]{0,1:T(8,128)(2,1)S(1)} %pad_maximum_fusion.2), channel_id=1, source_target_pairs={{0,4},{1,5},{2,6},{3,7},{4,0},{5,1},{6,2},{7,3},{8,12},{9,13},{10,... | collective-permute-start | bytes 196616 | tf_op jit(solution)/shard_map/ppermute | solution.py:43
  47.7 1.4 %collective-permute-done = bf16[128,256]{0,1:T(8,128)(2,1)S(1)} collective-permute-done((bf16[128,256]{0,1:T(8,128)(2,1)S(1)}, bf16[128,256]{0,1:T(8,128)(2,1)S(1)}, u32[]{:S(2)}, u32[]{:S(2)}) %collective-permute-start) | collective-permute-done | bytes 65568 | tf_op jit(solution)/shard_map/ppermute | solution.py:43
  50.4 4.8 %collective-permute-done.2 = bf16[128,256]{0,1:T(8,128)(2,1)S(1)} collective-permute-done((bf16[128,256]{0,1:T(8,128)(2,1)S(1)}, bf16[128,256]{0,1:T(8,128)(2,1)S(1)}, u32[]{:S(2)}, u32[]{:S(2)}) %collective-permute-start.2) | collective-permute-done | bytes 65568 | tf_op jit(solution)/shard_map/ppermute | solution.py:43
  57.5 2.0 %select_reduce_fusion = (f32[1024]{0:T(1024)S(1)}, f32[1024]{0:T(1024)S(1)}, f32[1024]{0:T(1024)S(1)}, f32[1024]{0:T(1024)S(1)}) fusion(f32[1024,1024]{0,1:T(8,128)S(1)} %get-tuple-element.68, s32[1024]{0:T(1024)S(1)} %bitcast.218, f32[1024]{0:T(1024)S(1)} %get-tuple-element.67, f32[1024,1024]{0,1:T(8,128)S(1)} %get-tuple-element.66, ...), kind=kLoop, calls=%fused_computation.2 | loop fusion | flops 9433088 | bytes 8417280 | tf_op jit(solution)/shard_map/reduce_sum | solution.py:91
  59.5 1.8 %collective-permute-start.7 = (f32[6,1024]{1,0:T(8,128)S(1)}, f32[6,1024]{1,0:T(8,128)S(1)}, u32[]{:S(2)}, u32[]{:S(2)}) collective-permute-start(f32[6,1024]{1,0:T(8,128)S(1)} %concatenate.47), channel_id=1, source_target_pairs={{0,1},{1,2},{2,3},{3,4},{4,5},{5,6},{6,7},{7,0},{8,9},{9,10},{10,1... | collective-permute-start | bytes 73736 | tf_op jit(solution)/shard_map/ppermute | solution.py:43
  61.4 2.6 %collective-permute-start.8 = (f32[6,1024]{1,0:T(8,128)S(1)}, f32[6,1024]{1,0:T(8,128)S(1)}, u32[]{:S(2)}, u32[]{:S(2)}) collective-permute-start(f32[6,1024]{1,0:T(8,128)S(1)} %concatenate.47), channel_id=1, source_target_pairs={{0,2},{1,3},{2,4},{3,5},{4,6},{5,7},{6,0},{7,1},{8,10},{9,11},{10,... | collective-permute-start | bytes 73736 | tf_op jit(solution)/shard_map/ppermute | solution.py:43
  64.2 2.7 %collective-permute-start.10 = (f32[6,1024]{1,0:T(8,128)S(1)}, f32[6,1024]{1,0:T(8,128)S(1)}, u32[]{:S(2)}, u32[]{:S(2)}) collective-permute-start(f32[6,1024]{1,0:T(8,128)S(1)} %concatenate.47), channel_id=1, source_target_pairs={{0,4},{1,5},{2,6},{3,7},{4,0},{5,1},{6,2},{7,3},{8,12},{9,13},{10,... | collective-permute-start | bytes 73736 | tf_op jit(solution)/shard_map/ppermute | solution.py:43
  67.0 2.1 %collective-permute-start.12 = (f32[6,1024]{1,0:T(8,128)S(1)}, f32[6,1024]{1,0:T(8,128)S(1)}, u32[]{:S(2)}, u32[]{:S(2)}) collective-permute-start(f32[6,1024]{1,0:T(8,128)S(1)} %concatenate.47), channel_id=1, source_target_pairs={{0,6},{1,7},{2,0},{3,1},{4,2},{5,3},{6,4},{7,5},{8,14},{9,15},{10,... | collective-permute-start | bytes 73736 | tf_op jit(solution)/shard_map/ppermute | solution.py:43
  72.9 1.5 %collective-permute-start.14 = (f32[2,22]{1,0:T(2,128)S(1)}, f32[2,22]{1,0:T(2,128)S(1)}, u32[]{:S(2)}, u32[]{:S(2)}) collective-permute-start(f32[2,22]{1,0:T(2,128)S(1)} %get-tuple-element.54), channel_id=1, source_target_pairs={{0,8},{8,16},{16,24},{24,0},{1,9},{9,17},{17,25},{25,1},{2,10},{10... | collective-permute-start | bytes 536 | tf_op jit(solution)/shard_map/ppermute | solution.py:43
  74.4 1.5 %collective-permute-start.15 = (f32[2,22]{1,0:T(2,128)S(1)}, f32[2,22]{1,0:T(2,128)S(1)}, u32[]{:S(2)}, u32[]{:S(2)}) collective-permute-start(f32[2,22]{1,0:T(2,128)S(1)} %get-tuple-element.54), channel_id=1, source_target_pairs={{0,16},{8,24},{16,0},{24,8},{1,17},{9,25},{17,1},{25,9},{2,18},{10... | collective-permute-start | bytes 536 | tf_op jit(solution)/shard_map/ppermute | solution.py:43
  75.9 1.4 %collective-permute-start.16 = (f32[2,22]{1,0:T(2,128)S(1)}, f32[2,22]{1,0:T(2,128)S(1)}, u32[]{:S(2)}, u32[]{:S(2)}) collective-permute-start(f32[2,22]{1,0:T(2,128)S(1)} %get-tuple-element.54), channel_id=1, source_target_pairs={{0,24},{8,0},{16,8},{24,16},{1,25},{9,1},{17,9},{25,17},{2,26},{10... | collective-permute-start | bytes 536 | tf_op jit(solution)/shard_map/ppermute | solution.py:43
  78.0 1.5 %collective-permute-done.16 = f32[2,22]{1,0:T(2,128)S(1)} collective-permute-done((f32[2,22]{1,0:T(2,128)S(1)}, f32[2,22]{1,0:T(2,128)S(1)}, u32[]{:S(2)}, u32[]{:S(2)}) %collective-permute-start.16) | collective-permute-done | bytes 208 | tf_op jit(solution)/shard_map/ppermute | solution.py:43
  81.4 1.8 %bitcast_divide_fusion = (f32[22]{0:T(128)S(1)}, f32[22]{0:T(128)}) fusion(f32[2,22]{1,0:T(2,128)S(1)} %fusion.33, f32[]{:T(128)} %fusion.42, f32[22]{0:T(128)S(1)} %get-tuple-element.19, f32[]{:T(128)} %get-tuple-element.18), kind=kLoop, calls=%fused_computation.158 | loop fusion | flops 132 | bytes 360 | tf_op jit(solution)/shard_map/div | solution.py:243
  83.9 3.5 %fusion.2 = f32[1024,128]{1,0:T(8,128)S(1)} fusion(bf16[1024,128]{1,0:T(8,128)(2,1)S(1)} %copy-done, f32[1024,1024]{0,1:T(8,128)} %copy-done.1, f32[1024]{0:T(1024)S(1)} %bitcast.222, f32[1024]{0:T(1024)S(1)} %broadcast_bitcast_fusion, s32[1024]{0:T(1024)S(1)} %bitcast.219), kind=kOutput, calls=%fused_computation.10 | convolution fusion | flops 274726912 | bytes 4993024 | tf_op jit(solution)/shard_map/dot_general | solution.py:113
  88.4 2.6 %collective-permute-start.19 = (f32[128,128]{1,0:T(8,128)S(1)}, f32[128,128]{1,0:T(8,128)S(1)}, u32[]{:S(2)}, u32[]{:S(2)}) collective-permute-start(f32[128,128]{1,0:T(8,128)S(1)} %get-tuple-element.32), channel_id=1, source_target_pairs={{0,3},{1,4},{2,5},{3,6},{4,7},{5,0},{6,1},{7,2},{8,11},{9,12},{10,... | collective-permute-start | bytes 196616 | tf_op jit(solution)/shard_map/ppermute | solution.py:54
  94.4 1.5 %collective-permute-start.23 = (f32[128,128]{1,0:T(8,128)S(1)}, f32[128,128]{1,0:T(8,128)S(1)}, u32[]{:S(2)}, u32[]{:S(2)}) collective-permute-start(f32[128,128]{1,0:T(8,128)S(1)} %get-tuple-element.28), channel_id=1, source_target_pairs={{0,7},{1,0},{2,1},{3,2},{4,3},{5,4},{6,5},{7,6},{8,15},{9,8},{10,9... | collective-permute-start | bytes 196616 | tf_op jit(solution)/shard_map/ppermute | solution.py:54
  95.9 3.4 %collective-permute-done.19 = f32[128,128]{1,0:T(8,128)S(1)} collective-permute-done((f32[128,128]{1,0:T(8,128)S(1)}, f32[128,128]{1,0:T(8,128)S(1)}, u32[]{:S(2)}, u32[]{:S(2)}) %collective-permute-start.19) | collective-permute-done | bytes 65568 | tf_op jit(solution)/shard_map/ppermute | solution.py:54
  99.6 1.5 %collective-permute-done.22 = f32[128,128]{1,0:T(8,128)S(1)} collective-permute-done((f32[128,128]{1,0:T(8,128)S(1)}, f32[128,128]{1,0:T(8,128)S(1)}, u32[]{:S(2)}, u32[]{:S(2)}) %collective-permute-start.22) | collective-permute-done | bytes 65568 | tf_op jit(solution)/shard_map/ppermute | solution.py:54
  103.3 2.4 %collective-permute-start.25 = (bf16[64,384]{1,0:T(8,128)(2,1)S(1)}, bf16[64,384]{1,0:T(8,128)(2,1)S(1)}, u32[]{:S(2)}, u32[]{:S(2)}) collective-permute-start(bf16[64,384]{1,0:T(8,128)(2,1)S(1)} %get-tuple-element.41), channel_id=1, source_target_pairs={{0,2},{1,3},{2,4},{3,5},{4,6},{5,7},{6,0},{7,1},{8,10},{9,11},{10,... | collective-permute-start | bytes 147464 | tf_op jit(solution)/shard_map/ppermute | solution.py:54
  106.0 2.3 %collective-permute-start.27 = (bf16[64,384]{1,0:T(8,128)(2,1)S(1)}, bf16[64,384]{1,0:T(8,128)(2,1)S(1)}, u32[]{:S(2)}, u32[]{:S(2)}) collective-permute-start(bf16[64,384]{1,0:T(8,128)(2,1)S(1)} %get-tuple-element.39), channel_id=1, source_target_pairs={{0,4},{1,5},{2,6},{3,7},{4,0},{5,1},{6,2},{7,3},{8,12},{9,13},{10,... | collective-permute-start | bytes 147464 | tf_op jit(solution)/shard_map/ppermute | solution.py:54
  108.9 1.5 %collective-permute-start.29 = (bf16[64,384]{1,0:T(8,128)(2,1)S(1)}, bf16[64,384]{1,0:T(8,128)(2,1)S(1)}, u32[]{:S(2)}, u32[]{:S(2)}) collective-permute-start(bf16[64,384]{1,0:T(8,128)(2,1)S(1)} %get-tuple-element.37), channel_id=1, source_target_pairs={{0,6},{1,7},{2,0},{3,1},{4,2},{5,3},{6,4},{7,5},{8,14},{9,15},{10,... | collective-permute-start | bytes 147464 | tf_op jit(solution)/shard_map/ppermute | solution.py:54
  110.4 1.4 %collective-permute-start.30 = (bf16[64,384]{1,0:T(8,128)(2,1)S(1)}, bf16[64,384]{1,0:T(8,128)(2,1)S(1)}, u32[]{:S(2)}, u32[]{:S(2)}) collective-permute-start(bf16[64,384]{1,0:T(8,128)(2,1)S(1)} %get-tuple-element.36), channel_id=1, source_target_pairs={{0,7},{1,0},{2,1},{3,2},{4,3},{5,4},{6,5},{7,6},{8,15},{9,8},{10,9... | collective-permute-start | bytes 147464 | tf_op jit(solution)/shard_map/ppermute | solution.py:54
  111.8 1.4 %collective-permute-done.26 = bf16[64,384]{1,0:T(8,128)(2,1)S(1)} collective-permute-done((bf16[64,384]{1,0:T(8,128)(2,1)S(1)}, bf16[64,384]{1,0:T(8,128)(2,1)S(1)}, u32[]{:S(2)}, u32[]{:S(2)}) %collective-permute-start.26) | collective-permute-done | bytes 49184 | tf_op jit(solution)/shard_map/ppermute | solution.py:54
  115.3 1.4 %collective-permute-start.31 = (f32[64,384]{1,0:T(8,128)S(1)}, f32[64,384]{1,0:T(8,128)S(1)}, u32[]{:S(2)}, u32[]{:S(2)}) collective-permute-start(f32[64,384]{1,0:T(8,128)S(1)} %convert_reduce_fusion), channel_id=1, source_target_pairs={{0,8},{8,16},{16,24},{24,0},{1,9},{9,17},{17,25},{25,1},{2,10},{10... | collective-permute-start | bytes 294920 | tf_op jit(solution)/shard_map/ppermute | solution.py:43
  116.7 1.5 %collective-permute-start.32 = (f32[64,384]{1,0:T(8,128)S(1)}, f32[64,384]{1,0:T(8,128)S(1)}, u32[]{:S(2)}, u32[]{:S(2)}) collective-permute-start(f32[64,384]{1,0:T(8,128)S(1)} %convert_reduce_fusion), channel_id=1, source_target_pairs={{0,16},{8,24},{16,0},{24,8},{1,17},{9,25},{17,1},{25,9},{2,18},{10... | collective-permute-start | bytes 294920 | tf_op jit(solution)/shard_map/ppermute | solution.py:43
  118.8 3.1 %collective-permute-done.31 = f32[64,384]{1,0:T(8,128)S(1)} collective-permute-done((f32[64,384]{1,0:T(8,128)S(1)}, f32[64,384]{1,0:T(8,128)S(1)}, u32[]{:S(2)}, u32[]{:S(2)}) %collective-permute-start.31) | collective-permute-done | bytes 98336 | tf_op jit(solution)/shard_map/ppermute | solution.py:43
  121.8 1.5 %collective-permute-done.32 = f32[64,384]{1,0:T(8,128)S(1)} collective-permute-done((f32[64,384]{1,0:T(8,128)S(1)}, f32[64,384]{1,0:T(8,128)S(1)}, u32[]{:S(2)}, u32[]{:S(2)}) %collective-permute-start.32) | collective-permute-done | bytes 98336 | tf_op jit(solution)/shard_map/ppermute | solution.py:43
  (160 shorter events, 30.3 us)
Async XLA Ops:
  26.9 14.6 %all-to-all-start = ((bf16[8,128,128]{2,1,0:T(8,128)(2,1)}), bf16[8,128,128]{2,1,0:T(8,128)(2,1)S(1)}, u32[]{:S(2)}, u32[]{:S(2)}) async-start(bf16[8,128,128]{2,1,0:T(8,128)(2,1)} %bitcast.7), calls=%async_computation | async-start | bytes 524288 | tf_op jit(solution)/shard_map/all_to_all | solution.py:51
  43.4 5.7 %collective-permute-start = (bf16[128,256]{0,1:T(8,128)(2,1)S(1)}, bf16[128,256]{0,1:T(8,128)(2,1)S(1)}, u32[]{:S(2)}, u32[]{:S(2)}) collective-permute-start(bf16[128,256]{0,1:T(8,128)(2,1)S(1)} %pad_maximum_fusion.2), channel_id=1, source_target_pairs={{0,1},{1,2},{2,3},{3,4},{4,5},{5,6},{6,7},{7,0},{8,9},{9,10},{10,1... | collective-permute-start | bytes 196616 | tf_op jit(solution)/shard_map/ppermute | solution.py:43
  43.4 6.9 %collective-permute-start.1 = (bf16[128,256]{0,1:T(8,128)(2,1)S(1)}, bf16[128,256]{0,1:T(8,128)(2,1)S(1)}, u32[]{:S(2)}, u32[]{:S(2)}) collective-permute-start(bf16[128,256]{0,1:T(8,128)(2,1)S(1)} %pad_maximum_fusion.2), channel_id=1, source_target_pairs={{0,2},{1,3},{2,4},{3,5},{4,6},{5,7},{6,0},{7,1},{8,10},{9,11},{10,... | collective-permute-start | bytes 196616 | tf_op jit(solution)/shard_map/ppermute | solution.py:43
  43.6 11.6 %collective-permute-start.2 = (bf16[128,256]{0,1:T(8,128)(2,1)S(1)}, bf16[128,256]{0,1:T(8,128)(2,1)S(1)}, u32[]{:S(2)}, u32[]{:S(2)}) collective-permute-start(bf16[128,256]{0,1:T(8,128)(2,1)S(1)} %pad_maximum_fusion.2), channel_id=1, source_target_pairs={{0,3},{1,4},{2,5},{3,6},{4,7},{5,0},{6,1},{7,2},{8,11},{9,12},{10,... | collective-permute-start | bytes 196616 | tf_op jit(solution)/shard_map/ppermute | solution.py:43
  45.2 10.2 %collective-permute-start.3 = (bf16[128,256]{0,1:T(8,128)(2,1)S(1)}, bf16[128,256]{0,1:T(8,128)(2,1)S(1)}, u32[]{:S(2)}, u32[]{:S(2)}) collective-permute-start(bf16[128,256]{0,1:T(8,128)(2,1)S(1)} %pad_maximum_fusion.2), channel_id=1, source_target_pairs={{0,4},{1,5},{2,6},{3,7},{4,0},{5,1},{6,2},{7,3},{8,12},{9,13},{10,... | collective-permute-start | bytes 196616 | tf_op jit(solution)/shard_map/ppermute | solution.py:43
  47.5 7.9 %collective-permute-start.4 = (bf16[128,256]{0,1:T(8,128)(2,1)S(1)}, bf16[128,256]{0,1:T(8,128)(2,1)S(1)}, u32[]{:S(2)}, u32[]{:S(2)}) collective-permute-start(bf16[128,256]{0,1:T(8,128)(2,1)S(1)} %pad_maximum_fusion.2), channel_id=1, source_target_pairs={{0,5},{1,6},{2,7},{3,0},{4,1},{5,2},{6,3},{7,4},{8,13},{9,14},{10,... | collective-permute-start | bytes 196616 | tf_op jit(solution)/shard_map/ppermute | solution.py:43
  49.1 6.4 %collective-permute-start.5 = (bf16[128,256]{0,1:T(8,128)(2,1)S(1)}, bf16[128,256]{0,1:T(8,128)(2,1)S(1)}, u32[]{:S(2)}, u32[]{:S(2)}) collective-permute-start(bf16[128,256]{0,1:T(8,128)(2,1)S(1)} %pad_maximum_fusion.2), channel_id=1, source_target_pairs={{0,6},{1,7},{2,0},{3,1},{4,2},{5,3},{6,4},{7,5},{8,14},{9,15},{10,... | collective-permute-start | bytes 196616 | tf_op jit(solution)/shard_map/ppermute | solution.py:43
  50.3 5.2 %collective-permute-start.6 = (bf16[128,256]{0,1:T(8,128)(2,1)S(1)}, bf16[128,256]{0,1:T(8,128)(2,1)S(1)}, u32[]{:S(2)}, u32[]{:S(2)}) collective-permute-start(bf16[128,256]{0,1:T(8,128)(2,1)S(1)} %pad_maximum_fusion.2), channel_id=1, source_target_pairs={{0,7},{1,0},{2,1},{3,2},{4,3},{5,4},{6,5},{7,6},{8,15},{9,8},{10,9... | collective-permute-start | bytes 196616 | tf_op jit(solution)/shard_map/ppermute | solution.py:43
  59.5 7.4 %collective-permute-start.7 = (f32[6,1024]{1,0:T(8,128)S(1)}, f32[6,1024]{1,0:T(8,128)S(1)}, u32[]{:S(2)}, u32[]{:S(2)}) collective-permute-start(f32[6,1024]{1,0:T(8,128)S(1)} %concatenate.47), channel_id=1, source_target_pairs={{0,1},{1,2},{2,3},{3,4},{4,5},{5,6},{6,7},{7,0},{8,9},{9,10},{10,1... | collective-permute-start | bytes 73736 | tf_op jit(solution)/shard_map/ppermute | solution.py:43
  61.4 7.7 %collective-permute-start.8 = (f32[6,1024]{1,0:T(8,128)S(1)}, f32[6,1024]{1,0:T(8,128)S(1)}, u32[]{:S(2)}, u32[]{:S(2)}) collective-permute-start(f32[6,1024]{1,0:T(8,128)S(1)} %concatenate.47), channel_id=1, source_target_pairs={{0,2},{1,3},{2,4},{3,5},{4,6},{5,7},{6,0},{7,1},{8,10},{9,11},{10,... | collective-permute-start | bytes 73736 | tf_op jit(solution)/shard_map/ppermute | solution.py:43
  64.1 6.3 %collective-permute-start.9 = (f32[6,1024]{1,0:T(8,128)S(1)}, f32[6,1024]{1,0:T(8,128)S(1)}, u32[]{:S(2)}, u32[]{:S(2)}) collective-permute-start(f32[6,1024]{1,0:T(8,128)S(1)} %concatenate.47), channel_id=1, source_target_pairs={{0,3},{1,4},{2,5},{3,6},{4,7},{5,0},{6,1},{7,2},{8,11},{9,12},{10,... | collective-permute-start | bytes 73736 | tf_op jit(solution)/shard_map/ppermute | solution.py:43
  64.2 6.3 %collective-permute-start.10 = (f32[6,1024]{1,0:T(8,128)S(1)}, f32[6,1024]{1,0:T(8,128)S(1)}, u32[]{:S(2)}, u32[]{:S(2)}) collective-permute-start(f32[6,1024]{1,0:T(8,128)S(1)} %concatenate.47), channel_id=1, source_target_pairs={{0,4},{1,5},{2,6},{3,7},{4,0},{5,1},{6,2},{7,3},{8,12},{9,13},{10,... | collective-permute-start | bytes 73736 | tf_op jit(solution)/shard_map/ppermute | solution.py:43
  66.9 3.6 %collective-permute-start.11 = (f32[6,1024]{1,0:T(8,128)S(1)}, f32[6,1024]{1,0:T(8,128)S(1)}, u32[]{:S(2)}, u32[]{:S(2)}) collective-permute-start(f32[6,1024]{1,0:T(8,128)S(1)} %concatenate.47), channel_id=1, source_target_pairs={{0,5},{1,6},{2,7},{3,0},{4,1},{5,2},{6,3},{7,4},{8,13},{9,14},{10,... | collective-permute-start | bytes 73736 | tf_op jit(solution)/shard_map/ppermute | solution.py:43
  67.0 4.1 %collective-permute-start.12 = (f32[6,1024]{1,0:T(8,128)S(1)}, f32[6,1024]{1,0:T(8,128)S(1)}, u32[]{:S(2)}, u32[]{:S(2)}) collective-permute-start(f32[6,1024]{1,0:T(8,128)S(1)} %concatenate.47), channel_id=1, source_target_pairs={{0,6},{1,7},{2,0},{3,1},{4,2},{5,3},{6,4},{7,5},{8,14},{9,15},{10,... | collective-permute-start | bytes 73736 | tf_op jit(solution)/shard_map/ppermute | solution.py:43
  72.9 4.5 %collective-permute-start.14 = (f32[2,22]{1,0:T(2,128)S(1)}, f32[2,22]{1,0:T(2,128)S(1)}, u32[]{:S(2)}, u32[]{:S(2)}) collective-permute-start(f32[2,22]{1,0:T(2,128)S(1)} %get-tuple-element.54), channel_id=1, source_target_pairs={{0,8},{8,16},{16,24},{24,0},{1,9},{9,17},{17,25},{25,1},{2,10},{10... | collective-permute-start | bytes 536 | tf_op jit(solution)/shard_map/ppermute | solution.py:43
  87.5 5.9 %collective-permute-start.17 = (f32[128,128]{1,0:T(8,128)S(1)}, f32[128,128]{1,0:T(8,128)S(1)}, u32[]{:S(2)}, u32[]{:S(2)}) collective-permute-start(f32[128,128]{1,0:T(8,128)S(1)} %get-tuple-element.34), channel_id=1, source_target_pairs={{0,1},{1,2},{2,3},{3,4},{4,5},{5,6},{6,7},{7,0},{8,9},{9,10},{10,1... | collective-permute-start | bytes 196616 | tf_op jit(solution)/shard_map/ppermute | solution.py:54
  87.6 6.9 %collective-permute-start.18 = (f32[128,128]{1,0:T(8,128)S(1)}, f32[128,128]{1,0:T(8,128)S(1)}, u32[]{:S(2)}, u32[]{:S(2)}) collective-permute-start(f32[128,128]{1,0:T(8,128)S(1)} %get-tuple-element.33), channel_id=1, source_target_pairs={{0,2},{1,3},{2,4},{3,5},{4,6},{5,7},{6,0},{7,1},{8,10},{9,11},{10,... | collective-permute-start | bytes 196616 | tf_op jit(solution)/shard_map/ppermute | solution.py:54
  88.4 10.9 %collective-permute-start.19 = (f32[128,128]{1,0:T(8,128)S(1)}, f32[128,128]{1,0:T(8,128)S(1)}, u32[]{:S(2)}, u32[]{:S(2)}) collective-permute-start(f32[128,128]{1,0:T(8,128)S(1)} %get-tuple-element.32), channel_id=1, source_target_pairs={{0,3},{1,4},{2,5},{3,6},{4,7},{5,0},{6,1},{7,2},{8,11},{9,12},{10,... | collective-permute-start | bytes 196616 | tf_op jit(solution)/shard_map/ppermute | solution.py:54
  91.0 8.5 %collective-permute-start.20 = (f32[128,128]{1,0:T(8,128)S(1)}, f32[128,128]{1,0:T(8,128)S(1)}, u32[]{:S(2)}, u32[]{:S(2)}) collective-permute-start(f32[128,128]{1,0:T(8,128)S(1)} %get-tuple-element.31), channel_id=1, source_target_pairs={{0,4},{1,5},{2,6},{3,7},{4,0},{5,1},{6,2},{7,3},{8,12},{9,13},{10,... | collective-permute-start | bytes 196616 | tf_op jit(solution)/shard_map/ppermute | solution.py:54
  92.2 7.4 %collective-permute-start.21 = (f32[128,128]{1,0:T(8,128)S(1)}, f32[128,128]{1,0:T(8,128)S(1)}, u32[]{:S(2)}, u32[]{:S(2)}) collective-permute-start(f32[128,128]{1,0:T(8,128)S(1)} %get-tuple-element.30), channel_id=1, source_target_pairs={{0,5},{1,6},{2,7},{3,0},{4,1},{5,2},{6,3},{7,4},{8,13},{9,14},{10,... | collective-permute-start | bytes 196616 | tf_op jit(solution)/shard_map/ppermute | solution.py:54
  93.5 7.7 %collective-permute-start.22 = (f32[128,128]{1,0:T(8,128)S(1)}, f32[128,128]{1,0:T(8,128)S(1)}, u32[]{:S(2)}, u32[]{:S(2)}) collective-permute-start(f32[128,128]{1,0:T(8,128)S(1)} %get-tuple-element.29), channel_id=1, source_target_pairs={{0,6},{1,7},{2,0},{3,1},{4,2},{5,3},{6,4},{7,5},{8,14},{9,15},{10,... | collective-permute-start | bytes 196616 | tf_op jit(solution)/shard_map/ppermute | solution.py:54
  94.4 6.7 %collective-permute-start.23 = (f32[128,128]{1,0:T(8,128)S(1)}, f32[128,128]{1,0:T(8,128)S(1)}, u32[]{:S(2)}, u32[]{:S(2)}) collective-permute-start(f32[128,128]{1,0:T(8,128)S(1)} %get-tuple-element.28), channel_id=1, source_target_pairs={{0,7},{1,0},{2,1},{3,2},{4,3},{5,4},{6,5},{7,6},{8,15},{9,8},{10,9... | collective-permute-start | bytes 196616 | tf_op jit(solution)/shard_map/ppermute | solution.py:54
  102.7 6.2 %collective-permute-start.24 = (bf16[64,384]{1,0:T(8,128)(2,1)S(1)}, bf16[64,384]{1,0:T(8,128)(2,1)S(1)}, u32[]{:S(2)}, u32[]{:S(2)}) collective-permute-start(bf16[64,384]{1,0:T(8,128)(2,1)S(1)} %get-tuple-element.42), channel_id=1, source_target_pairs={{0,1},{1,2},{2,3},{3,4},{4,5},{5,6},{6,7},{7,0},{8,9},{9,10},{10,1... | collective-permute-start | bytes 147464 | tf_op jit(solution)/shard_map/ppermute | solution.py:54
  103.3 7.2 %collective-permute-start.25 = (bf16[64,384]{1,0:T(8,128)(2,1)S(1)}, bf16[64,384]{1,0:T(8,128)(2,1)S(1)}, u32[]{:S(2)}, u32[]{:S(2)}) collective-permute-start(bf16[64,384]{1,0:T(8,128)(2,1)S(1)} %get-tuple-element.41), channel_id=1, source_target_pairs={{0,2},{1,3},{2,4},{3,5},{4,6},{5,7},{6,0},{7,1},{8,10},{9,11},{10,... | collective-permute-start | bytes 147464 | tf_op jit(solution)/shard_map/ppermute | solution.py:54
  105.6 7.7 %collective-permute-start.26 = (bf16[64,384]{1,0:T(8,128)(2,1)S(1)}, bf16[64,384]{1,0:T(8,128)(2,1)S(1)}, u32[]{:S(2)}, u32[]{:S(2)}) collective-permute-start(bf16[64,384]{1,0:T(8,128)(2,1)S(1)} %get-tuple-element.40), channel_id=1, source_target_pairs={{0,3},{1,4},{2,5},{3,6},{4,7},{5,0},{6,1},{7,2},{8,11},{9,12},{10,... | collective-permute-start | bytes 147464 | tf_op jit(solution)/shard_map/ppermute | solution.py:54
  106.0 7.6 %collective-permute-start.27 = (bf16[64,384]{1,0:T(8,128)(2,1)S(1)}, bf16[64,384]{1,0:T(8,128)(2,1)S(1)}, u32[]{:S(2)}, u32[]{:S(2)}) collective-permute-start(bf16[64,384]{1,0:T(8,128)(2,1)S(1)} %get-tuple-element.39), channel_id=1, source_target_pairs={{0,4},{1,5},{2,6},{3,7},{4,0},{5,1},{6,2},{7,3},{8,12},{9,13},{10,... | collective-permute-start | bytes 147464 | tf_op jit(solution)/shard_map/ppermute | solution.py:54
  108.3 5.3 %collective-permute-start.28 = (bf16[64,384]{1,0:T(8,128)(2,1)S(1)}, bf16[64,384]{1,0:T(8,128)(2,1)S(1)}, u32[]{:S(2)}, u32[]{:S(2)}) collective-permute-start(bf16[64,384]{1,0:T(8,128)(2,1)S(1)} %get-tuple-element.38), channel_id=1, source_target_pairs={{0,5},{1,6},{2,7},{3,0},{4,1},{5,2},{6,3},{7,4},{8,13},{9,14},{10,... | collective-permute-start | bytes 147464 | tf_op jit(solution)/shard_map/ppermute | solution.py:54
  108.9 6.1 %collective-permute-start.29 = (bf16[64,384]{1,0:T(8,128)(2,1)S(1)}, bf16[64,384]{1,0:T(8,128)(2,1)S(1)}, u32[]{:S(2)}, u32[]{:S(2)}) collective-permute-start(bf16[64,384]{1,0:T(8,128)(2,1)S(1)} %get-tuple-element.37), channel_id=1, source_target_pairs={{0,6},{1,7},{2,0},{3,1},{4,2},{5,3},{6,4},{7,5},{8,14},{9,15},{10,... | collective-permute-start | bytes 147464 | tf_op jit(solution)/shard_map/ppermute | solution.py:54
  110.4 4.5 %collective-permute-start.30 = (bf16[64,384]{1,0:T(8,128)(2,1)S(1)}, bf16[64,384]{1,0:T(8,128)(2,1)S(1)}, u32[]{:S(2)}, u32[]{:S(2)}) collective-permute-start(bf16[64,384]{1,0:T(8,128)(2,1)S(1)} %get-tuple-element.36), channel_id=1, source_target_pairs={{0,7},{1,0},{2,1},{3,2},{4,3},{5,4},{6,5},{7,6},{8,15},{9,8},{10,9... | collective-permute-start | bytes 147464 | tf_op jit(solution)/shard_map/ppermute | solution.py:54
  115.3 6.6 %collective-permute-start.31 = (f32[64,384]{1,0:T(8,128)S(1)}, f32[64,384]{1,0:T(8,128)S(1)}, u32[]{:S(2)}, u32[]{:S(2)}) collective-permute-start(f32[64,384]{1,0:T(8,128)S(1)} %convert_reduce_fusion), channel_id=1, source_target_pairs={{0,8},{8,16},{16,24},{24,0},{1,9},{9,17},{17,25},{25,1},{2,10},{10... | collective-permute-start | bytes 294920 | tf_op jit(solution)/shard_map/ppermute | solution.py:43
  116.7 6.6 %collective-permute-start.32 = (f32[64,384]{1,0:T(8,128)S(1)}, f32[64,384]{1,0:T(8,128)S(1)}, u32[]{:S(2)}, u32[]{:S(2)}) collective-permute-start(f32[64,384]{1,0:T(8,128)S(1)} %convert_reduce_fusion), channel_id=1, source_target_pairs={{0,16},{8,24},{16,0},{24,8},{1,17},{9,25},{17,1},{25,9},{2,18},{10... | collective-permute-start | bytes 294920 | tf_op jit(solution)/shard_map/ppermute | solution.py:43
  118.2 5.1 %collective-permute-start.33 = (f32[64,384]{1,0:T(8,128)S(1)}, f32[64,384]{1,0:T(8,128)S(1)}, u32[]{:S(2)}, u32[]{:S(2)}) collective-permute-start(f32[64,384]{1,0:T(8,128)S(1)} %convert_reduce_fusion), channel_id=1, source_target_pairs={{0,24},{8,0},{16,8},{24,16},{1,25},{9,1},{17,9},{25,17},{2,26},{10... | collective-permute-start | bytes 294920 | tf_op jit(solution)/shard_map/ppermute | solution.py:43
  (6 other events, 89.5 us)

commit v7 on v6

--- a/solution.py
+++ b/solution.py
@@ -200,7 +200,7 @@
     picked_rows = jnp.dot(token_hits, in_embed, preferred_element_type=jnp.float32).astype(
         jnp.bfloat16
     )
-    arrived = exchange_ordered(picked_rows.reshape(fsdp_size, per_device, width), "fsdp", True)
+    arrived = exchange_ordered(picked_rows.reshape(fsdp_size, per_device, width), "fsdp", False)
     embedded = jnp.sum(arrived.astype(jnp.float32), axis=0)
 
     normed = embedded * rms_scale(embedded)

time: 125 us -> 121 us (0.968)
  waiting for transfers between devices: 31.8 us -> 24.2 us
  starting transfers between devices: 46.5 us -> 50.9 us
    all_to_all x1 -> x0, waiting for transfers between devices: 9.09 us -> none  [exchange_ordered(): return lax.all_to_all(blocks, axis, 0, 0, tiled=True)]
    ppermute x14 -> x21, starting transfers between devices: 17.5 us -> 26.2 us  [exchange_ordered(): lax.ppermute(lax.dynamic_index_in_dim(blocks, (here + shift) % size, keep...]
    all_to_all x1 -> x0, starting transfers between devices: 4.81 us -> none  [exchange_ordered(): return lax.all_to_all(blocks, axis, 0, 0, tiled=True)]
    ppermute x14 -> x21, waiting for transfers between devices: 8.25 us -> 10.1 us  [exchange_ordered(): lax.ppermute(lax.dynamic_index_in_dim(blocks, (here + shift) % size, keep...]
    unnamed x31 -> x37, local copies, waits for them, and re-layouts: 4.6 us -> 4.61 us
  transfers between devices with their start and end apart: 35 -> 41, of which waited for: 16 -> 18; matrix products, arithmetic and copies ran while one was open for 1% -> 1% of each run, Pallas kernels for 0% -> 0%
where the time goes in v7:
time: 121 us
  starting transfers between devices  50.9 us (42%)
  waiting for transfers between devices  24.2 us (20%)
  blocking collectives  17.3 us (14%)
  other arithmetic  9.35 us (8%)
  matrix products  8.89 us (7%)
  local copies, waits for them, and re-layouts  7.88 us (7%)
  between operations  2.04 us (2%)
    ppermute x21, starting transfers between devices, exchange_ordered(): lax.ppermute(lax.dynamic_index_in_dim(blocks, (here + shift) % size, keep...  26.2 us
    ppermute x20, starting transfers between devices, gather_ordered(): lax.ppermute(value, axis, shift_pairs(size, shift))  24.7 us
    all_gather x1, blocking collectives, gather_ordered(): return lax.all_gather(value, axis)  17.3 us
    ppermute x20, waiting for transfers between devices, gather_ordered(): lax.ppermute(value, axis, shift_pairs(size, shift))  14 us
    ppermute x21, waiting for transfers between devices, exchange_ordered(): lax.ppermute(lax.dynamic_index_in_dim(blocks, (here + shift) % size, keep...  10.1 us
    unnamed x37, local copies, waits for them, and re-layouts  4.61 us
    dot_general x1, matrix products, one_block(): return jnp.dot(d_logits, table, preferred_element_type=jnp.float32)  3.49 us
  transfers between devices with their start and end apart: 41, of which 18 were waited for; matrix products, arithmetic and copies ran while one was open for 1% of the time, Pallas kernels for 0%

profile of v7, /device:TPU:0, one launch (start us, length us, event | category | flops | bytes accessed | tf_op | source)
XLA Modules:
  0.0 120.5 jit_solution(11247103721546426198)
XLA Ops:
  7.2 17.3 %all-gather.1 = bf16[8,389,128]{2,1,0:T(8,128)(2,1)S(1)} all-gather(bf16[1,389,128]{2,1,0:T(8,128)(2,1)S(1)} %bitcast.222), channel_id=2, replica_groups=mesh['dp'=4,'fsdp'=8] {'fsdp'}, dimensions={0}, use_global_device_ids=true | all-gather | bytes 896256 | tf_op jit(solution)/shard_map/all_gather | solution.py:41
  24.5 1.8 %fusion.3 = bf16[1024,128]{1,0:T(8,128)(2,1)S(1)} fusion(bf16[1024,128]{1,0:T(8,128)(2,1)} %param.19, s32[1024]{0:T(1024)S(1)} %bitcast.250), kind=kOutput, calls=%fused_computation.11 | convolution fusion | flops 269615104 | bytes 528384 | tf_op jit(solution)/shard_map/dot_general | solution.py:200
  26.8 1.6 %collective-permute-start.1 = (bf16[128,128]{1,0:T(8,128)(2,1)S(1)}, bf16[128,128]{1,0:T(8,128)(2,1)S(1)}, u32[]{:S(2)}, u32[]{:S(2)}) collective-permute-start(bf16[128,128]{1,0:T(8,128)(2,1)S(1)} %get-tuple-element.49), channel_id=1, source_target_pairs={{0,2},{1,3},{2,4},{3,5},{4,6},{5,7},{6,0},{7,1},{8,10},{9,11},{10,... | collective-permute-start | bytes 98312 | tf_op jit(solution)/shard_map/ppermute | solution.py:54
  28.4 2.1 %collective-permute-start.2 = (bf16[128,128]{1,0:T(8,128)(2,1)S(1)}, bf16[128,128]{1,0:T(8,128)(2,1)S(1)}, u32[]{:S(2)}, u32[]{:S(2)}) collective-permute-start(bf16[128,128]{1,0:T(8,128)(2,1)S(1)} %get-tuple-element.48), channel_id=1, source_target_pairs={{0,3},{1,4},{2,5},{3,6},{4,7},{5,0},{6,1},{7,2},{8,11},{9,12},{10,... | collective-permute-start | bytes 98312 | tf_op jit(solution)/shard_map/ppermute | solution.py:54
  31.8 1.4 %collective-permute-start.4 = (bf16[128,128]{1,0:T(8,128)(2,1)S(1)}, bf16[128,128]{1,0:T(8,128)(2,1)S(1)}, u32[]{:S(2)}, u32[]{:S(2)}) collective-permute-start(bf16[128,128]{1,0:T(8,128)(2,1)S(1)} %get-tuple-element.46), channel_id=1, source_target_pairs={{0,5},{1,6},{2,7},{3,0},{4,1},{5,2},{6,3},{7,4},{8,13},{9,14},{10,... | collective-permute-start | bytes 98312 | tf_op jit(solution)/shard_map/ppermute | solution.py:54
  36.2 1.7 %collective-permute-done.5 = bf16[128,128]{1,0:T(8,128)(2,1)S(1)} collective-permute-done((bf16[128,128]{1,0:T(8,128)(2,1)S(1)}, bf16[128,128]{1,0:T(8,128)(2,1)S(1)}, u32[]{:S(2)}, u32[]{:S(2)}) %collective-permute-start.5) | collective-permute-done | bytes 32800 | tf_op jit(solution)/shard_map/ppermute | solution.py:54
  41.2 2.0 %collective-permute-start.9 = (bf16[128,256]{0,1:T(8,128)(2,1)S(1)}, bf16[128,256]{0,1:T(8,128)(2,1)S(1)}, u32[]{:S(2)}, u32[]{:S(2)}) collective-permute-start(bf16[128,256]{0,1:T(8,128)(2,1)S(1)} %pad_maximum_fusion.2), channel_id=1, source_target_pairs={{0,3},{1,4},{2,5},{3,6},{4,7},{5,0},{6,1},{7,2},{8,11},{9,12},{10,... | collective-permute-start | bytes 196616 | tf_op jit(solution)/shard_map/ppermute | solution.py:43
  43.2 1.5 %collective-permute-start.10 = (bf16[128,256]{0,1:T(8,128)(2,1)S(1)}, bf16[128,256]{0,1:T(8,128)(2,1)S(1)}, u32[]{:S(2)}, u32[]{:S(2)}) collective-permute-start(bf16[128,256]{0,1:T(8,128)(2,1)S(1)} %pad_maximum_fusion.2), channel_id=1, source_target_pairs={{0,4},{1,5},{2,6},{3,7},{4,0},{5,1},{6,2},{7,3},{8,12},{9,13},{10,... | collective-permute-start | bytes 196616 | tf_op jit(solution)/shard_map/ppermute | solution.py:43
  45.9 1.5 %collective-permute-start.12 = (bf16[128,256]{0,1:T(8,128)(2,1)S(1)}, bf16[128,256]{0,1:T(8,128)(2,1)S(1)}, u32[]{:S(2)}, u32[]{:S(2)}) collective-permute-start(bf16[128,256]{0,1:T(8,128)(2,1)S(1)} %pad_maximum_fusion.2), channel_id=1, source_target_pairs={{0,6},{1,7},{2,0},{3,1},{4,2},{5,3},{6,4},{7,5},{8,14},{9,15},{10,... | collective-permute-start | bytes 196616 | tf_op jit(solution)/shard_map/ppermute | solution.py:43
  47.8 3.9 %collective-permute-done.9 = bf16[128,256]{0,1:T(8,128)(2,1)S(1)} collective-permute-done((bf16[128,256]{0,1:T(8,128)(2,1)S(1)}, bf16[128,256]{0,1:T(8,128)(2,1)S(1)}, u32[]{:S(2)}, u32[]{:S(2)}) %collective-permute-start.9) | collective-permute-done | bytes 65568 | tf_op jit(solution)/shard_map/ppermute | solution.py:43
  52.0 1.6 %collective-permute-done.12 = bf16[128,256]{0,1:T(8,128)(2,1)S(1)} collective-permute-done((bf16[128,256]{0,1:T(8,128)(2,1)S(1)}, bf16[128,256]{0,1:T(8,128)(2,1)S(1)}, u32[]{:S(2)}, u32[]{:S(2)}) %collective-permute-start.12) | collective-permute-done | bytes 65568 | tf_op jit(solution)/shard_map/ppermute | solution.py:43
  55.6 2.0 %select_reduce_fusion = (f32[1024]{0:T(1024)S(1)}, f32[1024]{0:T(1024)S(1)}, f32[1024]{0:T(1024)S(1)}, f32[1024]{0:T(1024)S(1)}) fusion(f32[1024,1024]{0,1:T(8,128)S(1)} %get-tuple-element.76, s32[1024]{0:T(1024)S(1)} %bitcast.247, f32[1024]{0:T(1024)S(1)} %get-tuple-element.75, f32[1024,1024]{0,1:T(8,128)S(1)} %get-tuple-element.74, ...), kind=kLoop, calls=%fused_computation.2 | loop fusion | flops 9433088 | bytes 8417280 | tf_op jit(solution)/shard_map/reduce_sum | solution.py:91
  58.2 2.3 %collective-permute-start.15 = (f32[6,1024]{1,0:T(8,128)S(1)}, f32[6,1024]{1,0:T(8,128)S(1)}, u32[]{:S(2)}, u32[]{:S(2)}) collective-permute-start(f32[6,1024]{1,0:T(8,128)S(1)} %concatenate.52), channel_id=1, source_target_pairs={{0,2},{1,3},{2,4},{3,5},{4,6},{5,7},{6,0},{7,1},{8,10},{9,11},{10,... | collective-permute-start | bytes 73736 | tf_op jit(solution)/shard_map/ppermute | solution.py:43
  61.4 2.0 %collective-permute-start.17 = (f32[6,1024]{1,0:T(8,128)S(1)}, f32[6,1024]{1,0:T(8,128)S(1)}, u32[]{:S(2)}, u32[]{:S(2)}) collective-permute-start(f32[6,1024]{1,0:T(8,128)S(1)} %concatenate.52), channel_id=1, source_target_pairs={{0,4},{1,5},{2,6},{3,7},{4,0},{5,1},{6,2},{7,3},{8,12},{9,13},{10,... | collective-permute-start | bytes 73736 | tf_op jit(solution)/shard_map/ppermute | solution.py:43
  69.5 1.5 %collective-permute-start.21 = (f32[2,22]{1,0:T(2,128)S(1)}, f32[2,22]{1,0:T(2,128)S(1)}, u32[]{:S(2)}, u32[]{:S(2)}) collective-permute-start(f32[2,22]{1,0:T(2,128)S(1)} %get-tuple-element.62), channel_id=1, source_target_pairs={{0,8},{8,16},{16,24},{24,0},{1,9},{9,17},{17,25},{25,1},{2,10},{10... | collective-permute-start | bytes 536 | tf_op jit(solution)/shard_map/ppermute | solution.py:43
  71.0 1.5 %collective-permute-start.22 = (f32[2,22]{1,0:T(2,128)S(1)}, f32[2,22]{1,0:T(2,128)S(1)}, u32[]{:S(2)}, u32[]{:S(2)}) collective-permute-start(f32[2,22]{1,0:T(2,128)S(1)} %get-tuple-element.62), channel_id=1, source_target_pairs={{0,16},{8,24},{16,0},{24,8},{1,17},{9,25},{17,1},{25,9},{2,18},{10... | collective-permute-start | bytes 536 | tf_op jit(solution)/shard_map/ppermute | solution.py:43
  72.6 1.4 %collective-permute-start.23 = (f32[2,22]{1,0:T(2,128)S(1)}, f32[2,22]{1,0:T(2,128)S(1)}, u32[]{:S(2)}, u32[]{:S(2)}) collective-permute-start(f32[2,22]{1,0:T(2,128)S(1)} %get-tuple-element.62), channel_id=1, source_target_pairs={{0,24},{8,0},{16,8},{24,16},{1,25},{9,1},{17,9},{25,17},{2,26},{10... | collective-permute-start | bytes 536 | tf_op jit(solution)/shard_map/ppermute | solution.py:43
  74.6 1.5 %collective-permute-done.23 = f32[2,22]{1,0:T(2,128)S(1)} collective-permute-done((f32[2,22]{1,0:T(2,128)S(1)}, f32[2,22]{1,0:T(2,128)S(1)}, u32[]{:S(2)}, u32[]{:S(2)}) %collective-permute-start.23) | collective-permute-done | bytes 208 | tf_op jit(solution)/shard_map/ppermute | solution.py:43
  78.0 1.8 %bitcast_divide_fusion = (f32[22]{0:T(128)S(1)}, f32[22]{0:T(128)}) fusion(f32[2,22]{1,0:T(2,128)S(1)} %fusion.34, f32[]{:T(128)} %fusion.43, f32[22]{0:T(128)S(1)} %get-tuple-element.19, f32[]{:T(128)} %get-tuple-element.18), kind=kLoop, calls=%fused_computation.176 | loop fusion | flops 132 | bytes 360 | tf_op jit(solution)/shard_map/div | solution.py:243
  80.6 3.5 %fusion.2 = f32[1024,128]{1,0:T(8,128)S(1)} fusion(bf16[1024,128]{1,0:T(8,128)(2,1)S(1)} %copy-done, f32[1024,1024]{0,1:T(8,128)} %copy-done.1, f32[1024]{0:T(1024)S(1)} %bitcast.251, f32[1024]{0:T(1024)S(1)} %broadcast_bitcast_fusion, s32[1024]{0:T(1024)S(1)} %bitcast.248), kind=kOutput, calls=%fused_computation.10 | convolution fusion | flops 274726912 | bytes 4993024 | tf_op jit(solution)/shard_map/dot_general | solution.py:113
  85.3 2.3 %collective-permute-start.26 = (f32[128,128]{1,0:T(8,128)S(1)}, f32[128,128]{1,0:T(8,128)S(1)}, u32[]{:S(2)}, u32[]{:S(2)}) collective-permute-start(f32[128,128]{1,0:T(8,128)S(1)} %get-tuple-element.32), channel_id=1, source_target_pairs={{0,3},{1,4},{2,5},{3,6},{4,7},{5,0},{6,1},{7,2},{8,11},{9,12},{10,... | collective-permute-start | bytes 196616 | tf_op jit(solution)/shard_map/ppermute | solution.py:54
  87.5 1.5 %collective-permute-start.27 = (f32[128,128]{1,0:T(8,128)S(1)}, f32[128,128]{1,0:T(8,128)S(1)}, u32[]{:S(2)}, u32[]{:S(2)}) collective-permute-start(f32[128,128]{1,0:T(8,128)S(1)} %get-tuple-element.31), channel_id=1, source_target_pairs={{0,4},{1,5},{2,6},{3,7},{4,0},{5,1},{6,2},{7,3},{8,12},{9,13},{10,... | collective-permute-start | bytes 196616 | tf_op jit(solution)/shard_map/ppermute | solution.py:54
  91.1 1.5 %collective-permute-start.30 = (f32[128,128]{1,0:T(8,128)S(1)}, f32[128,128]{1,0:T(8,128)S(1)}, u32[]{:S(2)}, u32[]{:S(2)}) collective-permute-start(f32[128,128]{1,0:T(8,128)S(1)} %get-tuple-element.28), channel_id=1, source_target_pairs={{0,7},{1,0},{2,1},{3,2},{4,3},{5,4},{6,5},{7,6},{8,15},{9,8},{10,9... | collective-permute-start | bytes 196616 | tf_op jit(solution)/shard_map/ppermute | solution.py:54
  92.6 3.4 %collective-permute-done.26 = f32[128,128]{1,0:T(8,128)S(1)} collective-permute-done((f32[128,128]{1,0:T(8,128)S(1)}, f32[128,128]{1,0:T(8,128)S(1)}, u32[]{:S(2)}, u32[]{:S(2)}) %collective-permute-start.26) | collective-permute-done | bytes 65568 | tf_op jit(solution)/shard_map/ppermute | solution.py:54
  99.8 2.5 %collective-permute-start.32 = (bf16[64,384]{1,0:T(8,128)(2,1)S(1)}, bf16[64,384]{1,0:T(8,128)(2,1)S(1)}, u32[]{:S(2)}, u32[]{:S(2)}) collective-permute-start(bf16[64,384]{1,0:T(8,128)(2,1)S(1)} %get-tuple-element.41), channel_id=1, source_target_pairs={{0,2},{1,3},{2,4},{3,5},{4,6},{5,7},{6,0},{7,1},{8,10},{9,11},{10,... | collective-permute-start | bytes 147464 | tf_op jit(solution)/shard_map/ppermute | solution.py:54
  102.6 2.3 %collective-permute-start.34 = (bf16[64,384]{1,0:T(8,128)(2,1)S(1)}, bf16[64,384]{1,0:T(8,128)(2,1)S(1)}, u32[]{:S(2)}, u32[]{:S(2)}) collective-permute-start(bf16[64,384]{1,0:T(8,128)(2,1)S(1)} %get-tuple-element.39), channel_id=1, source_target_pairs={{0,4},{1,5},{2,6},{3,7},{4,0},{5,1},{6,2},{7,3},{8,12},{9,13},{10,... | collective-permute-start | bytes 147464 | tf_op jit(solution)/shard_map/ppermute | solution.py:54
  105.5 1.5 %collective-permute-start.36 = (bf16[64,384]{1,0:T(8,128)(2,1)S(1)}, bf16[64,384]{1,0:T(8,128)(2,1)S(1)}, u32[]{:S(2)}, u32[]{:S(2)}) collective-permute-start(bf16[64,384]{1,0:T(8,128)(2,1)S(1)} %get-tuple-element.37), channel_id=1, source_target_pairs={{0,6},{1,7},{2,0},{3,1},{4,2},{5,3},{6,4},{7,5},{8,14},{9,15},{10,... | collective-permute-start | bytes 147464 | tf_op jit(solution)/shard_map/ppermute | solution.py:54
  107.1 1.4 %collective-permute-start.37 = (bf16[64,384]{1,0:T(8,128)(2,1)S(1)}, bf16[64,384]{1,0:T(8,128)(2,1)S(1)}, u32[]{:S(2)}, u32[]{:S(2)}) collective-permute-start(bf16[64,384]{1,0:T(8,128)(2,1)S(1)} %get-tuple-element.36), channel_id=1, source_target_pairs={{0,7},{1,0},{2,1},{3,2},{4,3},{5,4},{6,5},{7,6},{8,15},{9,8},{10,9... | collective-permute-start | bytes 147464 | tf_op jit(solution)/shard_map/ppermute | solution.py:54
  111.7 1.4 %collective-permute-start.38 = (f32[64,384]{1,0:T(8,128)S(1)}, f32[64,384]{1,0:T(8,128)S(1)}, u32[]{:S(2)}, u32[]{:S(2)}) collective-permute-start(f32[64,384]{1,0:T(8,128)S(1)} %convert_reduce_fusion), channel_id=1, source_target_pairs={{0,8},{8,16},{16,24},{24,0},{1,9},{9,17},{17,25},{25,1},{2,10},{10... | collective-permute-start | bytes 294920 | tf_op jit(solution)/shard_map/ppermute | solution.py:43
  113.1 1.5 %collective-permute-start.39 = (f32[64,384]{1,0:T(8,128)S(1)}, f32[64,384]{1,0:T(8,128)S(1)}, u32[]{:S(2)}, u32[]{:S(2)}) collective-permute-start(f32[64,384]{1,0:T(8,128)S(1)} %convert_reduce_fusion), channel_id=1, source_target_pairs={{0,16},{8,24},{16,0},{24,8},{1,17},{9,25},{17,1},{25,9},{2,18},{10... | collective-permute-start | bytes 294920 | tf_op jit(solution)/shard_map/ppermute | solution.py:43
  115.2 3.1 %collective-permute-done.38 = f32[64,384]{1,0:T(8,128)S(1)} collective-permute-done((f32[64,384]{1,0:T(8,128)S(1)}, f32[64,384]{1,0:T(8,128)S(1)}, u32[]{:S(2)}, u32[]{:S(2)}) %collective-permute-start.38) | collective-permute-done | bytes 98336 | tf_op jit(solution)/shard_map/ppermute | solution.py:43
  118.2 1.5 %collective-permute-done.39 = f32[64,384]{1,0:T(8,128)S(1)} collective-permute-done((f32[64,384]{1,0:T(8,128)S(1)}, f32[64,384]{1,0:T(8,128)S(1)}, u32[]{:S(2)}, u32[]{:S(2)}) %collective-permute-start.39) | collective-permute-done | bytes 98336 | tf_op jit(solution)/shard_map/ppermute | solution.py:43
  (181 shorter events, 40.6 us)
Async XLA Ops:
  26.3 7.5 %collective-permute-start = (bf16[128,128]{1,0:T(8,128)(2,1)S(1)}, bf16[128,128]{1,0:T(8,128)(2,1)S(1)}, u32[]{:S(2)}, u32[]{:S(2)}) collective-permute-start(bf16[128,128]{1,0:T(8,128)(2,1)S(1)} %get-tuple-element.50), channel_id=1, source_target_pairs={{0,1},{1,2},{2,3},{3,4},{4,5},{5,6},{6,7},{7,0},{8,9},{9,10},{10,1... | collective-permute-start | bytes 98312 | tf_op jit(solution)/shard_map/ppermute | solution.py:54
  26.8 7.9 %collective-permute-start.1 = (bf16[128,128]{1,0:T(8,128)(2,1)S(1)}, bf16[128,128]{1,0:T(8,128)(2,1)S(1)}, u32[]{:S(2)}, u32[]{:S(2)}) collective-permute-start(bf16[128,128]{1,0:T(8,128)(2,1)S(1)} %get-tuple-element.49), channel_id=1, source_target_pairs={{0,2},{1,3},{2,4},{3,5},{4,6},{5,7},{6,0},{7,1},{8,10},{9,11},{10,... | collective-permute-start | bytes 98312 | tf_op jit(solution)/shard_map/ppermute | solution.py:54
  28.4 7.0 %collective-permute-start.2 = (bf16[128,128]{1,0:T(8,128)(2,1)S(1)}, bf16[128,128]{1,0:T(8,128)(2,1)S(1)}, u32[]{:S(2)}, u32[]{:S(2)}) collective-permute-start(bf16[128,128]{1,0:T(8,128)(2,1)S(1)} %get-tuple-element.48), channel_id=1, source_target_pairs={{0,3},{1,4},{2,5},{3,6},{4,7},{5,0},{6,1},{7,2},{8,11},{9,12},{10,... | collective-permute-start | bytes 98312 | tf_op jit(solution)/shard_map/ppermute | solution.py:54
  30.5 5.6 %collective-permute-start.3 = (bf16[128,128]{1,0:T(8,128)(2,1)S(1)}, bf16[128,128]{1,0:T(8,128)(2,1)S(1)}, u32[]{:S(2)}, u32[]{:S(2)}) collective-permute-start(bf16[128,128]{1,0:T(8,128)(2,1)S(1)} %get-tuple-element.47), channel_id=1, source_target_pairs={{0,4},{1,5},{2,6},{3,7},{4,0},{5,1},{6,2},{7,3},{8,12},{9,13},{10,... | collective-permute-start | bytes 98312 | tf_op jit(solution)/shard_map/ppermute | solution.py:54
  39.9 6.0 %collective-permute-start.7 = (bf16[128,256]{0,1:T(8,128)(2,1)S(1)}, bf16[128,256]{0,1:T(8,128)(2,1)S(1)}, u32[]{:S(2)}, u32[]{:S(2)}) collective-permute-start(bf16[128,256]{0,1:T(8,128)(2,1)S(1)} %pad_maximum_fusion.2), channel_id=1, source_target_pairs={{0,1},{1,2},{2,3},{3,4},{4,5},{5,6},{6,7},{7,0},{8,9},{9,10},{10,1... | collective-permute-start | bytes 196616 | tf_op jit(solution)/shard_map/ppermute | solution.py:43
  40.9 6.7 %collective-permute-start.8 = (bf16[128,256]{0,1:T(8,128)(2,1)S(1)}, bf16[128,256]{0,1:T(8,128)(2,1)S(1)}, u32[]{:S(2)}, u32[]{:S(2)}) collective-permute-start(bf16[128,256]{0,1:T(8,128)(2,1)S(1)} %pad_maximum_fusion.2), channel_id=1, source_target_pairs={{0,2},{1,3},{2,4},{3,5},{4,6},{5,7},{6,0},{7,1},{8,10},{9,11},{10,... | collective-permute-start | bytes 196616 | tf_op jit(solution)/shard_map/ppermute | solution.py:43
  41.2 10.5 %collective-permute-start.9 = (bf16[128,256]{0,1:T(8,128)(2,1)S(1)}, bf16[128,256]{0,1:T(8,128)(2,1)S(1)}, u32[]{:S(2)}, u32[]{:S(2)}) collective-permute-start(bf16[128,256]{0,1:T(8,128)(2,1)S(1)} %pad_maximum_fusion.2), channel_id=1, source_target_pairs={{0,3},{1,4},{2,5},{3,6},{4,7},{5,0},{6,1},{7,2},{8,11},{9,12},{10,... | collective-permute-start | bytes 196616 | tf_op jit(solution)/shard_map/ppermute | solution.py:43
  43.2 8.7 %collective-permute-start.10 = (bf16[128,256]{0,1:T(8,128)(2,1)S(1)}, bf16[128,256]{0,1:T(8,128)(2,1)S(1)}, u32[]{:S(2)}, u32[]{:S(2)}) collective-permute-start(bf16[128,256]{0,1:T(8,128)(2,1)S(1)} %pad_maximum_fusion.2), channel_id=1, source_target_pairs={{0,4},{1,5},{2,6},{3,7},{4,0},{5,1},{6,2},{7,3},{8,12},{9,13},{10,... | collective-permute-start | bytes 196616 | tf_op jit(solution)/shard_map/ppermute | solution.py:43
  44.7 7.3 %collective-permute-start.11 = (bf16[128,256]{0,1:T(8,128)(2,1)S(1)}, bf16[128,256]{0,1:T(8,128)(2,1)S(1)}, u32[]{:S(2)}, u32[]{:S(2)}) collective-permute-start(bf16[128,256]{0,1:T(8,128)(2,1)S(1)} %pad_maximum_fusion.2), channel_id=1, source_target_pairs={{0,5},{1,6},{2,7},{3,0},{4,1},{5,2},{6,3},{7,4},{8,13},{9,14},{10,... | collective-permute-start | bytes 196616 | tf_op jit(solution)/shard_map/ppermute | solution.py:43
  45.9 7.6 %collective-permute-start.12 = (bf16[128,256]{0,1:T(8,128)(2,1)S(1)}, bf16[128,256]{0,1:T(8,128)(2,1)S(1)}, u32[]{:S(2)}, u32[]{:S(2)}) collective-permute-start(bf16[128,256]{0,1:T(8,128)(2,1)S(1)} %pad_maximum_fusion.2), channel_id=1, source_target_pairs={{0,6},{1,7},{2,0},{3,1},{4,2},{5,3},{6,4},{7,5},{8,14},{9,15},{10,... | collective-permute-start | bytes 196616 | tf_op jit(solution)/shard_map/ppermute | solution.py:43
  47.6 6.0 %collective-permute-start.13 = (bf16[128,256]{0,1:T(8,128)(2,1)S(1)}, bf16[128,256]{0,1:T(8,128)(2,1)S(1)}, u32[]{:S(2)}, u32[]{:S(2)}) collective-permute-start(bf16[128,256]{0,1:T(8,128)(2,1)S(1)} %pad_maximum_fusion.2), channel_id=1, source_target_pairs={{0,7},{1,0},{2,1},{3,2},{4,3},{5,4},{6,5},{7,6},{8,15},{9,8},{10,9... | collective-permute-start | bytes 196616 | tf_op jit(solution)/shard_map/ppermute | solution.py:43
  57.6 6.8 %collective-permute-start.14 = (f32[6,1024]{1,0:T(8,128)S(1)}, f32[6,1024]{1,0:T(8,128)S(1)}, u32[]{:S(2)}, u32[]{:S(2)}) collective-permute-start(f32[6,1024]{1,0:T(8,128)S(1)} %concatenate.52), channel_id=1, source_target_pairs={{0,1},{1,2},{2,3},{3,4},{4,5},{5,6},{6,7},{7,0},{8,9},{9,10},{10,1... | collective-permute-start | bytes 73736 | tf_op jit(solution)/shard_map/ppermute | solution.py:43
  58.2 7.4 %collective-permute-start.15 = (f32[6,1024]{1,0:T(8,128)S(1)}, f32[6,1024]{1,0:T(8,128)S(1)}, u32[]{:S(2)}, u32[]{:S(2)}) collective-permute-start(f32[6,1024]{1,0:T(8,128)S(1)} %concatenate.52), channel_id=1, source_target_pairs={{0,2},{1,3},{2,4},{3,5},{4,6},{5,7},{6,0},{7,1},{8,10},{9,11},{10,... | collective-permute-start | bytes 73736 | tf_op jit(solution)/shard_map/ppermute | solution.py:43
  60.6 6.3 %collective-permute-start.16 = (f32[6,1024]{1,0:T(8,128)S(1)}, f32[6,1024]{1,0:T(8,128)S(1)}, u32[]{:S(2)}, u32[]{:S(2)}) collective-permute-start(f32[6,1024]{1,0:T(8,128)S(1)} %concatenate.52), channel_id=1, source_target_pairs={{0,3},{1,4},{2,5},{3,6},{4,7},{5,0},{6,1},{7,2},{8,11},{9,12},{10,... | collective-permute-start | bytes 73736 | tf_op jit(solution)/shard_map/ppermute | solution.py:43
  61.4 6.2 %collective-permute-start.17 = (f32[6,1024]{1,0:T(8,128)S(1)}, f32[6,1024]{1,0:T(8,128)S(1)}, u32[]{:S(2)}, u32[]{:S(2)}) collective-permute-start(f32[6,1024]{1,0:T(8,128)S(1)} %concatenate.52), channel_id=1, source_target_pairs={{0,4},{1,5},{2,6},{3,7},{4,0},{5,1},{6,2},{7,3},{8,12},{9,13},{10,... | collective-permute-start | bytes 73736 | tf_op jit(solution)/shard_map/ppermute | solution.py:43
  69.5 4.5 %collective-permute-start.21 = (f32[2,22]{1,0:T(2,128)S(1)}, f32[2,22]{1,0:T(2,128)S(1)}, u32[]{:S(2)}, u32[]{:S(2)}) collective-permute-start(f32[2,22]{1,0:T(2,128)S(1)} %get-tuple-element.62), channel_id=1, source_target_pairs={{0,8},{8,16},{16,24},{24,0},{1,9},{9,17},{17,25},{25,1},{2,10},{10... | collective-permute-start | bytes 536 | tf_op jit(solution)/shard_map/ppermute | solution.py:43
  84.1 5.8 %collective-permute-start.24 = (f32[128,128]{1,0:T(8,128)S(1)}, f32[128,128]{1,0:T(8,128)S(1)}, u32[]{:S(2)}, u32[]{:S(2)}) collective-permute-start(f32[128,128]{1,0:T(8,128)S(1)} %get-tuple-element.34), channel_id=1, source_target_pairs={{0,1},{1,2},{2,3},{3,4},{4,5},{5,6},{6,7},{7,0},{8,9},{9,10},{10,1... | collective-permute-start | bytes 196616 | tf_op jit(solution)/shard_map/ppermute | solution.py:54
  84.2 6.9 %collective-permute-start.25 = (f32[128,128]{1,0:T(8,128)S(1)}, f32[128,128]{1,0:T(8,128)S(1)}, u32[]{:S(2)}, u32[]{:S(2)}) collective-permute-start(f32[128,128]{1,0:T(8,128)S(1)} %get-tuple-element.33), channel_id=1, source_target_pairs={{0,2},{1,3},{2,4},{3,5},{4,6},{5,7},{6,0},{7,1},{8,10},{9,11},{10,... | collective-permute-start | bytes 196616 | tf_op jit(solution)/shard_map/ppermute | solution.py:54
  85.3 10.7 %collective-permute-start.26 = (f32[128,128]{1,0:T(8,128)S(1)}, f32[128,128]{1,0:T(8,128)S(1)}, u32[]{:S(2)}, u32[]{:S(2)}) collective-permute-start(f32[128,128]{1,0:T(8,128)S(1)} %get-tuple-element.32), channel_id=1, source_target_pairs={{0,3},{1,4},{2,5},{3,6},{4,7},{5,0},{6,1},{7,2},{8,11},{9,12},{10,... | collective-permute-start | bytes 196616 | tf_op jit(solution)/shard_map/ppermute | solution.py:54
  87.5 8.7 %collective-permute-start.27 = (f32[128,128]{1,0:T(8,128)S(1)}, f32[128,128]{1,0:T(8,128)S(1)}, u32[]{:S(2)}, u32[]{:S(2)}) collective-permute-start(f32[128,128]{1,0:T(8,128)S(1)} %get-tuple-element.31), channel_id=1, source_target_pairs={{0,4},{1,5},{2,6},{3,7},{4,0},{5,1},{6,2},{7,3},{8,12},{9,13},{10,... | collective-permute-start | bytes 196616 | tf_op jit(solution)/shard_map/ppermute | solution.py:54
  89.0 7.2 %collective-permute-start.28 = (f32[128,128]{1,0:T(8,128)S(1)}, f32[128,128]{1,0:T(8,128)S(1)}, u32[]{:S(2)}, u32[]{:S(2)}) collective-permute-start(f32[128,128]{1,0:T(8,128)S(1)} %get-tuple-element.30), channel_id=1, source_target_pairs={{0,5},{1,6},{2,7},{3,0},{4,1},{5,2},{6,3},{7,4},{8,13},{9,14},{10,... | collective-permute-start | bytes 196616 | tf_op jit(solution)/shard_map/ppermute | solution.py:54
  90.0 7.5 %collective-permute-start.29 = (f32[128,128]{1,0:T(8,128)S(1)}, f32[128,128]{1,0:T(8,128)S(1)}, u32[]{:S(2)}, u32[]{:S(2)}) collective-permute-start(f32[128,128]{1,0:T(8,128)S(1)} %get-tuple-element.29), channel_id=1, source_target_pairs={{0,6},{1,7},{2,0},{3,1},{4,2},{5,3},{6,4},{7,5},{8,14},{9,15},{10,... | collective-permute-start | bytes 196616 | tf_op jit(solution)/shard_map/ppermute | solution.py:54
  91.1 6.4 %collective-permute-start.30 = (f32[128,128]{1,0:T(8,128)S(1)}, f32[128,128]{1,0:T(8,128)S(1)}, u32[]{:S(2)}, u32[]{:S(2)}) collective-permute-start(f32[128,128]{1,0:T(8,128)S(1)} %get-tuple-element.28), channel_id=1, source_target_pairs={{0,7},{1,0},{2,1},{3,2},{4,3},{5,4},{6,5},{7,6},{8,15},{9,8},{10,9... | collective-permute-start | bytes 196616 | tf_op jit(solution)/shard_map/ppermute | solution.py:54
  99.1 6.4 %collective-permute-start.31 = (bf16[64,384]{1,0:T(8,128)(2,1)S(1)}, bf16[64,384]{1,0:T(8,128)(2,1)S(1)}, u32[]{:S(2)}, u32[]{:S(2)}) collective-permute-start(bf16[64,384]{1,0:T(8,128)(2,1)S(1)} %get-tuple-element.42), channel_id=1, source_target_pairs={{0,1},{1,2},{2,3},{3,4},{4,5},{5,6},{6,7},{7,0},{8,9},{9,10},{10,1... | collective-permute-start | bytes 147464 | tf_op jit(solution)/shard_map/ppermute | solution.py:54
  99.8 7.3 %collective-permute-start.32 = (bf16[64,384]{1,0:T(8,128)(2,1)S(1)}, bf16[64,384]{1,0:T(8,128)(2,1)S(1)}, u32[]{:S(2)}, u32[]{:S(2)}) collective-permute-start(bf16[64,384]{1,0:T(8,128)(2,1)S(1)} %get-tuple-element.41), channel_id=1, source_target_pairs={{0,2},{1,3},{2,4},{3,5},{4,6},{5,7},{6,0},{7,1},{8,10},{9,11},{10,... | collective-permute-start | bytes 147464 | tf_op jit(solution)/shard_map/ppermute | solution.py:54
  102.2 7.0 %collective-permute-start.33 = (bf16[64,384]{1,0:T(8,128)(2,1)S(1)}, bf16[64,384]{1,0:T(8,128)(2,1)S(1)}, u32[]{:S(2)}, u32[]{:S(2)}) collective-permute-start(bf16[64,384]{1,0:T(8,128)(2,1)S(1)} %get-tuple-element.40), channel_id=1, source_target_pairs={{0,3},{1,4},{2,5},{3,6},{4,7},{5,0},{6,1},{7,2},{8,11},{9,12},{10,... | collective-permute-start | bytes 147464 | tf_op jit(solution)/shard_map/ppermute | solution.py:54
  102.6 7.6 %collective-permute-start.34 = (bf16[64,384]{1,0:T(8,128)(2,1)S(1)}, bf16[64,384]{1,0:T(8,128)(2,1)S(1)}, u32[]{:S(2)}, u32[]{:S(2)}) collective-permute-start(bf16[64,384]{1,0:T(8,128)(2,1)S(1)} %get-tuple-element.39), channel_id=1, source_target_pairs={{0,4},{1,5},{2,6},{3,7},{4,0},{5,1},{6,2},{7,3},{8,12},{9,13},{10,... | collective-permute-start | bytes 147464 | tf_op jit(solution)/shard_map/ppermute | solution.py:54
  105.0 5.3 %collective-permute-start.35 = (bf16[64,384]{1,0:T(8,128)(2,1)S(1)}, bf16[64,384]{1,0:T(8,128)(2,1)S(1)}, u32[]{:S(2)}, u32[]{:S(2)}) collective-permute-start(bf16[64,384]{1,0:T(8,128)(2,1)S(1)} %get-tuple-element.38), channel_id=1, source_target_pairs={{0,5},{1,6},{2,7},{3,0},{4,1},{5,2},{6,3},{7,4},{8,13},{9,14},{10,... | collective-permute-start | bytes 147464 | tf_op jit(solution)/shard_map/ppermute | solution.py:54
  105.5 5.9 %collective-permute-start.36 = (bf16[64,384]{1,0:T(8,128)(2,1)S(1)}, bf16[64,384]{1,0:T(8,128)(2,1)S(1)}, u32[]{:S(2)}, u32[]{:S(2)}) collective-permute-start(bf16[64,384]{1,0:T(8,128)(2,1)S(1)} %get-tuple-element.37), channel_id=1, source_target_pairs={{0,6},{1,7},{2,0},{3,1},{4,2},{5,3},{6,4},{7,5},{8,14},{9,15},{10,... | collective-permute-start | bytes 147464 | tf_op jit(solution)/shard_map/ppermute | solution.py:54
  111.7 6.6 %collective-permute-start.38 = (f32[64,384]{1,0:T(8,128)S(1)}, f32[64,384]{1,0:T(8,128)S(1)}, u32[]{:S(2)}, u32[]{:S(2)}) collective-permute-start(f32[64,384]{1,0:T(8,128)S(1)} %convert_reduce_fusion), channel_id=1, source_target_pairs={{0,8},{8,16},{16,24},{24,0},{1,9},{9,17},{17,25},{25,1},{2,10},{10... | collective-permute-start | bytes 294920 | tf_op jit(solution)/shard_map/ppermute | solution.py:43
  113.1 6.6 %collective-permute-start.39 = (f32[64,384]{1,0:T(8,128)S(1)}, f32[64,384]{1,0:T(8,128)S(1)}, u32[]{:S(2)}, u32[]{:S(2)}) collective-permute-start(f32[64,384]{1,0:T(8,128)S(1)} %convert_reduce_fusion), channel_id=1, source_target_pairs={{0,16},{8,24},{16,0},{24,8},{1,17},{9,25},{17,1},{25,9},{2,18},{10... | collective-permute-start | bytes 294920 | tf_op jit(solution)/shard_map/ppermute | solution.py:43
  114.6 5.1 %collective-permute-start.40 = (f32[64,384]{1,0:T(8,128)S(1)}, f32[64,384]{1,0:T(8,128)S(1)}, u32[]{:S(2)}, u32[]{:S(2)}) collective-permute-start(f32[64,384]{1,0:T(8,128)S(1)} %convert_reduce_fusion), channel_id=1, source_target_pairs={{0,24},{8,0},{16,8},{24,16},{1,25},{9,1},{17,9},{25,17},{2,26},{10... | collective-permute-start | bytes 294920 | tf_op jit(solution)/shard_map/ppermute | solution.py:43
  (12 other events, 110.3 us)

commit v8 on v7

--- a/solution.py
+++ b/solution.py
@@ -174,7 +174,7 @@
     extra_rows = small.reshape(small_count, width)[id_count:]
     matrix_rows = len(matrices) * unit_rows
     packed = jnp.concatenate(list(matrices) + [small.reshape(small_count, width)], axis=0)
-    gathered = gather_ordered(packed, "fsdp", True)
+    gathered = gather_ordered(packed, "fsdp", False)
     full_matrices = [
         gathered[:, index * unit_rows : (index + 1) * unit_rows].reshape(-1, width)
         for index in range(len(matrices))

time: 121 us -> 125 us (1.033)
  blocking collectives: 17.3 us -> 0 us
  starting transfers between devices: 50.9 us -> 65.9 us
  waiting for transfers between devices: 24.2 us -> 30.1 us
    all_gather x1 -> x0, blocking collectives: 17.3 us -> none  [gather_ordered(): return lax.all_gather(value, axis)]
    ppermute x20 -> x27, starting transfers between devices: 24.7 us -> 35.5 us  [gather_ordered(): lax.ppermute(value, axis, shift_pairs(size, shift))]
    ppermute x20 -> x27, waiting for transfers between devices: 14 us -> 19.7 us  [gather_ordered(): lax.ppermute(value, axis, shift_pairs(size, shift))]
    ppermute x21, starting transfers between devices: 26.2 us -> 30.4 us  [exchange_ordered(): lax.ppermute(lax.dynamic_index_in_dim(blocks, (here + shift) % size, keep...]
    unnamed x37 -> x46, local copies, waits for them, and re-layouts: 4.61 us -> 4.77 us
  transfers between devices with their start and end apart: 41 -> 48, of which waited for: 18 -> 19; matrix products, arithmetic and copies ran while one was open for 1% -> 1% of each run, Pallas kernels for 0% -> 0%
where the time goes in v8:
time: 125 us; the launch traced here: 124 us
  starting transfers between devices  65.9 us (53%)
  waiting for transfers between devices  30.1 us (24%)
  other arithmetic  9.67 us (8%)
  local copies, waits for them, and re-layouts  8.11 us (6%)
  matrix products  7.95 us (6%)
  between operations  2.2 us (2%)
    ppermute x27, starting transfers between devices, gather_ordered(): lax.ppermute(value, axis, shift_pairs(size, shift))  35.5 us
    ppermute x21, starting transfers between devices, exchange_ordered(): lax.ppermute(lax.dynamic_index_in_dim(blocks, (here + shift) % size, keep...  30.4 us
    ppermute x27, waiting for transfers between devices, gather_ordered(): lax.ppermute(value, axis, shift_pairs(size, shift))  19.7 us
    ppermute x21, waiting for transfers between devices, exchange_ordered(): lax.ppermute(lax.dynamic_index_in_dim(blocks, (here + shift) % size, keep...  10.4 us
    unnamed x46, local copies, waits for them, and re-layouts  4.77 us
    dot_general x1, matrix products, one_block(): return jnp.dot(d_logits, table, preferred_element_type=jnp.float32)  3.49 us
  transfers between devices with their start and end apart: 48, of which 19 were waited for; matrix products, arithmetic and copies ran while one was open for 1% of the time, Pallas kernels for 0%

profile of v8, /device:TPU:0, one launch (start us, length us, event | category | flops | bytes accessed | tf_op | source)
XLA Modules:
  0.0 123.9 jit_solution(9584480030515987664)
XLA Ops:
  7.7 2.6 %collective-permute-start.1 = (bf16[389,128]{1,0:T(8,128)(2,1)S(1)}, bf16[389,128]{1,0:T(8,128)(2,1)S(1)}, u32[]{:S(2)}, u32[]{:S(2)}) collective-permute-start(bf16[389,128]{1,0:T(8,128)(2,1)S(1)} %constant_dynamic-update-slice_fusion), channel_id=1, source_target_pairs={{0,2},{1,3},{2,4},{3,5},{4,6},{5,7},{6,0},{7,1},{8,10},{9,11},{10,... | collective-permute-start | bytes 298760 | tf_op jit(solution)/shard_map/ppermute | solution.py:43
  10.3 2.5 %collective-permute-start.2 = (bf16[389,128]{1,0:T(8,128)(2,1)S(1)}, bf16[389,128]{1,0:T(8,128)(2,1)S(1)}, u32[]{:S(2)}, u32[]{:S(2)}) collective-permute-start(bf16[389,128]{1,0:T(8,128)(2,1)S(1)} %constant_dynamic-update-slice_fusion), channel_id=1, source_target_pairs={{0,3},{1,4},{2,5},{3,6},{4,7},{5,0},{6,1},{7,2},{8,11},{9,12},{10,... | collective-permute-start | bytes 298760 | tf_op jit(solution)/shard_map/ppermute | solution.py:43
  15.4 1.4 %collective-permute-start.5 = (bf16[389,128]{1,0:T(8,128)(2,1)S(1)}, bf16[389,128]{1,0:T(8,128)(2,1)S(1)}, u32[]{:S(2)}, u32[]{:S(2)}) collective-permute-start(bf16[389,128]{1,0:T(8,128)(2,1)S(1)} %constant_dynamic-update-slice_fusion), channel_id=1, source_target_pairs={{0,6},{1,7},{2,0},{3,1},{4,2},{5,3},{6,4},{7,5},{8,14},{9,15},{10,... | collective-permute-start | bytes 298760 | tf_op jit(solution)/shard_map/ppermute | solution.py:43
  16.8 1.5 %collective-permute-start.6 = (bf16[389,128]{1,0:T(8,128)(2,1)S(1)}, bf16[389,128]{1,0:T(8,128)(2,1)S(1)}, u32[]{:S(2)}, u32[]{:S(2)}) collective-permute-start(bf16[389,128]{1,0:T(8,128)(2,1)S(1)} %constant_dynamic-update-slice_fusion), channel_id=1, source_target_pairs={{0,7},{1,0},{2,1},{3,2},{4,3},{5,4},{6,5},{7,6},{8,15},{9,8},{10,9... | collective-permute-start | bytes 298760 | tf_op jit(solution)/shard_map/ppermute | solution.py:43
  18.4 5.3 %collective-permute-done.2 = bf16[389,128]{1,0:T(8,128)(2,1)S(1)} collective-permute-done((bf16[389,128]{1,0:T(8,128)(2,1)S(1)}, bf16[389,128]{1,0:T(8,128)(2,1)S(1)}, u32[]{:S(2)}, u32[]{:S(2)}) %collective-permute-start.2) | collective-permute-done | bytes 99616 | tf_op jit(solution)/shard_map/ppermute | solution.py:43
  25.4 2.3 %collective-permute-start.7 = (bf16[128,128]{1,0:T(8,128)(2,1)S(1)}, bf16[128,128]{1,0:T(8,128)(2,1)S(1)}, u32[]{:S(2)}, u32[]{:S(2)}) collective-permute-start(bf16[128,128]{1,0:T(8,128)(2,1)S(1)} %get-tuple-element.50), channel_id=1, source_target_pairs={{0,1},{1,2},{2,3},{3,4},{4,5},{5,6},{6,7},{7,0},{8,9},{9,10},{10,1... | collective-permute-start | bytes 98312 | tf_op jit(solution)/shard_map/ppermute | solution.py:54
  28.0 4.3 %collective-permute-start.8 = (bf16[128,128]{1,0:T(8,128)(2,1)S(1)}, bf16[128,128]{1,0:T(8,128)(2,1)S(1)}, u32[]{:S(2)}, u32[]{:S(2)}) collective-permute-start(bf16[128,128]{1,0:T(8,128)(2,1)S(1)} %get-tuple-element.49), channel_id=1, source_target_pairs={{0,2},{1,3},{2,4},{3,5},{4,6},{5,7},{6,0},{7,1},{8,10},{9,11},{10,... | collective-permute-start | bytes 98312 | tf_op jit(solution)/shard_map/ppermute | solution.py:54
  33.2 2.0 %collective-permute-start.10 = (bf16[128,128]{1,0:T(8,128)(2,1)S(1)}, bf16[128,128]{1,0:T(8,128)(2,1)S(1)}, u32[]{:S(2)}, u32[]{:S(2)}) collective-permute-start(bf16[128,128]{1,0:T(8,128)(2,1)S(1)} %get-tuple-element.47), channel_id=1, source_target_pairs={{0,4},{1,5},{2,6},{3,7},{4,0},{5,1},{6,2},{7,3},{8,12},{9,13},{10,... | collective-permute-start | bytes 98312 | tf_op jit(solution)/shard_map/ppermute | solution.py:54
  35.2 1.7 %collective-permute-start.11 = (bf16[128,128]{1,0:T(8,128)(2,1)S(1)}, bf16[128,128]{1,0:T(8,128)(2,1)S(1)}, u32[]{:S(2)}, u32[]{:S(2)}) collective-permute-start(bf16[128,128]{1,0:T(8,128)(2,1)S(1)} %get-tuple-element.46), channel_id=1, source_target_pairs={{0,5},{1,6},{2,7},{3,0},{4,1},{5,2},{6,3},{7,4},{8,13},{9,14},{10,... | collective-permute-start | bytes 98312 | tf_op jit(solution)/shard_map/ppermute | solution.py:54
  38.9 2.2 %collective-permute-done.12 = bf16[128,128]{1,0:T(8,128)(2,1)S(1)} collective-permute-done((bf16[128,128]{1,0:T(8,128)(2,1)S(1)}, bf16[128,128]{1,0:T(8,128)(2,1)S(1)}, u32[]{:S(2)}, u32[]{:S(2)}) %collective-permute-start.12) | collective-permute-done | bytes 32800 | tf_op jit(solution)/shard_map/ppermute | solution.py:54
  44.5 1.5 %collective-permute-start.16 = (bf16[128,256]{0,1:T(8,128)(2,1)S(1)}, bf16[128,256]{0,1:T(8,128)(2,1)S(1)}, u32[]{:S(2)}, u32[]{:S(2)}) collective-permute-start(bf16[128,256]{0,1:T(8,128)(2,1)S(1)} %pad_maximum_fusion.2), channel_id=1, source_target_pairs={{0,3},{1,4},{2,5},{3,6},{4,7},{5,0},{6,1},{7,2},{8,11},{9,12},{10,... | collective-permute-start | bytes 196616 | tf_op jit(solution)/shard_map/ppermute | solution.py:43
  47.4 2.0 %collective-permute-start.18 = (bf16[128,256]{0,1:T(8,128)(2,1)S(1)}, bf16[128,256]{0,1:T(8,128)(2,1)S(1)}, u32[]{:S(2)}, u32[]{:S(2)}) collective-permute-start(bf16[128,256]{0,1:T(8,128)(2,1)S(1)} %pad_maximum_fusion.2), channel_id=1, source_target_pairs={{0,5},{1,6},{2,7},{3,0},{4,1},{5,2},{6,3},{7,4},{8,13},{9,14},{10,... | collective-permute-start | bytes 196616 | tf_op jit(solution)/shard_map/ppermute | solution.py:43
  50.9 4.2 %collective-permute-done.16 = bf16[128,256]{0,1:T(8,128)(2,1)S(1)} collective-permute-done((bf16[128,256]{0,1:T(8,128)(2,1)S(1)}, bf16[128,256]{0,1:T(8,128)(2,1)S(1)}, u32[]{:S(2)}, u32[]{:S(2)}) %collective-permute-start.16) | collective-permute-done | bytes 65568 | tf_op jit(solution)/shard_map/ppermute | solution.py:43
  55.3 1.6 %collective-permute-done.19 = bf16[128,256]{0,1:T(8,128)(2,1)S(1)} collective-permute-done((bf16[128,256]{0,1:T(8,128)(2,1)S(1)}, bf16[128,256]{0,1:T(8,128)(2,1)S(1)}, u32[]{:S(2)}, u32[]{:S(2)}) %collective-permute-start.19) | collective-permute-done | bytes 65568 | tf_op jit(solution)/shard_map/ppermute | solution.py:43
  58.9 2.0 %select_reduce_fusion = (f32[1024]{0:T(1024)S(1)}, f32[1024]{0:T(1024)S(1)}, f32[1024]{0:T(1024)S(1)}, f32[1024]{0:T(1024)S(1)}) fusion(f32[1024,1024]{0,1:T(8,128)S(1)} %get-tuple-element.76, s32[1024]{0:T(1024)S(1)} %bitcast.261, f32[1024]{0:T(1024)S(1)} %get-tuple-element.75, f32[1024,1024]{0,1:T(8,128)S(1)} %get-tuple-element.74, ...), kind=kLoop, calls=%fused_computation.2 | loop fusion | flops 9433088 | bytes 8417280 | tf_op jit(solution)/shard_map/reduce_sum | solution.py:91
  61.5 2.3 %collective-permute-start.22 = (f32[6,1024]{1,0:T(8,128)S(1)}, f32[6,1024]{1,0:T(8,128)S(1)}, u32[]{:S(2)}, u32[]{:S(2)}) collective-permute-start(f32[6,1024]{1,0:T(8,128)S(1)} %concatenate.57), channel_id=1, source_target_pairs={{0,2},{1,3},{2,4},{3,5},{4,6},{5,7},{6,0},{7,1},{8,10},{9,11},{10,... | collective-permute-start | bytes 73736 | tf_op jit(solution)/shard_map/ppermute | solution.py:43
  64.5 2.2 %collective-permute-start.24 = (f32[6,1024]{1,0:T(8,128)S(1)}, f32[6,1024]{1,0:T(8,128)S(1)}, u32[]{:S(2)}, u32[]{:S(2)}) collective-permute-start(f32[6,1024]{1,0:T(8,128)S(1)} %concatenate.57), channel_id=1, source_target_pairs={{0,4},{1,5},{2,6},{3,7},{4,0},{5,1},{6,2},{7,3},{8,12},{9,13},{10,... | collective-permute-start | bytes 73736 | tf_op jit(solution)/shard_map/ppermute | solution.py:43
  67.3 1.5 %collective-permute-start.26 = (f32[6,1024]{1,0:T(8,128)S(1)}, f32[6,1024]{1,0:T(8,128)S(1)}, u32[]{:S(2)}, u32[]{:S(2)}) collective-permute-start(f32[6,1024]{1,0:T(8,128)S(1)} %concatenate.57), channel_id=1, source_target_pairs={{0,6},{1,7},{2,0},{3,1},{4,2},{5,3},{6,4},{7,5},{8,14},{9,15},{10,... | collective-permute-start | bytes 73736 | tf_op jit(solution)/shard_map/ppermute | solution.py:43
  72.7 1.5 %collective-permute-start.28 = (f32[2,22]{1,0:T(2,128)S(1)}, f32[2,22]{1,0:T(2,128)S(1)}, u32[]{:S(2)}, u32[]{:S(2)}) collective-permute-start(f32[2,22]{1,0:T(2,128)S(1)} %get-tuple-element.62), channel_id=1, source_target_pairs={{0,8},{8,16},{16,24},{24,0},{1,9},{9,17},{17,25},{25,1},{2,10},{10... | collective-permute-start | bytes 536 | tf_op jit(solution)/shard_map/ppermute | solution.py:43
  74.3 1.5 %collective-permute-start.29 = (f32[2,22]{1,0:T(2,128)S(1)}, f32[2,22]{1,0:T(2,128)S(1)}, u32[]{:S(2)}, u32[]{:S(2)}) collective-permute-start(f32[2,22]{1,0:T(2,128)S(1)} %get-tuple-element.62), channel_id=1, source_target_pairs={{0,16},{8,24},{16,0},{24,8},{1,17},{9,25},{17,1},{25,9},{2,18},{10... | collective-permute-start | bytes 536 | tf_op jit(solution)/shard_map/ppermute | solution.py:43
  77.8 1.5 %collective-permute-done.30 = f32[2,22]{1,0:T(2,128)S(1)} collective-permute-done((f32[2,22]{1,0:T(2,128)S(1)}, f32[2,22]{1,0:T(2,128)S(1)}, u32[]{:S(2)}, u32[]{:S(2)}) %collective-permute-start.30) | collective-permute-done | bytes 208 | tf_op jit(solution)/shard_map/ppermute | solution.py:43
  81.3 1.8 %bitcast_divide_fusion = (f32[22]{0:T(128)S(1)}, f32[22]{0:T(128)}) fusion(f32[2,22]{1,0:T(2,128)S(1)} %fusion.35, f32[]{:T(128)} %fusion.44, f32[22]{0:T(128)S(1)} %get-tuple-element.19, f32[]{:T(128)} %get-tuple-element.18), kind=kLoop, calls=%fused_computation.187 | loop fusion | flops 132 | bytes 360 | tf_op jit(solution)/shard_map/div | solution.py:243
  83.8 3.5 %fusion.2 = f32[1024,128]{1,0:T(8,128)S(1)} fusion(bf16[1024,128]{1,0:T(8,128)(2,1)S(1)} %copy-done, f32[1024,1024]{0,1:T(8,128)} %copy-done.1, f32[1024]{0:T(1024)S(1)} %bitcast.265, f32[1024]{0:T(1024)S(1)} %broadcast_bitcast_fusion, s32[1024]{0:T(1024)S(1)} %bitcast.262), kind=kOutput, calls=%fused_computation.10 | convolution fusion | flops 274726912 | bytes 4993024 | tf_op jit(solution)/shard_map/dot_general | solution.py:113
  88.4 2.4 %collective-permute-start.33 = (f32[128,128]{1,0:T(8,128)S(1)}, f32[128,128]{1,0:T(8,128)S(1)}, u32[]{:S(2)}, u32[]{:S(2)}) collective-permute-start(f32[128,128]{1,0:T(8,128)S(1)} %get-tuple-element.32), channel_id=1, source_target_pairs={{0,3},{1,4},{2,5},{3,6},{4,7},{5,0},{6,1},{7,2},{8,11},{9,12},{10,... | collective-permute-start | bytes 196616 | tf_op jit(solution)/shard_map/ppermute | solution.py:54
  95.7 3.5 %collective-permute-done.33 = f32[128,128]{1,0:T(8,128)S(1)} collective-permute-done((f32[128,128]{1,0:T(8,128)S(1)}, f32[128,128]{1,0:T(8,128)S(1)}, u32[]{:S(2)}, u32[]{:S(2)}) %collective-permute-start.33) | collective-permute-done | bytes 65568 | tf_op jit(solution)/shard_map/ppermute | solution.py:54
  99.5 1.5 %collective-permute-done.36 = f32[128,128]{1,0:T(8,128)S(1)} collective-permute-done((f32[128,128]{1,0:T(8,128)S(1)}, f32[128,128]{1,0:T(8,128)S(1)}, u32[]{:S(2)}, u32[]{:S(2)}) %collective-permute-start.36) | collective-permute-done | bytes 65568 | tf_op jit(solution)/shard_map/ppermute | solution.py:54
  103.1 2.4 %collective-permute-start.39 = (bf16[64,384]{1,0:T(8,128)(2,1)S(1)}, bf16[64,384]{1,0:T(8,128)(2,1)S(1)}, u32[]{:S(2)}, u32[]{:S(2)}) collective-permute-start(bf16[64,384]{1,0:T(8,128)(2,1)S(1)} %get-tuple-element.41), channel_id=1, source_target_pairs={{0,2},{1,3},{2,4},{3,5},{4,6},{5,7},{6,0},{7,1},{8,10},{9,11},{10,... | collective-permute-start | bytes 147464 | tf_op jit(solution)/shard_map/ppermute | solution.py:54
  105.9 2.3 %collective-permute-start.41 = (bf16[64,384]{1,0:T(8,128)(2,1)S(1)}, bf16[64,384]{1,0:T(8,128)(2,1)S(1)}, u32[]{:S(2)}, u32[]{:S(2)}) collective-permute-start(bf16[64,384]{1,0:T(8,128)(2,1)S(1)} %get-tuple-element.39), channel_id=1, source_target_pairs={{0,4},{1,5},{2,6},{3,7},{4,0},{5,1},{6,2},{7,3},{8,12},{9,13},{10,... | collective-permute-start | bytes 147464 | tf_op jit(solution)/shard_map/ppermute | solution.py:54
  108.7 1.5 %collective-permute-start.43 = (bf16[64,384]{1,0:T(8,128)(2,1)S(1)}, bf16[64,384]{1,0:T(8,128)(2,1)S(1)}, u32[]{:S(2)}, u32[]{:S(2)}) collective-permute-start(bf16[64,384]{1,0:T(8,128)(2,1)S(1)} %get-tuple-element.37), channel_id=1, source_target_pairs={{0,6},{1,7},{2,0},{3,1},{4,2},{5,3},{6,4},{7,5},{8,14},{9,15},{10,... | collective-permute-start | bytes 147464 | tf_op jit(solution)/shard_map/ppermute | solution.py:54
  116.5 1.5 %collective-permute-start.46 = (f32[64,384]{1,0:T(8,128)S(1)}, f32[64,384]{1,0:T(8,128)S(1)}, u32[]{:S(2)}, u32[]{:S(2)}) collective-permute-start(f32[64,384]{1,0:T(8,128)S(1)} %convert_reduce_fusion), channel_id=1, source_target_pairs={{0,16},{8,24},{16,0},{24,8},{1,17},{9,25},{17,1},{25,9},{2,18},{10... | collective-permute-start | bytes 294920 | tf_op jit(solution)/shard_map/ppermute | solution.py:43
  118.5 3.1 %collective-permute-done.45 = f32[64,384]{1,0:T(8,128)S(1)} collective-permute-done((f32[64,384]{1,0:T(8,128)S(1)}, f32[64,384]{1,0:T(8,128)S(1)}, u32[]{:S(2)}, u32[]{:S(2)}) %collective-permute-start.45) | collective-permute-done | bytes 98336 | tf_op jit(solution)/shard_map/ppermute | solution.py:43
  121.6 1.5 %collective-permute-done.46 = f32[64,384]{1,0:T(8,128)S(1)} collective-permute-done((f32[64,384]{1,0:T(8,128)S(1)}, f32[64,384]{1,0:T(8,128)S(1)}, u32[]{:S(2)}, u32[]{:S(2)}) %collective-permute-start.46) | collective-permute-done | bytes 98336 | tf_op jit(solution)/shard_map/ppermute | solution.py:43
  (206 shorter events, 48.7 us)
Async XLA Ops:
  7.2 8.2 %collective-permute-start = (bf16[389,128]{1,0:T(8,128)(2,1)S(1)}, bf16[389,128]{1,0:T(8,128)(2,1)S(1)}, u32[]{:S(2)}, u32[]{:S(2)}) collective-permute-start(bf16[389,128]{1,0:T(8,128)(2,1)S(1)} %constant_dynamic-update-slice_fusion), channel_id=1, source_target_pairs={{0,1},{1,2},{2,3},{3,4},{4,5},{5,6},{6,7},{7,0},{8,9},{9,10},{10,1... | collective-permute-start | bytes 298760 | tf_op jit(solution)/shard_map/ppermute | solution.py:43
  7.7 9.2 %collective-permute-start.1 = (bf16[389,128]{1,0:T(8,128)(2,1)S(1)}, bf16[389,128]{1,0:T(8,128)(2,1)S(1)}, u32[]{:S(2)}, u32[]{:S(2)}) collective-permute-start(bf16[389,128]{1,0:T(8,128)(2,1)S(1)} %constant_dynamic-update-slice_fusion), channel_id=1, source_target_pairs={{0,2},{1,3},{2,4},{3,5},{4,6},{5,7},{6,0},{7,1},{8,10},{9,11},{10,... | collective-permute-start | bytes 298760 | tf_op jit(solution)/shard_map/ppermute | solution.py:43
  10.3 13.4 %collective-permute-start.2 = (bf16[389,128]{1,0:T(8,128)(2,1)S(1)}, bf16[389,128]{1,0:T(8,128)(2,1)S(1)}, u32[]{:S(2)}, u32[]{:S(2)}) collective-permute-start(bf16[389,128]{1,0:T(8,128)(2,1)S(1)} %constant_dynamic-update-slice_fusion), channel_id=1, source_target_pairs={{0,3},{1,4},{2,5},{3,6},{4,7},{5,0},{6,1},{7,2},{8,11},{9,12},{10,... | collective-permute-start | bytes 298760 | tf_op jit(solution)/shard_map/ppermute | solution.py:43
  12.8 11.1 %collective-permute-start.3 = (bf16[389,128]{1,0:T(8,128)(2,1)S(1)}, bf16[389,128]{1,0:T(8,128)(2,1)S(1)}, u32[]{:S(2)}, u32[]{:S(2)}) collective-permute-start(bf16[389,128]{1,0:T(8,128)(2,1)S(1)} %constant_dynamic-update-slice_fusion), channel_id=1, source_target_pairs={{0,4},{1,5},{2,6},{3,7},{4,0},{5,1},{6,2},{7,3},{8,12},{9,13},{10,... | collective-permute-start | bytes 298760 | tf_op jit(solution)/shard_map/ppermute | solution.py:43
  14.1 9.9 %collective-permute-start.4 = (bf16[389,128]{1,0:T(8,128)(2,1)S(1)}, bf16[389,128]{1,0:T(8,128)(2,1)S(1)}, u32[]{:S(2)}, u32[]{:S(2)}) collective-permute-start(bf16[389,128]{1,0:T(8,128)(2,1)S(1)} %constant_dynamic-update-slice_fusion), channel_id=1, source_target_pairs={{0,5},{1,6},{2,7},{3,0},{4,1},{5,2},{6,3},{7,4},{8,13},{9,14},{10,... | collective-permute-start | bytes 298760 | tf_op jit(solution)/shard_map/ppermute | solution.py:43
  15.4 8.6 %collective-permute-start.5 = (bf16[389,128]{1,0:T(8,128)(2,1)S(1)}, bf16[389,128]{1,0:T(8,128)(2,1)S(1)}, u32[]{:S(2)}, u32[]{:S(2)}) collective-permute-start(bf16[389,128]{1,0:T(8,128)(2,1)S(1)} %constant_dynamic-update-slice_fusion), channel_id=1, source_target_pairs={{0,6},{1,7},{2,0},{3,1},{4,2},{5,3},{6,4},{7,5},{8,14},{9,15},{10,... | collective-permute-start | bytes 298760 | tf_op jit(solution)/shard_map/ppermute | solution.py:43
  16.8 7.1 %collective-permute-start.6 = (bf16[389,128]{1,0:T(8,128)(2,1)S(1)}, bf16[389,128]{1,0:T(8,128)(2,1)S(1)}, u32[]{:S(2)}, u32[]{:S(2)}) collective-permute-start(bf16[389,128]{1,0:T(8,128)(2,1)S(1)} %constant_dynamic-update-slice_fusion), channel_id=1, source_target_pairs={{0,7},{1,0},{2,1},{3,2},{4,3},{5,4},{6,5},{7,6},{8,15},{9,8},{10,9... | collective-permute-start | bytes 298760 | tf_op jit(solution)/shard_map/ppermute | solution.py:43
  25.4 11.8 %collective-permute-start.7 = (bf16[128,128]{1,0:T(8,128)(2,1)S(1)}, bf16[128,128]{1,0:T(8,128)(2,1)S(1)}, u32[]{:S(2)}, u32[]{:S(2)}) collective-permute-start(bf16[128,128]{1,0:T(8,128)(2,1)S(1)} %get-tuple-element.50), channel_id=1, source_target_pairs={{0,1},{1,2},{2,3},{3,4},{4,5},{5,6},{6,7},{7,0},{8,9},{9,10},{10,1... | collective-permute-start | bytes 98312 | tf_op jit(solution)/shard_map/ppermute | solution.py:54
  28.0 9.6 %collective-permute-start.8 = (bf16[128,128]{1,0:T(8,128)(2,1)S(1)}, bf16[128,128]{1,0:T(8,128)(2,1)S(1)}, u32[]{:S(2)}, u32[]{:S(2)}) collective-permute-start(bf16[128,128]{1,0:T(8,128)(2,1)S(1)} %get-tuple-element.49), channel_id=1, source_target_pairs={{0,2},{1,3},{2,4},{3,5},{4,6},{5,7},{6,0},{7,1},{8,10},{9,11},{10,... | collective-permute-start | bytes 98312 | tf_op jit(solution)/shard_map/ppermute | solution.py:54
  32.3 6.6 %collective-permute-start.9 = (bf16[128,128]{1,0:T(8,128)(2,1)S(1)}, bf16[128,128]{1,0:T(8,128)(2,1)S(1)}, u32[]{:S(2)}, u32[]{:S(2)}) collective-permute-start(bf16[128,128]{1,0:T(8,128)(2,1)S(1)} %get-tuple-element.48), channel_id=1, source_target_pairs={{0,3},{1,4},{2,5},{3,6},{4,7},{5,0},{6,1},{7,2},{8,11},{9,12},{10,... | collective-permute-start | bytes 98312 | tf_op jit(solution)/shard_map/ppermute | solution.py:54
  43.2 6.2 %collective-permute-start.14 = (bf16[128,256]{0,1:T(8,128)(2,1)S(1)}, bf16[128,256]{0,1:T(8,128)(2,1)S(1)}, u32[]{:S(2)}, u32[]{:S(2)}) collective-permute-start(bf16[128,256]{0,1:T(8,128)(2,1)S(1)} %pad_maximum_fusion.2), channel_id=1, source_target_pairs={{0,1},{1,2},{2,3},{3,4},{4,5},{5,6},{6,7},{7,0},{8,9},{9,10},{10,1... | collective-permute-start | bytes 196616 | tf_op jit(solution)/shard_map/ppermute | solution.py:43
  43.4 6.8 %collective-permute-start.15 = (bf16[128,256]{0,1:T(8,128)(2,1)S(1)}, bf16[128,256]{0,1:T(8,128)(2,1)S(1)}, u32[]{:S(2)}, u32[]{:S(2)}) collective-permute-start(bf16[128,256]{0,1:T(8,128)(2,1)S(1)} %pad_maximum_fusion.2), channel_id=1, source_target_pairs={{0,2},{1,3},{2,4},{3,5},{4,6},{5,7},{6,0},{7,1},{8,10},{9,11},{10,... | collective-permute-start | bytes 196616 | tf_op jit(solution)/shard_map/ppermute | solution.py:43
  44.5 10.6 %collective-permute-start.16 = (bf16[128,256]{0,1:T(8,128)(2,1)S(1)}, bf16[128,256]{0,1:T(8,128)(2,1)S(1)}, u32[]{:S(2)}, u32[]{:S(2)}) collective-permute-start(bf16[128,256]{0,1:T(8,128)(2,1)S(1)} %pad_maximum_fusion.2), channel_id=1, source_target_pairs={{0,3},{1,4},{2,5},{3,6},{4,7},{5,0},{6,1},{7,2},{8,11},{9,12},{10,... | collective-permute-start | bytes 196616 | tf_op jit(solution)/shard_map/ppermute | solution.py:43
  46.0 9.3 %collective-permute-start.17 = (bf16[128,256]{0,1:T(8,128)(2,1)S(1)}, bf16[128,256]{0,1:T(8,128)(2,1)S(1)}, u32[]{:S(2)}, u32[]{:S(2)}) collective-permute-start(bf16[128,256]{0,1:T(8,128)(2,1)S(1)} %pad_maximum_fusion.2), channel_id=1, source_target_pairs={{0,4},{1,5},{2,6},{3,7},{4,0},{5,1},{6,2},{7,3},{8,12},{9,13},{10,... | collective-permute-start | bytes 196616 | tf_op jit(solution)/shard_map/ppermute | solution.py:43
  47.4 7.9 %collective-permute-start.18 = (bf16[128,256]{0,1:T(8,128)(2,1)S(1)}, bf16[128,256]{0,1:T(8,128)(2,1)S(1)}, u32[]{:S(2)}, u32[]{:S(2)}) collective-permute-start(bf16[128,256]{0,1:T(8,128)(2,1)S(1)} %pad_maximum_fusion.2), channel_id=1, source_target_pairs={{0,5},{1,6},{2,7},{3,0},{4,1},{5,2},{6,3},{7,4},{8,13},{9,14},{10,... | collective-permute-start | bytes 196616 | tf_op jit(solution)/shard_map/ppermute | solution.py:43
  49.4 7.5 %collective-permute-start.19 = (bf16[128,256]{0,1:T(8,128)(2,1)S(1)}, bf16[128,256]{0,1:T(8,128)(2,1)S(1)}, u32[]{:S(2)}, u32[]{:S(2)}) collective-permute-start(bf16[128,256]{0,1:T(8,128)(2,1)S(1)} %pad_maximum_fusion.2), channel_id=1, source_target_pairs={{0,6},{1,7},{2,0},{3,1},{4,2},{5,3},{6,4},{7,5},{8,14},{9,15},{10,... | collective-permute-start | bytes 196616 | tf_op jit(solution)/shard_map/ppermute | solution.py:43
  50.2 6.7 %collective-permute-start.20 = (bf16[128,256]{0,1:T(8,128)(2,1)S(1)}, bf16[128,256]{0,1:T(8,128)(2,1)S(1)}, u32[]{:S(2)}, u32[]{:S(2)}) collective-permute-start(bf16[128,256]{0,1:T(8,128)(2,1)S(1)} %pad_maximum_fusion.2), channel_id=1, source_target_pairs={{0,7},{1,0},{2,1},{3,2},{4,3},{5,4},{6,5},{7,6},{8,15},{9,8},{10,9... | collective-permute-start | bytes 196616 | tf_op jit(solution)/shard_map/ppermute | solution.py:43
  61.0 6.4 %collective-permute-start.21 = (f32[6,1024]{1,0:T(8,128)S(1)}, f32[6,1024]{1,0:T(8,128)S(1)}, u32[]{:S(2)}, u32[]{:S(2)}) collective-permute-start(f32[6,1024]{1,0:T(8,128)S(1)} %concatenate.57), channel_id=1, source_target_pairs={{0,1},{1,2},{2,3},{3,4},{4,5},{5,6},{6,7},{7,0},{8,9},{9,10},{10,1... | collective-permute-start | bytes 73736 | tf_op jit(solution)/shard_map/ppermute | solution.py:43
  61.5 7.4 %collective-permute-start.22 = (f32[6,1024]{1,0:T(8,128)S(1)}, f32[6,1024]{1,0:T(8,128)S(1)}, u32[]{:S(2)}, u32[]{:S(2)}) collective-permute-start(f32[6,1024]{1,0:T(8,128)S(1)} %concatenate.57), channel_id=1, source_target_pairs={{0,2},{1,3},{2,4},{3,5},{4,6},{5,7},{6,0},{7,1},{8,10},{9,11},{10,... | collective-permute-start | bytes 73736 | tf_op jit(solution)/shard_map/ppermute | solution.py:43
  63.9 6.3 %collective-permute-start.23 = (f32[6,1024]{1,0:T(8,128)S(1)}, f32[6,1024]{1,0:T(8,128)S(1)}, u32[]{:S(2)}, u32[]{:S(2)}) collective-permute-start(f32[6,1024]{1,0:T(8,128)S(1)} %concatenate.57), channel_id=1, source_target_pairs={{0,3},{1,4},{2,5},{3,6},{4,7},{5,0},{6,1},{7,2},{8,11},{9,12},{10,... | collective-permute-start | bytes 73736 | tf_op jit(solution)/shard_map/ppermute | solution.py:43
  87.4 6.9 %collective-permute-start.32 = (f32[128,128]{1,0:T(8,128)S(1)}, f32[128,128]{1,0:T(8,128)S(1)}, u32[]{:S(2)}, u32[]{:S(2)}) collective-permute-start(f32[128,128]{1,0:T(8,128)S(1)} %get-tuple-element.33), channel_id=1, source_target_pairs={{0,2},{1,3},{2,4},{3,5},{4,6},{5,7},{6,0},{7,1},{8,10},{9,11},{10,... | collective-permute-start | bytes 196616 | tf_op jit(solution)/shard_map/ppermute | solution.py:54
  88.4 10.8 %collective-permute-start.33 = (f32[128,128]{1,0:T(8,128)S(1)}, f32[128,128]{1,0:T(8,128)S(1)}, u32[]{:S(2)}, u32[]{:S(2)}) collective-permute-start(f32[128,128]{1,0:T(8,128)S(1)} %get-tuple-element.32), channel_id=1, source_target_pairs={{0,3},{1,4},{2,5},{3,6},{4,7},{5,0},{6,1},{7,2},{8,11},{9,12},{10,... | collective-permute-start | bytes 196616 | tf_op jit(solution)/shard_map/ppermute | solution.py:54
  90.9 8.6 %collective-permute-start.34 = (f32[128,128]{1,0:T(8,128)S(1)}, f32[128,128]{1,0:T(8,128)S(1)}, u32[]{:S(2)}, u32[]{:S(2)}) collective-permute-start(f32[128,128]{1,0:T(8,128)S(1)} %get-tuple-element.31), channel_id=1, source_target_pairs={{0,4},{1,5},{2,6},{3,7},{4,0},{5,1},{6,2},{7,3},{8,12},{9,13},{10,... | collective-permute-start | bytes 196616 | tf_op jit(solution)/shard_map/ppermute | solution.py:54
  92.2 7.2 %collective-permute-start.35 = (f32[128,128]{1,0:T(8,128)S(1)}, f32[128,128]{1,0:T(8,128)S(1)}, u32[]{:S(2)}, u32[]{:S(2)}) collective-permute-start(f32[128,128]{1,0:T(8,128)S(1)} %get-tuple-element.30), channel_id=1, source_target_pairs={{0,5},{1,6},{2,7},{3,0},{4,1},{5,2},{6,3},{7,4},{8,13},{9,14},{10,... | collective-permute-start | bytes 196616 | tf_op jit(solution)/shard_map/ppermute | solution.py:54
  93.3 7.6 %collective-permute-start.36 = (f32[128,128]{1,0:T(8,128)S(1)}, f32[128,128]{1,0:T(8,128)S(1)}, u32[]{:S(2)}, u32[]{:S(2)}) collective-permute-start(f32[128,128]{1,0:T(8,128)S(1)} %get-tuple-element.29), channel_id=1, source_target_pairs={{0,6},{1,7},{2,0},{3,1},{4,2},{5,3},{6,4},{7,5},{8,14},{9,15},{10,... | collective-permute-start | bytes 196616 | tf_op jit(solution)/shard_map/ppermute | solution.py:54
  94.3 6.6 %collective-permute-start.37 = (f32[128,128]{1,0:T(8,128)S(1)}, f32[128,128]{1,0:T(8,128)S(1)}, u32[]{:S(2)}, u32[]{:S(2)}) collective-permute-start(f32[128,128]{1,0:T(8,128)S(1)} %get-tuple-element.28), channel_id=1, source_target_pairs={{0,7},{1,0},{2,1},{3,2},{4,3},{5,4},{6,5},{7,6},{8,15},{9,8},{10,9... | collective-permute-start | bytes 196616 | tf_op jit(solution)/shard_map/ppermute | solution.py:54
  102.5 6.2 %collective-permute-start.38 = (bf16[64,384]{1,0:T(8,128)(2,1)S(1)}, bf16[64,384]{1,0:T(8,128)(2,1)S(1)}, u32[]{:S(2)}, u32[]{:S(2)}) collective-permute-start(bf16[64,384]{1,0:T(8,128)(2,1)S(1)} %get-tuple-element.42), channel_id=1, source_target_pairs={{0,1},{1,2},{2,3},{3,4},{4,5},{5,6},{6,7},{7,0},{8,9},{9,10},{10,1... | collective-permute-start | bytes 147464 | tf_op jit(solution)/shard_map/ppermute | solution.py:54
  103.1 7.2 %collective-permute-start.39 = (bf16[64,384]{1,0:T(8,128)(2,1)S(1)}, bf16[64,384]{1,0:T(8,128)(2,1)S(1)}, u32[]{:S(2)}, u32[]{:S(2)}) collective-permute-start(bf16[64,384]{1,0:T(8,128)(2,1)S(1)} %get-tuple-element.41), channel_id=1, source_target_pairs={{0,2},{1,3},{2,4},{3,5},{4,6},{5,7},{6,0},{7,1},{8,10},{9,11},{10,... | collective-permute-start | bytes 147464 | tf_op jit(solution)/shard_map/ppermute | solution.py:54
  105.5 7.6 %collective-permute-start.40 = (bf16[64,384]{1,0:T(8,128)(2,1)S(1)}, bf16[64,384]{1,0:T(8,128)(2,1)S(1)}, u32[]{:S(2)}, u32[]{:S(2)}) collective-permute-start(bf16[64,384]{1,0:T(8,128)(2,1)S(1)} %get-tuple-element.40), channel_id=1, source_target_pairs={{0,3},{1,4},{2,5},{3,6},{4,7},{5,0},{6,1},{7,2},{8,11},{9,12},{10,... | collective-permute-start | bytes 147464 | tf_op jit(solution)/shard_map/ppermute | solution.py:54
  105.9 7.6 %collective-permute-start.41 = (bf16[64,384]{1,0:T(8,128)(2,1)S(1)}, bf16[64,384]{1,0:T(8,128)(2,1)S(1)}, u32[]{:S(2)}, u32[]{:S(2)}) collective-permute-start(bf16[64,384]{1,0:T(8,128)(2,1)S(1)} %get-tuple-element.39), channel_id=1, source_target_pairs={{0,4},{1,5},{2,6},{3,7},{4,0},{5,1},{6,2},{7,3},{8,12},{9,13},{10,... | collective-permute-start | bytes 147464 | tf_op jit(solution)/shard_map/ppermute | solution.py:54
  115.1 6.6 %collective-permute-start.45 = (f32[64,384]{1,0:T(8,128)S(1)}, f32[64,384]{1,0:T(8,128)S(1)}, u32[]{:S(2)}, u32[]{:S(2)}) collective-permute-start(f32[64,384]{1,0:T(8,128)S(1)} %convert_reduce_fusion), channel_id=1, source_target_pairs={{0,8},{8,16},{16,24},{24,0},{1,9},{9,17},{17,25},{25,1},{2,10},{10... | collective-permute-start | bytes 294920 | tf_op jit(solution)/shard_map/ppermute | solution.py:43
  116.5 6.6 %collective-permute-start.46 = (f32[64,384]{1,0:T(8,128)S(1)}, f32[64,384]{1,0:T(8,128)S(1)}, u32[]{:S(2)}, u32[]{:S(2)}) collective-permute-start(f32[64,384]{1,0:T(8,128)S(1)} %convert_reduce_fusion), channel_id=1, source_target_pairs={{0,16},{8,24},{16,0},{24,8},{1,17},{9,25},{17,1},{25,9},{2,18},{10... | collective-permute-start | bytes 294920 | tf_op jit(solution)/shard_map/ppermute | solution.py:43
  (20 other events, 175.8 us)

commit v9 on v7

--- a/solution.py
+++ b/solution.py
@@ -3,6 +3,8 @@
 import jax
 import jax.numpy as jnp
 from jax import lax
+from jax.experimental import pallas as pl
+from jax.experimental.pallas import tpu as pltpu
 from jax.sharding import PartitionSpec as P
 
 EPSILON = 1e-05
@@ -59,6 +61,33 @@
         for shift in range(1, size)
     ]
     return to_absolute(jnp.stack(pieces), axis)
+
+
+def pack_rows(parts):
+    counts = [part.shape[0] for part in parts]
+    width = parts[0].shape[1]
+
+    def kernel(*refs):
+        sources, target, semaphores = refs[: len(parts)], refs[len(parts)], refs[-1]
+        copies = []
+        start = 0
+        for index, (source, count) in enumerate(zip(sources, counts)):
+            copy = pltpu.make_async_copy(
+                source, target.at[pl.ds(start, count)], semaphores.at[index]
+            )
+            copy.start()
+            copies.append(copy)
+            start += count
+        for copy in copies:
+            copy.wait()
+
+    return pl.pallas_call(
+        kernel,
+        out_shape=jax.ShapeDtypeStruct((sum(counts), width), parts[0].dtype),
+        in_specs=[pl.BlockSpec(memory_space=pl.ANY)] * len(parts),
+        out_specs=pl.BlockSpec(memory_space=pl.ANY),
+        scratch_shapes=[pltpu.SemaphoreType.DMA((len(parts),))],
+    )(*parts)
 
 
 def feed_forward(embedded, normed, weights):
@@ -162,7 +191,7 @@
     id_count = 4 * per_device // width
     extra_size = rows_here + len(gains) * gain_here
     extra_count = -(-extra_size // width)
-    small_count = id_count + extra_count
+    small_count = -(-(id_count + extra_count) // 16) * 16
     id_pieces = (tokens // ID_BASE, tokens % ID_BASE, targets // ID_BASE, targets % ID_BASE)
     small = jnp.zeros((small_count * width,), jnp.bfloat16)
     start = 0
@@ -170,10 +199,8 @@
         piece = piece.astype(jnp.bfloat16)
         small = small + jnp.pad(piece, (start, small_count * width - start - piece.shape[0]))
         start += piece.shape[0]
-    id_rows = small.reshape(small_count, width)[:id_count]
-    extra_rows = small.reshape(small_count, width)[id_count:]
     matrix_rows = len(matrices) * unit_rows
-    packed = jnp.concatenate(list(matrices) + [small.reshape(small_count, width)], axis=0)
+    packed = pack_rows(list(matrices) + [small.reshape(small_count, width)])
     gathered = gather_ordered(packed, "fsdp", True)
     full_matrices = [
         gathered[:, index * unit_rows : (index + 1) * unit_rows].reshape(-1, width)

time: 121 us -> 147 us (1.21)
  waiting for transfers between devices: 24.2 us -> 59.6 us
  starting transfers between devices: 50.9 us -> 40.5 us
  local copies, waits for them, and re-layouts: 7.88 us -> 3.56 us
  Pallas kernels: 0 us -> 4.26 us
    ppermute x21, waiting for transfers between devices: 10.1 us -> 34.6 us  [exchange_ordered(): lax.ppermute(lax.dynamic_index_in_dim(blocks, (here + shift) % size, keep...]
    ppermute x20, waiting for transfers between devices: 14 us -> 25 us  [gather_ordered(): lax.ppermute(value, axis, shift_pairs(size, shift))]
    ppermute x21, starting transfers between devices: 26.2 us -> 20.5 us  [exchange_ordered(): lax.ppermute(lax.dynamic_index_in_dim(blocks, (here + shift) % size, keep...]
    ppermute x20, starting transfers between devices: 24.7 us -> 20 us  [gather_ordered(): lax.ppermute(value, axis, shift_pairs(size, shift))]
    unnamed x37 -> x31, local copies, waits for them, and re-layouts: 4.61 us -> 0.29 us
    pallas_call x0 -> x1, Pallas kernels: none -> 4.26 us  [pack_rows(): pl.pallas_call(kernel, out_shape=jax.ShapeDtypeStruct((sum(counts), width...]
  transfers between devices with their start and end apart: 41 -> 41, of which waited for: 18 -> 17; matrix products, arithmetic and copies ran while one was open for 1% -> 1% of each run, Pallas kernels for 0% -> 0%
where the time goes in v9:
time: 147 us; the launch traced here: 146 us
  waiting for transfers between devices  59.6 us (41%)
  starting transfers between devices  40.5 us (28%)
  blocking collectives  17.5 us (12%)
  other arithmetic  9.94 us (7%)
  matrix products  8.9 us (6%)
  Pallas kernels  4.26 us (3%)
  local copies, waits for them, and re-layouts  3.56 us (2%)
  between operations  2.13 us (1%)
    ppermute x21, waiting for transfers between devices, exchange_ordered(): lax.ppermute(lax.dynamic_index_in_dim(blocks, (here + shift) % size, keep...  34.6 us
    ppermute x20, waiting for transfers between devices, gather_ordered(): lax.ppermute(value, axis, shift_pairs(size, shift))  25 us
    ppermute x21, starting transfers between devices, exchange_ordered(): lax.ppermute(lax.dynamic_index_in_dim(blocks, (here + shift) % size, keep...  20.5 us
    ppermute x20, starting transfers between devices, gather_ordered(): lax.ppermute(value, axis, shift_pairs(size, shift))  20 us
    all_gather x1, blocking collectives, gather_ordered(): return lax.all_gather(value, axis)  17.5 us
    pallas_call x1, Pallas kernels, pack_rows(): pl.pallas_call(kernel, out_shape=jax.ShapeDtypeStruct((sum(counts), width...  4.26 us
    dot_general x1, matrix products, one_block(): return jnp.dot(d_logits, table, preferred_element_type=jnp.float32)  3.49 us
  transfers between devices with their start and end apart: 41, of which 17 were waited for; matrix products, arithmetic and copies ran while one was open for 1% of the time, Pallas kernels for 0%

profile of v9, /device:TPU:0, one launch (start us, length us, event | category | flops | bytes accessed | tf_op | source)
XLA Modules:
  0.0 146.4 jit_solution(13486020342666801429)
XLA Ops:
  3.5 4.3 %shard_map.183 = bf16[400,128]{1,0:T(8,128)(2,1)} custom-call(bf16[64,128]{1,0:T(8,128)(2,1)} %refs_0_.1, bf16[64,128]{1,0:T(8,128)(2,1)} %refs_1_.1, bf16[64,128]{1,0:T(8,128)(2,1)} %refs_2_.1, bf16[64,128]{1,0:T(8,128)(2,1)} %refs_3_.1, bf16[64,128]{1,0:T(8,128)(2,1)} %refs_4_.1, bf16[64,128]{1,0:T(8,128)(2,1)} %refs_5_.1, ...), custom_call_target="tpu_custom_call" | custom-call | tf_op jit(solution)/shard_map/pallas_call | solution.py:84
  7.7 17.5 %all-gather = bf16[3200,128]{1,0:T(8,128)(2,1)S(1)} all-gather(bf16[400,128]{1,0:T(8,128)(2,1)} %shard_map.183), channel_id=2, replica_groups=mesh['dp'=4,'fsdp'=8] {'fsdp'}, dimensions={0}, use_global_device_ids=true | all-gather | bytes 921600 | tf_op jit(solution)/shard_map/all_gather | solution.py:43
  25.3 1.8 %fusion.3 = bf16[1024,128]{1,0:T(8,128)(2,1)S(1)} fusion(bf16[1024,128]{1,0:T(8,128)(2,1)} %param.19, s32[1024]{0:T(1024)S(1)} %bitcast.252), kind=kOutput, calls=%fused_computation.11 | convolution fusion | flops 269615104 | bytes 528384 | tf_op jit(solution)/shard_map/dot_general | solution.py:227
  27.1 3.6 %collective-permute-start.6 = (bf16[128,128]{1,0:T(8,128)(2,1)S(1)}, bf16[128,128]{1,0:T(8,128)(2,1)S(1)}, u32[]{:S(2)}, u32[]{:S(2)}) collective-permute-start(bf16[128,128]{1,0:T(8,128)(2,1)S(1)} %get-tuple-element.44), channel_id=1, source_target_pairs={{0,7},{1,0},{2,1},{3,2},{4,3},{5,4},{6,5},{7,6},{8,15},{9,8},{10,9... | collective-permute-start | bytes 98312 | tf_op jit(solution)/shard_map/ppermute | solution.py:56
  30.8 2.7 %collective-permute-start.3 = (bf16[128,128]{1,0:T(8,128)(2,1)S(1)}, bf16[128,128]{1,0:T(8,128)(2,1)S(1)}, u32[]{:S(2)}, u32[]{:S(2)}) collective-permute-start(bf16[128,128]{1,0:T(8,128)(2,1)S(1)} %get-tuple-element.47), channel_id=1, source_target_pairs={{0,4},{1,5},{2,6},{3,7},{4,0},{5,1},{6,2},{7,3},{8,12},{9,13},{10,... | collective-permute-start | bytes 98312 | tf_op jit(solution)/shard_map/ppermute | solution.py:56
  34.7 3.9 %collective-permute-done = bf16[128,128]{1,0:T(8,128)(2,1)S(1)} collective-permute-done((bf16[128,128]{1,0:T(8,128)(2,1)S(1)}, bf16[128,128]{1,0:T(8,128)(2,1)S(1)}, u32[]{:S(2)}, u32[]{:S(2)}) %collective-permute-start) | collective-permute-done | bytes 32800 | tf_op jit(solution)/shard_map/ppermute | solution.py:56
  38.6 5.7 %collective-permute-done.1 = bf16[128,128]{1,0:T(8,128)(2,1)S(1)} collective-permute-done((bf16[128,128]{1,0:T(8,128)(2,1)S(1)}, bf16[128,128]{1,0:T(8,128)(2,1)S(1)}, u32[]{:S(2)}, u32[]{:S(2)}) %collective-permute-start.1) | collective-permute-done | bytes 32800 | tf_op jit(solution)/shard_map/ppermute | solution.py:56
  44.3 4.2 %collective-permute-done.2 = bf16[128,128]{1,0:T(8,128)(2,1)S(1)} collective-permute-done((bf16[128,128]{1,0:T(8,128)(2,1)S(1)}, bf16[128,128]{1,0:T(8,128)(2,1)S(1)}, u32[]{:S(2)}, u32[]{:S(2)}) %collective-permute-start.2) | collective-permute-done | bytes 32800 | tf_op jit(solution)/shard_map/ppermute | solution.py:56
  51.0 1.5 %collective-permute-start.9 = (bf16[128,256]{0,1:T(8,128)(2,1)S(1)}, bf16[128,256]{0,1:T(8,128)(2,1)S(1)}, u32[]{:S(2)}, u32[]{:S(2)}) collective-permute-start(bf16[128,256]{0,1:T(8,128)(2,1)S(1)} %pad_maximum_fusion.2), channel_id=1, source_target_pairs={{0,3},{1,4},{2,5},{3,6},{4,7},{5,0},{6,1},{7,2},{8,11},{9,12},{10,... | collective-permute-start | bytes 196616 | tf_op jit(solution)/shard_map/ppermute | solution.py:45
  52.5 1.5 %collective-permute-start.7 = (bf16[128,256]{0,1:T(8,128)(2,1)S(1)}, bf16[128,256]{0,1:T(8,128)(2,1)S(1)}, u32[]{:S(2)}, u32[]{:S(2)}) collective-permute-start(bf16[128,256]{0,1:T(8,128)(2,1)S(1)} %pad_maximum_fusion.2), channel_id=1, source_target_pairs={{0,1},{1,2},{2,3},{3,4},{4,5},{5,6},{6,7},{7,0},{8,9},{9,10},{10,1... | collective-permute-start | bytes 196616 | tf_op jit(solution)/shard_map/ppermute | solution.py:45
  54.1 4.7 %collective-permute-done.7 = bf16[128,256]{0,1:T(8,128)(2,1)S(1)} collective-permute-done((bf16[128,256]{0,1:T(8,128)(2,1)S(1)}, bf16[128,256]{0,1:T(8,128)(2,1)S(1)}, u32[]{:S(2)}, u32[]{:S(2)}) %collective-permute-start.7) | collective-permute-done | bytes 65568 | tf_op jit(solution)/shard_map/ppermute | solution.py:45
  59.3 6.0 %collective-permute-done.8 = bf16[128,256]{0,1:T(8,128)(2,1)S(1)} collective-permute-done((bf16[128,256]{0,1:T(8,128)(2,1)S(1)}, bf16[128,256]{0,1:T(8,128)(2,1)S(1)}, u32[]{:S(2)}, u32[]{:S(2)}) %collective-permute-start.8) | collective-permute-done | bytes 65568 | tf_op jit(solution)/shard_map/ppermute | solution.py:45
  65.5 1.8 %collective-permute-done.13 = bf16[128,256]{0,1:T(8,128)(2,1)S(1)} collective-permute-done((bf16[128,256]{0,1:T(8,128)(2,1)S(1)}, bf16[128,256]{0,1:T(8,128)(2,1)S(1)}, u32[]{:S(2)}, u32[]{:S(2)}) %collective-permute-start.13) | collective-permute-done | bytes 65568 | tf_op jit(solution)/shard_map/ppermute | solution.py:45
  69.2 2.0 %select_reduce_fusion = (f32[1024]{0:T(1024)S(1)}, f32[1024]{0:T(1024)S(1)}, f32[1024]{0:T(1024)S(1)}, f32[1024]{0:T(1024)S(1)}) fusion(f32[1024,1024]{0,1:T(8,128)S(1)} %get-tuple-element.76, s32[1024]{0:T(1024)S(1)} %bitcast.249, f32[1024]{0:T(1024)S(1)} %get-tuple-element.75, f32[1024,1024]{0,1:T(8,128)S(1)} %get-tuple-element.74, ...), kind=kLoop, calls=%fused_computation.2 | loop fusion | flops 9433088 | bytes 8417280 | tf_op jit(solution)/shard_map/reduce_sum | solution.py:120
  71.3 2.1 %collective-permute-start.19 = (f32[6,1024]{1,0:T(8,128)S(1)}, f32[6,1024]{1,0:T(8,128)S(1)}, u32[]{:S(2)}, u32[]{:S(2)}) collective-permute-start(f32[6,1024]{1,0:T(8,128)S(1)} %concatenate.48), channel_id=1, source_target_pairs={{0,6},{1,7},{2,0},{3,1},{4,2},{5,3},{6,4},{7,5},{8,14},{9,15},{10,... | collective-permute-start | bytes 73736 | tf_op jit(solution)/shard_map/ppermute | solution.py:45
  75.2 2.6 %collective-permute-start.17 = (f32[6,1024]{1,0:T(8,128)S(1)}, f32[6,1024]{1,0:T(8,128)S(1)}, u32[]{:S(2)}, u32[]{:S(2)}) collective-permute-start(f32[6,1024]{1,0:T(8,128)S(1)} %concatenate.48), channel_id=1, source_target_pairs={{0,4},{1,5},{2,6},{3,7},{4,0},{5,1},{6,2},{7,3},{8,12},{9,13},{10,... | collective-permute-start | bytes 73736 | tf_op jit(solution)/shard_map/ppermute | solution.py:45
  78.5 1.5 %collective-permute-start.14 = (f32[6,1024]{1,0:T(8,128)S(1)}, f32[6,1024]{1,0:T(8,128)S(1)}, u32[]{:S(2)}, u32[]{:S(2)}) collective-permute-start(f32[6,1024]{1,0:T(8,128)S(1)} %concatenate.48), channel_id=1, source_target_pairs={{0,1},{1,2},{2,3},{3,4},{4,5},{5,6},{6,7},{7,0},{8,9},{9,10},{10,1... | collective-permute-start | bytes 73736 | tf_op jit(solution)/shard_map/ppermute | solution.py:45
  82.1 1.9 %collective-permute-done.15 = f32[6,1024]{1,0:T(8,128)S(1)} collective-permute-done((f32[6,1024]{1,0:T(8,128)S(1)}, f32[6,1024]{1,0:T(8,128)S(1)}, u32[]{:S(2)}, u32[]{:S(2)}) %collective-permute-start.15) | collective-permute-done | bytes 24608 | tf_op jit(solution)/shard_map/ppermute | solution.py:45
  85.1 1.6 %collective-permute-start.22 = (f32[2,22]{1,0:T(2,128)S(1)}, f32[2,22]{1,0:T(2,128)S(1)}, u32[]{:S(2)}, u32[]{:S(2)}) collective-permute-start(f32[2,22]{1,0:T(2,128)S(1)} %get-tuple-element.62), channel_id=1, source_target_pairs={{0,16},{8,24},{16,0},{24,8},{1,17},{9,25},{17,1},{25,9},{2,18},{10... | collective-permute-start | bytes 536 | tf_op jit(solution)/shard_map/ppermute | solution.py:45
  89.6 1.5 %collective-permute-done.21 = f32[2,22]{1,0:T(2,128)S(1)} collective-permute-done((f32[2,22]{1,0:T(2,128)S(1)}, f32[2,22]{1,0:T(2,128)S(1)}, u32[]{:S(2)}, u32[]{:S(2)}) %collective-permute-start.21) | collective-permute-done | bytes 208 | tf_op jit(solution)/shard_map/ppermute | solution.py:45
  93.7 1.8 %bitcast_divide_fusion = (f32[22]{0:T(128)S(1)}, f32[22]{0:T(128)}) fusion(f32[2,22]{1,0:T(2,128)S(1)} %fusion.34, f32[]{:T(128)} %fusion.43, f32[22]{0:T(128)S(1)} %get-tuple-element.19, f32[]{:T(128)} %get-tuple-element.18), kind=kLoop, calls=%fused_computation.170 | loop fusion | flops 132 | bytes 360 | tf_op jit(solution)/shard_map/div | solution.py:270
  96.2 3.5 %fusion.2 = f32[1024,128]{1,0:T(8,128)S(1)} fusion(bf16[1024,128]{1,0:T(8,128)(2,1)S(1)} %copy-done, f32[1024,1024]{0,1:T(8,128)} %copy-done.1, f32[1024]{0:T(1024)S(1)} %bitcast.253, f32[1024]{0:T(1024)S(1)} %broadcast_bitcast_fusion, s32[1024]{0:T(1024)S(1)} %bitcast.250), kind=kOutput, calls=%fused_computation.10 | convolution fusion | flops 274726912 | bytes 4993024 | tf_op jit(solution)/shard_map/dot_general | solution.py:142
  99.8 3.5 %collective-permute-start.30 = (f32[128,128]{1,0:T(8,128)S(1)}, f32[128,128]{1,0:T(8,128)S(1)}, u32[]{:S(2)}, u32[]{:S(2)}) collective-permute-start(f32[128,128]{1,0:T(8,128)S(1)} %get-tuple-element.28), channel_id=1, source_target_pairs={{0,7},{1,0},{2,1},{3,2},{4,3},{5,4},{6,5},{7,6},{8,15},{9,8},{10,9... | collective-permute-start | bytes 196616 | tf_op jit(solution)/shard_map/ppermute | solution.py:56
  103.4 2.7 %collective-permute-start.27 = (f32[128,128]{1,0:T(8,128)S(1)}, f32[128,128]{1,0:T(8,128)S(1)}, u32[]{:S(2)}, u32[]{:S(2)}) collective-permute-start(f32[128,128]{1,0:T(8,128)S(1)} %get-tuple-element.31), channel_id=1, source_target_pairs={{0,4},{1,5},{2,6},{3,7},{4,0},{5,1},{6,2},{7,3},{8,12},{9,13},{10,... | collective-permute-start | bytes 196616 | tf_op jit(solution)/shard_map/ppermute | solution.py:56
  106.0 6.5 %collective-permute-done.25 = f32[128,128]{1,0:T(8,128)S(1)} collective-permute-done((f32[128,128]{1,0:T(8,128)S(1)}, f32[128,128]{1,0:T(8,128)S(1)}, u32[]{:S(2)}, u32[]{:S(2)}) %collective-permute-start.25) | collective-permute-done | bytes 65568 | tf_op jit(solution)/shard_map/ppermute | solution.py:56
  112.8 4.4 %collective-permute-done.26 = f32[128,128]{1,0:T(8,128)S(1)} collective-permute-done((f32[128,128]{1,0:T(8,128)S(1)}, f32[128,128]{1,0:T(8,128)S(1)}, u32[]{:S(2)}, u32[]{:S(2)}) %collective-permute-start.26) | collective-permute-done | bytes 65568 | tf_op jit(solution)/shard_map/ppermute | solution.py:56
  120.2 2.2 %collective-permute-start.37 = (bf16[64,384]{1,0:T(8,128)(2,1)S(1)}, bf16[64,384]{1,0:T(8,128)(2,1)S(1)}, u32[]{:S(2)}, u32[]{:S(2)}) collective-permute-start(bf16[64,384]{1,0:T(8,128)(2,1)S(1)} %get-tuple-element.36), channel_id=1, source_target_pairs={{0,7},{1,0},{2,1},{3,2},{4,3},{5,4},{6,5},{7,6},{8,15},{9,8},{10,9... | collective-permute-start | bytes 147464 | tf_op jit(solution)/shard_map/ppermute | solution.py:56
  126.0 5.3 %collective-permute-done.32 = bf16[64,384]{1,0:T(8,128)(2,1)S(1)} collective-permute-done((bf16[64,384]{1,0:T(8,128)(2,1)S(1)}, bf16[64,384]{1,0:T(8,128)(2,1)S(1)}, u32[]{:S(2)}, u32[]{:S(2)}) %collective-permute-start.32) | collective-permute-done | bytes 49184 | tf_op jit(solution)/shard_map/ppermute | solution.py:56
  131.3 4.4 %collective-permute-done.33 = bf16[64,384]{1,0:T(8,128)(2,1)S(1)} collective-permute-done((bf16[64,384]{1,0:T(8,128)(2,1)S(1)}, bf16[64,384]{1,0:T(8,128)(2,1)S(1)}, u32[]{:S(2)}, u32[]{:S(2)}) %collective-permute-start.33) | collective-permute-done | bytes 49184 | tf_op jit(solution)/shard_map/ppermute | solution.py:56
  136.1 2.4 %collective-permute-start.40 = (f32[64,384]{1,0:T(8,128)S(1)}, f32[64,384]{1,0:T(8,128)S(1)}, u32[]{:S(2)}, u32[]{:S(2)}) collective-permute-start(f32[64,384]{1,0:T(8,128)S(1)} %convert_reduce_fusion), channel_id=1, source_target_pairs={{0,24},{8,0},{16,8},{24,16},{1,25},{9,1},{17,9},{25,17},{2,26},{10... | collective-permute-start | bytes 294920 | tf_op jit(solution)/shard_map/ppermute | solution.py:45
  139.1 2.5 %collective-permute-done.40 = f32[64,384]{1,0:T(8,128)S(1)} collective-permute-done((f32[64,384]{1,0:T(8,128)S(1)}, f32[64,384]{1,0:T(8,128)S(1)}, u32[]{:S(2)}, u32[]{:S(2)}) %collective-permute-start.40) | collective-permute-done | bytes 98336 | tf_op jit(solution)/shard_map/ppermute | solution.py:45
  141.6 4.0 %collective-permute-done.39 = f32[64,384]{1,0:T(8,128)S(1)} collective-permute-done((f32[64,384]{1,0:T(8,128)S(1)}, f32[64,384]{1,0:T(8,128)S(1)}, u32[]{:S(2)}, u32[]{:S(2)}) %collective-permute-start.39) | collective-permute-done | bytes 98336 | tf_op jit(solution)/shard_map/ppermute | solution.py:45
  (176 shorter events, 28.5 us)
Async XLA Ops:
  27.1 21.5 %collective-permute-start.6 = (bf16[128,128]{1,0:T(8,128)(2,1)S(1)}, bf16[128,128]{1,0:T(8,128)(2,1)S(1)}, u32[]{:S(2)}, u32[]{:S(2)}) collective-permute-start(bf16[128,128]{1,0:T(8,128)(2,1)S(1)} %get-tuple-element.44), channel_id=1, source_target_pairs={{0,7},{1,0},{2,1},{3,2},{4,3},{5,4},{6,5},{7,6},{8,15},{9,8},{10,9... | collective-permute-start | bytes 98312 | tf_op jit(solution)/shard_map/ppermute | solution.py:56
  30.7 17.9 %collective-permute-start.5 = (bf16[128,128]{1,0:T(8,128)(2,1)S(1)}, bf16[128,128]{1,0:T(8,128)(2,1)S(1)}, u32[]{:S(2)}, u32[]{:S(2)}) collective-permute-start(bf16[128,128]{1,0:T(8,128)(2,1)S(1)} %get-tuple-element.45), channel_id=1, source_target_pairs={{0,6},{1,7},{2,0},{3,1},{4,2},{5,3},{6,4},{7,5},{8,14},{9,15},{10,... | collective-permute-start | bytes 98312 | tf_op jit(solution)/shard_map/ppermute | solution.py:56
  30.8 17.8 %collective-permute-start.4 = (bf16[128,128]{1,0:T(8,128)(2,1)S(1)}, bf16[128,128]{1,0:T(8,128)(2,1)S(1)}, u32[]{:S(2)}, u32[]{:S(2)}) collective-permute-start(bf16[128,128]{1,0:T(8,128)(2,1)S(1)} %get-tuple-element.46), channel_id=1, source_target_pairs={{0,5},{1,6},{2,7},{3,0},{4,1},{5,2},{6,3},{7,4},{8,13},{9,14},{10,... | collective-permute-start | bytes 98312 | tf_op jit(solution)/shard_map/ppermute | solution.py:56
  30.8 17.8 %collective-permute-start.3 = (bf16[128,128]{1,0:T(8,128)(2,1)S(1)}, bf16[128,128]{1,0:T(8,128)(2,1)S(1)}, u32[]{:S(2)}, u32[]{:S(2)}) collective-permute-start(bf16[128,128]{1,0:T(8,128)(2,1)S(1)} %get-tuple-element.47), channel_id=1, source_target_pairs={{0,4},{1,5},{2,6},{3,7},{4,0},{5,1},{6,2},{7,3},{8,12},{9,13},{10,... | collective-permute-start | bytes 98312 | tf_op jit(solution)/shard_map/ppermute | solution.py:56
  33.5 5.1 %collective-permute-start = (bf16[128,128]{1,0:T(8,128)(2,1)S(1)}, bf16[128,128]{1,0:T(8,128)(2,1)S(1)}, u32[]{:S(2)}, u32[]{:S(2)}) collective-permute-start(bf16[128,128]{1,0:T(8,128)(2,1)S(1)} %get-tuple-element.50), channel_id=1, source_target_pairs={{0,1},{1,2},{2,3},{3,4},{4,5},{5,6},{6,7},{7,0},{8,9},{9,10},{10,1... | collective-permute-start | bytes 98312 | tf_op jit(solution)/shard_map/ppermute | solution.py:56
  38.6 5.7 %collective-permute-start.1 = (bf16[128,128]{1,0:T(8,128)(2,1)S(1)}, bf16[128,128]{1,0:T(8,128)(2,1)S(1)}, u32[]{:S(2)}, u32[]{:S(2)}) collective-permute-start(bf16[128,128]{1,0:T(8,128)(2,1)S(1)} %get-tuple-element.49), channel_id=1, source_target_pairs={{0,2},{1,3},{2,4},{3,5},{4,6},{5,7},{6,0},{7,1},{8,10},{9,11},{10,... | collective-permute-start | bytes 98312 | tf_op jit(solution)/shard_map/ppermute | solution.py:56
  50.7 14.8 %collective-permute-start.12 = (bf16[128,256]{0,1:T(8,128)(2,1)S(1)}, bf16[128,256]{0,1:T(8,128)(2,1)S(1)}, u32[]{:S(2)}, u32[]{:S(2)}) collective-permute-start(bf16[128,256]{0,1:T(8,128)(2,1)S(1)} %pad_maximum_fusion.2), channel_id=1, source_target_pairs={{0,6},{1,7},{2,0},{3,1},{4,2},{5,3},{6,4},{7,5},{8,14},{9,15},{10,... | collective-permute-start | bytes 196616 | tf_op jit(solution)/shard_map/ppermute | solution.py:45
  50.7 14.7 %collective-permute-start.11 = (bf16[128,256]{0,1:T(8,128)(2,1)S(1)}, bf16[128,256]{0,1:T(8,128)(2,1)S(1)}, u32[]{:S(2)}, u32[]{:S(2)}) collective-permute-start(bf16[128,256]{0,1:T(8,128)(2,1)S(1)} %pad_maximum_fusion.2), channel_id=1, source_target_pairs={{0,5},{1,6},{2,7},{3,0},{4,1},{5,2},{6,3},{7,4},{8,13},{9,14},{10,... | collective-permute-start | bytes 196616 | tf_op jit(solution)/shard_map/ppermute | solution.py:45
  51.0 14.4 %collective-permute-start.10 = (bf16[128,256]{0,1:T(8,128)(2,1)S(1)}, bf16[128,256]{0,1:T(8,128)(2,1)S(1)}, u32[]{:S(2)}, u32[]{:S(2)}) collective-permute-start(bf16[128,256]{0,1:T(8,128)(2,1)S(1)} %pad_maximum_fusion.2), channel_id=1, source_target_pairs={{0,4},{1,5},{2,6},{3,7},{4,0},{5,1},{6,2},{7,3},{8,12},{9,13},{10,... | collective-permute-start | bytes 196616 | tf_op jit(solution)/shard_map/ppermute | solution.py:45
  51.0 14.4 %collective-permute-start.9 = (bf16[128,256]{0,1:T(8,128)(2,1)S(1)}, bf16[128,256]{0,1:T(8,128)(2,1)S(1)}, u32[]{:S(2)}, u32[]{:S(2)}) collective-permute-start(bf16[128,256]{0,1:T(8,128)(2,1)S(1)} %pad_maximum_fusion.2), channel_id=1, source_target_pairs={{0,3},{1,4},{2,5},{3,6},{4,7},{5,0},{6,1},{7,2},{8,11},{9,12},{10,... | collective-permute-start | bytes 196616 | tf_op jit(solution)/shard_map/ppermute | solution.py:45
  52.5 6.2 %collective-permute-start.7 = (bf16[128,256]{0,1:T(8,128)(2,1)S(1)}, bf16[128,256]{0,1:T(8,128)(2,1)S(1)}, u32[]{:S(2)}, u32[]{:S(2)}) collective-permute-start(bf16[128,256]{0,1:T(8,128)(2,1)S(1)} %pad_maximum_fusion.2), channel_id=1, source_target_pairs={{0,1},{1,2},{2,3},{3,4},{4,5},{5,6},{6,7},{7,0},{8,9},{9,10},{10,1... | collective-permute-start | bytes 196616 | tf_op jit(solution)/shard_map/ppermute | solution.py:45
  58.8 6.6 %collective-permute-start.8 = (bf16[128,256]{0,1:T(8,128)(2,1)S(1)}, bf16[128,256]{0,1:T(8,128)(2,1)S(1)}, u32[]{:S(2)}, u32[]{:S(2)}) collective-permute-start(bf16[128,256]{0,1:T(8,128)(2,1)S(1)} %pad_maximum_fusion.2), channel_id=1, source_target_pairs={{0,2},{1,3},{2,4},{3,5},{4,6},{5,7},{6,0},{7,1},{8,10},{9,11},{10,... | collective-permute-start | bytes 196616 | tf_op jit(solution)/shard_map/ppermute | solution.py:45
  71.3 6.6 %collective-permute-start.19 = (f32[6,1024]{1,0:T(8,128)S(1)}, f32[6,1024]{1,0:T(8,128)S(1)}, u32[]{:S(2)}, u32[]{:S(2)}) collective-permute-start(f32[6,1024]{1,0:T(8,128)S(1)} %concatenate.48), channel_id=1, source_target_pairs={{0,6},{1,7},{2,0},{3,1},{4,2},{5,3},{6,4},{7,5},{8,14},{9,15},{10,... | collective-permute-start | bytes 73736 | tf_op jit(solution)/shard_map/ppermute | solution.py:45
  74.8 9.3 %collective-permute-start.20 = (f32[6,1024]{1,0:T(8,128)S(1)}, f32[6,1024]{1,0:T(8,128)S(1)}, u32[]{:S(2)}, u32[]{:S(2)}) collective-permute-start(f32[6,1024]{1,0:T(8,128)S(1)} %concatenate.48), channel_id=1, source_target_pairs={{0,7},{1,0},{2,1},{3,2},{4,3},{5,4},{6,5},{7,6},{8,15},{9,8},{10,9... | collective-permute-start | bytes 73736 | tf_op jit(solution)/shard_map/ppermute | solution.py:45
  75.2 6.4 %collective-permute-start.17 = (f32[6,1024]{1,0:T(8,128)S(1)}, f32[6,1024]{1,0:T(8,128)S(1)}, u32[]{:S(2)}, u32[]{:S(2)}) collective-permute-start(f32[6,1024]{1,0:T(8,128)S(1)} %concatenate.48), channel_id=1, source_target_pairs={{0,4},{1,5},{2,6},{3,7},{4,0},{5,1},{6,2},{7,3},{8,12},{9,13},{10,... | collective-permute-start | bytes 73736 | tf_op jit(solution)/shard_map/ppermute | solution.py:45
  77.9 6.2 %collective-permute-start.15 = (f32[6,1024]{1,0:T(8,128)S(1)}, f32[6,1024]{1,0:T(8,128)S(1)}, u32[]{:S(2)}, u32[]{:S(2)}) collective-permute-start(f32[6,1024]{1,0:T(8,128)S(1)} %concatenate.48), channel_id=1, source_target_pairs={{0,2},{1,3},{2,4},{3,5},{4,6},{5,7},{6,0},{7,1},{8,10},{9,11},{10,... | collective-permute-start | bytes 73736 | tf_op jit(solution)/shard_map/ppermute | solution.py:45
  78.5 5.6 %collective-permute-start.14 = (f32[6,1024]{1,0:T(8,128)S(1)}, f32[6,1024]{1,0:T(8,128)S(1)}, u32[]{:S(2)}, u32[]{:S(2)}) collective-permute-start(f32[6,1024]{1,0:T(8,128)S(1)} %concatenate.48), channel_id=1, source_target_pairs={{0,1},{1,2},{2,3},{3,4},{4,5},{5,6},{6,7},{7,0},{8,9},{9,10},{10,1... | collective-permute-start | bytes 73736 | tf_op jit(solution)/shard_map/ppermute | solution.py:45
  99.8 6.3 %collective-permute-start.24 = (f32[128,128]{1,0:T(8,128)S(1)}, f32[128,128]{1,0:T(8,128)S(1)}, u32[]{:S(2)}, u32[]{:S(2)}) collective-permute-start(f32[128,128]{1,0:T(8,128)S(1)} %get-tuple-element.34), channel_id=1, source_target_pairs={{0,1},{1,2},{2,3},{3,4},{4,5},{5,6},{6,7},{7,0},{8,9},{9,10},{10,1... | collective-permute-start | bytes 196616 | tf_op jit(solution)/shard_map/ppermute | solution.py:56
  99.8 17.4 %collective-permute-start.30 = (f32[128,128]{1,0:T(8,128)S(1)}, f32[128,128]{1,0:T(8,128)S(1)}, u32[]{:S(2)}, u32[]{:S(2)}) collective-permute-start(f32[128,128]{1,0:T(8,128)S(1)} %get-tuple-element.28), channel_id=1, source_target_pairs={{0,7},{1,0},{2,1},{3,2},{4,3},{5,4},{6,5},{7,6},{8,15},{9,8},{10,9... | collective-permute-start | bytes 196616 | tf_op jit(solution)/shard_map/ppermute | solution.py:56
  103.3 13.9 %collective-permute-start.29 = (f32[128,128]{1,0:T(8,128)S(1)}, f32[128,128]{1,0:T(8,128)S(1)}, u32[]{:S(2)}, u32[]{:S(2)}) collective-permute-start(f32[128,128]{1,0:T(8,128)S(1)} %get-tuple-element.29), channel_id=1, source_target_pairs={{0,6},{1,7},{2,0},{3,1},{4,2},{5,3},{6,4},{7,5},{8,14},{9,15},{10,... | collective-permute-start | bytes 196616 | tf_op jit(solution)/shard_map/ppermute | solution.py:56
  103.4 13.8 %collective-permute-start.28 = (f32[128,128]{1,0:T(8,128)S(1)}, f32[128,128]{1,0:T(8,128)S(1)}, u32[]{:S(2)}, u32[]{:S(2)}) collective-permute-start(f32[128,128]{1,0:T(8,128)S(1)} %get-tuple-element.30), channel_id=1, source_target_pairs={{0,5},{1,6},{2,7},{3,0},{4,1},{5,2},{6,3},{7,4},{8,13},{9,14},{10,... | collective-permute-start | bytes 196616 | tf_op jit(solution)/shard_map/ppermute | solution.py:56
  103.4 13.8 %collective-permute-start.27 = (f32[128,128]{1,0:T(8,128)S(1)}, f32[128,128]{1,0:T(8,128)S(1)}, u32[]{:S(2)}, u32[]{:S(2)}) collective-permute-start(f32[128,128]{1,0:T(8,128)S(1)} %get-tuple-element.31), channel_id=1, source_target_pairs={{0,4},{1,5},{2,6},{3,7},{4,0},{5,1},{6,2},{7,3},{8,12},{9,13},{10,... | collective-permute-start | bytes 196616 | tf_op jit(solution)/shard_map/ppermute | solution.py:56
  106.0 6.5 %collective-permute-start.25 = (f32[128,128]{1,0:T(8,128)S(1)}, f32[128,128]{1,0:T(8,128)S(1)}, u32[]{:S(2)}, u32[]{:S(2)}) collective-permute-start(f32[128,128]{1,0:T(8,128)S(1)} %get-tuple-element.33), channel_id=1, source_target_pairs={{0,2},{1,3},{2,4},{3,5},{4,6},{5,7},{6,0},{7,1},{8,10},{9,11},{10,... | collective-permute-start | bytes 196616 | tf_op jit(solution)/shard_map/ppermute | solution.py:56
  118.8 6.3 %collective-permute-start.31 = (bf16[64,384]{1,0:T(8,128)(2,1)S(1)}, bf16[64,384]{1,0:T(8,128)(2,1)S(1)}, u32[]{:S(2)}, u32[]{:S(2)}) collective-permute-start(bf16[64,384]{1,0:T(8,128)(2,1)S(1)} %get-tuple-element.42), channel_id=1, source_target_pairs={{0,1},{1,2},{2,3},{3,4},{4,5},{5,6},{6,7},{7,0},{8,9},{9,10},{10,1... | collective-permute-start | bytes 147464 | tf_op jit(solution)/shard_map/ppermute | solution.py:56
  120.2 15.6 %collective-permute-start.37 = (bf16[64,384]{1,0:T(8,128)(2,1)S(1)}, bf16[64,384]{1,0:T(8,128)(2,1)S(1)}, u32[]{:S(2)}, u32[]{:S(2)}) collective-permute-start(bf16[64,384]{1,0:T(8,128)(2,1)S(1)} %get-tuple-element.36), channel_id=1, source_target_pairs={{0,7},{1,0},{2,1},{3,2},{4,3},{5,4},{6,5},{7,6},{8,15},{9,8},{10,9... | collective-permute-start | bytes 147464 | tf_op jit(solution)/shard_map/ppermute | solution.py:56
  122.4 13.4 %collective-permute-start.36 = (bf16[64,384]{1,0:T(8,128)(2,1)S(1)}, bf16[64,384]{1,0:T(8,128)(2,1)S(1)}, u32[]{:S(2)}, u32[]{:S(2)}) collective-permute-start(bf16[64,384]{1,0:T(8,128)(2,1)S(1)} %get-tuple-element.37), channel_id=1, source_target_pairs={{0,6},{1,7},{2,0},{3,1},{4,2},{5,3},{6,4},{7,5},{8,14},{9,15},{10,... | collective-permute-start | bytes 147464 | tf_op jit(solution)/shard_map/ppermute | solution.py:56
  122.4 13.3 %collective-permute-start.35 = (bf16[64,384]{1,0:T(8,128)(2,1)S(1)}, bf16[64,384]{1,0:T(8,128)(2,1)S(1)}, u32[]{:S(2)}, u32[]{:S(2)}) collective-permute-start(bf16[64,384]{1,0:T(8,128)(2,1)S(1)} %get-tuple-element.38), channel_id=1, source_target_pairs={{0,5},{1,6},{2,7},{3,0},{4,1},{5,2},{6,3},{7,4},{8,13},{9,14},{10,... | collective-permute-start | bytes 147464 | tf_op jit(solution)/shard_map/ppermute | solution.py:56
  123.7 12.1 %collective-permute-start.34 = (bf16[64,384]{1,0:T(8,128)(2,1)S(1)}, bf16[64,384]{1,0:T(8,128)(2,1)S(1)}, u32[]{:S(2)}, u32[]{:S(2)}) collective-permute-start(bf16[64,384]{1,0:T(8,128)(2,1)S(1)} %get-tuple-element.39), channel_id=1, source_target_pairs={{0,4},{1,5},{2,6},{3,7},{4,0},{5,1},{6,2},{7,3},{8,12},{9,13},{10,... | collective-permute-start | bytes 147464 | tf_op jit(solution)/shard_map/ppermute | solution.py:56
  125.1 6.2 %collective-permute-start.32 = (bf16[64,384]{1,0:T(8,128)(2,1)S(1)}, bf16[64,384]{1,0:T(8,128)(2,1)S(1)}, u32[]{:S(2)}, u32[]{:S(2)}) collective-permute-start(bf16[64,384]{1,0:T(8,128)(2,1)S(1)} %get-tuple-element.41), channel_id=1, source_target_pairs={{0,2},{1,3},{2,4},{3,5},{4,6},{5,7},{6,0},{7,1},{8,10},{9,11},{10,... | collective-permute-start | bytes 147464 | tf_op jit(solution)/shard_map/ppermute | solution.py:56
  136.1 5.5 %collective-permute-start.40 = (f32[64,384]{1,0:T(8,128)S(1)}, f32[64,384]{1,0:T(8,128)S(1)}, u32[]{:S(2)}, u32[]{:S(2)}) collective-permute-start(f32[64,384]{1,0:T(8,128)S(1)} %convert_reduce_fusion), channel_id=1, source_target_pairs={{0,24},{8,0},{16,8},{24,16},{1,25},{9,1},{17,9},{25,17},{2,26},{10... | collective-permute-start | bytes 294920 | tf_op jit(solution)/shard_map/ppermute | solution.py:45
  138.5 7.1 %collective-permute-start.39 = (f32[64,384]{1,0:T(8,128)S(1)}, f32[64,384]{1,0:T(8,128)S(1)}, u32[]{:S(2)}, u32[]{:S(2)}) collective-permute-start(f32[64,384]{1,0:T(8,128)S(1)} %convert_reduce_fusion), channel_id=1, source_target_pairs={{0,16},{8,24},{16,0},{24,8},{1,17},{9,25},{17,1},{25,9},{2,18},{10... | collective-permute-start | bytes 294920 | tf_op jit(solution)/shard_map/ppermute | solution.py:45
  139.0 6.6 %collective-permute-start.38 = (f32[64,384]{1,0:T(8,128)S(1)}, f32[64,384]{1,0:T(8,128)S(1)}, u32[]{:S(2)}, u32[]{:S(2)}) collective-permute-start(f32[64,384]{1,0:T(8,128)S(1)} %convert_reduce_fusion), channel_id=1, source_target_pairs={{0,8},{8,16},{16,24},{24,0},{1,9},{9,17},{17,25},{25,1},{2,10},{10... | collective-permute-start | bytes 294920 | tf_op jit(solution)/shard_map/ppermute | solution.py:45
  (12 other events, 129.5 us)

commit v10 on v7

--- a/solution.py
+++ b/solution.py
@@ -99,32 +99,31 @@
     return jnp.moveaxis(result, 1, 0).reshape(3, total)
 
 
-def head_gradient(inputs, table, log_total, weight, targets):
+def head_residual(inputs, table, log_total, targets):
     total = inputs.shape[0]
     rows = block_rows_of(total)
     columns = jnp.arange(table.shape[0], dtype=jnp.int32)
 
     def one_block(block):
-        block_in, block_total, block_weight, block_target = block
+        block_in, block_total, block_target = block
         logits = contract_last(block_in, table)
         probs = jnp.exp(logits - block_total[:, None])
         hits = (block_target[:, None] == columns[None, :]).astype(jnp.float32)
-        d_logits = (block_weight[:, None] * (probs - hits)).astype(jnp.bfloat16)
-        return jnp.dot(d_logits, table, preferred_element_type=jnp.float32)
+        return probs - hits
 
     if rows == total:
-        return one_block((inputs, log_total, weight, targets))
+        return one_block((inputs, log_total, targets))
     count = total // rows
     result = lax.map(
         one_block,
-        (
-            inputs.reshape(count, rows, -1),
-            log_total.reshape(count, rows),
-            weight.reshape(count, rows),
-            targets.reshape(count, rows),
-        ),
+        (inputs.reshape(count, rows, -1), log_total.reshape(count, rows), targets.reshape(count, rows)),
     )
     return result.reshape(total, -1)
+
+
+def head_gradient(residual, table, weight):
+    d_logits = (weight[:, None] * residual).astype(jnp.bfloat16)
+    return jnp.dot(d_logits, table, preferred_element_type=jnp.float32)
 
 
 def body(
@@ -234,6 +233,10 @@
     group_sums = jnp.sum(row_hits * row_excess[:, None], axis=0)
     group_counts = jnp.sum(row_hits, axis=0) * seq_len
 
+    residual = lax.optimization_barrier(
+        head_residual(prx_group, out_embed, log_total[1], target_local)
+    )
+
     summed = jnp.sum(gather_ordered(jnp.stack([group_sums, group_counts]), "dp", False), axis=0)
     total_sums = summed[0]
     domain_counts = summed[1]
@@ -244,7 +247,7 @@
     row_weight = jnp.take(token_ratio, row_domains)
     token_weight = jnp.repeat(row_weight, seq_len)
 
-    d_second_part = head_gradient(prx_group, out_embed, log_total[1], token_weight, target_local)
+    d_second_part = head_gradient(residual, out_embed, token_weight)
 
     d_second = jnp.sum(
         exchange_ordered(d_second_part.reshape(fsdp_size, per_device, width), "fsdp", False),

time: 121 us -> 123 us (1.017)
  other arithmetic: 9.35 us -> 14.6 us
  waiting for transfers between devices: 24.2 us -> 22 us
    sub x0 -> x1, other arithmetic: none -> 5.21 us  [one_block(): return probs - hits]
    ppermute x20, waiting for transfers between devices: 14 us -> 11.3 us  [gather_ordered(): lax.ppermute(value, axis, shift_pairs(size, shift))]
  transfers between devices with their start and end apart: 41 -> 41, of which waited for: 18 -> 16; matrix products, arithmetic and copies ran while one was open for 1% -> 5% of each run, Pallas kernels for 0% -> 0%
where the time goes in v10:
time: 123 us
  starting transfers between devices  50.6 us (41%)
  waiting for transfers between devices  22 us (18%)
  blocking collectives  17.3 us (14%)
  other arithmetic  14.6 us (12%)
  matrix products  8.33 us (7%)
  local copies, waits for them, and re-layouts  7.87 us (6%)
  between operations  2.05 us (2%)
    ppermute x21, starting transfers between devices, exchange_ordered(): lax.ppermute(lax.dynamic_index_in_dim(blocks, (here + shift) % size, keep...  25.9 us
    ppermute x20, starting transfers between devices, gather_ordered(): lax.ppermute(value, axis, shift_pairs(size, shift))  24.7 us
    all_gather x1, blocking collectives, gather_ordered(): return lax.all_gather(value, axis)  17.3 us
    ppermute x20, waiting for transfers between devices, gather_ordered(): lax.ppermute(value, axis, shift_pairs(size, shift))  11.3 us
    ppermute x21, waiting for transfers between devices, exchange_ordered(): lax.ppermute(lax.dynamic_index_in_dim(blocks, (here + shift) % size, keep...  10.7 us
    sub x1, other arithmetic, one_block(): return probs - hits  5.21 us
    unnamed x37, local copies, waits for them, and re-layouts  4.61 us
    dot_general x1, matrix products, head_gradient(): return jnp.dot(d_logits, table, preferred_element_type=jnp.float32)  2.93 us
  transfers between devices with their start and end apart: 41, of which 16 were waited for; matrix products, arithmetic and copies ran while one was open for 5% of the time, Pallas kernels for 0%

profile of v10, /device:TPU:0, one launch (start us, length us, event | category | flops | bytes accessed | tf_op | source)
XLA Modules:
  0.0 122.7 jit_solution(1365246014158621293)
XLA Ops:
  7.2 17.3 %all-gather.1 = bf16[8,389,128]{2,1,0:T(8,128)(2,1)S(1)} all-gather(bf16[1,389,128]{2,1,0:T(8,128)(2,1)S(1)} %bitcast.222), channel_id=2, replica_groups=mesh['dp'=4,'fsdp'=8] {'fsdp'}, dimensions={0}, use_global_device_ids=true | all-gather | bytes 896256 | tf_op jit(solution)/shard_map/all_gather | solution.py:41
  24.5 1.8 %fusion.4 = bf16[1024,128]{1,0:T(8,128)(2,1)S(1)} fusion(bf16[1024,128]{1,0:T(8,128)(2,1)} %param.19, s32[1024]{0:T(1024)S(1)} %bitcast.251), kind=kOutput, calls=%fused_computation.13 | convolution fusion | flops 269615104 | bytes 528384 | tf_op jit(solution)/shard_map/dot_general | solution.py:199
  26.8 1.6 %collective-permute-start.1 = (bf16[128,128]{1,0:T(8,128)(2,1)S(1)}, bf16[128,128]{1,0:T(8,128)(2,1)S(1)}, u32[]{:S(2)}, u32[]{:S(2)}) collective-permute-start(bf16[128,128]{1,0:T(8,128)(2,1)S(1)} %get-tuple-element.49), channel_id=1, source_target_pairs={{0,2},{1,3},{2,4},{3,5},{4,6},{5,7},{6,0},{7,1},{8,10},{9,11},{10,... | collective-permute-start | bytes 98312 | tf_op jit(solution)/shard_map/ppermute | solution.py:54
  28.4 2.1 %collective-permute-start.2 = (bf16[128,128]{1,0:T(8,128)(2,1)S(1)}, bf16[128,128]{1,0:T(8,128)(2,1)S(1)}, u32[]{:S(2)}, u32[]{:S(2)}) collective-permute-start(bf16[128,128]{1,0:T(8,128)(2,1)S(1)} %get-tuple-element.48), channel_id=1, source_target_pairs={{0,3},{1,4},{2,5},{3,6},{4,7},{5,0},{6,1},{7,2},{8,11},{9,12},{10,... | collective-permute-start | bytes 98312 | tf_op jit(solution)/shard_map/ppermute | solution.py:54
  31.8 1.4 %collective-permute-start.4 = (bf16[128,128]{1,0:T(8,128)(2,1)S(1)}, bf16[128,128]{1,0:T(8,128)(2,1)S(1)}, u32[]{:S(2)}, u32[]{:S(2)}) collective-permute-start(bf16[128,128]{1,0:T(8,128)(2,1)S(1)} %get-tuple-element.46), channel_id=1, source_target_pairs={{0,5},{1,6},{2,7},{3,0},{4,1},{5,2},{6,3},{7,4},{8,13},{9,14},{10,... | collective-permute-start | bytes 98312 | tf_op jit(solution)/shard_map/ppermute | solution.py:54
  36.2 1.7 %collective-permute-done.5 = bf16[128,128]{1,0:T(8,128)(2,1)S(1)} collective-permute-done((bf16[128,128]{1,0:T(8,128)(2,1)S(1)}, bf16[128,128]{1,0:T(8,128)(2,1)S(1)}, u32[]{:S(2)}, u32[]{:S(2)}) %collective-permute-start.5) | collective-permute-done | bytes 32800 | tf_op jit(solution)/shard_map/ppermute | solution.py:54
  41.2 2.0 %collective-permute-start.9 = (bf16[128,256]{0,1:T(8,128)(2,1)S(1)}, bf16[128,256]{0,1:T(8,128)(2,1)S(1)}, u32[]{:S(2)}, u32[]{:S(2)}) collective-permute-start(bf16[128,256]{0,1:T(8,128)(2,1)S(1)} %pad_maximum_fusion.2), channel_id=1, source_target_pairs={{0,3},{1,4},{2,5},{3,6},{4,7},{5,0},{6,1},{7,2},{8,11},{9,12},{10,... | collective-permute-start | bytes 196616 | tf_op jit(solution)/shard_map/ppermute | solution.py:43
  43.2 1.5 %collective-permute-start.10 = (bf16[128,256]{0,1:T(8,128)(2,1)S(1)}, bf16[128,256]{0,1:T(8,128)(2,1)S(1)}, u32[]{:S(2)}, u32[]{:S(2)}) collective-permute-start(bf16[128,256]{0,1:T(8,128)(2,1)S(1)} %pad_maximum_fusion.2), channel_id=1, source_target_pairs={{0,4},{1,5},{2,6},{3,7},{4,0},{5,1},{6,2},{7,3},{8,12},{9,13},{10,... | collective-permute-start | bytes 196616 | tf_op jit(solution)/shard_map/ppermute | solution.py:43
  45.9 1.5 %collective-permute-start.12 = (bf16[128,256]{0,1:T(8,128)(2,1)S(1)}, bf16[128,256]{0,1:T(8,128)(2,1)S(1)}, u32[]{:S(2)}, u32[]{:S(2)}) collective-permute-start(bf16[128,256]{0,1:T(8,128)(2,1)S(1)} %pad_maximum_fusion.2), channel_id=1, source_target_pairs={{0,6},{1,7},{2,0},{3,1},{4,2},{5,3},{6,4},{7,5},{8,14},{9,15},{10,... | collective-permute-start | bytes 196616 | tf_op jit(solution)/shard_map/ppermute | solution.py:43
  47.8 3.9 %collective-permute-done.9 = bf16[128,256]{0,1:T(8,128)(2,1)S(1)} collective-permute-done((bf16[128,256]{0,1:T(8,128)(2,1)S(1)}, bf16[128,256]{0,1:T(8,128)(2,1)S(1)}, u32[]{:S(2)}, u32[]{:S(2)}) %collective-permute-start.9) | collective-permute-done | bytes 65568 | tf_op jit(solution)/shard_map/ppermute | solution.py:43
  52.0 1.6 %collective-permute-done.12 = bf16[128,256]{0,1:T(8,128)(2,1)S(1)} collective-permute-done((bf16[128,256]{0,1:T(8,128)(2,1)S(1)}, bf16[128,256]{0,1:T(8,128)(2,1)S(1)}, u32[]{:S(2)}, u32[]{:S(2)}) %collective-permute-start.12) | collective-permute-done | bytes 65568 | tf_op jit(solution)/shard_map/ppermute | solution.py:43
  55.6 2.0 %select_reduce_fusion = (f32[1024]{0:T(1024)S(1)}, f32[1024]{0:T(1024)S(1)}, f32[1024]{0:T(1024)S(1)}, f32[1024]{0:T(1024)S(1)}) fusion(f32[1024,1024]{0,1:T(8,128)S(1)} %get-tuple-element.76, s32[1024]{0:T(1024)S(1)} %bitcast.235, f32[1024]{0:T(1024)S(1)} %get-tuple-element.75, f32[1024,1024]{0,1:T(8,128)S(1)} %get-tuple-element.74, ...), kind=kLoop, calls=%fused_computation.3 | loop fusion | flops 9433088 | bytes 8417280 | tf_op jit(solution)/shard_map/reduce_sum | solution.py:91
  58.2 2.3 %collective-permute-start.15 = (f32[6,1024]{1,0:T(8,128)S(1)}, f32[6,1024]{1,0:T(8,128)S(1)}, u32[]{:S(2)}, u32[]{:S(2)}) collective-permute-start(f32[6,1024]{1,0:T(8,128)S(1)} %concatenate.52), channel_id=1, source_target_pairs={{0,2},{1,3},{2,4},{3,5},{4,6},{5,7},{6,0},{7,1},{8,10},{9,11},{10,... | collective-permute-start | bytes 73736 | tf_op jit(solution)/shard_map/ppermute | solution.py:43
  61.4 2.0 %collective-permute-start.17 = (f32[6,1024]{1,0:T(8,128)S(1)}, f32[6,1024]{1,0:T(8,128)S(1)}, u32[]{:S(2)}, u32[]{:S(2)}) collective-permute-start(f32[6,1024]{1,0:T(8,128)S(1)} %concatenate.52), channel_id=1, source_target_pairs={{0,4},{1,5},{2,6},{3,7},{4,0},{5,1},{6,2},{7,3},{8,12},{9,13},{10,... | collective-permute-start | bytes 73736 | tf_op jit(solution)/shard_map/ppermute | solution.py:43
  69.5 1.5 %collective-permute-start.21 = (f32[2,22]{1,0:T(2,128)S(1)}, f32[2,22]{1,0:T(2,128)S(1)}, u32[]{:S(2)}, u32[]{:S(2)}) collective-permute-start(f32[2,22]{1,0:T(2,128)S(1)} %get-tuple-element.62), channel_id=1, source_target_pairs={{0,8},{8,16},{16,24},{24,0},{1,9},{9,17},{17,25},{25,1},{2,10},{10... | collective-permute-start | bytes 536 | tf_op jit(solution)/shard_map/ppermute | solution.py:43
  71.0 1.5 %collective-permute-start.22 = (f32[2,22]{1,0:T(2,128)S(1)}, f32[2,22]{1,0:T(2,128)S(1)}, u32[]{:S(2)}, u32[]{:S(2)}) collective-permute-start(f32[2,22]{1,0:T(2,128)S(1)} %get-tuple-element.62), channel_id=1, source_target_pairs={{0,16},{8,24},{16,0},{24,8},{1,17},{9,25},{17,1},{25,9},{2,18},{10... | collective-permute-start | bytes 536 | tf_op jit(solution)/shard_map/ppermute | solution.py:43
  72.5 1.4 %collective-permute-start.23 = (f32[2,22]{1,0:T(2,128)S(1)}, f32[2,22]{1,0:T(2,128)S(1)}, u32[]{:S(2)}, u32[]{:S(2)}) collective-permute-start(f32[2,22]{1,0:T(2,128)S(1)} %get-tuple-element.62), channel_id=1, source_target_pairs={{0,24},{8,0},{16,8},{24,16},{1,25},{9,1},{17,9},{25,17},{2,26},{10... | collective-permute-start | bytes 536 | tf_op jit(solution)/shard_map/ppermute | solution.py:43
  74.0 5.2 %convert_subtract_fusion = f32[1024,1024]{0,1:T(8,128)} fusion(f32[1024,1024]{0,1:T(8,128)} %copy-done.1, f32[1024]{0:T(1024)S(1)} %bitcast.245, s32[1024]{0:T(1024)S(1)} %bitcast.236), kind=kLoop, calls=%fused_computation.2 | loop fusion | flops 4194304 | bytes 8396800 | tf_op jit(solution)/shard_map/sub | solution.py:112
  81.1 1.8 %bitcast_divide_fusion = (f32[22]{0:T(128)S(1)}, f32[22]{0:T(128)}) fusion(f32[2,22]{1,0:T(2,128)S(1)} %fusion.35, f32[]{:T(128)} %fusion.44, f32[22]{0:T(128)S(1)} %get-tuple-element.19, f32[]{:T(128)} %get-tuple-element.18), kind=kLoop, calls=%fused_computation.178 | loop fusion | flops 132 | bytes 360 | tf_op jit(solution)/shard_map/div | solution.py:246
  83.7 2.9 %fusion.1 = f32[1024,128]{1,0:T(8,128)S(1)} fusion(bf16[1024,128]{1,0:T(8,128)(2,1)S(1)} %copy-done, f32[1024,1024]{0,1:T(8,128)} %convert_subtract_fusion, f32[1024]{0:T(1024)S(1)} %broadcast_bitcast_fusion), kind=kOutput, calls=%fused_computation.10 | convolution fusion | flops 270532608 | bytes 4984832 | tf_op jit(solution)/shard_map/dot_general | solution.py:126
  87.8 2.3 %collective-permute-start.26 = (f32[128,128]{1,0:T(8,128)S(1)}, f32[128,128]{1,0:T(8,128)S(1)}, u32[]{:S(2)}, u32[]{:S(2)}) collective-permute-start(f32[128,128]{1,0:T(8,128)S(1)} %get-tuple-element.32), channel_id=1, source_target_pairs={{0,3},{1,4},{2,5},{3,6},{4,7},{5,0},{6,1},{7,2},{8,11},{9,12},{10,... | collective-permute-start | bytes 196616 | tf_op jit(solution)/shard_map/ppermute | solution.py:54
  90.1 1.5 %collective-permute-start.27 = (f32[128,128]{1,0:T(8,128)S(1)}, f32[128,128]{1,0:T(8,128)S(1)}, u32[]{:S(2)}, u32[]{:S(2)}) collective-permute-start(f32[128,128]{1,0:T(8,128)S(1)} %get-tuple-element.31), channel_id=1, source_target_pairs={{0,4},{1,5},{2,6},{3,7},{4,0},{5,1},{6,2},{7,3},{8,12},{9,13},{10,... | collective-permute-start | bytes 196616 | tf_op jit(solution)/shard_map/ppermute | solution.py:54
  93.7 1.5 %collective-permute-start.30 = (f32[128,128]{1,0:T(8,128)S(1)}, f32[128,128]{1,0:T(8,128)S(1)}, u32[]{:S(2)}, u32[]{:S(2)}) collective-permute-start(f32[128,128]{1,0:T(8,128)S(1)} %get-tuple-element.28), channel_id=1, source_target_pairs={{0,7},{1,0},{2,1},{3,2},{4,3},{5,4},{6,5},{7,6},{8,15},{9,8},{10,9... | collective-permute-start | bytes 196616 | tf_op jit(solution)/shard_map/ppermute | solution.py:54
  95.1 3.4 %collective-permute-done.26 = f32[128,128]{1,0:T(8,128)S(1)} collective-permute-done((f32[128,128]{1,0:T(8,128)S(1)}, f32[128,128]{1,0:T(8,128)S(1)}, u32[]{:S(2)}, u32[]{:S(2)}) %collective-permute-start.26) | collective-permute-done | bytes 65568 | tf_op jit(solution)/shard_map/ppermute | solution.py:54
  98.8 1.6 %collective-permute-done.29 = f32[128,128]{1,0:T(8,128)S(1)} collective-permute-done((f32[128,128]{1,0:T(8,128)S(1)}, f32[128,128]{1,0:T(8,128)S(1)}, u32[]{:S(2)}, u32[]{:S(2)}) %collective-permute-start.29) | collective-permute-done | bytes 65568 | tf_op jit(solution)/shard_map/ppermute | solution.py:54
  102.4 2.3 %collective-permute-start.32 = (bf16[64,384]{1,0:T(8,128)(2,1)S(1)}, bf16[64,384]{1,0:T(8,128)(2,1)S(1)}, u32[]{:S(2)}, u32[]{:S(2)}) collective-permute-start(bf16[64,384]{1,0:T(8,128)(2,1)S(1)} %get-tuple-element.41), channel_id=1, source_target_pairs={{0,2},{1,3},{2,4},{3,5},{4,6},{5,7},{6,0},{7,1},{8,10},{9,11},{10,... | collective-permute-start | bytes 147464 | tf_op jit(solution)/shard_map/ppermute | solution.py:54
  105.2 2.3 %collective-permute-start.34 = (bf16[64,384]{1,0:T(8,128)(2,1)S(1)}, bf16[64,384]{1,0:T(8,128)(2,1)S(1)}, u32[]{:S(2)}, u32[]{:S(2)}) collective-permute-start(bf16[64,384]{1,0:T(8,128)(2,1)S(1)} %get-tuple-element.39), channel_id=1, source_target_pairs={{0,4},{1,5},{2,6},{3,7},{4,0},{5,1},{6,2},{7,3},{8,12},{9,13},{10,... | collective-permute-start | bytes 147464 | tf_op jit(solution)/shard_map/ppermute | solution.py:54
  108.0 1.5 %collective-permute-start.36 = (bf16[64,384]{1,0:T(8,128)(2,1)S(1)}, bf16[64,384]{1,0:T(8,128)(2,1)S(1)}, u32[]{:S(2)}, u32[]{:S(2)}) collective-permute-start(bf16[64,384]{1,0:T(8,128)(2,1)S(1)} %get-tuple-element.37), channel_id=1, source_target_pairs={{0,6},{1,7},{2,0},{3,1},{4,2},{5,3},{6,4},{7,5},{8,14},{9,15},{10,... | collective-permute-start | bytes 147464 | tf_op jit(solution)/shard_map/ppermute | solution.py:54
  109.6 1.4 %collective-permute-start.37 = (bf16[64,384]{1,0:T(8,128)(2,1)S(1)}, bf16[64,384]{1,0:T(8,128)(2,1)S(1)}, u32[]{:S(2)}, u32[]{:S(2)}) collective-permute-start(bf16[64,384]{1,0:T(8,128)(2,1)S(1)} %get-tuple-element.36), channel_id=1, source_target_pairs={{0,7},{1,0},{2,1},{3,2},{4,3},{5,4},{6,5},{7,6},{8,15},{9,8},{10,9... | collective-permute-start | bytes 147464 | tf_op jit(solution)/shard_map/ppermute | solution.py:54
  111.0 1.5 %collective-permute-done.33 = bf16[64,384]{1,0:T(8,128)(2,1)S(1)} collective-permute-done((bf16[64,384]{1,0:T(8,128)(2,1)S(1)}, bf16[64,384]{1,0:T(8,128)(2,1)S(1)}, u32[]{:S(2)}, u32[]{:S(2)}) %collective-permute-start.33) | collective-permute-done | bytes 49184 | tf_op jit(solution)/shard_map/ppermute | solution.py:54
  115.6 2.3 %collective-permute-start.40 = (f32[64,384]{1,0:T(8,128)S(1)}, f32[64,384]{1,0:T(8,128)S(1)}, u32[]{:S(2)}, u32[]{:S(2)}) collective-permute-start(f32[64,384]{1,0:T(8,128)S(1)} %convert_reduce_fusion), channel_id=1, source_target_pairs={{0,24},{8,0},{16,8},{24,16},{1,25},{9,1},{17,9},{25,17},{2,26},{10... | collective-permute-start | bytes 294920 | tf_op jit(solution)/shard_map/ppermute | solution.py:43
  118.0 3.1 %collective-permute-done.38 = f32[64,384]{1,0:T(8,128)S(1)} collective-permute-done((f32[64,384]{1,0:T(8,128)S(1)}, f32[64,384]{1,0:T(8,128)S(1)}, u32[]{:S(2)}, u32[]{:S(2)}) %collective-permute-start.38) | collective-permute-done | bytes 98336 | tf_op jit(solution)/shard_map/ppermute | solution.py:43
  (182 shorter events, 38.9 us)
Async XLA Ops:
  26.3 7.5 %collective-permute-start = (bf16[128,128]{1,0:T(8,128)(2,1)S(1)}, bf16[128,128]{1,0:T(8,128)(2,1)S(1)}, u32[]{:S(2)}, u32[]{:S(2)}) collective-permute-start(bf16[128,128]{1,0:T(8,128)(2,1)S(1)} %get-tuple-element.50), channel_id=1, source_target_pairs={{0,1},{1,2},{2,3},{3,4},{4,5},{5,6},{6,7},{7,0},{8,9},{9,10},{10,1... | collective-permute-start | bytes 98312 | tf_op jit(solution)/shard_map/ppermute | solution.py:54
  26.8 7.9 %collective-permute-start.1 = (bf16[128,128]{1,0:T(8,128)(2,1)S(1)}, bf16[128,128]{1,0:T(8,128)(2,1)S(1)}, u32[]{:S(2)}, u32[]{:S(2)}) collective-permute-start(bf16[128,128]{1,0:T(8,128)(2,1)S(1)} %get-tuple-element.49), channel_id=1, source_target_pairs={{0,2},{1,3},{2,4},{3,5},{4,6},{5,7},{6,0},{7,1},{8,10},{9,11},{10,... | collective-permute-start | bytes 98312 | tf_op jit(solution)/shard_map/ppermute | solution.py:54
  28.4 7.0 %collective-permute-start.2 = (bf16[128,128]{1,0:T(8,128)(2,1)S(1)}, bf16[128,128]{1,0:T(8,128)(2,1)S(1)}, u32[]{:S(2)}, u32[]{:S(2)}) collective-permute-start(bf16[128,128]{1,0:T(8,128)(2,1)S(1)} %get-tuple-element.48), channel_id=1, source_target_pairs={{0,3},{1,4},{2,5},{3,6},{4,7},{5,0},{6,1},{7,2},{8,11},{9,12},{10,... | collective-permute-start | bytes 98312 | tf_op jit(solution)/shard_map/ppermute | solution.py:54
  39.9 6.0 %collective-permute-start.7 = (bf16[128,256]{0,1:T(8,128)(2,1)S(1)}, bf16[128,256]{0,1:T(8,128)(2,1)S(1)}, u32[]{:S(2)}, u32[]{:S(2)}) collective-permute-start(bf16[128,256]{0,1:T(8,128)(2,1)S(1)} %pad_maximum_fusion.2), channel_id=1, source_target_pairs={{0,1},{1,2},{2,3},{3,4},{4,5},{5,6},{6,7},{7,0},{8,9},{9,10},{10,1... | collective-permute-start | bytes 196616 | tf_op jit(solution)/shard_map/ppermute | solution.py:43
  40.9 6.7 %collective-permute-start.8 = (bf16[128,256]{0,1:T(8,128)(2,1)S(1)}, bf16[128,256]{0,1:T(8,128)(2,1)S(1)}, u32[]{:S(2)}, u32[]{:S(2)}) collective-permute-start(bf16[128,256]{0,1:T(8,128)(2,1)S(1)} %pad_maximum_fusion.2), channel_id=1, source_target_pairs={{0,2},{1,3},{2,4},{3,5},{4,6},{5,7},{6,0},{7,1},{8,10},{9,11},{10,... | collective-permute-start | bytes 196616 | tf_op jit(solution)/shard_map/ppermute | solution.py:43
  41.2 10.5 %collective-permute-start.9 = (bf16[128,256]{0,1:T(8,128)(2,1)S(1)}, bf16[128,256]{0,1:T(8,128)(2,1)S(1)}, u32[]{:S(2)}, u32[]{:S(2)}) collective-permute-start(bf16[128,256]{0,1:T(8,128)(2,1)S(1)} %pad_maximum_fusion.2), channel_id=1, source_target_pairs={{0,3},{1,4},{2,5},{3,6},{4,7},{5,0},{6,1},{7,2},{8,11},{9,12},{10,... | collective-permute-start | bytes 196616 | tf_op jit(solution)/shard_map/ppermute | solution.py:43
  43.2 8.7 %collective-permute-start.10 = (bf16[128,256]{0,1:T(8,128)(2,1)S(1)}, bf16[128,256]{0,1:T(8,128)(2,1)S(1)}, u32[]{:S(2)}, u32[]{:S(2)}) collective-permute-start(bf16[128,256]{0,1:T(8,128)(2,1)S(1)} %pad_maximum_fusion.2), channel_id=1, source_target_pairs={{0,4},{1,5},{2,6},{3,7},{4,0},{5,1},{6,2},{7,3},{8,12},{9,13},{10,... | collective-permute-start | bytes 196616 | tf_op jit(solution)/shard_map/ppermute | solution.py:43
  44.7 7.3 %collective-permute-start.11 = (bf16[128,256]{0,1:T(8,128)(2,1)S(1)}, bf16[128,256]{0,1:T(8,128)(2,1)S(1)}, u32[]{:S(2)}, u32[]{:S(2)}) collective-permute-start(bf16[128,256]{0,1:T(8,128)(2,1)S(1)} %pad_maximum_fusion.2), channel_id=1, source_target_pairs={{0,5},{1,6},{2,7},{3,0},{4,1},{5,2},{6,3},{7,4},{8,13},{9,14},{10,... | collective-permute-start | bytes 196616 | tf_op jit(solution)/shard_map/ppermute | solution.py:43
  45.9 7.6 %collective-permute-start.12 = (bf16[128,256]{0,1:T(8,128)(2,1)S(1)}, bf16[128,256]{0,1:T(8,128)(2,1)S(1)}, u32[]{:S(2)}, u32[]{:S(2)}) collective-permute-start(bf16[128,256]{0,1:T(8,128)(2,1)S(1)} %pad_maximum_fusion.2), channel_id=1, source_target_pairs={{0,6},{1,7},{2,0},{3,1},{4,2},{5,3},{6,4},{7,5},{8,14},{9,15},{10,... | collective-permute-start | bytes 196616 | tf_op jit(solution)/shard_map/ppermute | solution.py:43
  47.6 6.0 %collective-permute-start.13 = (bf16[128,256]{0,1:T(8,128)(2,1)S(1)}, bf16[128,256]{0,1:T(8,128)(2,1)S(1)}, u32[]{:S(2)}, u32[]{:S(2)}) collective-permute-start(bf16[128,256]{0,1:T(8,128)(2,1)S(1)} %pad_maximum_fusion.2), channel_id=1, source_target_pairs={{0,7},{1,0},{2,1},{3,2},{4,3},{5,4},{6,5},{7,6},{8,15},{9,8},{10,9... | collective-permute-start | bytes 196616 | tf_op jit(solution)/shard_map/ppermute | solution.py:43
  57.6 6.8 %collective-permute-start.14 = (f32[6,1024]{1,0:T(8,128)S(1)}, f32[6,1024]{1,0:T(8,128)S(1)}, u32[]{:S(2)}, u32[]{:S(2)}) collective-permute-start(f32[6,1024]{1,0:T(8,128)S(1)} %concatenate.52), channel_id=1, source_target_pairs={{0,1},{1,2},{2,3},{3,4},{4,5},{5,6},{6,7},{7,0},{8,9},{9,10},{10,1... | collective-permute-start | bytes 73736 | tf_op jit(solution)/shard_map/ppermute | solution.py:43
  58.2 7.4 %collective-permute-start.15 = (f32[6,1024]{1,0:T(8,128)S(1)}, f32[6,1024]{1,0:T(8,128)S(1)}, u32[]{:S(2)}, u32[]{:S(2)}) collective-permute-start(f32[6,1024]{1,0:T(8,128)S(1)} %concatenate.52), channel_id=1, source_target_pairs={{0,2},{1,3},{2,4},{3,5},{4,6},{5,7},{6,0},{7,1},{8,10},{9,11},{10,... | collective-permute-start | bytes 73736 | tf_op jit(solution)/shard_map/ppermute | solution.py:43
  60.6 6.3 %collective-permute-start.16 = (f32[6,1024]{1,0:T(8,128)S(1)}, f32[6,1024]{1,0:T(8,128)S(1)}, u32[]{:S(2)}, u32[]{:S(2)}) collective-permute-start(f32[6,1024]{1,0:T(8,128)S(1)} %concatenate.52), channel_id=1, source_target_pairs={{0,3},{1,4},{2,5},{3,6},{4,7},{5,0},{6,1},{7,2},{8,11},{9,12},{10,... | collective-permute-start | bytes 73736 | tf_op jit(solution)/shard_map/ppermute | solution.py:43
  61.4 6.2 %collective-permute-start.17 = (f32[6,1024]{1,0:T(8,128)S(1)}, f32[6,1024]{1,0:T(8,128)S(1)}, u32[]{:S(2)}, u32[]{:S(2)}) collective-permute-start(f32[6,1024]{1,0:T(8,128)S(1)} %concatenate.52), channel_id=1, source_target_pairs={{0,4},{1,5},{2,6},{3,7},{4,0},{5,1},{6,2},{7,3},{8,12},{9,13},{10,... | collective-permute-start | bytes 73736 | tf_op jit(solution)/shard_map/ppermute | solution.py:43
  69.5 9.7 %collective-permute-start.21 = (f32[2,22]{1,0:T(2,128)S(1)}, f32[2,22]{1,0:T(2,128)S(1)}, u32[]{:S(2)}, u32[]{:S(2)}) collective-permute-start(f32[2,22]{1,0:T(2,128)S(1)} %get-tuple-element.62), channel_id=1, source_target_pairs={{0,8},{8,16},{16,24},{24,0},{1,9},{9,17},{17,25},{25,1},{2,10},{10... | collective-permute-start | bytes 536 | tf_op jit(solution)/shard_map/ppermute | solution.py:43
  71.0 8.2 %collective-permute-start.22 = (f32[2,22]{1,0:T(2,128)S(1)}, f32[2,22]{1,0:T(2,128)S(1)}, u32[]{:S(2)}, u32[]{:S(2)}) collective-permute-start(f32[2,22]{1,0:T(2,128)S(1)} %get-tuple-element.62), channel_id=1, source_target_pairs={{0,16},{8,24},{16,0},{24,8},{1,17},{9,25},{17,1},{25,9},{2,18},{10... | collective-permute-start | bytes 536 | tf_op jit(solution)/shard_map/ppermute | solution.py:43
  72.5 6.7 %collective-permute-start.23 = (f32[2,22]{1,0:T(2,128)S(1)}, f32[2,22]{1,0:T(2,128)S(1)}, u32[]{:S(2)}, u32[]{:S(2)}) collective-permute-start(f32[2,22]{1,0:T(2,128)S(1)} %get-tuple-element.62), channel_id=1, source_target_pairs={{0,24},{8,0},{16,8},{24,16},{1,25},{9,1},{17,9},{25,17},{2,26},{10... | collective-permute-start | bytes 536 | tf_op jit(solution)/shard_map/ppermute | solution.py:43
  86.7 6.0 %collective-permute-start.24 = (f32[128,128]{1,0:T(8,128)S(1)}, f32[128,128]{1,0:T(8,128)S(1)}, u32[]{:S(2)}, u32[]{:S(2)}) collective-permute-start(f32[128,128]{1,0:T(8,128)S(1)} %get-tuple-element.34), channel_id=1, source_target_pairs={{0,1},{1,2},{2,3},{3,4},{4,5},{5,6},{6,7},{7,0},{8,9},{9,10},{10,1... | collective-permute-start | bytes 196616 | tf_op jit(solution)/shard_map/ppermute | solution.py:54
  86.7 6.9 %collective-permute-start.25 = (f32[128,128]{1,0:T(8,128)S(1)}, f32[128,128]{1,0:T(8,128)S(1)}, u32[]{:S(2)}, u32[]{:S(2)}) collective-permute-start(f32[128,128]{1,0:T(8,128)S(1)} %get-tuple-element.33), channel_id=1, source_target_pairs={{0,2},{1,3},{2,4},{3,5},{4,6},{5,7},{6,0},{7,1},{8,10},{9,11},{10,... | collective-permute-start | bytes 196616 | tf_op jit(solution)/shard_map/ppermute | solution.py:54
  87.8 10.7 %collective-permute-start.26 = (f32[128,128]{1,0:T(8,128)S(1)}, f32[128,128]{1,0:T(8,128)S(1)}, u32[]{:S(2)}, u32[]{:S(2)}) collective-permute-start(f32[128,128]{1,0:T(8,128)S(1)} %get-tuple-element.32), channel_id=1, source_target_pairs={{0,3},{1,4},{2,5},{3,6},{4,7},{5,0},{6,1},{7,2},{8,11},{9,12},{10,... | collective-permute-start | bytes 196616 | tf_op jit(solution)/shard_map/ppermute | solution.py:54
  90.1 8.7 %collective-permute-start.27 = (f32[128,128]{1,0:T(8,128)S(1)}, f32[128,128]{1,0:T(8,128)S(1)}, u32[]{:S(2)}, u32[]{:S(2)}) collective-permute-start(f32[128,128]{1,0:T(8,128)S(1)} %get-tuple-element.31), channel_id=1, source_target_pairs={{0,4},{1,5},{2,6},{3,7},{4,0},{5,1},{6,2},{7,3},{8,12},{9,13},{10,... | collective-permute-start | bytes 196616 | tf_op jit(solution)/shard_map/ppermute | solution.py:54
  91.6 7.2 %collective-permute-start.28 = (f32[128,128]{1,0:T(8,128)S(1)}, f32[128,128]{1,0:T(8,128)S(1)}, u32[]{:S(2)}, u32[]{:S(2)}) collective-permute-start(f32[128,128]{1,0:T(8,128)S(1)} %get-tuple-element.30), channel_id=1, source_target_pairs={{0,5},{1,6},{2,7},{3,0},{4,1},{5,2},{6,3},{7,4},{8,13},{9,14},{10,... | collective-permute-start | bytes 196616 | tf_op jit(solution)/shard_map/ppermute | solution.py:54
  92.6 7.7 %collective-permute-start.29 = (f32[128,128]{1,0:T(8,128)S(1)}, f32[128,128]{1,0:T(8,128)S(1)}, u32[]{:S(2)}, u32[]{:S(2)}) collective-permute-start(f32[128,128]{1,0:T(8,128)S(1)} %get-tuple-element.29), channel_id=1, source_target_pairs={{0,6},{1,7},{2,0},{3,1},{4,2},{5,3},{6,4},{7,5},{8,14},{9,15},{10,... | collective-permute-start | bytes 196616 | tf_op jit(solution)/shard_map/ppermute | solution.py:54
  93.7 6.7 %collective-permute-start.30 = (f32[128,128]{1,0:T(8,128)S(1)}, f32[128,128]{1,0:T(8,128)S(1)}, u32[]{:S(2)}, u32[]{:S(2)}) collective-permute-start(f32[128,128]{1,0:T(8,128)S(1)} %get-tuple-element.28), channel_id=1, source_target_pairs={{0,7},{1,0},{2,1},{3,2},{4,3},{5,4},{6,5},{7,6},{8,15},{9,8},{10,9... | collective-permute-start | bytes 196616 | tf_op jit(solution)/shard_map/ppermute | solution.py:54
  101.9 6.2 %collective-permute-start.31 = (bf16[64,384]{1,0:T(8,128)(2,1)S(1)}, bf16[64,384]{1,0:T(8,128)(2,1)S(1)}, u32[]{:S(2)}, u32[]{:S(2)}) collective-permute-start(bf16[64,384]{1,0:T(8,128)(2,1)S(1)} %get-tuple-element.42), channel_id=1, source_target_pairs={{0,1},{1,2},{2,3},{3,4},{4,5},{5,6},{6,7},{7,0},{8,9},{9,10},{10,1... | collective-permute-start | bytes 147464 | tf_op jit(solution)/shard_map/ppermute | solution.py:54
  102.4 7.2 %collective-permute-start.32 = (bf16[64,384]{1,0:T(8,128)(2,1)S(1)}, bf16[64,384]{1,0:T(8,128)(2,1)S(1)}, u32[]{:S(2)}, u32[]{:S(2)}) collective-permute-start(bf16[64,384]{1,0:T(8,128)(2,1)S(1)} %get-tuple-element.41), channel_id=1, source_target_pairs={{0,2},{1,3},{2,4},{3,5},{4,6},{5,7},{6,0},{7,1},{8,10},{9,11},{10,... | collective-permute-start | bytes 147464 | tf_op jit(solution)/shard_map/ppermute | solution.py:54
  104.8 7.7 %collective-permute-start.33 = (bf16[64,384]{1,0:T(8,128)(2,1)S(1)}, bf16[64,384]{1,0:T(8,128)(2,1)S(1)}, u32[]{:S(2)}, u32[]{:S(2)}) collective-permute-start(bf16[64,384]{1,0:T(8,128)(2,1)S(1)} %get-tuple-element.40), channel_id=1, source_target_pairs={{0,3},{1,4},{2,5},{3,6},{4,7},{5,0},{6,1},{7,2},{8,11},{9,12},{10,... | collective-permute-start | bytes 147464 | tf_op jit(solution)/shard_map/ppermute | solution.py:54
  105.2 7.6 %collective-permute-start.34 = (bf16[64,384]{1,0:T(8,128)(2,1)S(1)}, bf16[64,384]{1,0:T(8,128)(2,1)S(1)}, u32[]{:S(2)}, u32[]{:S(2)}) collective-permute-start(bf16[64,384]{1,0:T(8,128)(2,1)S(1)} %get-tuple-element.39), channel_id=1, source_target_pairs={{0,4},{1,5},{2,6},{3,7},{4,0},{5,1},{6,2},{7,3},{8,12},{9,13},{10,... | collective-permute-start | bytes 147464 | tf_op jit(solution)/shard_map/ppermute | solution.py:54
  108.0 6.1 %collective-permute-start.36 = (bf16[64,384]{1,0:T(8,128)(2,1)S(1)}, bf16[64,384]{1,0:T(8,128)(2,1)S(1)}, u32[]{:S(2)}, u32[]{:S(2)}) collective-permute-start(bf16[64,384]{1,0:T(8,128)(2,1)S(1)} %get-tuple-element.37), channel_id=1, source_target_pairs={{0,6},{1,7},{2,0},{3,1},{4,2},{5,3},{6,4},{7,5},{8,14},{9,15},{10,... | collective-permute-start | bytes 147464 | tf_op jit(solution)/shard_map/ppermute | solution.py:54
  114.5 6.6 %collective-permute-start.38 = (f32[64,384]{1,0:T(8,128)S(1)}, f32[64,384]{1,0:T(8,128)S(1)}, u32[]{:S(2)}, u32[]{:S(2)}) collective-permute-start(f32[64,384]{1,0:T(8,128)S(1)} %convert_reduce_fusion), channel_id=1, source_target_pairs={{0,8},{8,16},{16,24},{24,0},{1,9},{9,17},{17,25},{25,1},{2,10},{10... | collective-permute-start | bytes 294920 | tf_op jit(solution)/shard_map/ppermute | solution.py:43
  115.1 6.8 %collective-permute-start.39 = (f32[64,384]{1,0:T(8,128)S(1)}, f32[64,384]{1,0:T(8,128)S(1)}, u32[]{:S(2)}, u32[]{:S(2)}) collective-permute-start(f32[64,384]{1,0:T(8,128)S(1)} %convert_reduce_fusion), channel_id=1, source_target_pairs={{0,16},{8,24},{16,0},{24,8},{1,17},{9,25},{17,1},{25,9},{2,18},{10... | collective-permute-start | bytes 294920 | tf_op jit(solution)/shard_map/ppermute | solution.py:43
  115.6 6.3 %collective-permute-start.40 = (f32[64,384]{1,0:T(8,128)S(1)}, f32[64,384]{1,0:T(8,128)S(1)}, u32[]{:S(2)}, u32[]{:S(2)}) collective-permute-start(f32[64,384]{1,0:T(8,128)S(1)} %convert_reduce_fusion), channel_id=1, source_target_pairs={{0,24},{8,0},{16,8},{24,16},{1,25},{9,1},{17,9},{25,17},{2,26},{10... | collective-permute-start | bytes 294920 | tf_op jit(solution)/shard_map/ppermute | solution.py:43
  (12 other events, 99.0 us)

commit v11 on v7

--- a/solution.py
+++ b/solution.py
@@ -35,10 +35,17 @@
     return jnp.roll(stack[::-1], lax.axis_index(axis) + 1, axis=0)
 
 
-def gather_ordered(value, axis, native):
+def gather_ordered(value, axis, native, paired=False):
     size = lax.axis_size(axis)
     if native or size > FAN_OUT_MAX:
         return lax.all_gather(value, axis)
+    if paired and size & (size - 1) == 0:
+        pieces = [value] + [
+            lax.ppermute(value, axis, [(source, source ^ mask) for source in range(size)])
+            for mask in range(1, size)
+        ]
+        order = jnp.bitwise_xor(lax.axis_index(axis), jnp.arange(size))
+        return jnp.take(jnp.stack(pieces), order, axis=0)
     pieces = [value] + [
         lax.ppermute(value, axis, shift_pairs(size, shift)) for shift in range(1, size)
     ]
@@ -234,7 +241,7 @@
     group_sums = jnp.sum(row_hits * row_excess[:, None], axis=0)
     group_counts = jnp.sum(row_hits, axis=0) * seq_len
 
-    summed = jnp.sum(gather_ordered(jnp.stack([group_sums, group_counts]), "dp", False), axis=0)
+    summed = jnp.sum(gather_ordered(jnp.stack([group_sums, group_counts]), "dp", False, True), axis=0)
     total_sums = summed[0]
     domain_counts = summed[1]
     softmax_mix = jax.nn.softmax(jnp.log(alpha_prev) + total_sums / domain_counts)
@@ -276,7 +283,7 @@
     )
     local_grad = jnp.sum(arrived_grad.astype(jnp.float32), axis=0)
 
-    grad_shard = jnp.sum(gather_ordered(local_grad, "dp", False), axis=0)
+    grad_shard = jnp.sum(gather_ordered(local_grad, "dp", False, True), axis=0)
     return (
         alpha_new,
         grad_shard[:, :width],

time: 121 us -> 123 us (1.017)
    ppermute x20 -> x14, starting transfers between devices: 24.7 us -> 16.7 us  [gather_ordered(): lax.ppermute(value, axis, shift_pairs(size, shift))]
    ppermute x0 -> x6, waiting for transfers between devices: none -> 7.88 us  [gather_ordered(): lax.ppermute(value, axis, [(source, source ^ mask) for source in range(si...]
    ppermute x0 -> x6, starting transfers between devices: none -> 7.11 us  [gather_ordered(): lax.ppermute(value, axis, [(source, source ^ mask) for source in range(si...]
    ppermute x20 -> x14, waiting for transfers between devices: 14 us -> 7.33 us  [gather_ordered(): lax.ppermute(value, axis, shift_pairs(size, shift))]
where the time goes in v11:
time: 123 us; the launch traced here: 122 us
  starting transfers between devices  51.1 us (42%)
  waiting for transfers between devices  24.2 us (20%)
  blocking collectives  17.3 us (14%)
  other arithmetic  9.46 us (8%)
  local copies, waits for them, and re-layouts  8.99 us (7%)
  matrix products  8.89 us (7%)
  between operations  2.07 us (2%)
    ppermute x21, starting transfers between devices, exchange_ordered(): lax.ppermute(lax.dynamic_index_in_dim(blocks, (here + shift) % size, keep...  27.2 us
    all_gather x1, blocking collectives, gather_ordered(): return lax.all_gather(value, axis)  17.3 us
    ppermute x14, starting transfers between devices, gather_ordered(): lax.ppermute(value, axis, shift_pairs(size, shift))  16.7 us
    ppermute x21, waiting for transfers between devices, exchange_ordered(): lax.ppermute(lax.dynamic_index_in_dim(blocks, (here + shift) % size, keep...  9.04 us
    ppermute x6, waiting for transfers between devices, gather_ordered(): lax.ppermute(value, axis, [(source, source ^ mask) for source in range(si...  7.88 us
    ppermute x14, waiting for transfers between devices, gather_ordered(): lax.ppermute(value, axis, shift_pairs(size, shift))  7.33 us
    ppermute x6, starting transfers between devices, gather_ordered(): lax.ppermute(value, axis, [(source, source ^ mask) for source in range(si...  7.11 us
    unnamed x37, local copies, waits for them, and re-layouts  4.61 us
  transfers between devices with their start and end apart: 41, of which 18 were waited for; matrix products, arithmetic and copies ran while one was open for 1% of the time, Pallas kernels for 0%

profile of v11, /device:TPU:0, one launch (start us, length us, event | category | flops | bytes accessed | tf_op | source)
XLA Modules:
  0.0 122.0 jit_solution(16671131226576963942)
XLA Ops:
  7.2 17.3 %all-gather.1 = bf16[8,389,128]{2,1,0:T(8,128)(2,1)S(1)} all-gather(bf16[1,389,128]{2,1,0:T(8,128)(2,1)S(1)} %bitcast.224), channel_id=2, replica_groups=mesh['dp'=4,'fsdp'=8] {'fsdp'}, dimensions={0}, use_global_device_ids=true | all-gather | bytes 896256 | tf_op jit(solution)/shard_map/all_gather | solution.py:41
  24.5 1.8 %fusion.3 = bf16[1024,128]{1,0:T(8,128)(2,1)S(1)} fusion(bf16[1024,128]{1,0:T(8,128)(2,1)} %param.19, s32[1024]{0:T(1024)S(1)} %bitcast.252), kind=kOutput, calls=%fused_computation.13 | convolution fusion | flops 269615104 | bytes 528384 | tf_op jit(solution)/shard_map/dot_general | solution.py:207
  26.8 1.6 %collective-permute-start.1 = (bf16[128,128]{1,0:T(8,128)(2,1)S(1)}, bf16[128,128]{1,0:T(8,128)(2,1)S(1)}, u32[]{:S(2)}, u32[]{:S(2)}) collective-permute-start(bf16[128,128]{1,0:T(8,128)(2,1)S(1)} %get-tuple-element.49), channel_id=1, source_target_pairs={{0,2},{1,3},{2,4},{3,5},{4,6},{5,7},{6,0},{7,1},{8,10},{9,11},{10,... | collective-permute-start | bytes 98312 | tf_op jit(solution)/shard_map/ppermute | solution.py:61
  28.4 2.1 %collective-permute-start.2 = (bf16[128,128]{1,0:T(8,128)(2,1)S(1)}, bf16[128,128]{1,0:T(8,128)(2,1)S(1)}, u32[]{:S(2)}, u32[]{:S(2)}) collective-permute-start(bf16[128,128]{1,0:T(8,128)(2,1)S(1)} %get-tuple-element.48), channel_id=1, source_target_pairs={{0,3},{1,4},{2,5},{3,6},{4,7},{5,0},{6,1},{7,2},{8,11},{9,12},{10,... | collective-permute-start | bytes 98312 | tf_op jit(solution)/shard_map/ppermute | solution.py:61
  30.5 1.3 %collective-permute-start.3 = (bf16[128,128]{1,0:T(8,128)(2,1)S(1)}, bf16[128,128]{1,0:T(8,128)(2,1)S(1)}, u32[]{:S(2)}, u32[]{:S(2)}) collective-permute-start(bf16[128,128]{1,0:T(8,128)(2,1)S(1)} %get-tuple-element.47), channel_id=1, source_target_pairs={{0,4},{1,5},{2,6},{3,7},{4,0},{5,1},{6,2},{7,3},{8,12},{9,13},{10,... | collective-permute-start | bytes 98312 | tf_op jit(solution)/shard_map/ppermute | solution.py:61
  31.8 1.4 %collective-permute-start.4 = (bf16[128,128]{1,0:T(8,128)(2,1)S(1)}, bf16[128,128]{1,0:T(8,128)(2,1)S(1)}, u32[]{:S(2)}, u32[]{:S(2)}) collective-permute-start(bf16[128,128]{1,0:T(8,128)(2,1)S(1)} %get-tuple-element.46), channel_id=1, source_target_pairs={{0,5},{1,6},{2,7},{3,0},{4,1},{5,2},{6,3},{7,4},{8,13},{9,14},{10,... | collective-permute-start | bytes 98312 | tf_op jit(solution)/shard_map/ppermute | solution.py:61
  36.2 1.9 %collective-permute-done.5 = bf16[128,128]{1,0:T(8,128)(2,1)S(1)} collective-permute-done((bf16[128,128]{1,0:T(8,128)(2,1)S(1)}, bf16[128,128]{1,0:T(8,128)(2,1)S(1)}, u32[]{:S(2)}, u32[]{:S(2)}) %collective-permute-start.5) | collective-permute-done | bytes 32800 | tf_op jit(solution)/shard_map/ppermute | solution.py:61
  41.4 2.0 %collective-permute-start.9 = (bf16[128,256]{0,1:T(8,128)(2,1)S(1)}, bf16[128,256]{0,1:T(8,128)(2,1)S(1)}, u32[]{:S(2)}, u32[]{:S(2)}) collective-permute-start(bf16[128,256]{0,1:T(8,128)(2,1)S(1)} %pad_maximum_fusion.2), channel_id=1, source_target_pairs={{0,3},{1,4},{2,5},{3,6},{4,7},{5,0},{6,1},{7,2},{8,11},{9,12},{10,... | collective-permute-start | bytes 196616 | tf_op jit(solution)/shard_map/ppermute | solution.py:50
  43.4 1.5 %collective-permute-start.10 = (bf16[128,256]{0,1:T(8,128)(2,1)S(1)}, bf16[128,256]{0,1:T(8,128)(2,1)S(1)}, u32[]{:S(2)}, u32[]{:S(2)}) collective-permute-start(bf16[128,256]{0,1:T(8,128)(2,1)S(1)} %pad_maximum_fusion.2), channel_id=1, source_target_pairs={{0,4},{1,5},{2,6},{3,7},{4,0},{5,1},{6,2},{7,3},{8,12},{9,13},{10,... | collective-permute-start | bytes 196616 | tf_op jit(solution)/shard_map/ppermute | solution.py:50
  46.1 1.5 %collective-permute-start.12 = (bf16[128,256]{0,1:T(8,128)(2,1)S(1)}, bf16[128,256]{0,1:T(8,128)(2,1)S(1)}, u32[]{:S(2)}, u32[]{:S(2)}) collective-permute-start(bf16[128,256]{0,1:T(8,128)(2,1)S(1)} %pad_maximum_fusion.2), channel_id=1, source_target_pairs={{0,6},{1,7},{2,0},{3,1},{4,2},{5,3},{6,4},{7,5},{8,14},{9,15},{10,... | collective-permute-start | bytes 196616 | tf_op jit(solution)/shard_map/ppermute | solution.py:50
  48.0 3.9 %collective-permute-done.9 = bf16[128,256]{0,1:T(8,128)(2,1)S(1)} collective-permute-done((bf16[128,256]{0,1:T(8,128)(2,1)S(1)}, bf16[128,256]{0,1:T(8,128)(2,1)S(1)}, u32[]{:S(2)}, u32[]{:S(2)}) %collective-permute-start.9) | collective-permute-done | bytes 65568 | tf_op jit(solution)/shard_map/ppermute | solution.py:50
  52.2 1.6 %collective-permute-done.12 = bf16[128,256]{0,1:T(8,128)(2,1)S(1)} collective-permute-done((bf16[128,256]{0,1:T(8,128)(2,1)S(1)}, bf16[128,256]{0,1:T(8,128)(2,1)S(1)}, u32[]{:S(2)}, u32[]{:S(2)}) %collective-permute-start.12) | collective-permute-done | bytes 65568 | tf_op jit(solution)/shard_map/ppermute | solution.py:50
  55.8 2.0 %select_reduce_fusion = (f32[1024]{0:T(1024)S(1)}, f32[1024]{0:T(1024)S(1)}, f32[1024]{0:T(1024)S(1)}, f32[1024]{0:T(1024)S(1)}) fusion(f32[1024,1024]{0,1:T(8,128)S(1)} %get-tuple-element.76, s32[1024]{0:T(1024)S(1)} %bitcast.249, f32[1024]{0:T(1024)S(1)} %get-tuple-element.75, f32[1024,1024]{0,1:T(8,128)S(1)} %get-tuple-element.74, ...), kind=kLoop, calls=%fused_computation.4 | loop fusion | flops 9433088 | bytes 8417280 | tf_op jit(solution)/shard_map/reduce_sum | solution.py:98
  58.4 2.3 %collective-permute-start.15 = (f32[6,1024]{1,0:T(8,128)S(1)}, f32[6,1024]{1,0:T(8,128)S(1)}, u32[]{:S(2)}, u32[]{:S(2)}) collective-permute-start(f32[6,1024]{1,0:T(8,128)S(1)} %concatenate.44), channel_id=1, source_target_pairs={{0,2},{1,3},{2,4},{3,5},{4,6},{5,7},{6,0},{7,1},{8,10},{9,11},{10,... | collective-permute-start | bytes 73736 | tf_op jit(solution)/shard_map/ppermute | solution.py:50
  61.4 2.0 %collective-permute-start.17 = (f32[6,1024]{1,0:T(8,128)S(1)}, f32[6,1024]{1,0:T(8,128)S(1)}, u32[]{:S(2)}, u32[]{:S(2)}) collective-permute-start(f32[6,1024]{1,0:T(8,128)S(1)} %concatenate.44), channel_id=1, source_target_pairs={{0,4},{1,5},{2,6},{3,7},{4,0},{5,1},{6,2},{7,3},{8,12},{9,13},{10,... | collective-permute-start | bytes 73736 | tf_op jit(solution)/shard_map/ppermute | solution.py:50
  69.5 1.6 %collective-permute-start.21 = (f32[2,22]{1,0:T(2,128)S(1)}, f32[2,22]{1,0:T(2,128)S(1)}, u32[]{:S(2)}, u32[]{:S(2)}) collective-permute-start(f32[2,22]{1,0:T(2,128)S(1)} %get-tuple-element.62), channel_id=1, source_target_pairs={{0,8},{8,0},{16,24},{24,16},{1,9},{9,1},{17,25},{25,17},{2,10},{10... | collective-permute-start | bytes 536 | tf_op jit(solution)/shard_map/ppermute | solution.py:44
  71.0 1.5 %collective-permute-start.22 = (f32[2,22]{1,0:T(2,128)S(1)}, f32[2,22]{1,0:T(2,128)S(1)}, u32[]{:S(2)}, u32[]{:S(2)}) collective-permute-start(f32[2,22]{1,0:T(2,128)S(1)} %get-tuple-element.62), channel_id=1, source_target_pairs={{0,16},{8,24},{16,0},{24,8},{1,17},{9,25},{17,1},{25,9},{2,18},{10... | collective-permute-start | bytes 536 | tf_op jit(solution)/shard_map/ppermute | solution.py:44
  73.1 1.5 %collective-permute-done.22 = f32[2,22]{1,0:T(2,128)S(1)} collective-permute-done((f32[2,22]{1,0:T(2,128)S(1)}, f32[2,22]{1,0:T(2,128)S(1)}, u32[]{:S(2)}, u32[]{:S(2)}) %collective-permute-start.22) | collective-permute-done | bytes 208 | tf_op jit(solution)/shard_map/ppermute | solution.py:44
  74.6 2.4 %collective-permute-done.23 = f32[2,22]{1,0:T(2,128)S(1)} collective-permute-done((f32[2,22]{1,0:T(2,128)S(1)}, f32[2,22]{1,0:T(2,128)S(1)}, u32[]{:S(2)}, u32[]{:S(2)}) %collective-permute-start.23) | collective-permute-done | bytes 208 | tf_op jit(solution)/shard_map/ppermute | solution.py:44
  79.6 1.8 %bitcast_divide_fusion = (f32[22]{0:T(128)S(1)}, f32[22]{0:T(128)}) fusion(f32[2,22]{1,0:T(2,128)S(1)} %select_reduce_fusion.3, f32[]{:T(128)} %fusion.40, f32[22]{0:T(128)S(1)} %get-tuple-element.19, f32[]{:T(128)} %get-tuple-element.18), kind=kLoop, calls=%fused_computation.177 | loop fusion | flops 132 | bytes 360 | tf_op jit(solution)/shard_map/div | solution.py:250
  82.1 3.5 %fusion.2 = f32[1024,128]{1,0:T(8,128)S(1)} fusion(bf16[1024,128]{1,0:T(8,128)(2,1)S(1)} %copy-done, f32[1024,1024]{0,1:T(8,128)} %copy-done.1, f32[1024]{0:T(1024)S(1)} %bitcast.253, f32[1024]{0:T(1024)S(1)} %broadcast_bitcast_fusion, s32[1024]{0:T(1024)S(1)} %bitcast.250), kind=kOutput, calls=%fused_computation.12 | convolution fusion | flops 274726912 | bytes 4993024 | tf_op jit(solution)/shard_map/dot_general | solution.py:120
  86.8 2.3 %collective-permute-start.26 = (f32[128,128]{1,0:T(8,128)S(1)}, f32[128,128]{1,0:T(8,128)S(1)}, u32[]{:S(2)}, u32[]{:S(2)}) collective-permute-start(f32[128,128]{1,0:T(8,128)S(1)} %get-tuple-element.32), channel_id=1, source_target_pairs={{0,3},{1,4},{2,5},{3,6},{4,7},{5,0},{6,1},{7,2},{8,11},{9,12},{10,... | collective-permute-start | bytes 196616 | tf_op jit(solution)/shard_map/ppermute | solution.py:61
  89.0 1.5 %collective-permute-start.27 = (f32[128,128]{1,0:T(8,128)S(1)}, f32[128,128]{1,0:T(8,128)S(1)}, u32[]{:S(2)}, u32[]{:S(2)}) collective-permute-start(f32[128,128]{1,0:T(8,128)S(1)} %get-tuple-element.31), channel_id=1, source_target_pairs={{0,4},{1,5},{2,6},{3,7},{4,0},{5,1},{6,2},{7,3},{8,12},{9,13},{10,... | collective-permute-start | bytes 196616 | tf_op jit(solution)/shard_map/ppermute | solution.py:61
  93.9 3.6 %collective-permute-done.26 = f32[128,128]{1,0:T(8,128)S(1)} collective-permute-done((f32[128,128]{1,0:T(8,128)S(1)}, f32[128,128]{1,0:T(8,128)S(1)}, u32[]{:S(2)}, u32[]{:S(2)}) %collective-permute-start.26) | collective-permute-done | bytes 65568 | tf_op jit(solution)/shard_map/ppermute | solution.py:61
  99.3 1.9 %collective-permute-start.31 = (bf16[64,384]{1,0:T(8,128)(2,1)S(1)}, bf16[64,384]{1,0:T(8,128)(2,1)S(1)}, u32[]{:S(2)}, u32[]{:S(2)}) collective-permute-start(bf16[64,384]{1,0:T(8,128)(2,1)S(1)} %get-tuple-element.42), channel_id=1, source_target_pairs={{0,1},{1,2},{2,3},{3,4},{4,5},{5,6},{6,7},{7,0},{8,9},{9,10},{10,1... | collective-permute-start | bytes 147464 | tf_op jit(solution)/shard_map/ppermute | solution.py:61
  101.3 2.5 %collective-permute-start.32 = (bf16[64,384]{1,0:T(8,128)(2,1)S(1)}, bf16[64,384]{1,0:T(8,128)(2,1)S(1)}, u32[]{:S(2)}, u32[]{:S(2)}) collective-permute-start(bf16[64,384]{1,0:T(8,128)(2,1)S(1)} %get-tuple-element.41), channel_id=1, source_target_pairs={{0,2},{1,3},{2,4},{3,5},{4,6},{5,7},{6,0},{7,1},{8,10},{9,11},{10,... | collective-permute-start | bytes 147464 | tf_op jit(solution)/shard_map/ppermute | solution.py:61
  104.2 2.3 %collective-permute-start.34 = (bf16[64,384]{1,0:T(8,128)(2,1)S(1)}, bf16[64,384]{1,0:T(8,128)(2,1)S(1)}, u32[]{:S(2)}, u32[]{:S(2)}) collective-permute-start(bf16[64,384]{1,0:T(8,128)(2,1)S(1)} %get-tuple-element.39), channel_id=1, source_target_pairs={{0,4},{1,5},{2,6},{3,7},{4,0},{5,1},{6,2},{7,3},{8,12},{9,13},{10,... | collective-permute-start | bytes 147464 | tf_op jit(solution)/shard_map/ppermute | solution.py:61
  107.0 1.6 %collective-permute-start.36 = (bf16[64,384]{1,0:T(8,128)(2,1)S(1)}, bf16[64,384]{1,0:T(8,128)(2,1)S(1)}, u32[]{:S(2)}, u32[]{:S(2)}) collective-permute-start(bf16[64,384]{1,0:T(8,128)(2,1)S(1)} %get-tuple-element.37), channel_id=1, source_target_pairs={{0,6},{1,7},{2,0},{3,1},{4,2},{5,3},{6,4},{7,5},{8,14},{9,15},{10,... | collective-permute-start | bytes 147464 | tf_op jit(solution)/shard_map/ppermute | solution.py:61
  108.6 1.4 %collective-permute-start.37 = (bf16[64,384]{1,0:T(8,128)(2,1)S(1)}, bf16[64,384]{1,0:T(8,128)(2,1)S(1)}, u32[]{:S(2)}, u32[]{:S(2)}) collective-permute-start(bf16[64,384]{1,0:T(8,128)(2,1)S(1)} %get-tuple-element.36), channel_id=1, source_target_pairs={{0,7},{1,0},{2,1},{3,2},{4,3},{5,4},{6,5},{7,6},{8,15},{9,8},{10,9... | collective-permute-start | bytes 147464 | tf_op jit(solution)/shard_map/ppermute | solution.py:61
  114.3 2.5 %collective-permute-start.40 = (f32[64,384]{1,0:T(8,128)S(1)}, f32[64,384]{1,0:T(8,128)S(1)}, u32[]{:S(2)}, u32[]{:S(2)}) collective-permute-start(f32[64,384]{1,0:T(8,128)S(1)} %convert_reduce_fusion), channel_id=1, source_target_pairs={{0,24},{8,16},{16,8},{24,0},{1,25},{9,17},{17,9},{25,1},{2,26},{10... | collective-permute-start | bytes 294920 | tf_op jit(solution)/shard_map/ppermute | solution.py:44
  116.7 2.1 %collective-permute-done.38 = f32[64,384]{1,0:T(8,128)S(1)} collective-permute-done((f32[64,384]{1,0:T(8,128)S(1)}, f32[64,384]{1,0:T(8,128)S(1)}, u32[]{:S(2)}, u32[]{:S(2)}) %collective-permute-start.38) | collective-permute-done | bytes 98336 | tf_op jit(solution)/shard_map/ppermute | solution.py:44
  118.9 1.8 %collective-permute-done.39 = f32[64,384]{1,0:T(8,128)S(1)} collective-permute-done((f32[64,384]{1,0:T(8,128)S(1)}, f32[64,384]{1,0:T(8,128)S(1)}, u32[]{:S(2)}, u32[]{:S(2)}) %collective-permute-start.39) | collective-permute-done | bytes 98336 | tf_op jit(solution)/shard_map/ppermute | solution.py:44
  (184 shorter events, 40.0 us)
Async XLA Ops:
  26.3 7.7 %collective-permute-start = (bf16[128,128]{1,0:T(8,128)(2,1)S(1)}, bf16[128,128]{1,0:T(8,128)(2,1)S(1)}, u32[]{:S(2)}, u32[]{:S(2)}) collective-permute-start(bf16[128,128]{1,0:T(8,128)(2,1)S(1)} %get-tuple-element.50), channel_id=1, source_target_pairs={{0,1},{1,2},{2,3},{3,4},{4,5},{5,6},{6,7},{7,0},{8,9},{9,10},{10,1... | collective-permute-start | bytes 98312 | tf_op jit(solution)/shard_map/ppermute | solution.py:61
  26.8 8.0 %collective-permute-start.1 = (bf16[128,128]{1,0:T(8,128)(2,1)S(1)}, bf16[128,128]{1,0:T(8,128)(2,1)S(1)}, u32[]{:S(2)}, u32[]{:S(2)}) collective-permute-start(bf16[128,128]{1,0:T(8,128)(2,1)S(1)} %get-tuple-element.49), channel_id=1, source_target_pairs={{0,2},{1,3},{2,4},{3,5},{4,6},{5,7},{6,0},{7,1},{8,10},{9,11},{10,... | collective-permute-start | bytes 98312 | tf_op jit(solution)/shard_map/ppermute | solution.py:61
  28.4 7.2 %collective-permute-start.2 = (bf16[128,128]{1,0:T(8,128)(2,1)S(1)}, bf16[128,128]{1,0:T(8,128)(2,1)S(1)}, u32[]{:S(2)}, u32[]{:S(2)}) collective-permute-start(bf16[128,128]{1,0:T(8,128)(2,1)S(1)} %get-tuple-element.48), channel_id=1, source_target_pairs={{0,3},{1,4},{2,5},{3,6},{4,7},{5,0},{6,1},{7,2},{8,11},{9,12},{10,... | collective-permute-start | bytes 98312 | tf_op jit(solution)/shard_map/ppermute | solution.py:61
  30.5 5.6 %collective-permute-start.3 = (bf16[128,128]{1,0:T(8,128)(2,1)S(1)}, bf16[128,128]{1,0:T(8,128)(2,1)S(1)}, u32[]{:S(2)}, u32[]{:S(2)}) collective-permute-start(bf16[128,128]{1,0:T(8,128)(2,1)S(1)} %get-tuple-element.47), channel_id=1, source_target_pairs={{0,4},{1,5},{2,6},{3,7},{4,0},{5,1},{6,2},{7,3},{8,12},{9,13},{10,... | collective-permute-start | bytes 98312 | tf_op jit(solution)/shard_map/ppermute | solution.py:61
  40.1 6.0 %collective-permute-start.7 = (bf16[128,256]{0,1:T(8,128)(2,1)S(1)}, bf16[128,256]{0,1:T(8,128)(2,1)S(1)}, u32[]{:S(2)}, u32[]{:S(2)}) collective-permute-start(bf16[128,256]{0,1:T(8,128)(2,1)S(1)} %pad_maximum_fusion.2), channel_id=1, source_target_pairs={{0,1},{1,2},{2,3},{3,4},{4,5},{5,6},{6,7},{7,0},{8,9},{9,10},{10,1... | collective-permute-start | bytes 196616 | tf_op jit(solution)/shard_map/ppermute | solution.py:50
  41.1 6.7 %collective-permute-start.8 = (bf16[128,256]{0,1:T(8,128)(2,1)S(1)}, bf16[128,256]{0,1:T(8,128)(2,1)S(1)}, u32[]{:S(2)}, u32[]{:S(2)}) collective-permute-start(bf16[128,256]{0,1:T(8,128)(2,1)S(1)} %pad_maximum_fusion.2), channel_id=1, source_target_pairs={{0,2},{1,3},{2,4},{3,5},{4,6},{5,7},{6,0},{7,1},{8,10},{9,11},{10,... | collective-permute-start | bytes 196616 | tf_op jit(solution)/shard_map/ppermute | solution.py:50
  41.4 10.5 %collective-permute-start.9 = (bf16[128,256]{0,1:T(8,128)(2,1)S(1)}, bf16[128,256]{0,1:T(8,128)(2,1)S(1)}, u32[]{:S(2)}, u32[]{:S(2)}) collective-permute-start(bf16[128,256]{0,1:T(8,128)(2,1)S(1)} %pad_maximum_fusion.2), channel_id=1, source_target_pairs={{0,3},{1,4},{2,5},{3,6},{4,7},{5,0},{6,1},{7,2},{8,11},{9,12},{10,... | collective-permute-start | bytes 196616 | tf_op jit(solution)/shard_map/ppermute | solution.py:50
  43.4 8.7 %collective-permute-start.10 = (bf16[128,256]{0,1:T(8,128)(2,1)S(1)}, bf16[128,256]{0,1:T(8,128)(2,1)S(1)}, u32[]{:S(2)}, u32[]{:S(2)}) collective-permute-start(bf16[128,256]{0,1:T(8,128)(2,1)S(1)} %pad_maximum_fusion.2), channel_id=1, source_target_pairs={{0,4},{1,5},{2,6},{3,7},{4,0},{5,1},{6,2},{7,3},{8,12},{9,13},{10,... | collective-permute-start | bytes 196616 | tf_op jit(solution)/shard_map/ppermute | solution.py:50
  44.8 7.3 %collective-permute-start.11 = (bf16[128,256]{0,1:T(8,128)(2,1)S(1)}, bf16[128,256]{0,1:T(8,128)(2,1)S(1)}, u32[]{:S(2)}, u32[]{:S(2)}) collective-permute-start(bf16[128,256]{0,1:T(8,128)(2,1)S(1)} %pad_maximum_fusion.2), channel_id=1, source_target_pairs={{0,5},{1,6},{2,7},{3,0},{4,1},{5,2},{6,3},{7,4},{8,13},{9,14},{10,... | collective-permute-start | bytes 196616 | tf_op jit(solution)/shard_map/ppermute | solution.py:50
  46.1 7.6 %collective-permute-start.12 = (bf16[128,256]{0,1:T(8,128)(2,1)S(1)}, bf16[128,256]{0,1:T(8,128)(2,1)S(1)}, u32[]{:S(2)}, u32[]{:S(2)}) collective-permute-start(bf16[128,256]{0,1:T(8,128)(2,1)S(1)} %pad_maximum_fusion.2), channel_id=1, source_target_pairs={{0,6},{1,7},{2,0},{3,1},{4,2},{5,3},{6,4},{7,5},{8,14},{9,15},{10,... | collective-permute-start | bytes 196616 | tf_op jit(solution)/shard_map/ppermute | solution.py:50
  47.8 6.0 %collective-permute-start.13 = (bf16[128,256]{0,1:T(8,128)(2,1)S(1)}, bf16[128,256]{0,1:T(8,128)(2,1)S(1)}, u32[]{:S(2)}, u32[]{:S(2)}) collective-permute-start(bf16[128,256]{0,1:T(8,128)(2,1)S(1)} %pad_maximum_fusion.2), channel_id=1, source_target_pairs={{0,7},{1,0},{2,1},{3,2},{4,3},{5,4},{6,5},{7,6},{8,15},{9,8},{10,9... | collective-permute-start | bytes 196616 | tf_op jit(solution)/shard_map/ppermute | solution.py:50
  57.8 6.6 %collective-permute-start.14 = (f32[6,1024]{1,0:T(8,128)S(1)}, f32[6,1024]{1,0:T(8,128)S(1)}, u32[]{:S(2)}, u32[]{:S(2)}) collective-permute-start(f32[6,1024]{1,0:T(8,128)S(1)} %concatenate.44), channel_id=1, source_target_pairs={{0,1},{1,2},{2,3},{3,4},{4,5},{5,6},{6,7},{7,0},{8,9},{9,10},{10,1... | collective-permute-start | bytes 73736 | tf_op jit(solution)/shard_map/ppermute | solution.py:50
  58.4 7.2 %collective-permute-start.15 = (f32[6,1024]{1,0:T(8,128)S(1)}, f32[6,1024]{1,0:T(8,128)S(1)}, u32[]{:S(2)}, u32[]{:S(2)}) collective-permute-start(f32[6,1024]{1,0:T(8,128)S(1)} %concatenate.44), channel_id=1, source_target_pairs={{0,2},{1,3},{2,4},{3,5},{4,6},{5,7},{6,0},{7,1},{8,10},{9,11},{10,... | collective-permute-start | bytes 73736 | tf_op jit(solution)/shard_map/ppermute | solution.py:50
  60.7 6.3 %collective-permute-start.16 = (f32[6,1024]{1,0:T(8,128)S(1)}, f32[6,1024]{1,0:T(8,128)S(1)}, u32[]{:S(2)}, u32[]{:S(2)}) collective-permute-start(f32[6,1024]{1,0:T(8,128)S(1)} %concatenate.44), channel_id=1, source_target_pairs={{0,3},{1,4},{2,5},{3,6},{4,7},{5,0},{6,1},{7,2},{8,11},{9,12},{10,... | collective-permute-start | bytes 73736 | tf_op jit(solution)/shard_map/ppermute | solution.py:50
  61.4 6.2 %collective-permute-start.17 = (f32[6,1024]{1,0:T(8,128)S(1)}, f32[6,1024]{1,0:T(8,128)S(1)}, u32[]{:S(2)}, u32[]{:S(2)}) collective-permute-start(f32[6,1024]{1,0:T(8,128)S(1)} %concatenate.44), channel_id=1, source_target_pairs={{0,4},{1,5},{2,6},{3,7},{4,0},{5,1},{6,2},{7,3},{8,12},{9,13},{10,... | collective-permute-start | bytes 73736 | tf_op jit(solution)/shard_map/ppermute | solution.py:50
  72.6 4.5 %collective-permute-start.23 = (f32[2,22]{1,0:T(2,128)S(1)}, f32[2,22]{1,0:T(2,128)S(1)}, u32[]{:S(2)}, u32[]{:S(2)}) collective-permute-start(f32[2,22]{1,0:T(2,128)S(1)} %get-tuple-element.62), channel_id=1, source_target_pairs={{0,24},{8,16},{16,8},{24,0},{1,25},{9,17},{17,9},{25,1},{2,26},{10... | collective-permute-start | bytes 536 | tf_op jit(solution)/shard_map/ppermute | solution.py:44
  85.7 5.8 %collective-permute-start.24 = (f32[128,128]{1,0:T(8,128)S(1)}, f32[128,128]{1,0:T(8,128)S(1)}, u32[]{:S(2)}, u32[]{:S(2)}) collective-permute-start(f32[128,128]{1,0:T(8,128)S(1)} %get-tuple-element.34), channel_id=1, source_target_pairs={{0,1},{1,2},{2,3},{3,4},{4,5},{5,6},{6,7},{7,0},{8,9},{9,10},{10,1... | collective-permute-start | bytes 196616 | tf_op jit(solution)/shard_map/ppermute | solution.py:61
  85.7 6.9 %collective-permute-start.25 = (f32[128,128]{1,0:T(8,128)S(1)}, f32[128,128]{1,0:T(8,128)S(1)}, u32[]{:S(2)}, u32[]{:S(2)}) collective-permute-start(f32[128,128]{1,0:T(8,128)S(1)} %get-tuple-element.33), channel_id=1, source_target_pairs={{0,2},{1,3},{2,4},{3,5},{4,6},{5,7},{6,0},{7,1},{8,10},{9,11},{10,... | collective-permute-start | bytes 196616 | tf_op jit(solution)/shard_map/ppermute | solution.py:61
  86.8 10.7 %collective-permute-start.26 = (f32[128,128]{1,0:T(8,128)S(1)}, f32[128,128]{1,0:T(8,128)S(1)}, u32[]{:S(2)}, u32[]{:S(2)}) collective-permute-start(f32[128,128]{1,0:T(8,128)S(1)} %get-tuple-element.32), channel_id=1, source_target_pairs={{0,3},{1,4},{2,5},{3,6},{4,7},{5,0},{6,1},{7,2},{8,11},{9,12},{10,... | collective-permute-start | bytes 196616 | tf_op jit(solution)/shard_map/ppermute | solution.py:61
  89.0 8.7 %collective-permute-start.27 = (f32[128,128]{1,0:T(8,128)S(1)}, f32[128,128]{1,0:T(8,128)S(1)}, u32[]{:S(2)}, u32[]{:S(2)}) collective-permute-start(f32[128,128]{1,0:T(8,128)S(1)} %get-tuple-element.31), channel_id=1, source_target_pairs={{0,4},{1,5},{2,6},{3,7},{4,0},{5,1},{6,2},{7,3},{8,12},{9,13},{10,... | collective-permute-start | bytes 196616 | tf_op jit(solution)/shard_map/ppermute | solution.py:61
  90.5 7.2 %collective-permute-start.28 = (f32[128,128]{1,0:T(8,128)S(1)}, f32[128,128]{1,0:T(8,128)S(1)}, u32[]{:S(2)}, u32[]{:S(2)}) collective-permute-start(f32[128,128]{1,0:T(8,128)S(1)} %get-tuple-element.30), channel_id=1, source_target_pairs={{0,5},{1,6},{2,7},{3,0},{4,1},{5,2},{6,3},{7,4},{8,13},{9,14},{10,... | collective-permute-start | bytes 196616 | tf_op jit(solution)/shard_map/ppermute | solution.py:61
  91.5 6.3 %collective-permute-start.29 = (f32[128,128]{1,0:T(8,128)S(1)}, f32[128,128]{1,0:T(8,128)S(1)}, u32[]{:S(2)}, u32[]{:S(2)}) collective-permute-start(f32[128,128]{1,0:T(8,128)S(1)} %get-tuple-element.29), channel_id=1, source_target_pairs={{0,6},{1,7},{2,0},{3,1},{4,2},{5,3},{6,4},{7,5},{8,14},{9,15},{10,... | collective-permute-start | bytes 196616 | tf_op jit(solution)/shard_map/ppermute | solution.py:61
  92.6 5.1 %collective-permute-start.30 = (f32[128,128]{1,0:T(8,128)S(1)}, f32[128,128]{1,0:T(8,128)S(1)}, u32[]{:S(2)}, u32[]{:S(2)}) collective-permute-start(f32[128,128]{1,0:T(8,128)S(1)} %get-tuple-element.28), channel_id=1, source_target_pairs={{0,7},{1,0},{2,1},{3,2},{4,3},{5,4},{6,5},{7,6},{8,15},{9,8},{10,9... | collective-permute-start | bytes 196616 | tf_op jit(solution)/shard_map/ppermute | solution.py:61
  99.3 7.7 %collective-permute-start.31 = (bf16[64,384]{1,0:T(8,128)(2,1)S(1)}, bf16[64,384]{1,0:T(8,128)(2,1)S(1)}, u32[]{:S(2)}, u32[]{:S(2)}) collective-permute-start(bf16[64,384]{1,0:T(8,128)(2,1)S(1)} %get-tuple-element.42), channel_id=1, source_target_pairs={{0,1},{1,2},{2,3},{3,4},{4,5},{5,6},{6,7},{7,0},{8,9},{9,10},{10,1... | collective-permute-start | bytes 147464 | tf_op jit(solution)/shard_map/ppermute | solution.py:61
  101.3 7.3 %collective-permute-start.32 = (bf16[64,384]{1,0:T(8,128)(2,1)S(1)}, bf16[64,384]{1,0:T(8,128)(2,1)S(1)}, u32[]{:S(2)}, u32[]{:S(2)}) collective-permute-start(bf16[64,384]{1,0:T(8,128)(2,1)S(1)} %get-tuple-element.41), channel_id=1, source_target_pairs={{0,2},{1,3},{2,4},{3,5},{4,6},{5,7},{6,0},{7,1},{8,10},{9,11},{10,... | collective-permute-start | bytes 147464 | tf_op jit(solution)/shard_map/ppermute | solution.py:61
  103.8 6.9 %collective-permute-start.33 = (bf16[64,384]{1,0:T(8,128)(2,1)S(1)}, bf16[64,384]{1,0:T(8,128)(2,1)S(1)}, u32[]{:S(2)}, u32[]{:S(2)}) collective-permute-start(bf16[64,384]{1,0:T(8,128)(2,1)S(1)} %get-tuple-element.40), channel_id=1, source_target_pairs={{0,3},{1,4},{2,5},{3,6},{4,7},{5,0},{6,1},{7,2},{8,11},{9,12},{10,... | collective-permute-start | bytes 147464 | tf_op jit(solution)/shard_map/ppermute | solution.py:61
  104.2 7.6 %collective-permute-start.34 = (bf16[64,384]{1,0:T(8,128)(2,1)S(1)}, bf16[64,384]{1,0:T(8,128)(2,1)S(1)}, u32[]{:S(2)}, u32[]{:S(2)}) collective-permute-start(bf16[64,384]{1,0:T(8,128)(2,1)S(1)} %get-tuple-element.39), channel_id=1, source_target_pairs={{0,4},{1,5},{2,6},{3,7},{4,0},{5,1},{6,2},{7,3},{8,12},{9,13},{10,... | collective-permute-start | bytes 147464 | tf_op jit(solution)/shard_map/ppermute | solution.py:61
  106.5 5.3 %collective-permute-start.35 = (bf16[64,384]{1,0:T(8,128)(2,1)S(1)}, bf16[64,384]{1,0:T(8,128)(2,1)S(1)}, u32[]{:S(2)}, u32[]{:S(2)}) collective-permute-start(bf16[64,384]{1,0:T(8,128)(2,1)S(1)} %get-tuple-element.38), channel_id=1, source_target_pairs={{0,5},{1,6},{2,7},{3,0},{4,1},{5,2},{6,3},{7,4},{8,13},{9,14},{10,... | collective-permute-start | bytes 147464 | tf_op jit(solution)/shard_map/ppermute | solution.py:61
  107.0 5.8 %collective-permute-start.36 = (bf16[64,384]{1,0:T(8,128)(2,1)S(1)}, bf16[64,384]{1,0:T(8,128)(2,1)S(1)}, u32[]{:S(2)}, u32[]{:S(2)}) collective-permute-start(bf16[64,384]{1,0:T(8,128)(2,1)S(1)} %get-tuple-element.37), channel_id=1, source_target_pairs={{0,6},{1,7},{2,0},{3,1},{4,2},{5,3},{6,4},{7,5},{8,14},{9,15},{10,... | collective-permute-start | bytes 147464 | tf_op jit(solution)/shard_map/ppermute | solution.py:61
  113.2 5.7 %collective-permute-start.38 = (f32[64,384]{1,0:T(8,128)S(1)}, f32[64,384]{1,0:T(8,128)S(1)}, u32[]{:S(2)}, u32[]{:S(2)}) collective-permute-start(f32[64,384]{1,0:T(8,128)S(1)} %convert_reduce_fusion), channel_id=1, source_target_pairs={{0,8},{8,0},{16,24},{24,16},{1,9},{9,1},{17,25},{25,17},{2,10},{10... | collective-permute-start | bytes 294920 | tf_op jit(solution)/shard_map/ppermute | solution.py:44
  113.8 6.8 %collective-permute-start.39 = (f32[64,384]{1,0:T(8,128)S(1)}, f32[64,384]{1,0:T(8,128)S(1)}, u32[]{:S(2)}, u32[]{:S(2)}) collective-permute-start(f32[64,384]{1,0:T(8,128)S(1)} %convert_reduce_fusion), channel_id=1, source_target_pairs={{0,16},{8,24},{16,0},{24,8},{1,17},{9,25},{17,1},{25,9},{2,18},{10... | collective-permute-start | bytes 294920 | tf_op jit(solution)/shard_map/ppermute | solution.py:44
  114.3 6.3 %collective-permute-start.40 = (f32[64,384]{1,0:T(8,128)S(1)}, f32[64,384]{1,0:T(8,128)S(1)}, u32[]{:S(2)}, u32[]{:S(2)}) collective-permute-start(f32[64,384]{1,0:T(8,128)S(1)} %convert_reduce_fusion), channel_id=1, source_target_pairs={{0,24},{8,16},{16,8},{24,0},{1,25},{9,17},{17,9},{25,1},{2,26},{10... | collective-permute-start | bytes 294920 | tf_op jit(solution)/shard_map/ppermute | solution.py:44
  (12 other events, 111.9 us)

commit v12 on v7

--- a/solution.py
+++ b/solution.py
@@ -35,10 +35,19 @@
     return jnp.roll(stack[::-1], lax.axis_index(axis) + 1, axis=0)
 
 
-def gather_ordered(value, axis, native):
+def gather_ordered(value, axis, native, two_rounds=False):
     size = lax.axis_size(axis)
     if native or size > FAN_OUT_MAX:
         return lax.all_gather(value, axis)
+    if two_rounds and size > 2 and size & (size - 1) == 0:
+        sibling = lax.ppermute(value, axis, [(source, source ^ 1) for source in range(size)])
+        pair = jnp.stack([value, sibling])
+        pieces = [value, sibling]
+        for mask in range(2, size, 2):
+            arrived = lax.ppermute(pair, axis, [(source, source ^ mask) for source in range(size)])
+            pieces += [arrived[0], arrived[1]]
+        order = jnp.bitwise_xor(lax.axis_index(axis), jnp.arange(size))
+        return jnp.take(jnp.stack(pieces), order, axis=0)
     pieces = [value] + [
         lax.ppermute(value, axis, shift_pairs(size, shift)) for shift in range(1, size)
     ]
@@ -216,7 +225,7 @@
     ref_stats = vocab_stats(ref_group, out_embed, target_local)
     prx_stats = vocab_stats(prx_group, out_embed, target_local)
 
-    all_stats = gather_ordered(jnp.concatenate([ref_stats, prx_stats]), "fsdp", False)
+    all_stats = gather_ordered(jnp.concatenate([ref_stats, prx_stats]), "fsdp", False, True)
     tops = all_stats[:, 0::3]
     exp_totals = all_stats[:, 1::3]
     picks = all_stats[:, 2::3]

time: 121 us -> 123 us (1.017)
  waiting for transfers between devices: 24.2 us -> 27.6 us
  starting transfers between devices: 50.9 us -> 48.6 us
    ppermute x20 -> x13, starting transfers between devices: 24.7 us -> 15.7 us  [gather_ordered(): lax.ppermute(value, axis, shift_pairs(size, shift))]
    ppermute x0 -> x4, waiting for transfers between devices: none -> 6.17 us  [the longest x3 5.32 us: gather_ordered(): lax.ppermute(pair, axis, [(source, source ^ mask) for source in range(siz...]
    ppermute x0 -> x4, starting transfers between devices: none -> 5.34 us  [the longest x3 4.79 us: gather_ordered(): lax.ppermute(pair, axis, [(source, source ^ mask) for source in range(siz...]
    ppermute x20 -> x13, waiting for transfers between devices: 14 us -> 12.6 us  [gather_ordered(): lax.ppermute(value, axis, shift_pairs(size, shift))]
    ppermute x21, starting transfers between devices: 26.2 us -> 27.6 us  [exchange_ordered(): lax.ppermute(lax.dynamic_index_in_dim(blocks, (here + shift) % size, keep...]
    ppermute x21, waiting for transfers between devices: 10.1 us -> 8.86 us  [exchange_ordered(): lax.ppermute(lax.dynamic_index_in_dim(blocks, (here + shift) % size, keep...]
    unnamed x37 -> x41, local copies, waits for them, and re-layouts: 4.61 us -> 4.63 us
  transfers between devices with their start and end apart: 41 -> 38, of which waited for: 18 -> 18; matrix products, arithmetic and copies ran while one was open for 1% -> 1% of each run, Pallas kernels for 0% -> 0%
where the time goes in v12:
time: 123 us; the launch traced here: 122 us
  starting transfers between devices  48.6 us (40%)
  waiting for transfers between devices  27.6 us (22%)
  blocking collectives  17.3 us (14%)
  other arithmetic  9.57 us (8%)
  matrix products  8.91 us (7%)
  local copies, waits for them, and re-layouts  8.19 us (7%)
  between operations  2.05 us (2%)
    ppermute x21, starting transfers between devices, exchange_ordered(): lax.ppermute(lax.dynamic_index_in_dim(blocks, (here + shift) % size, keep...  27.6 us
    all_gather x1, blocking collectives, gather_ordered(): return lax.all_gather(value, axis)  17.3 us
    ppermute x13, starting transfers between devices, gather_ordered(): lax.ppermute(value, axis, shift_pairs(size, shift))  15.7 us
    ppermute x13, waiting for transfers between devices, gather_ordered(): lax.ppermute(value, axis, shift_pairs(size, shift))  12.6 us
    ppermute x21, waiting for transfers between devices, exchange_ordered(): lax.ppermute(lax.dynamic_index_in_dim(blocks, (here + shift) % size, keep...  8.86 us
    ppermute x3, waiting for transfers between devices, gather_ordered(): lax.ppermute(pair, axis, [(source, source ^ mask) for source in range(siz...  5.32 us
    ppermute x3, starting transfers between devices, gather_ordered(): lax.ppermute(pair, axis, [(source, source ^ mask) for source in range(siz...  4.79 us
    unnamed x41, local copies, waits for them, and re-layouts  4.63 us
  transfers between devices with their start and end apart: 38, of which 18 were waited for; matrix products, arithmetic and copies ran while one was open for 1% of the time, Pallas kernels for 0%

profile of v12, /device:TPU:0, one launch (start us, length us, event | category | flops | bytes accessed | tf_op | source)
XLA Modules:
  0.0 122.2 jit_solution(6324570471833201547)
XLA Ops:
  7.2 17.3 %all-gather.1 = bf16[8,389,128]{2,1,0:T(8,128)(2,1)S(1)} all-gather(bf16[1,389,128]{2,1,0:T(8,128)(2,1)S(1)} %bitcast.220), channel_id=2, replica_groups=mesh['dp'=4,'fsdp'=8] {'fsdp'}, dimensions={0}, use_global_device_ids=true | all-gather | bytes 896256 | tf_op jit(solution)/shard_map/all_gather | solution.py:41
  24.5 1.8 %fusion.3 = bf16[1024,128]{1,0:T(8,128)(2,1)S(1)} fusion(bf16[1024,128]{1,0:T(8,128)(2,1)} %param.19, s32[1024]{0:T(1024)S(1)} %bitcast.242), kind=kOutput, calls=%fused_computation.12 | convolution fusion | flops 269615104 | bytes 528384 | tf_op jit(solution)/shard_map/dot_general | solution.py:209
  26.8 1.6 %collective-permute-start.1 = (bf16[128,128]{1,0:T(8,128)(2,1)S(1)}, bf16[128,128]{1,0:T(8,128)(2,1)S(1)}, u32[]{:S(2)}, u32[]{:S(2)}) collective-permute-start(bf16[128,128]{1,0:T(8,128)(2,1)S(1)} %get-tuple-element.47), channel_id=1, source_target_pairs={{0,2},{1,3},{2,4},{3,5},{4,6},{5,7},{6,0},{7,1},{8,10},{9,11},{10,... | collective-permute-start | bytes 98312 | tf_op jit(solution)/shard_map/ppermute | solution.py:63
  28.4 2.1 %collective-permute-start.2 = (bf16[128,128]{1,0:T(8,128)(2,1)S(1)}, bf16[128,128]{1,0:T(8,128)(2,1)S(1)}, u32[]{:S(2)}, u32[]{:S(2)}) collective-permute-start(bf16[128,128]{1,0:T(8,128)(2,1)S(1)} %get-tuple-element.46), channel_id=1, source_target_pairs={{0,3},{1,4},{2,5},{3,6},{4,7},{5,0},{6,1},{7,2},{8,11},{9,12},{10,... | collective-permute-start | bytes 98312 | tf_op jit(solution)/shard_map/ppermute | solution.py:63
  36.2 2.0 %collective-permute-done.5 = bf16[128,128]{1,0:T(8,128)(2,1)S(1)} collective-permute-done((bf16[128,128]{1,0:T(8,128)(2,1)S(1)}, bf16[128,128]{1,0:T(8,128)(2,1)S(1)}, u32[]{:S(2)}, u32[]{:S(2)}) %collective-permute-start.5) | collective-permute-done | bytes 32800 | tf_op jit(solution)/shard_map/ppermute | solution.py:63
  41.5 2.0 %collective-permute-start.9 = (bf16[128,256]{0,1:T(8,128)(2,1)S(1)}, bf16[128,256]{0,1:T(8,128)(2,1)S(1)}, u32[]{:S(2)}, u32[]{:S(2)}) collective-permute-start(bf16[128,256]{0,1:T(8,128)(2,1)S(1)} %pad_maximum_fusion.2), channel_id=1, source_target_pairs={{0,3},{1,4},{2,5},{3,6},{4,7},{5,0},{6,1},{7,2},{8,11},{9,12},{10,... | collective-permute-start | bytes 196616 | tf_op jit(solution)/shard_map/ppermute | solution.py:52
  43.5 1.5 %collective-permute-start.10 = (bf16[128,256]{0,1:T(8,128)(2,1)S(1)}, bf16[128,256]{0,1:T(8,128)(2,1)S(1)}, u32[]{:S(2)}, u32[]{:S(2)}) collective-permute-start(bf16[128,256]{0,1:T(8,128)(2,1)S(1)} %pad_maximum_fusion.2), channel_id=1, source_target_pairs={{0,4},{1,5},{2,6},{3,7},{4,0},{5,1},{6,2},{7,3},{8,12},{9,13},{10,... | collective-permute-start | bytes 196616 | tf_op jit(solution)/shard_map/ppermute | solution.py:52
  46.3 1.5 %collective-permute-start.12 = (bf16[128,256]{0,1:T(8,128)(2,1)S(1)}, bf16[128,256]{0,1:T(8,128)(2,1)S(1)}, u32[]{:S(2)}, u32[]{:S(2)}) collective-permute-start(bf16[128,256]{0,1:T(8,128)(2,1)S(1)} %pad_maximum_fusion.2), channel_id=1, source_target_pairs={{0,6},{1,7},{2,0},{3,1},{4,2},{5,3},{6,4},{7,5},{8,14},{9,15},{10,... | collective-permute-start | bytes 196616 | tf_op jit(solution)/shard_map/ppermute | solution.py:52
  48.1 3.9 %collective-permute-done.9 = bf16[128,256]{0,1:T(8,128)(2,1)S(1)} collective-permute-done((bf16[128,256]{0,1:T(8,128)(2,1)S(1)}, bf16[128,256]{0,1:T(8,128)(2,1)S(1)}, u32[]{:S(2)}, u32[]{:S(2)}) %collective-permute-start.9) | collective-permute-done | bytes 65568 | tf_op jit(solution)/shard_map/ppermute | solution.py:52
  52.3 1.6 %collective-permute-done.12 = bf16[128,256]{0,1:T(8,128)(2,1)S(1)} collective-permute-done((bf16[128,256]{0,1:T(8,128)(2,1)S(1)}, bf16[128,256]{0,1:T(8,128)(2,1)S(1)}, u32[]{:S(2)}, u32[]{:S(2)}) %collective-permute-start.12) | collective-permute-done | bytes 65568 | tf_op jit(solution)/shard_map/ppermute | solution.py:52
  55.9 2.0 %select_reduce_fusion = (f32[1024]{0:T(1024)S(1)}, f32[1024]{0:T(1024)S(1)}, f32[1024]{0:T(1024)S(1)}, f32[1024]{0:T(1024)S(1)}) fusion(f32[1024,1024]{0,1:T(8,128)S(1)} %get-tuple-element.74, s32[1024]{0:T(1024)S(1)} %bitcast.239, f32[1024]{0:T(1024)S(1)} %get-tuple-element.73, f32[1024,1024]{0,1:T(8,128)S(1)} %get-tuple-element.72, ...), kind=kLoop, calls=%fused_computation.3 | loop fusion | flops 9433088 | bytes 8417280 | tf_op jit(solution)/shard_map/reduce_sum | solution.py:100
  59.4 2.3 %collective-permute-start.15 = (f32[2,6,1024]{2,1,0:T(8,128)S(1)}, f32[2,6,1024]{2,1,0:T(8,128)S(1)}, u32[]{:S(2)}, u32[]{:S(2)}) collective-permute-start(f32[2,6,1024]{2,1,0:T(8,128)S(1)} %pad_maximum_fusion.3), channel_id=1, source_target_pairs={{0,2},{1,3},{2,0},{3,1},{4,6},{5,7},{6,4},{7,5},{8,10},{9,11},{10,... | collective-permute-start | bytes 147464 | tf_op jit(solution)/shard_map/ppermute | solution.py:47
  61.7 1.4 %collective-permute-start.16 = (f32[2,6,1024]{2,1,0:T(8,128)S(1)}, f32[2,6,1024]{2,1,0:T(8,128)S(1)}, u32[]{:S(2)}, u32[]{:S(2)}) collective-permute-start(f32[2,6,1024]{2,1,0:T(8,128)S(1)} %pad_maximum_fusion.3), channel_id=1, source_target_pairs={{0,4},{1,5},{2,6},{3,7},{4,0},{5,1},{6,2},{7,3},{8,12},{9,13},{10,... | collective-permute-start | bytes 147464 | tf_op jit(solution)/shard_map/ppermute | solution.py:47
  64.4 5.1 %collective-permute-done.16 = f32[2,6,1024]{2,1,0:T(8,128)S(1)} collective-permute-done((f32[2,6,1024]{2,1,0:T(8,128)S(1)}, f32[2,6,1024]{2,1,0:T(8,128)S(1)}, u32[]{:S(2)}, u32[]{:S(2)}) %collective-permute-start.16) | collective-permute-done | bytes 49184 | tf_op jit(solution)/shard_map/ppermute | solution.py:47
  71.0 1.5 %collective-permute-start.18 = (f32[2,22]{1,0:T(2,128)S(1)}, f32[2,22]{1,0:T(2,128)S(1)}, u32[]{:S(2)}, u32[]{:S(2)}) collective-permute-start(f32[2,22]{1,0:T(2,128)S(1)} %get-tuple-element.60), channel_id=1, source_target_pairs={{0,8},{8,16},{16,24},{24,0},{1,9},{9,17},{17,25},{25,1},{2,10},{10... | collective-permute-start | bytes 536 | tf_op jit(solution)/shard_map/ppermute | solution.py:52
  72.6 1.5 %collective-permute-start.19 = (f32[2,22]{1,0:T(2,128)S(1)}, f32[2,22]{1,0:T(2,128)S(1)}, u32[]{:S(2)}, u32[]{:S(2)}) collective-permute-start(f32[2,22]{1,0:T(2,128)S(1)} %get-tuple-element.60), channel_id=1, source_target_pairs={{0,16},{8,24},{16,0},{24,8},{1,17},{9,25},{17,1},{25,9},{2,18},{10... | collective-permute-start | bytes 536 | tf_op jit(solution)/shard_map/ppermute | solution.py:52
  74.1 1.4 %collective-permute-start.20 = (f32[2,22]{1,0:T(2,128)S(1)}, f32[2,22]{1,0:T(2,128)S(1)}, u32[]{:S(2)}, u32[]{:S(2)}) collective-permute-start(f32[2,22]{1,0:T(2,128)S(1)} %get-tuple-element.60), channel_id=1, source_target_pairs={{0,24},{8,0},{16,8},{24,16},{1,25},{9,1},{17,9},{25,17},{2,26},{10... | collective-permute-start | bytes 536 | tf_op jit(solution)/shard_map/ppermute | solution.py:52
  76.2 1.5 %collective-permute-done.20 = f32[2,22]{1,0:T(2,128)S(1)} collective-permute-done((f32[2,22]{1,0:T(2,128)S(1)}, f32[2,22]{1,0:T(2,128)S(1)}, u32[]{:S(2)}, u32[]{:S(2)}) %collective-permute-start.20) | collective-permute-done | bytes 208 | tf_op jit(solution)/shard_map/ppermute | solution.py:52
  79.6 1.8 %bitcast_divide_fusion = (f32[22]{0:T(128)S(1)}, f32[22]{0:T(128)}) fusion(f32[2,22]{1,0:T(2,128)S(1)} %fusion.34, f32[]{:T(128)} %fusion.43, f32[22]{0:T(128)S(1)} %get-tuple-element.17, f32[]{:T(128)} %get-tuple-element.16), kind=kLoop, calls=%fused_computation.184 | loop fusion | flops 132 | bytes 360 | tf_op jit(solution)/shard_map/div | solution.py:252
  82.1 3.5 %fusion.2 = f32[1024,128]{1,0:T(8,128)S(1)} fusion(bf16[1024,128]{1,0:T(8,128)(2,1)S(1)} %copy-done, f32[1024,1024]{0,1:T(8,128)} %copy-done.1, f32[1024]{0:T(1024)S(1)} %bitcast.243, f32[1024]{0:T(1024)S(1)} %broadcast_bitcast_fusion, s32[1024]{0:T(1024)S(1)} %bitcast.240), kind=kOutput, calls=%fused_computation.11 | convolution fusion | flops 274726912 | bytes 4993024 | tf_op jit(solution)/shard_map/dot_general | solution.py:122
  85.8 1.9 %collective-permute-start.22 = (f32[128,128]{1,0:T(8,128)S(1)}, f32[128,128]{1,0:T(8,128)S(1)}, u32[]{:S(2)}, u32[]{:S(2)}) collective-permute-start(f32[128,128]{1,0:T(8,128)S(1)} %get-tuple-element.31), channel_id=1, source_target_pairs={{0,2},{1,3},{2,4},{3,5},{4,6},{5,7},{6,0},{7,1},{8,10},{9,11},{10,... | collective-permute-start | bytes 196616 | tf_op jit(solution)/shard_map/ppermute | solution.py:63
  87.8 3.6 %collective-permute-start.24 = (f32[128,128]{1,0:T(8,128)S(1)}, f32[128,128]{1,0:T(8,128)S(1)}, u32[]{:S(2)}, u32[]{:S(2)}) collective-permute-start(f32[128,128]{1,0:T(8,128)S(1)} %get-tuple-element.29), channel_id=1, source_target_pairs={{0,4},{1,5},{2,6},{3,7},{4,0},{5,1},{6,2},{7,3},{8,12},{9,13},{10,... | collective-permute-start | bytes 196616 | tf_op jit(solution)/shard_map/ppermute | solution.py:63
  91.4 2.1 %collective-permute-start.26 = (f32[128,128]{1,0:T(8,128)S(1)}, f32[128,128]{1,0:T(8,128)S(1)}, u32[]{:S(2)}, u32[]{:S(2)}) collective-permute-start(f32[128,128]{1,0:T(8,128)S(1)} %get-tuple-element.27), channel_id=1, source_target_pairs={{0,6},{1,7},{2,0},{3,1},{4,2},{5,3},{6,4},{7,5},{8,14},{9,15},{10,... | collective-permute-start | bytes 196616 | tf_op jit(solution)/shard_map/ppermute | solution.py:63
  94.3 3.2 %collective-permute-done.23 = f32[128,128]{1,0:T(8,128)S(1)} collective-permute-done((f32[128,128]{1,0:T(8,128)S(1)}, f32[128,128]{1,0:T(8,128)S(1)}, u32[]{:S(2)}, u32[]{:S(2)}) %collective-permute-start.23) | collective-permute-done | bytes 65568 | tf_op jit(solution)/shard_map/ppermute | solution.py:63
  99.5 1.8 %collective-permute-start.28 = (bf16[64,384]{1,0:T(8,128)(2,1)S(1)}, bf16[64,384]{1,0:T(8,128)(2,1)S(1)}, u32[]{:S(2)}, u32[]{:S(2)}) collective-permute-start(bf16[64,384]{1,0:T(8,128)(2,1)S(1)} %get-tuple-element.40), channel_id=1, source_target_pairs={{0,1},{1,2},{2,3},{3,4},{4,5},{5,6},{6,7},{7,0},{8,9},{9,10},{10,1... | collective-permute-start | bytes 147464 | tf_op jit(solution)/shard_map/ppermute | solution.py:63
  101.3 2.5 %collective-permute-start.29 = (bf16[64,384]{1,0:T(8,128)(2,1)S(1)}, bf16[64,384]{1,0:T(8,128)(2,1)S(1)}, u32[]{:S(2)}, u32[]{:S(2)}) collective-permute-start(bf16[64,384]{1,0:T(8,128)(2,1)S(1)} %get-tuple-element.39), channel_id=1, source_target_pairs={{0,2},{1,3},{2,4},{3,5},{4,6},{5,7},{6,0},{7,1},{8,10},{9,11},{10,... | collective-permute-start | bytes 147464 | tf_op jit(solution)/shard_map/ppermute | solution.py:63
  104.2 2.4 %collective-permute-start.31 = (bf16[64,384]{1,0:T(8,128)(2,1)S(1)}, bf16[64,384]{1,0:T(8,128)(2,1)S(1)}, u32[]{:S(2)}, u32[]{:S(2)}) collective-permute-start(bf16[64,384]{1,0:T(8,128)(2,1)S(1)} %get-tuple-element.37), channel_id=1, source_target_pairs={{0,4},{1,5},{2,6},{3,7},{4,0},{5,1},{6,2},{7,3},{8,12},{9,13},{10,... | collective-permute-start | bytes 147464 | tf_op jit(solution)/shard_map/ppermute | solution.py:63
  107.1 1.6 %collective-permute-start.33 = (bf16[64,384]{1,0:T(8,128)(2,1)S(1)}, bf16[64,384]{1,0:T(8,128)(2,1)S(1)}, u32[]{:S(2)}, u32[]{:S(2)}) collective-permute-start(bf16[64,384]{1,0:T(8,128)(2,1)S(1)} %get-tuple-element.35), channel_id=1, source_target_pairs={{0,6},{1,7},{2,0},{3,1},{4,2},{5,3},{6,4},{7,5},{8,14},{9,15},{10,... | collective-permute-start | bytes 147464 | tf_op jit(solution)/shard_map/ppermute | solution.py:63
  113.4 1.4 %collective-permute-start.35 = (f32[64,384]{1,0:T(8,128)S(1)}, f32[64,384]{1,0:T(8,128)S(1)}, u32[]{:S(2)}, u32[]{:S(2)}) collective-permute-start(f32[64,384]{1,0:T(8,128)S(1)} %convert_reduce_fusion), channel_id=1, source_target_pairs={{0,8},{8,16},{16,24},{24,0},{1,9},{9,17},{17,25},{25,1},{2,10},{10... | collective-permute-start | bytes 294920 | tf_op jit(solution)/shard_map/ppermute | solution.py:52
  114.8 1.5 %collective-permute-start.36 = (f32[64,384]{1,0:T(8,128)S(1)}, f32[64,384]{1,0:T(8,128)S(1)}, u32[]{:S(2)}, u32[]{:S(2)}) collective-permute-start(f32[64,384]{1,0:T(8,128)S(1)} %convert_reduce_fusion), channel_id=1, source_target_pairs={{0,16},{8,24},{16,0},{24,8},{1,17},{9,25},{17,1},{25,9},{2,18},{10... | collective-permute-start | bytes 294920 | tf_op jit(solution)/shard_map/ppermute | solution.py:52
  116.8 3.1 %collective-permute-done.35 = f32[64,384]{1,0:T(8,128)S(1)} collective-permute-done((f32[64,384]{1,0:T(8,128)S(1)}, f32[64,384]{1,0:T(8,128)S(1)}, u32[]{:S(2)}, u32[]{:S(2)}) %collective-permute-start.35) | collective-permute-done | bytes 98336 | tf_op jit(solution)/shard_map/ppermute | solution.py:52
  119.9 1.5 %collective-permute-done.36 = f32[64,384]{1,0:T(8,128)S(1)} collective-permute-done((f32[64,384]{1,0:T(8,128)S(1)}, f32[64,384]{1,0:T(8,128)S(1)}, u32[]{:S(2)}, u32[]{:S(2)}) %collective-permute-start.36) | collective-permute-done | bytes 98336 | tf_op jit(solution)/shard_map/ppermute | solution.py:52
  (179 shorter events, 36.0 us)
Async XLA Ops:
  26.3 7.9 %collective-permute-start = (bf16[128,128]{1,0:T(8,128)(2,1)S(1)}, bf16[128,128]{1,0:T(8,128)(2,1)S(1)}, u32[]{:S(2)}, u32[]{:S(2)}) collective-permute-start(bf16[128,128]{1,0:T(8,128)(2,1)S(1)} %get-tuple-element.48), channel_id=1, source_target_pairs={{0,1},{1,2},{2,3},{3,4},{4,5},{5,6},{6,7},{7,0},{8,9},{9,10},{10,1... | collective-permute-start | bytes 98312 | tf_op jit(solution)/shard_map/ppermute | solution.py:63
  26.8 8.2 %collective-permute-start.1 = (bf16[128,128]{1,0:T(8,128)(2,1)S(1)}, bf16[128,128]{1,0:T(8,128)(2,1)S(1)}, u32[]{:S(2)}, u32[]{:S(2)}) collective-permute-start(bf16[128,128]{1,0:T(8,128)(2,1)S(1)} %get-tuple-element.47), channel_id=1, source_target_pairs={{0,2},{1,3},{2,4},{3,5},{4,6},{5,7},{6,0},{7,1},{8,10},{9,11},{10,... | collective-permute-start | bytes 98312 | tf_op jit(solution)/shard_map/ppermute | solution.py:63
  28.4 7.4 %collective-permute-start.2 = (bf16[128,128]{1,0:T(8,128)(2,1)S(1)}, bf16[128,128]{1,0:T(8,128)(2,1)S(1)}, u32[]{:S(2)}, u32[]{:S(2)}) collective-permute-start(bf16[128,128]{1,0:T(8,128)(2,1)S(1)} %get-tuple-element.46), channel_id=1, source_target_pairs={{0,3},{1,4},{2,5},{3,6},{4,7},{5,0},{6,1},{7,2},{8,11},{9,12},{10,... | collective-permute-start | bytes 98312 | tf_op jit(solution)/shard_map/ppermute | solution.py:63
  30.5 5.6 %collective-permute-start.3 = (bf16[128,128]{1,0:T(8,128)(2,1)S(1)}, bf16[128,128]{1,0:T(8,128)(2,1)S(1)}, u32[]{:S(2)}, u32[]{:S(2)}) collective-permute-start(bf16[128,128]{1,0:T(8,128)(2,1)S(1)} %get-tuple-element.45), channel_id=1, source_target_pairs={{0,4},{1,5},{2,6},{3,7},{4,0},{5,1},{6,2},{7,3},{8,12},{9,13},{10,... | collective-permute-start | bytes 98312 | tf_op jit(solution)/shard_map/ppermute | solution.py:63
  40.2 6.0 %collective-permute-start.7 = (bf16[128,256]{0,1:T(8,128)(2,1)S(1)}, bf16[128,256]{0,1:T(8,128)(2,1)S(1)}, u32[]{:S(2)}, u32[]{:S(2)}) collective-permute-start(bf16[128,256]{0,1:T(8,128)(2,1)S(1)} %pad_maximum_fusion.2), channel_id=1, source_target_pairs={{0,1},{1,2},{2,3},{3,4},{4,5},{5,6},{6,7},{7,0},{8,9},{9,10},{10,1... | collective-permute-start | bytes 196616 | tf_op jit(solution)/shard_map/ppermute | solution.py:52
  41.2 6.7 %collective-permute-start.8 = (bf16[128,256]{0,1:T(8,128)(2,1)S(1)}, bf16[128,256]{0,1:T(8,128)(2,1)S(1)}, u32[]{:S(2)}, u32[]{:S(2)}) collective-permute-start(bf16[128,256]{0,1:T(8,128)(2,1)S(1)} %pad_maximum_fusion.2), channel_id=1, source_target_pairs={{0,2},{1,3},{2,4},{3,5},{4,6},{5,7},{6,0},{7,1},{8,10},{9,11},{10,... | collective-permute-start | bytes 196616 | tf_op jit(solution)/shard_map/ppermute | solution.py:52
  41.5 10.5 %collective-permute-start.9 = (bf16[128,256]{0,1:T(8,128)(2,1)S(1)}, bf16[128,256]{0,1:T(8,128)(2,1)S(1)}, u32[]{:S(2)}, u32[]{:S(2)}) collective-permute-start(bf16[128,256]{0,1:T(8,128)(2,1)S(1)} %pad_maximum_fusion.2), channel_id=1, source_target_pairs={{0,3},{1,4},{2,5},{3,6},{4,7},{5,0},{6,1},{7,2},{8,11},{9,12},{10,... | collective-permute-start | bytes 196616 | tf_op jit(solution)/shard_map/ppermute | solution.py:52
  43.5 8.7 %collective-permute-start.10 = (bf16[128,256]{0,1:T(8,128)(2,1)S(1)}, bf16[128,256]{0,1:T(8,128)(2,1)S(1)}, u32[]{:S(2)}, u32[]{:S(2)}) collective-permute-start(bf16[128,256]{0,1:T(8,128)(2,1)S(1)} %pad_maximum_fusion.2), channel_id=1, source_target_pairs={{0,4},{1,5},{2,6},{3,7},{4,0},{5,1},{6,2},{7,3},{8,12},{9,13},{10,... | collective-permute-start | bytes 196616 | tf_op jit(solution)/shard_map/ppermute | solution.py:52
  45.0 7.3 %collective-permute-start.11 = (bf16[128,256]{0,1:T(8,128)(2,1)S(1)}, bf16[128,256]{0,1:T(8,128)(2,1)S(1)}, u32[]{:S(2)}, u32[]{:S(2)}) collective-permute-start(bf16[128,256]{0,1:T(8,128)(2,1)S(1)} %pad_maximum_fusion.2), channel_id=1, source_target_pairs={{0,5},{1,6},{2,7},{3,0},{4,1},{5,2},{6,3},{7,4},{8,13},{9,14},{10,... | collective-permute-start | bytes 196616 | tf_op jit(solution)/shard_map/ppermute | solution.py:52
  46.3 7.6 %collective-permute-start.12 = (bf16[128,256]{0,1:T(8,128)(2,1)S(1)}, bf16[128,256]{0,1:T(8,128)(2,1)S(1)}, u32[]{:S(2)}, u32[]{:S(2)}) collective-permute-start(bf16[128,256]{0,1:T(8,128)(2,1)S(1)} %pad_maximum_fusion.2), channel_id=1, source_target_pairs={{0,6},{1,7},{2,0},{3,1},{4,2},{5,3},{6,4},{7,5},{8,14},{9,15},{10,... | collective-permute-start | bytes 196616 | tf_op jit(solution)/shard_map/ppermute | solution.py:52
  47.9 6.0 %collective-permute-start.13 = (bf16[128,256]{0,1:T(8,128)(2,1)S(1)}, bf16[128,256]{0,1:T(8,128)(2,1)S(1)}, u32[]{:S(2)}, u32[]{:S(2)}) collective-permute-start(bf16[128,256]{0,1:T(8,128)(2,1)S(1)} %pad_maximum_fusion.2), channel_id=1, source_target_pairs={{0,7},{1,0},{2,1},{3,2},{4,3},{5,4},{6,5},{7,6},{8,15},{9,8},{10,9... | collective-permute-start | bytes 196616 | tf_op jit(solution)/shard_map/ppermute | solution.py:52
  59.4 5.0 %collective-permute-start.15 = (f32[2,6,1024]{2,1,0:T(8,128)S(1)}, f32[2,6,1024]{2,1,0:T(8,128)S(1)}, u32[]{:S(2)}, u32[]{:S(2)}) collective-permute-start(f32[2,6,1024]{2,1,0:T(8,128)S(1)} %pad_maximum_fusion.3), channel_id=1, source_target_pairs={{0,2},{1,3},{2,0},{3,1},{4,6},{5,7},{6,4},{7,5},{8,10},{9,11},{10,... | collective-permute-start | bytes 147464 | tf_op jit(solution)/shard_map/ppermute | solution.py:47
  61.7 7.8 %collective-permute-start.16 = (f32[2,6,1024]{2,1,0:T(8,128)S(1)}, f32[2,6,1024]{2,1,0:T(8,128)S(1)}, u32[]{:S(2)}, u32[]{:S(2)}) collective-permute-start(f32[2,6,1024]{2,1,0:T(8,128)S(1)} %pad_maximum_fusion.3), channel_id=1, source_target_pairs={{0,4},{1,5},{2,6},{3,7},{4,0},{5,1},{6,2},{7,3},{8,12},{9,13},{10,... | collective-permute-start | bytes 147464 | tf_op jit(solution)/shard_map/ppermute | solution.py:47
  63.2 6.4 %collective-permute-start.17 = (f32[2,6,1024]{2,1,0:T(8,128)S(1)}, f32[2,6,1024]{2,1,0:T(8,128)S(1)}, u32[]{:S(2)}, u32[]{:S(2)}) collective-permute-start(f32[2,6,1024]{2,1,0:T(8,128)S(1)} %pad_maximum_fusion.3), channel_id=1, source_target_pairs={{0,6},{1,7},{2,4},{3,5},{4,2},{5,3},{6,0},{7,1},{8,14},{9,15},{10,... | collective-permute-start | bytes 147464 | tf_op jit(solution)/shard_map/ppermute | solution.py:47
  71.0 4.5 %collective-permute-start.18 = (f32[2,22]{1,0:T(2,128)S(1)}, f32[2,22]{1,0:T(2,128)S(1)}, u32[]{:S(2)}, u32[]{:S(2)}) collective-permute-start(f32[2,22]{1,0:T(2,128)S(1)} %get-tuple-element.60), channel_id=1, source_target_pairs={{0,8},{8,16},{16,24},{24,0},{1,9},{9,17},{17,25},{25,1},{2,10},{10... | collective-permute-start | bytes 536 | tf_op jit(solution)/shard_map/ppermute | solution.py:52
  85.7 5.7 %collective-permute-start.21 = (f32[128,128]{1,0:T(8,128)S(1)}, f32[128,128]{1,0:T(8,128)S(1)}, u32[]{:S(2)}, u32[]{:S(2)}) collective-permute-start(f32[128,128]{1,0:T(8,128)S(1)} %get-tuple-element.32), channel_id=1, source_target_pairs={{0,1},{1,2},{2,3},{3,4},{4,5},{5,6},{6,7},{7,0},{8,9},{9,10},{10,1... | collective-permute-start | bytes 196616 | tf_op jit(solution)/shard_map/ppermute | solution.py:63
  85.8 7.8 %collective-permute-start.22 = (f32[128,128]{1,0:T(8,128)S(1)}, f32[128,128]{1,0:T(8,128)S(1)}, u32[]{:S(2)}, u32[]{:S(2)}) collective-permute-start(f32[128,128]{1,0:T(8,128)S(1)} %get-tuple-element.31), channel_id=1, source_target_pairs={{0,2},{1,3},{2,4},{3,5},{4,6},{5,7},{6,0},{7,1},{8,10},{9,11},{10,... | collective-permute-start | bytes 196616 | tf_op jit(solution)/shard_map/ppermute | solution.py:63
  87.7 9.8 %collective-permute-start.23 = (f32[128,128]{1,0:T(8,128)S(1)}, f32[128,128]{1,0:T(8,128)S(1)}, u32[]{:S(2)}, u32[]{:S(2)}) collective-permute-start(f32[128,128]{1,0:T(8,128)S(1)} %get-tuple-element.30), channel_id=1, source_target_pairs={{0,3},{1,4},{2,5},{3,6},{4,7},{5,0},{6,1},{7,2},{8,11},{9,12},{10,... | collective-permute-start | bytes 196616 | tf_op jit(solution)/shard_map/ppermute | solution.py:63
  87.8 10.0 %collective-permute-start.24 = (f32[128,128]{1,0:T(8,128)S(1)}, f32[128,128]{1,0:T(8,128)S(1)}, u32[]{:S(2)}, u32[]{:S(2)}) collective-permute-start(f32[128,128]{1,0:T(8,128)S(1)} %get-tuple-element.29), channel_id=1, source_target_pairs={{0,4},{1,5},{2,6},{3,7},{4,0},{5,1},{6,2},{7,3},{8,12},{9,13},{10,... | collective-permute-start | bytes 196616 | tf_op jit(solution)/shard_map/ppermute | solution.py:63
  91.4 6.4 %collective-permute-start.25 = (f32[128,128]{1,0:T(8,128)S(1)}, f32[128,128]{1,0:T(8,128)S(1)}, u32[]{:S(2)}, u32[]{:S(2)}) collective-permute-start(f32[128,128]{1,0:T(8,128)S(1)} %get-tuple-element.28), channel_id=1, source_target_pairs={{0,5},{1,6},{2,7},{3,0},{4,1},{5,2},{6,3},{7,4},{8,13},{9,14},{10,... | collective-permute-start | bytes 196616 | tf_op jit(solution)/shard_map/ppermute | solution.py:63
  91.4 6.4 %collective-permute-start.26 = (f32[128,128]{1,0:T(8,128)S(1)}, f32[128,128]{1,0:T(8,128)S(1)}, u32[]{:S(2)}, u32[]{:S(2)}) collective-permute-start(f32[128,128]{1,0:T(8,128)S(1)} %get-tuple-element.27), channel_id=1, source_target_pairs={{0,6},{1,7},{2,0},{3,1},{4,2},{5,3},{6,4},{7,5},{8,14},{9,15},{10,... | collective-permute-start | bytes 196616 | tf_op jit(solution)/shard_map/ppermute | solution.py:63
  93.5 4.4 %collective-permute-start.27 = (f32[128,128]{1,0:T(8,128)S(1)}, f32[128,128]{1,0:T(8,128)S(1)}, u32[]{:S(2)}, u32[]{:S(2)}) collective-permute-start(f32[128,128]{1,0:T(8,128)S(1)} %get-tuple-element.26), channel_id=1, source_target_pairs={{0,7},{1,0},{2,1},{3,2},{4,3},{5,4},{6,5},{7,6},{8,15},{9,8},{10,9... | collective-permute-start | bytes 196616 | tf_op jit(solution)/shard_map/ppermute | solution.py:63
  99.5 7.6 %collective-permute-start.28 = (bf16[64,384]{1,0:T(8,128)(2,1)S(1)}, bf16[64,384]{1,0:T(8,128)(2,1)S(1)}, u32[]{:S(2)}, u32[]{:S(2)}) collective-permute-start(bf16[64,384]{1,0:T(8,128)(2,1)S(1)} %get-tuple-element.40), channel_id=1, source_target_pairs={{0,1},{1,2},{2,3},{3,4},{4,5},{5,6},{6,7},{7,0},{8,9},{9,10},{10,1... | collective-permute-start | bytes 147464 | tf_op jit(solution)/shard_map/ppermute | solution.py:63
  101.3 7.4 %collective-permute-start.29 = (bf16[64,384]{1,0:T(8,128)(2,1)S(1)}, bf16[64,384]{1,0:T(8,128)(2,1)S(1)}, u32[]{:S(2)}, u32[]{:S(2)}) collective-permute-start(bf16[64,384]{1,0:T(8,128)(2,1)S(1)} %get-tuple-element.39), channel_id=1, source_target_pairs={{0,2},{1,3},{2,4},{3,5},{4,6},{5,7},{6,0},{7,1},{8,10},{9,11},{10,... | collective-permute-start | bytes 147464 | tf_op jit(solution)/shard_map/ppermute | solution.py:63
  103.8 7.5 %collective-permute-start.30 = (bf16[64,384]{1,0:T(8,128)(2,1)S(1)}, bf16[64,384]{1,0:T(8,128)(2,1)S(1)}, u32[]{:S(2)}, u32[]{:S(2)}) collective-permute-start(bf16[64,384]{1,0:T(8,128)(2,1)S(1)} %get-tuple-element.38), channel_id=1, source_target_pairs={{0,3},{1,4},{2,5},{3,6},{4,7},{5,0},{6,1},{7,2},{8,11},{9,12},{10,... | collective-permute-start | bytes 147464 | tf_op jit(solution)/shard_map/ppermute | solution.py:63
  104.2 7.6 %collective-permute-start.31 = (bf16[64,384]{1,0:T(8,128)(2,1)S(1)}, bf16[64,384]{1,0:T(8,128)(2,1)S(1)}, u32[]{:S(2)}, u32[]{:S(2)}) collective-permute-start(bf16[64,384]{1,0:T(8,128)(2,1)S(1)} %get-tuple-element.37), channel_id=1, source_target_pairs={{0,4},{1,5},{2,6},{3,7},{4,0},{5,1},{6,2},{7,3},{8,12},{9,13},{10,... | collective-permute-start | bytes 147464 | tf_op jit(solution)/shard_map/ppermute | solution.py:63
  106.6 5.2 %collective-permute-start.32 = (bf16[64,384]{1,0:T(8,128)(2,1)S(1)}, bf16[64,384]{1,0:T(8,128)(2,1)S(1)}, u32[]{:S(2)}, u32[]{:S(2)}) collective-permute-start(bf16[64,384]{1,0:T(8,128)(2,1)S(1)} %get-tuple-element.36), channel_id=1, source_target_pairs={{0,5},{1,6},{2,7},{3,0},{4,1},{5,2},{6,3},{7,4},{8,13},{9,14},{10,... | collective-permute-start | bytes 147464 | tf_op jit(solution)/shard_map/ppermute | solution.py:63
  107.1 6.0 %collective-permute-start.33 = (bf16[64,384]{1,0:T(8,128)(2,1)S(1)}, bf16[64,384]{1,0:T(8,128)(2,1)S(1)}, u32[]{:S(2)}, u32[]{:S(2)}) collective-permute-start(bf16[64,384]{1,0:T(8,128)(2,1)S(1)} %get-tuple-element.35), channel_id=1, source_target_pairs={{0,6},{1,7},{2,0},{3,1},{4,2},{5,3},{6,4},{7,5},{8,14},{9,15},{10,... | collective-permute-start | bytes 147464 | tf_op jit(solution)/shard_map/ppermute | solution.py:63
  108.7 4.3 %collective-permute-start.34 = (bf16[64,384]{1,0:T(8,128)(2,1)S(1)}, bf16[64,384]{1,0:T(8,128)(2,1)S(1)}, u32[]{:S(2)}, u32[]{:S(2)}) collective-permute-start(bf16[64,384]{1,0:T(8,128)(2,1)S(1)} %get-tuple-element.34), channel_id=1, source_target_pairs={{0,7},{1,0},{2,1},{3,2},{4,3},{5,4},{6,5},{7,6},{8,15},{9,8},{10,9... | collective-permute-start | bytes 147464 | tf_op jit(solution)/shard_map/ppermute | solution.py:63
  113.4 6.6 %collective-permute-start.35 = (f32[64,384]{1,0:T(8,128)S(1)}, f32[64,384]{1,0:T(8,128)S(1)}, u32[]{:S(2)}, u32[]{:S(2)}) collective-permute-start(f32[64,384]{1,0:T(8,128)S(1)} %convert_reduce_fusion), channel_id=1, source_target_pairs={{0,8},{8,16},{16,24},{24,0},{1,9},{9,17},{17,25},{25,1},{2,10},{10... | collective-permute-start | bytes 294920 | tf_op jit(solution)/shard_map/ppermute | solution.py:52
  114.8 6.7 %collective-permute-start.36 = (f32[64,384]{1,0:T(8,128)S(1)}, f32[64,384]{1,0:T(8,128)S(1)}, u32[]{:S(2)}, u32[]{:S(2)}) collective-permute-start(f32[64,384]{1,0:T(8,128)S(1)} %convert_reduce_fusion), channel_id=1, source_target_pairs={{0,16},{8,24},{16,0},{24,8},{1,17},{9,25},{17,1},{25,9},{2,18},{10... | collective-permute-start | bytes 294920 | tf_op jit(solution)/shard_map/ppermute | solution.py:52
  116.3 5.1 %collective-permute-start.37 = (f32[64,384]{1,0:T(8,128)S(1)}, f32[64,384]{1,0:T(8,128)S(1)}, u32[]{:S(2)}, u32[]{:S(2)}) collective-permute-start(f32[64,384]{1,0:T(8,128)S(1)} %convert_reduce_fusion), channel_id=1, source_target_pairs={{0,24},{8,0},{16,8},{24,16},{1,25},{9,1},{17,9},{25,17},{2,26},{10... | collective-permute-start | bytes 294920 | tf_op jit(solution)/shard_map/ppermute | solution.py:52
  (9 other events, 97.8 us)

commit v13 on v7

--- a/solution.py
+++ b/solution.py
@@ -88,7 +88,11 @@
         logits = contract_last(block_in, table)
         top_logit = jnp.max(logits, axis=1)
         exp_total = jnp.sum(jnp.exp(logits - top_logit[:, None]), axis=1)
-        picked = jnp.sum(jnp.where(block_target[:, None] == columns[None, :], logits, 0.0), axis=1)
+        inside = (block_target >= 0) & (block_target < table.shape[0])
+        clipped = jnp.clip(block_target, 0, table.shape[0] - 1)
+        picked = jnp.where(
+            inside, jnp.take_along_axis(logits, clipped[:, None], axis=1)[:, 0], 0.0
+        )
         return jnp.stack([top_logit, exp_total, picked])
 
     if rows == total:

time: 121 us -> 243 us (2.01); the launches traced: 121 us -> 240 us
  local copies, waits for them, and re-layouts: 7.88 us -> 91.2 us
  waiting for transfers between devices: 24.2 us -> 70.8 us
  starting transfers between devices: 50.9 us -> 36.1 us
    gather x0 -> x2, local copies, waits for them, and re-layouts: none -> 83.5 us  [one_block(): jnp.take_along_axis(logits, clipped[:, None], axis=1)[:, 0]]
    ppermute x21, waiting for transfers between devices: 10.1 us -> 34.3 us  [exchange_ordered(): lax.ppermute(lax.dynamic_index_in_dim(blocks, (here + shift) % size, keep...]
    ppermute x20, waiting for transfers between devices: 14 us -> 36.4 us  [gather_ordered(): lax.ppermute(value, axis, shift_pairs(size, shift))]
    ppermute x20, starting transfers between devices: 24.7 us -> 15.6 us  [gather_ordered(): lax.ppermute(value, axis, shift_pairs(size, shift))]
    ppermute x21, starting transfers between devices: 26.2 us -> 20.5 us  [exchange_ordered(): lax.ppermute(lax.dynamic_index_in_dim(blocks, (here + shift) % size, keep...]
  transfers between devices with their start and end apart: 41 -> 41, of which waited for: 18 -> 17; matrix products, arithmetic and copies ran while one was open for 1% -> 0% of each run, Pallas kernels for 0% -> 0%
where the time goes in v13:
time: 243 us; the launch traced here: 240 us
  local copies, waits for them, and re-layouts  91.2 us (38%)
  waiting for transfers between devices  70.8 us (29%)
  starting transfers between devices  36.1 us (15%)
  blocking collectives  17.3 us (7%)
  matrix products  11.3 us (5%)
  other arithmetic  10.9 us (4%)
    gather x2, local copies, waits for them, and re-layouts, one_block(): jnp.take_along_axis(logits, clipped[:, None], axis=1)[:, 0]  83.5 us
    ppermute x20, waiting for transfers between devices, gather_ordered(): lax.ppermute(value, axis, shift_pairs(size, shift))  36.4 us
    ppermute x21, waiting for transfers between devices, exchange_ordered(): lax.ppermute(lax.dynamic_index_in_dim(blocks, (here + shift) % size, keep...  34.3 us
    ppermute x21, starting transfers between devices, exchange_ordered(): lax.ppermute(lax.dynamic_index_in_dim(blocks, (here + shift) % size, keep...  20.5 us
    all_gather x1, blocking collectives, gather_ordered(): return lax.all_gather(value, axis)  17.3 us
    ppermute x20, starting transfers between devices, gather_ordered(): lax.ppermute(value, axis, shift_pairs(size, shift))  15.6 us
  transfers between devices with their start and end apart: 41, of which 17 were waited for; matrix products, arithmetic and copies ran while one was open for 0% of the time, Pallas kernels for 0%

profile of v13, /device:TPU:0, one launch (start us, length us, event | category | flops | bytes accessed | tf_op | source)
XLA Modules:
  0.0 239.7 jit_solution(14417934373637831212)
XLA Ops:
  7.2 17.3 %all-gather.1 = bf16[8,389,128]{2,1,0:T(8,128)(2,1)S(1)} all-gather(bf16[1,389,128]{2,1,0:T(8,128)(2,1)S(1)} %bitcast.258), channel_id=2, replica_groups=mesh['dp'=4,'fsdp'=8] {'fsdp'}, dimensions={0}, use_global_device_ids=true | all-gather | bytes 896256 | tf_op jit(solution)/shard_map/all_gather | solution.py:41
  24.5 1.8 fusion.3
  26.3 3.6 %collective-permute-start.6 = (bf16[128,128]{1,0:T(8,128)(2,1)S(1)}, bf16[128,128]{1,0:T(8,128)(2,1)S(1)}, u32[]{:S(2)}, u32[]{:S(2)}) collective-permute-start(bf16[128,128]{1,0:T(8,128)(2,1)S(1)} %get-tuple-element.39), channel_id=1, source_target_pairs={{0,7},{1,0},{2,1},{3,2},{4,3},{5,4},{6,5},{7,6},{8,15},{9,8},{10,9... | collective-permute-start | bytes 98312 | tf_op jit(solution)/shard_map/ppermute | solution.py:54
  30.0 2.7 %collective-permute-start.3 = (bf16[128,128]{1,0:T(8,128)(2,1)S(1)}, bf16[128,128]{1,0:T(8,128)(2,1)S(1)}, u32[]{:S(2)}, u32[]{:S(2)}) collective-permute-start(bf16[128,128]{1,0:T(8,128)(2,1)S(1)} %get-tuple-element.42), channel_id=1, source_target_pairs={{0,4},{1,5},{2,6},{3,7},{4,0},{5,1},{6,2},{7,3},{8,12},{9,13},{10,... | collective-permute-start | bytes 98312 | tf_op jit(solution)/shard_map/ppermute | solution.py:54
  34.1 3.7 %collective-permute-done = bf16[128,128]{1,0:T(8,128)(2,1)S(1)} collective-permute-done((bf16[128,128]{1,0:T(8,128)(2,1)S(1)}, bf16[128,128]{1,0:T(8,128)(2,1)S(1)}, u32[]{:S(2)}, u32[]{:S(2)}) %collective-permute-start) | collective-permute-done | bytes 32800 | tf_op jit(solution)/shard_map/ppermute | solution.py:54
  37.8 5.7 %collective-permute-done.1 = bf16[128,128]{1,0:T(8,128)(2,1)S(1)} collective-permute-done((bf16[128,128]{1,0:T(8,128)(2,1)S(1)}, bf16[128,128]{1,0:T(8,128)(2,1)S(1)}, u32[]{:S(2)}, u32[]{:S(2)}) %collective-permute-start.1) | collective-permute-done | bytes 32800 | tf_op jit(solution)/shard_map/ppermute | solution.py:54
  43.5 4.2 %collective-permute-done.2 = bf16[128,128]{1,0:T(8,128)(2,1)S(1)} collective-permute-done((bf16[128,128]{1,0:T(8,128)(2,1)S(1)}, bf16[128,128]{1,0:T(8,128)(2,1)S(1)}, u32[]{:S(2)}, u32[]{:S(2)}) %collective-permute-start.2) | collective-permute-done | bytes 32800 | tf_op jit(solution)/shard_map/ppermute | solution.py:54
  53.3 4.7 %collective-permute-done.7 = bf16[128,256]{0,1:T(8,128)(2,1)S(1)} collective-permute-done((bf16[128,256]{0,1:T(8,128)(2,1)S(1)}, bf16[128,256]{0,1:T(8,128)(2,1)S(1)}, u32[]{:S(2)}, u32[]{:S(2)}) %collective-permute-start.7) | collective-permute-done | bytes 65568 | tf_op jit(solution)/shard_map/ppermute | solution.py:43
  58.5 6.0 %collective-permute-done.8 = bf16[128,256]{0,1:T(8,128)(2,1)S(1)} collective-permute-done((bf16[128,256]{0,1:T(8,128)(2,1)S(1)}, bf16[128,256]{0,1:T(8,128)(2,1)S(1)}, u32[]{:S(2)}, u32[]{:S(2)}) %collective-permute-start.8) | collective-permute-done | bytes 65568 | tf_op jit(solution)/shard_map/ppermute | solution.py:43
  64.7 1.8 collective-permute-done.13
  67.7 3.1 %fusion.56 = (f32[1024]{0:T(1024)S(1)}, f32[1024,1024]{0,1:T(8,128)}) fusion(bf16[1024,128]{1,0:T(8,128)(2,1)S(1)} %copy-done, bf16[1024,256]{1,0:T(8,128)(2,1)S(1)} %bitcast.249), kind=kOutput, calls=%fused_computation.219 | convolution fusion | flops 269483008 | bytes 4722688 | tf_op jit(solution)/shard_map/dot_general | solution.py:19
  71.4 41.7 %gather_fusion.2 = f32[1024]{0:T(1024)S(1)} fusion(f32[1024,1024]{0,1:T(8,128)} %copy-done.1, s32[1024]{0:T(1024)S(1)} %bitcast.246), kind=kCustom, calls=%fused_computation.1.clone | custom fusion | bytes 16384 | tf_op jit(solution)/shard_map/jit(take_along_axis)/gather | solution.py:94
  113.1 41.8 %gather_fusion.1 = f32[1024]{0:T(1024)S(1)} fusion(f32[1024,1024]{0,1:T(8,128)} %get-tuple-element.69, s32[1024]{0:T(1024)S(1)} %bitcast.247), kind=kCustom, calls=%fused_computation.clone | custom fusion | bytes 16384 | tf_op jit(solution)/shard_map/jit(take_along_axis)/gather | solution.py:94
  155.0 2.8 %exponential_reduce_fusion.1 = f32[1024]{0:T(1024)S(1)} fusion(f32[1024,1024]{0,1:T(8,128)} %get-tuple-element.69, f32[1024]{0:T(1024)S(1)} %get-tuple-element.68), kind=kLoop, calls=%fused_computation.6 | loop fusion | flops 2096128 | bytes 4202496 | tf_op jit(solution)/shard_map/reduce_sum | solution.py:90
  158.1 2.9 %collective-permute-start.17 = (f32[6,1024]{1,0:T(8,128)S(1)}, f32[6,1024]{1,0:T(8,128)S(1)}, u32[]{:S(2)}, u32[]{:S(2)}) collective-permute-start(f32[6,1024]{1,0:T(8,128)S(1)} %concatenate.52), channel_id=1, source_target_pairs={{0,4},{1,5},{2,6},{3,7},{4,0},{5,1},{6,2},{7,3},{8,12},{9,13},{10,... | collective-permute-start | bytes 73736 | tf_op jit(solution)/shard_map/ppermute | solution.py:43
  161.3 4.8 %collective-permute-done.14 = f32[6,1024]{1,0:T(8,128)S(1)} collective-permute-done((f32[6,1024]{1,0:T(8,128)S(1)}, f32[6,1024]{1,0:T(8,128)S(1)}, u32[]{:S(2)}, u32[]{:S(2)}) %collective-permute-start.14) | collective-permute-done | bytes 24608 | tf_op jit(solution)/shard_map/ppermute | solution.py:43
  166.1 5.7 %collective-permute-done.15 = f32[6,1024]{1,0:T(8,128)S(1)} collective-permute-done((f32[6,1024]{1,0:T(8,128)S(1)}, f32[6,1024]{1,0:T(8,128)S(1)}, u32[]{:S(2)}, u32[]{:S(2)}) %collective-permute-start.15) | collective-permute-done | bytes 24608 | tf_op jit(solution)/shard_map/ppermute | solution.py:43
  171.8 4.2 %collective-permute-done.16 = f32[6,1024]{1,0:T(8,128)S(1)} collective-permute-done((f32[6,1024]{1,0:T(8,128)S(1)}, f32[6,1024]{1,0:T(8,128)S(1)}, u32[]{:S(2)}, u32[]{:S(2)}) %collective-permute-start.16) | collective-permute-done | bytes 24608 | tf_op jit(solution)/shard_map/ppermute | solution.py:43
  177.1 2.9 %collective-permute-start.22 = (f32[2,22]{1,0:T(2,128)S(1)}, f32[2,22]{1,0:T(2,128)S(1)}, u32[]{:S(2)}, u32[]{:S(2)}) collective-permute-start(f32[2,22]{1,0:T(2,128)S(1)} %get-tuple-element.57), channel_id=1, source_target_pairs={{0,16},{8,24},{16,0},{24,8},{1,17},{9,25},{17,1},{25,9},{2,18},{10... | collective-permute-start | bytes 536 | tf_op jit(solution)/shard_map/ppermute | solution.py:43
  180.0 2.6 %collective-permute-start.21 = (f32[2,22]{1,0:T(2,128)S(1)}, f32[2,22]{1,0:T(2,128)S(1)}, u32[]{:S(2)}, u32[]{:S(2)}) collective-permute-start(f32[2,22]{1,0:T(2,128)S(1)} %get-tuple-element.57), channel_id=1, source_target_pairs={{0,8},{8,16},{16,24},{24,0},{1,9},{9,17},{17,25},{25,1},{2,10},{10... | collective-permute-start | bytes 536 | tf_op jit(solution)/shard_map/ppermute | solution.py:43
  184.5 1.7 collective-permute-done.23
  188.1 1.8 bitcast_divide_fusion
  190.6 3.5 %fusion.2 = f32[1024,128]{1,0:T(8,128)S(1)} fusion(bf16[1024,128]{1,0:T(8,128)(2,1)S(1)} %copy-done, f32[1024,1024]{0,1:T(8,128)} %copy-done.1, s32[1024]{0:T(1024)S(1)} %bitcast.273, f32[1024]{0:T(1024)S(1)} %bitcast.279, f32[1024]{0:T(1024)S(1)} %broadcast_bitcast_fusion), kind=kOutput, calls=%fused_computation.10 | convolution fusion | flops 274726912 | bytes 4993024 | tf_op jit(solution)/shard_map/dot_general | solution.py:117
  194.2 3.5 %collective-permute-start.30 = (f32[128,128]{1,0:T(8,128)S(1)}, f32[128,128]{1,0:T(8,128)S(1)}, u32[]{:S(2)}, u32[]{:S(2)}) collective-permute-start(f32[128,128]{1,0:T(8,128)S(1)} %get-tuple-element.23), channel_id=1, source_target_pairs={{0,7},{1,0},{2,1},{3,2},{4,3},{5,4},{6,5},{7,6},{8,15},{9,8},{10,9... | collective-permute-start | bytes 196616 | tf_op jit(solution)/shard_map/ppermute | solution.py:54
  197.8 2.7 %collective-permute-start.27 = (f32[128,128]{1,0:T(8,128)S(1)}, f32[128,128]{1,0:T(8,128)S(1)}, u32[]{:S(2)}, u32[]{:S(2)}) collective-permute-start(f32[128,128]{1,0:T(8,128)S(1)} %get-tuple-element.26), channel_id=1, source_target_pairs={{0,4},{1,5},{2,6},{3,7},{4,0},{5,1},{6,2},{7,3},{8,12},{9,13},{10,... | collective-permute-start | bytes 196616 | tf_op jit(solution)/shard_map/ppermute | solution.py:54
  200.5 6.5 %collective-permute-done.25 = f32[128,128]{1,0:T(8,128)S(1)} collective-permute-done((f32[128,128]{1,0:T(8,128)S(1)}, f32[128,128]{1,0:T(8,128)S(1)}, u32[]{:S(2)}, u32[]{:S(2)}) %collective-permute-start.25) | collective-permute-done | bytes 65568 | tf_op jit(solution)/shard_map/ppermute | solution.py:54
  207.2 4.4 %collective-permute-done.26 = f32[128,128]{1,0:T(8,128)S(1)} collective-permute-done((f32[128,128]{1,0:T(8,128)S(1)}, f32[128,128]{1,0:T(8,128)S(1)}, u32[]{:S(2)}, u32[]{:S(2)}) %collective-permute-start.26) | collective-permute-done | bytes 65568 | tf_op jit(solution)/shard_map/ppermute | solution.py:54
  214.6 2.2 collective-permute-start.37
  220.4 5.3 %collective-permute-done.32 = bf16[64,384]{1,0:T(8,128)(2,1)S(1)} collective-permute-done((bf16[64,384]{1,0:T(8,128)(2,1)S(1)}, bf16[64,384]{1,0:T(8,128)(2,1)S(1)}, u32[]{:S(2)}, u32[]{:S(2)}) %collective-permute-start.32) | collective-permute-done | bytes 49184 | tf_op jit(solution)/shard_map/ppermute | solution.py:54
  225.7 4.4 %collective-permute-done.33 = bf16[64,384]{1,0:T(8,128)(2,1)S(1)} collective-permute-done((bf16[64,384]{1,0:T(8,128)(2,1)S(1)}, bf16[64,384]{1,0:T(8,128)(2,1)S(1)}, u32[]{:S(2)}, u32[]{:S(2)}) %collective-permute-start.33) | collective-permute-done | bytes 49184 | tf_op jit(solution)/shard_map/ppermute | solution.py:54
  232.9 2.9 %collective-permute-done.40 = f32[64,384]{1,0:T(8,128)S(1)} collective-permute-done((f32[64,384]{1,0:T(8,128)S(1)}, f32[64,384]{1,0:T(8,128)S(1)}, u32[]{:S(2)}, u32[]{:S(2)}) %collective-permute-start.40) | collective-permute-done | bytes 98336 | tf_op jit(solution)/shard_map/ppermute | solution.py:43
  235.9 3.1 %collective-permute-done.39 = f32[64,384]{1,0:T(8,128)S(1)} collective-permute-done((f32[64,384]{1,0:T(8,128)S(1)}, f32[64,384]{1,0:T(8,128)S(1)}, u32[]{:S(2)}, u32[]{:S(2)}) %collective-permute-start.39) | collective-permute-done | bytes 98336 | tf_op jit(solution)/shard_map/ppermute | solution.py:43
  (192 shorter events, 31.5 us)
Async XLA Ops:
  26.3 21.5 %collective-permute-start.6 = (bf16[128,128]{1,0:T(8,128)(2,1)S(1)}, bf16[128,128]{1,0:T(8,128)(2,1)S(1)}, u32[]{:S(2)}, u32[]{:S(2)}) collective-permute-start(bf16[128,128]{1,0:T(8,128)(2,1)S(1)} %get-tuple-element.39), channel_id=1, source_target_pairs={{0,7},{1,0},{2,1},{3,2},{4,3},{5,4},{6,5},{7,6},{8,15},{9,8},{10,9... | collective-permute-start | bytes 98312 | tf_op jit(solution)/shard_map/ppermute | solution.py:54
  29.9 17.9 %collective-permute-start.5 = (bf16[128,128]{1,0:T(8,128)(2,1)S(1)}, bf16[128,128]{1,0:T(8,128)(2,1)S(1)}, u32[]{:S(2)}, u32[]{:S(2)}) collective-permute-start(bf16[128,128]{1,0:T(8,128)(2,1)S(1)} %get-tuple-element.40), channel_id=1, source_target_pairs={{0,6},{1,7},{2,0},{3,1},{4,2},{5,3},{6,4},{7,5},{8,14},{9,15},{10,... | collective-permute-start | bytes 98312 | tf_op jit(solution)/shard_map/ppermute | solution.py:54
  30.0 17.8 %collective-permute-start.4 = (bf16[128,128]{1,0:T(8,128)(2,1)S(1)}, bf16[128,128]{1,0:T(8,128)(2,1)S(1)}, u32[]{:S(2)}, u32[]{:S(2)}) collective-permute-start(bf16[128,128]{1,0:T(8,128)(2,1)S(1)} %get-tuple-element.41), channel_id=1, source_target_pairs={{0,5},{1,6},{2,7},{3,0},{4,1},{5,2},{6,3},{7,4},{8,13},{9,14},{10,... | collective-permute-start | bytes 98312 | tf_op jit(solution)/shard_map/ppermute | solution.py:54
  30.0 17.8 %collective-permute-start.3 = (bf16[128,128]{1,0:T(8,128)(2,1)S(1)}, bf16[128,128]{1,0:T(8,128)(2,1)S(1)}, u32[]{:S(2)}, u32[]{:S(2)}) collective-permute-start(bf16[128,128]{1,0:T(8,128)(2,1)S(1)} %get-tuple-element.42), channel_id=1, source_target_pairs={{0,4},{1,5},{2,6},{3,7},{4,0},{5,1},{6,2},{7,3},{8,12},{9,13},{10,... | collective-permute-start | bytes 98312 | tf_op jit(solution)/shard_map/ppermute | solution.py:54
  37.8 5.7 %collective-permute-start.1 = (bf16[128,128]{1,0:T(8,128)(2,1)S(1)}, bf16[128,128]{1,0:T(8,128)(2,1)S(1)}, u32[]{:S(2)}, u32[]{:S(2)}) collective-permute-start(bf16[128,128]{1,0:T(8,128)(2,1)S(1)} %get-tuple-element.44), channel_id=1, source_target_pairs={{0,2},{1,3},{2,4},{3,5},{4,6},{5,7},{6,0},{7,1},{8,10},{9,11},{10,... | collective-permute-start | bytes 98312 | tf_op jit(solution)/shard_map/ppermute | solution.py:54
  49.9 14.8 %collective-permute-start.12 = (bf16[128,256]{0,1:T(8,128)(2,1)S(1)}, bf16[128,256]{0,1:T(8,128)(2,1)S(1)}, u32[]{:S(2)}, u32[]{:S(2)}) collective-permute-start(bf16[128,256]{0,1:T(8,128)(2,1)S(1)} %pad_maximum_fusion.2), channel_id=1, source_target_pairs={{0,6},{1,7},{2,0},{3,1},{4,2},{5,3},{6,4},{7,5},{8,14},{9,15},{10,... | collective-permute-start | bytes 196616 | tf_op jit(solution)/shard_map/ppermute | solution.py:43
  49.9 14.7 %collective-permute-start.11 = (bf16[128,256]{0,1:T(8,128)(2,1)S(1)}, bf16[128,256]{0,1:T(8,128)(2,1)S(1)}, u32[]{:S(2)}, u32[]{:S(2)}) collective-permute-start(bf16[128,256]{0,1:T(8,128)(2,1)S(1)} %pad_maximum_fusion.2), channel_id=1, source_target_pairs={{0,5},{1,6},{2,7},{3,0},{4,1},{5,2},{6,3},{7,4},{8,13},{9,14},{10,... | collective-permute-start | bytes 196616 | tf_op jit(solution)/shard_map/ppermute | solution.py:43
  50.2 14.4 %collective-permute-start.10 = (bf16[128,256]{0,1:T(8,128)(2,1)S(1)}, bf16[128,256]{0,1:T(8,128)(2,1)S(1)}, u32[]{:S(2)}, u32[]{:S(2)}) collective-permute-start(bf16[128,256]{0,1:T(8,128)(2,1)S(1)} %pad_maximum_fusion.2), channel_id=1, source_target_pairs={{0,4},{1,5},{2,6},{3,7},{4,0},{5,1},{6,2},{7,3},{8,12},{9,13},{10,... | collective-permute-start | bytes 196616 | tf_op jit(solution)/shard_map/ppermute | solution.py:43
  50.2 14.4 %collective-permute-start.9 = (bf16[128,256]{0,1:T(8,128)(2,1)S(1)}, bf16[128,256]{0,1:T(8,128)(2,1)S(1)}, u32[]{:S(2)}, u32[]{:S(2)}) collective-permute-start(bf16[128,256]{0,1:T(8,128)(2,1)S(1)} %pad_maximum_fusion.2), channel_id=1, source_target_pairs={{0,3},{1,4},{2,5},{3,6},{4,7},{5,0},{6,1},{7,2},{8,11},{9,12},{10,... | collective-permute-start | bytes 196616 | tf_op jit(solution)/shard_map/ppermute | solution.py:43
  51.7 6.2 %collective-permute-start.7 = (bf16[128,256]{0,1:T(8,128)(2,1)S(1)}, bf16[128,256]{0,1:T(8,128)(2,1)S(1)}, u32[]{:S(2)}, u32[]{:S(2)}) collective-permute-start(bf16[128,256]{0,1:T(8,128)(2,1)S(1)} %pad_maximum_fusion.2), channel_id=1, source_target_pairs={{0,1},{1,2},{2,3},{3,4},{4,5},{5,6},{6,7},{7,0},{8,9},{9,10},{10,1... | collective-permute-start | bytes 196616 | tf_op jit(solution)/shard_map/ppermute | solution.py:43
  58.0 6.6 %collective-permute-start.8 = (bf16[128,256]{0,1:T(8,128)(2,1)S(1)}, bf16[128,256]{0,1:T(8,128)(2,1)S(1)}, u32[]{:S(2)}, u32[]{:S(2)}) collective-permute-start(bf16[128,256]{0,1:T(8,128)(2,1)S(1)} %pad_maximum_fusion.2), channel_id=1, source_target_pairs={{0,2},{1,3},{2,4},{3,5},{4,6},{5,7},{6,0},{7,1},{8,10},{9,11},{10,... | collective-permute-start | bytes 196616 | tf_op jit(solution)/shard_map/ppermute | solution.py:43
  157.9 18.3 %collective-permute-start.20 = (f32[6,1024]{1,0:T(8,128)S(1)}, f32[6,1024]{1,0:T(8,128)S(1)}, u32[]{:S(2)}, u32[]{:S(2)}) collective-permute-start(f32[6,1024]{1,0:T(8,128)S(1)} %concatenate.52), channel_id=1, source_target_pairs={{0,7},{1,0},{2,1},{3,2},{4,3},{5,4},{6,5},{7,6},{8,15},{9,8},{10,9... | collective-permute-start | bytes 73736 | tf_op jit(solution)/shard_map/ppermute | solution.py:43
  157.9 18.2 %collective-permute-start.19 = (f32[6,1024]{1,0:T(8,128)S(1)}, f32[6,1024]{1,0:T(8,128)S(1)}, u32[]{:S(2)}, u32[]{:S(2)}) collective-permute-start(f32[6,1024]{1,0:T(8,128)S(1)} %concatenate.52), channel_id=1, source_target_pairs={{0,6},{1,7},{2,0},{3,1},{4,2},{5,3},{6,4},{7,5},{8,14},{9,15},{10,... | collective-permute-start | bytes 73736 | tf_op jit(solution)/shard_map/ppermute | solution.py:43
  158.0 18.1 %collective-permute-start.18 = (f32[6,1024]{1,0:T(8,128)S(1)}, f32[6,1024]{1,0:T(8,128)S(1)}, u32[]{:S(2)}, u32[]{:S(2)}) collective-permute-start(f32[6,1024]{1,0:T(8,128)S(1)} %concatenate.52), channel_id=1, source_target_pairs={{0,5},{1,6},{2,7},{3,0},{4,1},{5,2},{6,3},{7,4},{8,13},{9,14},{10,... | collective-permute-start | bytes 73736 | tf_op jit(solution)/shard_map/ppermute | solution.py:43
  158.1 18.0 %collective-permute-start.17 = (f32[6,1024]{1,0:T(8,128)S(1)}, f32[6,1024]{1,0:T(8,128)S(1)}, u32[]{:S(2)}, u32[]{:S(2)}) collective-permute-start(f32[6,1024]{1,0:T(8,128)S(1)} %concatenate.52), channel_id=1, source_target_pairs={{0,4},{1,5},{2,6},{3,7},{4,0},{5,1},{6,2},{7,3},{8,12},{9,13},{10,... | collective-permute-start | bytes 73736 | tf_op jit(solution)/shard_map/ppermute | solution.py:43
  166.1 5.7 %collective-permute-start.15 = (f32[6,1024]{1,0:T(8,128)S(1)}, f32[6,1024]{1,0:T(8,128)S(1)}, u32[]{:S(2)}, u32[]{:S(2)}) collective-permute-start(f32[6,1024]{1,0:T(8,128)S(1)} %concatenate.52), channel_id=1, source_target_pairs={{0,2},{1,3},{2,4},{3,5},{4,6},{5,7},{6,0},{7,1},{8,10},{9,11},{10,... | collective-permute-start | bytes 73736 | tf_op jit(solution)/shard_map/ppermute | solution.py:43
  177.1 5.9 %collective-permute-start.22 = (f32[2,22]{1,0:T(2,128)S(1)}, f32[2,22]{1,0:T(2,128)S(1)}, u32[]{:S(2)}, u32[]{:S(2)}) collective-permute-start(f32[2,22]{1,0:T(2,128)S(1)} %get-tuple-element.57), channel_id=1, source_target_pairs={{0,16},{8,24},{16,0},{24,8},{1,17},{9,25},{17,1},{25,9},{2,18},{10... | collective-permute-start | bytes 536 | tf_op jit(solution)/shard_map/ppermute | solution.py:43
  194.2 6.3 %collective-permute-start.24 = (f32[128,128]{1,0:T(8,128)S(1)}, f32[128,128]{1,0:T(8,128)S(1)}, u32[]{:S(2)}, u32[]{:S(2)}) collective-permute-start(f32[128,128]{1,0:T(8,128)S(1)} %get-tuple-element.29), channel_id=1, source_target_pairs={{0,1},{1,2},{2,3},{3,4},{4,5},{5,6},{6,7},{7,0},{8,9},{9,10},{10,1... | collective-permute-start | bytes 196616 | tf_op jit(solution)/shard_map/ppermute | solution.py:54
  194.2 17.4 %collective-permute-start.30 = (f32[128,128]{1,0:T(8,128)S(1)}, f32[128,128]{1,0:T(8,128)S(1)}, u32[]{:S(2)}, u32[]{:S(2)}) collective-permute-start(f32[128,128]{1,0:T(8,128)S(1)} %get-tuple-element.23), channel_id=1, source_target_pairs={{0,7},{1,0},{2,1},{3,2},{4,3},{5,4},{6,5},{7,6},{8,15},{9,8},{10,9... | collective-permute-start | bytes 196616 | tf_op jit(solution)/shard_map/ppermute | solution.py:54
  197.8 13.9 %collective-permute-start.29 = (f32[128,128]{1,0:T(8,128)S(1)}, f32[128,128]{1,0:T(8,128)S(1)}, u32[]{:S(2)}, u32[]{:S(2)}) collective-permute-start(f32[128,128]{1,0:T(8,128)S(1)} %get-tuple-element.24), channel_id=1, source_target_pairs={{0,6},{1,7},{2,0},{3,1},{4,2},{5,3},{6,4},{7,5},{8,14},{9,15},{10,... | collective-permute-start | bytes 196616 | tf_op jit(solution)/shard_map/ppermute | solution.py:54
  197.8 13.8 %collective-permute-start.28 = (f32[128,128]{1,0:T(8,128)S(1)}, f32[128,128]{1,0:T(8,128)S(1)}, u32[]{:S(2)}, u32[]{:S(2)}) collective-permute-start(f32[128,128]{1,0:T(8,128)S(1)} %get-tuple-element.25), channel_id=1, source_target_pairs={{0,5},{1,6},{2,7},{3,0},{4,1},{5,2},{6,3},{7,4},{8,13},{9,14},{10,... | collective-permute-start | bytes 196616 | tf_op jit(solution)/shard_map/ppermute | solution.py:54
  197.8 13.8 %collective-permute-start.27 = (f32[128,128]{1,0:T(8,128)S(1)}, f32[128,128]{1,0:T(8,128)S(1)}, u32[]{:S(2)}, u32[]{:S(2)}) collective-permute-start(f32[128,128]{1,0:T(8,128)S(1)} %get-tuple-element.26), channel_id=1, source_target_pairs={{0,4},{1,5},{2,6},{3,7},{4,0},{5,1},{6,2},{7,3},{8,12},{9,13},{10,... | collective-permute-start | bytes 196616 | tf_op jit(solution)/shard_map/ppermute | solution.py:54
  200.4 6.5 %collective-permute-start.25 = (f32[128,128]{1,0:T(8,128)S(1)}, f32[128,128]{1,0:T(8,128)S(1)}, u32[]{:S(2)}, u32[]{:S(2)}) collective-permute-start(f32[128,128]{1,0:T(8,128)S(1)} %get-tuple-element.28), channel_id=1, source_target_pairs={{0,2},{1,3},{2,4},{3,5},{4,6},{5,7},{6,0},{7,1},{8,10},{9,11},{10,... | collective-permute-start | bytes 196616 | tf_op jit(solution)/shard_map/ppermute | solution.py:54
  213.2 6.3 %collective-permute-start.31 = (bf16[64,384]{1,0:T(8,128)(2,1)S(1)}, bf16[64,384]{1,0:T(8,128)(2,1)S(1)}, u32[]{:S(2)}, u32[]{:S(2)}) collective-permute-start(bf16[64,384]{1,0:T(8,128)(2,1)S(1)} %get-tuple-element.37), channel_id=1, source_target_pairs={{0,1},{1,2},{2,3},{3,4},{4,5},{5,6},{6,7},{7,0},{8,9},{9,10},{10,1... | collective-permute-start | bytes 147464 | tf_op jit(solution)/shard_map/ppermute | solution.py:54
  214.6 15.6 %collective-permute-start.37 = (bf16[64,384]{1,0:T(8,128)(2,1)S(1)}, bf16[64,384]{1,0:T(8,128)(2,1)S(1)}, u32[]{:S(2)}, u32[]{:S(2)}) collective-permute-start(bf16[64,384]{1,0:T(8,128)(2,1)S(1)} %get-tuple-element.31), channel_id=1, source_target_pairs={{0,7},{1,0},{2,1},{3,2},{4,3},{5,4},{6,5},{7,6},{8,15},{9,8},{10,9... | collective-permute-start | bytes 147464 | tf_op jit(solution)/shard_map/ppermute | solution.py:54
  216.8 13.4 %collective-permute-start.36 = (bf16[64,384]{1,0:T(8,128)(2,1)S(1)}, bf16[64,384]{1,0:T(8,128)(2,1)S(1)}, u32[]{:S(2)}, u32[]{:S(2)}) collective-permute-start(bf16[64,384]{1,0:T(8,128)(2,1)S(1)} %get-tuple-element.32), channel_id=1, source_target_pairs={{0,6},{1,7},{2,0},{3,1},{4,2},{5,3},{6,4},{7,5},{8,14},{9,15},{10,... | collective-permute-start | bytes 147464 | tf_op jit(solution)/shard_map/ppermute | solution.py:54
  216.8 13.3 %collective-permute-start.35 = (bf16[64,384]{1,0:T(8,128)(2,1)S(1)}, bf16[64,384]{1,0:T(8,128)(2,1)S(1)}, u32[]{:S(2)}, u32[]{:S(2)}) collective-permute-start(bf16[64,384]{1,0:T(8,128)(2,1)S(1)} %get-tuple-element.33), channel_id=1, source_target_pairs={{0,5},{1,6},{2,7},{3,0},{4,1},{5,2},{6,3},{7,4},{8,13},{9,14},{10,... | collective-permute-start | bytes 147464 | tf_op jit(solution)/shard_map/ppermute | solution.py:54
  218.1 12.1 %collective-permute-start.34 = (bf16[64,384]{1,0:T(8,128)(2,1)S(1)}, bf16[64,384]{1,0:T(8,128)(2,1)S(1)}, u32[]{:S(2)}, u32[]{:S(2)}) collective-permute-start(bf16[64,384]{1,0:T(8,128)(2,1)S(1)} %get-tuple-element.34), channel_id=1, source_target_pairs={{0,4},{1,5},{2,6},{3,7},{4,0},{5,1},{6,2},{7,3},{8,12},{9,13},{10,... | collective-permute-start | bytes 147464 | tf_op jit(solution)/shard_map/ppermute | solution.py:54
  219.5 6.2 %collective-permute-start.32 = (bf16[64,384]{1,0:T(8,128)(2,1)S(1)}, bf16[64,384]{1,0:T(8,128)(2,1)S(1)}, u32[]{:S(2)}, u32[]{:S(2)}) collective-permute-start(bf16[64,384]{1,0:T(8,128)(2,1)S(1)} %get-tuple-element.36), channel_id=1, source_target_pairs={{0,2},{1,3},{2,4},{3,5},{4,6},{5,7},{6,0},{7,1},{8,10},{9,11},{10,... | collective-permute-start | bytes 147464 | tf_op jit(solution)/shard_map/ppermute | solution.py:54
  230.5 5.3 %collective-permute-start.40 = (f32[64,384]{1,0:T(8,128)S(1)}, f32[64,384]{1,0:T(8,128)S(1)}, u32[]{:S(2)}, u32[]{:S(2)}) collective-permute-start(f32[64,384]{1,0:T(8,128)S(1)} %convert_reduce_fusion), channel_id=1, source_target_pairs={{0,24},{8,0},{16,8},{24,16},{1,25},{9,1},{17,9},{25,17},{2,26},{10... | collective-permute-start | bytes 294920 | tf_op jit(solution)/shard_map/ppermute | solution.py:43
  231.8 7.1 %collective-permute-start.39 = (f32[64,384]{1,0:T(8,128)S(1)}, f32[64,384]{1,0:T(8,128)S(1)}, u32[]{:S(2)}, u32[]{:S(2)}) collective-permute-start(f32[64,384]{1,0:T(8,128)S(1)} %convert_reduce_fusion), channel_id=1, source_target_pairs={{0,16},{8,24},{16,0},{24,8},{1,17},{9,25},{17,1},{25,9},{2,18},{10... | collective-permute-start | bytes 294920 | tf_op jit(solution)/shard_map/ppermute | solution.py:43
  232.9 6.0 %collective-permute-start.38 = (f32[64,384]{1,0:T(8,128)S(1)}, f32[64,384]{1,0:T(8,128)S(1)}, u32[]{:S(2)}, u32[]{:S(2)}) collective-permute-start(f32[64,384]{1,0:T(8,128)S(1)} %convert_reduce_fusion), channel_id=1, source_target_pairs={{0,8},{8,16},{16,24},{24,0},{1,9},{9,17},{17,25},{25,1},{2,10},{10... | collective-permute-start | bytes 294920 | tf_op jit(solution)/shard_map/ppermute | solution.py:43
  (12 other events, 139.0 us)

commit v14 on v7

--- a/solution.py
+++ b/solution.py
@@ -58,7 +58,7 @@
         )
         for shift in range(1, size)
     ]
-    return to_absolute(jnp.stack(pieces), axis)
+    return jnp.stack(pieces)
 
 
 def feed_forward(embedded, normed, weights):

time: 121 us -> 121 us (level)
    unnamed x37 -> x39, local copies, waits for them, and re-layouts: 4.61 us -> 5.27 us
where the time goes in v14:
time: 121 us
  starting transfers between devices  50.5 us (42%)
  waiting for transfers between devices  24.6 us (20%)
  blocking collectives  17.3 us (14%)
  other arithmetic  8.94 us (7%)
  matrix products  8.9 us (7%)
  local copies, waits for them, and re-layouts  8.35 us (7%)
  between operations  2.03 us (2%)
    ppermute x21, starting transfers between devices, exchange_ordered(): lax.ppermute(lax.dynamic_index_in_dim(blocks, (here + shift) % size, keep...  25.8 us
    ppermute x20, starting transfers between devices, gather_ordered(): lax.ppermute(value, axis, shift_pairs(size, shift))  24.7 us
    all_gather x1, blocking collectives, gather_ordered(): return lax.all_gather(value, axis)  17.3 us
    ppermute x20, waiting for transfers between devices, gather_ordered(): lax.ppermute(value, axis, shift_pairs(size, shift))  14 us
    ppermute x21, waiting for transfers between devices, exchange_ordered(): lax.ppermute(lax.dynamic_index_in_dim(blocks, (here + shift) % size, keep...  10.5 us
    unnamed x39, local copies, waits for them, and re-layouts  5.27 us
    dot_general x1, matrix products, one_block(): return jnp.dot(d_logits, table, preferred_element_type=jnp.float32)  3.49 us
  transfers between devices with their start and end apart: 41, of which 18 were waited for; matrix products, arithmetic and copies ran while one was open for 1% of the time, Pallas kernels for 0%

profile of v14, /device:TPU:0, one launch (start us, length us, event | category | flops | bytes accessed | tf_op | source)
XLA Modules:
  0.0 120.6 jit_solution(10994364037601334719)
XLA Ops:
  7.2 17.3 %all-gather.1 = bf16[8,389,128]{2,1,0:T(8,128)(2,1)S(1)} all-gather(bf16[1,389,128]{2,1,0:T(8,128)(2,1)S(1)} %bitcast.218), channel_id=2, replica_groups=mesh['dp'=4,'fsdp'=8] {'fsdp'}, dimensions={0}, use_global_device_ids=true | all-gather | bytes 896256 | tf_op jit(solution)/shard_map/all_gather | solution.py:41
  24.5 1.8 %fusion.3 = bf16[1024,128]{1,0:T(8,128)(2,1)S(1)} fusion(bf16[1024,128]{1,0:T(8,128)(2,1)} %param.19, s32[1024]{0:T(1024)S(1)} %bitcast.253), kind=kOutput, calls=%fused_computation.11 | convolution fusion | flops 269615104 | bytes 528384 | tf_op jit(solution)/shard_map/dot_general | solution.py:200
  26.8 1.6 %collective-permute-start.1 = (bf16[128,128]{1,0:T(8,128)(2,1)S(1)}, bf16[128,128]{1,0:T(8,128)(2,1)S(1)}, u32[]{:S(2)}, u32[]{:S(2)}) collective-permute-start(bf16[128,128]{1,0:T(8,128)(2,1)S(1)} %get-tuple-element.51), channel_id=1, source_target_pairs={{0,2},{1,3},{2,4},{3,5},{4,6},{5,7},{6,0},{7,1},{8,10},{9,11},{10,... | collective-permute-start | bytes 98312 | tf_op jit(solution)/shard_map/ppermute | solution.py:54
  28.4 2.1 %collective-permute-start.2 = (bf16[128,128]{1,0:T(8,128)(2,1)S(1)}, bf16[128,128]{1,0:T(8,128)(2,1)S(1)}, u32[]{:S(2)}, u32[]{:S(2)}) collective-permute-start(bf16[128,128]{1,0:T(8,128)(2,1)S(1)} %get-tuple-element.50), channel_id=1, source_target_pairs={{0,3},{1,4},{2,5},{3,6},{4,7},{5,0},{6,1},{7,2},{8,11},{9,12},{10,... | collective-permute-start | bytes 98312 | tf_op jit(solution)/shard_map/ppermute | solution.py:54
  31.8 1.4 %collective-permute-start.4 = (bf16[128,128]{1,0:T(8,128)(2,1)S(1)}, bf16[128,128]{1,0:T(8,128)(2,1)S(1)}, u32[]{:S(2)}, u32[]{:S(2)}) collective-permute-start(bf16[128,128]{1,0:T(8,128)(2,1)S(1)} %get-tuple-element.48), channel_id=1, source_target_pairs={{0,5},{1,6},{2,7},{3,0},{4,1},{5,2},{6,3},{7,4},{8,13},{9,14},{10,... | collective-permute-start | bytes 98312 | tf_op jit(solution)/shard_map/ppermute | solution.py:54
  36.2 1.7 %collective-permute-done.5 = bf16[128,128]{1,0:T(8,128)(2,1)S(1)} collective-permute-done((bf16[128,128]{1,0:T(8,128)(2,1)S(1)}, bf16[128,128]{1,0:T(8,128)(2,1)S(1)}, u32[]{:S(2)}, u32[]{:S(2)}) %collective-permute-start.5) | collective-permute-done | bytes 32800 | tf_op jit(solution)/shard_map/ppermute | solution.py:54
  41.1 2.0 %collective-permute-start.9 = (bf16[128,256]{0,1:T(8,128)(2,1)S(1)}, bf16[128,256]{0,1:T(8,128)(2,1)S(1)}, u32[]{:S(2)}, u32[]{:S(2)}) collective-permute-start(bf16[128,256]{0,1:T(8,128)(2,1)S(1)} %pad_maximum_fusion.2), channel_id=1, source_target_pairs={{0,3},{1,4},{2,5},{3,6},{4,7},{5,0},{6,1},{7,2},{8,11},{9,12},{10,... | collective-permute-start | bytes 196616 | tf_op jit(solution)/shard_map/ppermute | solution.py:43
  43.1 1.5 %collective-permute-start.10 = (bf16[128,256]{0,1:T(8,128)(2,1)S(1)}, bf16[128,256]{0,1:T(8,128)(2,1)S(1)}, u32[]{:S(2)}, u32[]{:S(2)}) collective-permute-start(bf16[128,256]{0,1:T(8,128)(2,1)S(1)} %pad_maximum_fusion.2), channel_id=1, source_target_pairs={{0,4},{1,5},{2,6},{3,7},{4,0},{5,1},{6,2},{7,3},{8,12},{9,13},{10,... | collective-permute-start | bytes 196616 | tf_op jit(solution)/shard_map/ppermute | solution.py:43
  45.8 1.5 %collective-permute-start.12 = (bf16[128,256]{0,1:T(8,128)(2,1)S(1)}, bf16[128,256]{0,1:T(8,128)(2,1)S(1)}, u32[]{:S(2)}, u32[]{:S(2)}) collective-permute-start(bf16[128,256]{0,1:T(8,128)(2,1)S(1)} %pad_maximum_fusion.2), channel_id=1, source_target_pairs={{0,6},{1,7},{2,0},{3,1},{4,2},{5,3},{6,4},{7,5},{8,14},{9,15},{10,... | collective-permute-start | bytes 196616 | tf_op jit(solution)/shard_map/ppermute | solution.py:43
  47.7 3.9 %collective-permute-done.9 = bf16[128,256]{0,1:T(8,128)(2,1)S(1)} collective-permute-done((bf16[128,256]{0,1:T(8,128)(2,1)S(1)}, bf16[128,256]{0,1:T(8,128)(2,1)S(1)}, u32[]{:S(2)}, u32[]{:S(2)}) %collective-permute-start.9) | collective-permute-done | bytes 65568 | tf_op jit(solution)/shard_map/ppermute | solution.py:43
  51.9 1.6 %collective-permute-done.12 = bf16[128,256]{0,1:T(8,128)(2,1)S(1)} collective-permute-done((bf16[128,256]{0,1:T(8,128)(2,1)S(1)}, bf16[128,256]{0,1:T(8,128)(2,1)S(1)}, u32[]{:S(2)}, u32[]{:S(2)}) %collective-permute-start.12) | collective-permute-done | bytes 65568 | tf_op jit(solution)/shard_map/ppermute | solution.py:43
  55.4 2.0 %select_reduce_fusion = (f32[1024]{0:T(1024)S(1)}, f32[1024]{0:T(1024)S(1)}, f32[1024]{0:T(1024)S(1)}, f32[1024]{0:T(1024)S(1)}) fusion(f32[1024,1024]{0,1:T(8,128)S(1)} %get-tuple-element.78, s32[1024]{0:T(1024)S(1)} %bitcast.250, f32[1024]{0:T(1024)S(1)} %get-tuple-element.77, f32[1024,1024]{0,1:T(8,128)S(1)} %get-tuple-element.76, ...), kind=kLoop, calls=%fused_computation.2 | loop fusion | flops 9433088 | bytes 8417280 | tf_op jit(solution)/shard_map/reduce_sum | solution.py:91
  58.1 2.3 %collective-permute-start.15 = (f32[6,1024]{1,0:T(8,128)S(1)}, f32[6,1024]{1,0:T(8,128)S(1)}, u32[]{:S(2)}, u32[]{:S(2)}) collective-permute-start(f32[6,1024]{1,0:T(8,128)S(1)} %concatenate.39), channel_id=1, source_target_pairs={{0,2},{1,3},{2,4},{3,5},{4,6},{5,7},{6,0},{7,1},{8,10},{9,11},{10,... | collective-permute-start | bytes 73736 | tf_op jit(solution)/shard_map/ppermute | solution.py:43
  61.3 2.0 %collective-permute-start.17 = (f32[6,1024]{1,0:T(8,128)S(1)}, f32[6,1024]{1,0:T(8,128)S(1)}, u32[]{:S(2)}, u32[]{:S(2)}) collective-permute-start(f32[6,1024]{1,0:T(8,128)S(1)} %concatenate.39), channel_id=1, source_target_pairs={{0,4},{1,5},{2,6},{3,7},{4,0},{5,1},{6,2},{7,3},{8,12},{9,13},{10,... | collective-permute-start | bytes 73736 | tf_op jit(solution)/shard_map/ppermute | solution.py:43
  69.4 1.5 %collective-permute-start.21 = (f32[2,22]{1,0:T(2,128)S(1)}, f32[2,22]{1,0:T(2,128)S(1)}, u32[]{:S(2)}, u32[]{:S(2)}) collective-permute-start(f32[2,22]{1,0:T(2,128)S(1)} %get-tuple-element.64), channel_id=1, source_target_pairs={{0,8},{8,16},{16,24},{24,0},{1,9},{9,17},{17,25},{25,1},{2,10},{10... | collective-permute-start | bytes 536 | tf_op jit(solution)/shard_map/ppermute | solution.py:43
  70.9 1.5 %collective-permute-start.22 = (f32[2,22]{1,0:T(2,128)S(1)}, f32[2,22]{1,0:T(2,128)S(1)}, u32[]{:S(2)}, u32[]{:S(2)}) collective-permute-start(f32[2,22]{1,0:T(2,128)S(1)} %get-tuple-element.64), channel_id=1, source_target_pairs={{0,16},{8,24},{16,0},{24,8},{1,17},{9,25},{17,1},{25,9},{2,18},{10... | collective-permute-start | bytes 536 | tf_op jit(solution)/shard_map/ppermute | solution.py:43
  72.4 1.4 %collective-permute-start.23 = (f32[2,22]{1,0:T(2,128)S(1)}, f32[2,22]{1,0:T(2,128)S(1)}, u32[]{:S(2)}, u32[]{:S(2)}) collective-permute-start(f32[2,22]{1,0:T(2,128)S(1)} %get-tuple-element.64), channel_id=1, source_target_pairs={{0,24},{8,0},{16,8},{24,16},{1,25},{9,1},{17,9},{25,17},{2,26},{10... | collective-permute-start | bytes 536 | tf_op jit(solution)/shard_map/ppermute | solution.py:43
  74.5 1.5 %collective-permute-done.23 = f32[2,22]{1,0:T(2,128)S(1)} collective-permute-done((f32[2,22]{1,0:T(2,128)S(1)}, f32[2,22]{1,0:T(2,128)S(1)}, u32[]{:S(2)}, u32[]{:S(2)}) %collective-permute-start.23) | collective-permute-done | bytes 208 | tf_op jit(solution)/shard_map/ppermute | solution.py:43
  77.9 1.8 %bitcast_divide_fusion = (f32[22]{0:T(128)S(1)}, f32[22]{0:T(128)}) fusion(f32[2,22]{1,0:T(2,128)S(1)} %fusion.37, f32[]{:T(128)} %fusion.46, f32[22]{0:T(128)S(1)} %get-tuple-element.21, f32[]{:T(128)} %get-tuple-element.20), kind=kLoop, calls=%fused_computation.167 | loop fusion | flops 132 | bytes 360 | tf_op jit(solution)/shard_map/div | solution.py:243
  80.5 3.5 %fusion.2 = f32[1024,128]{1,0:T(8,128)S(1)} fusion(bf16[1024,128]{1,0:T(8,128)(2,1)S(1)} %copy-done, f32[1024,1024]{0,1:T(8,128)} %copy-done.1, f32[1024]{0:T(1024)S(1)} %bitcast.254, f32[1024]{0:T(1024)S(1)} %broadcast_bitcast_fusion, s32[1024]{0:T(1024)S(1)} %bitcast.251), kind=kOutput, calls=%fused_computation.10 | convolution fusion | flops 274726912 | bytes 4993024 | tf_op jit(solution)/shard_map/dot_general | solution.py:113
  85.4 2.4 %collective-permute-start.26 = (f32[128,128]{0,1:T(8,128)S(1)}, f32[128,128]{0,1:T(8,128)S(1)}, u32[]{:S(2)}, u32[]{:S(2)}) collective-permute-start(f32[128,128]{0,1:T(8,128)S(1)} %bitcast.231), channel_id=1, source_target_pairs={{0,3},{1,4},{2,5},{3,6},{4,7},{5,0},{6,1},{7,2},{8,11},{9,12},{10,... | collective-permute-start | bytes 196616 | tf_op jit(solution)/shard_map/ppermute | solution.py:54
  87.9 1.6 %collective-permute-start.27 = (f32[128,128]{0,1:T(8,128)S(1)}, f32[128,128]{0,1:T(8,128)S(1)}, u32[]{:S(2)}, u32[]{:S(2)}) collective-permute-start(f32[128,128]{0,1:T(8,128)S(1)} %bitcast.232), channel_id=1, source_target_pairs={{0,4},{1,5},{2,6},{3,7},{4,0},{5,1},{6,2},{7,3},{8,12},{9,13},{10,... | collective-permute-start | bytes 196616 | tf_op jit(solution)/shard_map/ppermute | solution.py:54
  93.3 2.7 %collective-permute-done.26 = f32[128,128]{0,1:T(8,128)S(1)} collective-permute-done((f32[128,128]{0,1:T(8,128)S(1)}, f32[128,128]{0,1:T(8,128)S(1)}, u32[]{:S(2)}, u32[]{:S(2)}) %collective-permute-start.26) | collective-permute-done | bytes 65568 | tf_op jit(solution)/shard_map/ppermute | solution.py:54
  96.2 1.8 %collective-permute-done.29 = f32[128,128]{0,1:T(8,128)S(1)} collective-permute-done((f32[128,128]{0,1:T(8,128)S(1)}, f32[128,128]{0,1:T(8,128)S(1)}, u32[]{:S(2)}, u32[]{:S(2)}) %collective-permute-start.29) | collective-permute-done | bytes 65568 | tf_op jit(solution)/shard_map/ppermute | solution.py:54
  99.9 2.0 %collective-permute-start.32 = (bf16[64,384]{1,0:T(8,128)(2,1)S(1)}, bf16[64,384]{1,0:T(8,128)(2,1)S(1)}, u32[]{:S(2)}, u32[]{:S(2)}) collective-permute-start(bf16[64,384]{1,0:T(8,128)(2,1)S(1)} %get-tuple-element.43), channel_id=1, source_target_pairs={{0,2},{1,3},{2,4},{3,5},{4,6},{5,7},{6,0},{7,1},{8,10},{9,11},{10,... | collective-permute-start | bytes 147464 | tf_op jit(solution)/shard_map/ppermute | solution.py:54
  102.5 2.1 %collective-permute-start.34 = (bf16[64,384]{1,0:T(8,128)(2,1)S(1)}, bf16[64,384]{1,0:T(8,128)(2,1)S(1)}, u32[]{:S(2)}, u32[]{:S(2)}) collective-permute-start(bf16[64,384]{1,0:T(8,128)(2,1)S(1)} %get-tuple-element.41), channel_id=1, source_target_pairs={{0,4},{1,5},{2,6},{3,7},{4,0},{5,1},{6,2},{7,3},{8,12},{9,13},{10,... | collective-permute-start | bytes 147464 | tf_op jit(solution)/shard_map/ppermute | solution.py:54
  106.7 1.4 %collective-permute-start.37 = (bf16[64,384]{1,0:T(8,128)(2,1)S(1)}, bf16[64,384]{1,0:T(8,128)(2,1)S(1)}, u32[]{:S(2)}, u32[]{:S(2)}) collective-permute-start(bf16[64,384]{1,0:T(8,128)(2,1)S(1)} %get-tuple-element.38), channel_id=1, source_target_pairs={{0,7},{1,0},{2,1},{3,2},{4,3},{5,4},{6,5},{7,6},{8,15},{9,8},{10,9... | collective-permute-start | bytes 147464 | tf_op jit(solution)/shard_map/ppermute | solution.py:54
  108.2 1.8 %collective-permute-done.33 = bf16[64,384]{1,0:T(8,128)(2,1)S(1)} collective-permute-done((bf16[64,384]{1,0:T(8,128)(2,1)S(1)}, bf16[64,384]{1,0:T(8,128)(2,1)S(1)}, u32[]{:S(2)}, u32[]{:S(2)}) %collective-permute-start.33) | collective-permute-done | bytes 49184 | tf_op jit(solution)/shard_map/ppermute | solution.py:54
  111.7 1.4 %collective-permute-start.38 = (f32[64,384]{1,0:T(8,128)S(1)}, f32[64,384]{1,0:T(8,128)S(1)}, u32[]{:S(2)}, u32[]{:S(2)}) collective-permute-start(f32[64,384]{1,0:T(8,128)S(1)} %convert_reduce_fusion), channel_id=1, source_target_pairs={{0,8},{8,16},{16,24},{24,0},{1,9},{9,17},{17,25},{25,1},{2,10},{10... | collective-permute-start | bytes 294920 | tf_op jit(solution)/shard_map/ppermute | solution.py:43
  113.1 1.5 %collective-permute-start.39 = (f32[64,384]{1,0:T(8,128)S(1)}, f32[64,384]{1,0:T(8,128)S(1)}, u32[]{:S(2)}, u32[]{:S(2)}) collective-permute-start(f32[64,384]{1,0:T(8,128)S(1)} %convert_reduce_fusion), channel_id=1, source_target_pairs={{0,16},{8,24},{16,0},{24,8},{1,17},{9,25},{17,1},{25,9},{2,18},{10... | collective-permute-start | bytes 294920 | tf_op jit(solution)/shard_map/ppermute | solution.py:43
  115.2 3.1 %collective-permute-done.38 = f32[64,384]{1,0:T(8,128)S(1)} collective-permute-done((f32[64,384]{1,0:T(8,128)S(1)}, f32[64,384]{1,0:T(8,128)S(1)}, u32[]{:S(2)}, u32[]{:S(2)}) %collective-permute-start.38) | collective-permute-done | bytes 98336 | tf_op jit(solution)/shard_map/ppermute | solution.py:43
  118.3 1.5 %collective-permute-done.39 = f32[64,384]{1,0:T(8,128)S(1)} collective-permute-done((f32[64,384]{1,0:T(8,128)S(1)}, f32[64,384]{1,0:T(8,128)S(1)}, u32[]{:S(2)}, u32[]{:S(2)}) %collective-permute-start.39) | collective-permute-done | bytes 98336 | tf_op jit(solution)/shard_map/ppermute | solution.py:43
  (177 shorter events, 41.2 us)
Async XLA Ops:
  26.3 7.5 %collective-permute-start = (bf16[128,128]{1,0:T(8,128)(2,1)S(1)}, bf16[128,128]{1,0:T(8,128)(2,1)S(1)}, u32[]{:S(2)}, u32[]{:S(2)}) collective-permute-start(bf16[128,128]{1,0:T(8,128)(2,1)S(1)} %get-tuple-element.52), channel_id=1, source_target_pairs={{0,1},{1,2},{2,3},{3,4},{4,5},{5,6},{6,7},{7,0},{8,9},{9,10},{10,1... | collective-permute-start | bytes 98312 | tf_op jit(solution)/shard_map/ppermute | solution.py:54
  26.8 7.9 %collective-permute-start.1 = (bf16[128,128]{1,0:T(8,128)(2,1)S(1)}, bf16[128,128]{1,0:T(8,128)(2,1)S(1)}, u32[]{:S(2)}, u32[]{:S(2)}) collective-permute-start(bf16[128,128]{1,0:T(8,128)(2,1)S(1)} %get-tuple-element.51), channel_id=1, source_target_pairs={{0,2},{1,3},{2,4},{3,5},{4,6},{5,7},{6,0},{7,1},{8,10},{9,11},{10,... | collective-permute-start | bytes 98312 | tf_op jit(solution)/shard_map/ppermute | solution.py:54
  28.4 7.0 %collective-permute-start.2 = (bf16[128,128]{1,0:T(8,128)(2,1)S(1)}, bf16[128,128]{1,0:T(8,128)(2,1)S(1)}, u32[]{:S(2)}, u32[]{:S(2)}) collective-permute-start(bf16[128,128]{1,0:T(8,128)(2,1)S(1)} %get-tuple-element.50), channel_id=1, source_target_pairs={{0,3},{1,4},{2,5},{3,6},{4,7},{5,0},{6,1},{7,2},{8,11},{9,12},{10,... | collective-permute-start | bytes 98312 | tf_op jit(solution)/shard_map/ppermute | solution.py:54
  30.5 5.6 %collective-permute-start.3 = (bf16[128,128]{1,0:T(8,128)(2,1)S(1)}, bf16[128,128]{1,0:T(8,128)(2,1)S(1)}, u32[]{:S(2)}, u32[]{:S(2)}) collective-permute-start(bf16[128,128]{1,0:T(8,128)(2,1)S(1)} %get-tuple-element.49), channel_id=1, source_target_pairs={{0,4},{1,5},{2,6},{3,7},{4,0},{5,1},{6,2},{7,3},{8,12},{9,13},{10,... | collective-permute-start | bytes 98312 | tf_op jit(solution)/shard_map/ppermute | solution.py:54
  39.8 6.0 %collective-permute-start.7 = (bf16[128,256]{0,1:T(8,128)(2,1)S(1)}, bf16[128,256]{0,1:T(8,128)(2,1)S(1)}, u32[]{:S(2)}, u32[]{:S(2)}) collective-permute-start(bf16[128,256]{0,1:T(8,128)(2,1)S(1)} %pad_maximum_fusion.2), channel_id=1, source_target_pairs={{0,1},{1,2},{2,3},{3,4},{4,5},{5,6},{6,7},{7,0},{8,9},{9,10},{10,1... | collective-permute-start | bytes 196616 | tf_op jit(solution)/shard_map/ppermute | solution.py:43
  40.8 6.7 %collective-permute-start.8 = (bf16[128,256]{0,1:T(8,128)(2,1)S(1)}, bf16[128,256]{0,1:T(8,128)(2,1)S(1)}, u32[]{:S(2)}, u32[]{:S(2)}) collective-permute-start(bf16[128,256]{0,1:T(8,128)(2,1)S(1)} %pad_maximum_fusion.2), channel_id=1, source_target_pairs={{0,2},{1,3},{2,4},{3,5},{4,6},{5,7},{6,0},{7,1},{8,10},{9,11},{10,... | collective-permute-start | bytes 196616 | tf_op jit(solution)/shard_map/ppermute | solution.py:43
  41.1 10.5 %collective-permute-start.9 = (bf16[128,256]{0,1:T(8,128)(2,1)S(1)}, bf16[128,256]{0,1:T(8,128)(2,1)S(1)}, u32[]{:S(2)}, u32[]{:S(2)}) collective-permute-start(bf16[128,256]{0,1:T(8,128)(2,1)S(1)} %pad_maximum_fusion.2), channel_id=1, source_target_pairs={{0,3},{1,4},{2,5},{3,6},{4,7},{5,0},{6,1},{7,2},{8,11},{9,12},{10,... | collective-permute-start | bytes 196616 | tf_op jit(solution)/shard_map/ppermute | solution.py:43
  43.1 8.7 %collective-permute-start.10 = (bf16[128,256]{0,1:T(8,128)(2,1)S(1)}, bf16[128,256]{0,1:T(8,128)(2,1)S(1)}, u32[]{:S(2)}, u32[]{:S(2)}) collective-permute-start(bf16[128,256]{0,1:T(8,128)(2,1)S(1)} %pad_maximum_fusion.2), channel_id=1, source_target_pairs={{0,4},{1,5},{2,6},{3,7},{4,0},{5,1},{6,2},{7,3},{8,12},{9,13},{10,... | collective-permute-start | bytes 196616 | tf_op jit(solution)/shard_map/ppermute | solution.py:43
  44.5 7.3 %collective-permute-start.11 = (bf16[128,256]{0,1:T(8,128)(2,1)S(1)}, bf16[128,256]{0,1:T(8,128)(2,1)S(1)}, u32[]{:S(2)}, u32[]{:S(2)}) collective-permute-start(bf16[128,256]{0,1:T(8,128)(2,1)S(1)} %pad_maximum_fusion.2), channel_id=1, source_target_pairs={{0,5},{1,6},{2,7},{3,0},{4,1},{5,2},{6,3},{7,4},{8,13},{9,14},{10,... | collective-permute-start | bytes 196616 | tf_op jit(solution)/shard_map/ppermute | solution.py:43
  45.8 7.7 %collective-permute-start.12 = (bf16[128,256]{0,1:T(8,128)(2,1)S(1)}, bf16[128,256]{0,1:T(8,128)(2,1)S(1)}, u32[]{:S(2)}, u32[]{:S(2)}) collective-permute-start(bf16[128,256]{0,1:T(8,128)(2,1)S(1)} %pad_maximum_fusion.2), channel_id=1, source_target_pairs={{0,6},{1,7},{2,0},{3,1},{4,2},{5,3},{6,4},{7,5},{8,14},{9,15},{10,... | collective-permute-start | bytes 196616 | tf_op jit(solution)/shard_map/ppermute | solution.py:43
  47.5 6.0 %collective-permute-start.13 = (bf16[128,256]{0,1:T(8,128)(2,1)S(1)}, bf16[128,256]{0,1:T(8,128)(2,1)S(1)}, u32[]{:S(2)}, u32[]{:S(2)}) collective-permute-start(bf16[128,256]{0,1:T(8,128)(2,1)S(1)} %pad_maximum_fusion.2), channel_id=1, source_target_pairs={{0,7},{1,0},{2,1},{3,2},{4,3},{5,4},{6,5},{7,6},{8,15},{9,8},{10,9... | collective-permute-start | bytes 196616 | tf_op jit(solution)/shard_map/ppermute | solution.py:43
  57.5 6.8 %collective-permute-start.14 = (f32[6,1024]{1,0:T(8,128)S(1)}, f32[6,1024]{1,0:T(8,128)S(1)}, u32[]{:S(2)}, u32[]{:S(2)}) collective-permute-start(f32[6,1024]{1,0:T(8,128)S(1)} %concatenate.39), channel_id=1, source_target_pairs={{0,1},{1,2},{2,3},{3,4},{4,5},{5,6},{6,7},{7,0},{8,9},{9,10},{10,1... | collective-permute-start | bytes 73736 | tf_op jit(solution)/shard_map/ppermute | solution.py:43
  58.1 7.4 %collective-permute-start.15 = (f32[6,1024]{1,0:T(8,128)S(1)}, f32[6,1024]{1,0:T(8,128)S(1)}, u32[]{:S(2)}, u32[]{:S(2)}) collective-permute-start(f32[6,1024]{1,0:T(8,128)S(1)} %concatenate.39), channel_id=1, source_target_pairs={{0,2},{1,3},{2,4},{3,5},{4,6},{5,7},{6,0},{7,1},{8,10},{9,11},{10,... | collective-permute-start | bytes 73736 | tf_op jit(solution)/shard_map/ppermute | solution.py:43
  60.5 6.3 %collective-permute-start.16 = (f32[6,1024]{1,0:T(8,128)S(1)}, f32[6,1024]{1,0:T(8,128)S(1)}, u32[]{:S(2)}, u32[]{:S(2)}) collective-permute-start(f32[6,1024]{1,0:T(8,128)S(1)} %concatenate.39), channel_id=1, source_target_pairs={{0,3},{1,4},{2,5},{3,6},{4,7},{5,0},{6,1},{7,2},{8,11},{9,12},{10,... | collective-permute-start | bytes 73736 | tf_op jit(solution)/shard_map/ppermute | solution.py:43
  61.3 6.2 %collective-permute-start.17 = (f32[6,1024]{1,0:T(8,128)S(1)}, f32[6,1024]{1,0:T(8,128)S(1)}, u32[]{:S(2)}, u32[]{:S(2)}) collective-permute-start(f32[6,1024]{1,0:T(8,128)S(1)} %concatenate.39), channel_id=1, source_target_pairs={{0,4},{1,5},{2,6},{3,7},{4,0},{5,1},{6,2},{7,3},{8,12},{9,13},{10,... | collective-permute-start | bytes 73736 | tf_op jit(solution)/shard_map/ppermute | solution.py:43
  84.1 6.6 %collective-permute-start.24 = (f32[128,128]{0,1:T(8,128)S(1)}, f32[128,128]{0,1:T(8,128)S(1)}, u32[]{:S(2)}, u32[]{:S(2)}) collective-permute-start(f32[128,128]{0,1:T(8,128)S(1)} %bitcast.237), channel_id=1, source_target_pairs={{0,1},{1,2},{2,3},{3,4},{4,5},{5,6},{6,7},{7,0},{8,9},{9,10},{10,1... | collective-permute-start | bytes 196616 | tf_op jit(solution)/shard_map/ppermute | solution.py:54
  84.3 7.7 %collective-permute-start.25 = (f32[128,128]{0,1:T(8,128)S(1)}, f32[128,128]{0,1:T(8,128)S(1)}, u32[]{:S(2)}, u32[]{:S(2)}) collective-permute-start(f32[128,128]{0,1:T(8,128)S(1)} %bitcast.235), channel_id=1, source_target_pairs={{0,2},{1,3},{2,4},{3,5},{4,6},{5,7},{6,0},{7,1},{8,10},{9,11},{10,... | collective-permute-start | bytes 196616 | tf_op jit(solution)/shard_map/ppermute | solution.py:54
  85.4 10.6 %collective-permute-start.26 = (f32[128,128]{0,1:T(8,128)S(1)}, f32[128,128]{0,1:T(8,128)S(1)}, u32[]{:S(2)}, u32[]{:S(2)}) collective-permute-start(f32[128,128]{0,1:T(8,128)S(1)} %bitcast.231), channel_id=1, source_target_pairs={{0,3},{1,4},{2,5},{3,6},{4,7},{5,0},{6,1},{7,2},{8,11},{9,12},{10,... | collective-permute-start | bytes 196616 | tf_op jit(solution)/shard_map/ppermute | solution.py:54
  87.9 8.3 %collective-permute-start.27 = (f32[128,128]{0,1:T(8,128)S(1)}, f32[128,128]{0,1:T(8,128)S(1)}, u32[]{:S(2)}, u32[]{:S(2)}) collective-permute-start(f32[128,128]{0,1:T(8,128)S(1)} %bitcast.232), channel_id=1, source_target_pairs={{0,4},{1,5},{2,6},{3,7},{4,0},{5,1},{6,2},{7,3},{8,12},{9,13},{10,... | collective-permute-start | bytes 196616 | tf_op jit(solution)/shard_map/ppermute | solution.py:54
  89.5 6.6 %collective-permute-start.28 = (f32[128,128]{0,1:T(8,128)S(1)}, f32[128,128]{0,1:T(8,128)S(1)}, u32[]{:S(2)}, u32[]{:S(2)}) collective-permute-start(f32[128,128]{0,1:T(8,128)S(1)} %bitcast.233), channel_id=1, source_target_pairs={{0,5},{1,6},{2,7},{3,0},{4,1},{5,2},{6,3},{7,4},{8,13},{9,14},{10,... | collective-permute-start | bytes 196616 | tf_op jit(solution)/shard_map/ppermute | solution.py:54
  90.7 7.3 %collective-permute-start.29 = (f32[128,128]{0,1:T(8,128)S(1)}, f32[128,128]{0,1:T(8,128)S(1)}, u32[]{:S(2)}, u32[]{:S(2)}) collective-permute-start(f32[128,128]{0,1:T(8,128)S(1)} %bitcast.236), channel_id=1, source_target_pairs={{0,6},{1,7},{2,0},{3,1},{4,2},{5,3},{6,4},{7,5},{8,14},{9,15},{10,... | collective-permute-start | bytes 196616 | tf_op jit(solution)/shard_map/ppermute | solution.py:54
  92.0 6.0 %collective-permute-start.30 = (f32[128,128]{0,1:T(8,128)S(1)}, f32[128,128]{0,1:T(8,128)S(1)}, u32[]{:S(2)}, u32[]{:S(2)}) collective-permute-start(f32[128,128]{0,1:T(8,128)S(1)} %bitcast.234), channel_id=1, source_target_pairs={{0,7},{1,0},{2,1},{3,2},{4,3},{5,4},{6,5},{7,6},{8,15},{9,8},{10,9... | collective-permute-start | bytes 196616 | tf_op jit(solution)/shard_map/ppermute | solution.py:54
  99.2 6.2 %collective-permute-start.31 = (bf16[64,384]{1,0:T(8,128)(2,1)S(1)}, bf16[64,384]{1,0:T(8,128)(2,1)S(1)}, u32[]{:S(2)}, u32[]{:S(2)}) collective-permute-start(bf16[64,384]{1,0:T(8,128)(2,1)S(1)} %get-tuple-element.44), channel_id=1, source_target_pairs={{0,1},{1,2},{2,3},{3,4},{4,5},{5,6},{6,7},{7,0},{8,9},{9,10},{10,1... | collective-permute-start | bytes 147464 | tf_op jit(solution)/shard_map/ppermute | solution.py:54
  99.9 6.8 %collective-permute-start.32 = (bf16[64,384]{1,0:T(8,128)(2,1)S(1)}, bf16[64,384]{1,0:T(8,128)(2,1)S(1)}, u32[]{:S(2)}, u32[]{:S(2)}) collective-permute-start(bf16[64,384]{1,0:T(8,128)(2,1)S(1)} %get-tuple-element.43), channel_id=1, source_target_pairs={{0,2},{1,3},{2,4},{3,5},{4,6},{5,7},{6,0},{7,1},{8,10},{9,11},{10,... | collective-permute-start | bytes 147464 | tf_op jit(solution)/shard_map/ppermute | solution.py:54
  101.9 8.1 %collective-permute-start.33 = (bf16[64,384]{1,0:T(8,128)(2,1)S(1)}, bf16[64,384]{1,0:T(8,128)(2,1)S(1)}, u32[]{:S(2)}, u32[]{:S(2)}) collective-permute-start(bf16[64,384]{1,0:T(8,128)(2,1)S(1)} %get-tuple-element.42), channel_id=1, source_target_pairs={{0,3},{1,4},{2,5},{3,6},{4,7},{5,0},{6,1},{7,2},{8,11},{9,12},{10,... | collective-permute-start | bytes 147464 | tf_op jit(solution)/shard_map/ppermute | solution.py:54
  102.5 7.7 %collective-permute-start.34 = (bf16[64,384]{1,0:T(8,128)(2,1)S(1)}, bf16[64,384]{1,0:T(8,128)(2,1)S(1)}, u32[]{:S(2)}, u32[]{:S(2)}) collective-permute-start(bf16[64,384]{1,0:T(8,128)(2,1)S(1)} %get-tuple-element.41), channel_id=1, source_target_pairs={{0,4},{1,5},{2,6},{3,7},{4,0},{5,1},{6,2},{7,3},{8,12},{9,13},{10,... | collective-permute-start | bytes 147464 | tf_op jit(solution)/shard_map/ppermute | solution.py:54
  104.6 5.6 %collective-permute-start.35 = (bf16[64,384]{1,0:T(8,128)(2,1)S(1)}, bf16[64,384]{1,0:T(8,128)(2,1)S(1)}, u32[]{:S(2)}, u32[]{:S(2)}) collective-permute-start(bf16[64,384]{1,0:T(8,128)(2,1)S(1)} %get-tuple-element.40), channel_id=1, source_target_pairs={{0,5},{1,6},{2,7},{3,0},{4,1},{5,2},{6,3},{7,4},{8,13},{9,14},{10,... | collective-permute-start | bytes 147464 | tf_op jit(solution)/shard_map/ppermute | solution.py:54
  105.4 6.2 %collective-permute-start.36 = (bf16[64,384]{1,0:T(8,128)(2,1)S(1)}, bf16[64,384]{1,0:T(8,128)(2,1)S(1)}, u32[]{:S(2)}, u32[]{:S(2)}) collective-permute-start(bf16[64,384]{1,0:T(8,128)(2,1)S(1)} %get-tuple-element.39), channel_id=1, source_target_pairs={{0,6},{1,7},{2,0},{3,1},{4,2},{5,3},{6,4},{7,5},{8,14},{9,15},{10,... | collective-permute-start | bytes 147464 | tf_op jit(solution)/shard_map/ppermute | solution.py:54
  106.7 4.9 %collective-permute-start.37 = (bf16[64,384]{1,0:T(8,128)(2,1)S(1)}, bf16[64,384]{1,0:T(8,128)(2,1)S(1)}, u32[]{:S(2)}, u32[]{:S(2)}) collective-permute-start(bf16[64,384]{1,0:T(8,128)(2,1)S(1)} %get-tuple-element.38), channel_id=1, source_target_pairs={{0,7},{1,0},{2,1},{3,2},{4,3},{5,4},{6,5},{7,6},{8,15},{9,8},{10,9... | collective-permute-start | bytes 147464 | tf_op jit(solution)/shard_map/ppermute | solution.py:54
  111.7 6.6 %collective-permute-start.38 = (f32[64,384]{1,0:T(8,128)S(1)}, f32[64,384]{1,0:T(8,128)S(1)}, u32[]{:S(2)}, u32[]{:S(2)}) collective-permute-start(f32[64,384]{1,0:T(8,128)S(1)} %convert_reduce_fusion), channel_id=1, source_target_pairs={{0,8},{8,16},{16,24},{24,0},{1,9},{9,17},{17,25},{25,1},{2,10},{10... | collective-permute-start | bytes 294920 | tf_op jit(solution)/shard_map/ppermute | solution.py:43
  113.1 6.7 %collective-permute-start.39 = (f32[64,384]{1,0:T(8,128)S(1)}, f32[64,384]{1,0:T(8,128)S(1)}, u32[]{:S(2)}, u32[]{:S(2)}) collective-permute-start(f32[64,384]{1,0:T(8,128)S(1)} %convert_reduce_fusion), channel_id=1, source_target_pairs={{0,16},{8,24},{16,0},{24,8},{1,17},{9,25},{17,1},{25,9},{2,18},{10... | collective-permute-start | bytes 294920 | tf_op jit(solution)/shard_map/ppermute | solution.py:43
  114.7 5.1 %collective-permute-start.40 = (f32[64,384]{1,0:T(8,128)S(1)}, f32[64,384]{1,0:T(8,128)S(1)}, u32[]{:S(2)}, u32[]{:S(2)}) collective-permute-start(f32[64,384]{1,0:T(8,128)S(1)} %convert_reduce_fusion), channel_id=1, source_target_pairs={{0,24},{8,0},{16,8},{24,16},{1,25},{9,1},{17,9},{25,17},{2,26},{10... | collective-permute-start | bytes 294920 | tf_op jit(solution)/shard_map/ppermute | solution.py:43
  (12 other events, 110.4 us)

commit v15 on v14

--- a/solution.py
+++ b/solution.py
@@ -59,6 +59,24 @@
         for shift in range(1, size)
     ]
     return jnp.stack(pieces)
+
+
+def exchange_summed(blocks, axis, native):
+    size = lax.axis_size(axis)
+    if native or size > FAN_OUT_MAX or size < 4 or size & (size - 1):
+        return jnp.sum(exchange_ordered(blocks, axis, native), axis=0)
+    here = lax.axis_index(axis)
+    core = here % 2
+    chips = jnp.arange(size // 2) * 2
+    sent = lax.ppermute(
+        jnp.take(blocks, chips + 1 - core, axis=0), axis, [(source, source ^ 1) for source in range(size)]
+    )
+    combined = jnp.take(blocks, chips + core, axis=0) + sent
+    total = lax.dynamic_index_in_dim(combined, here // 2, keepdims=False)
+    for mask in range(2, size, 2):
+        piece = lax.dynamic_index_in_dim(combined, (here ^ mask) // 2, keepdims=False)
+        total = total + lax.ppermute(piece, axis, [(source, source ^ mask) for source in range(size)])
+    return total
 
 
 def feed_forward(embedded, normed, weights):
@@ -200,8 +218,9 @@
     picked_rows = jnp.dot(token_hits, in_embed, preferred_element_type=jnp.float32).astype(
         jnp.bfloat16
     )
-    arrived = exchange_ordered(picked_rows.reshape(fsdp_size, per_device, width), "fsdp", False)
-    embedded = jnp.sum(arrived.astype(jnp.float32), axis=0)
+    embedded = exchange_summed(
+        picked_rows.reshape(fsdp_size, per_device, width), "fsdp", False
+    ).astype(jnp.float32)
 
     normed = embedded * rms_scale(embedded)
     ref_own = feed_forward(embedded, normed, ref_weights)[0]
@@ -246,9 +265,8 @@
 
     d_second_part = head_gradient(prx_group, out_embed, log_total[1], token_weight, target_local)
 
-    d_second = jnp.sum(
-        exchange_ordered(d_second_part.reshape(fsdp_size, per_device, width), "fsdp", False),
-        axis=0,
+    d_second = exchange_summed(
+        d_second_part.reshape(fsdp_size, per_device, width), "fsdp", False
     )
     first_in, gate_act, up_act, hidden, second_scale, unit_stream = saved_state
     d_unit = d_second * prx_weights[4].astype(jnp.float32)

time: 121 us -> 119 us (0.983)
  starting transfers between devices: 50.5 us -> 41.4 us
  waiting for transfers between devices: 24.6 us -> 28.8 us
  local copies, waits for them, and re-layouts: 8.35 us -> 10.6 us
    ppermute x21 -> x7, starting transfers between devices: 25.8 us -> 7.66 us  [exchange_ordered(): lax.ppermute(lax.dynamic_index_in_dim(blocks, (here + shift) % size, keep...]
    ppermute x0 -> x8, waiting for transfers between devices: none -> 11 us  [the longest x6 9.95 us: exchange_summed(): lax.ppermute(piece, axis, [(source, source ^ mask) for source in range(si...]
    ppermute x0 -> x8, starting transfers between devices: none -> 9.65 us  [the longest x6 9.17 us: exchange_summed(): lax.ppermute(piece, axis, [(source, source ^ mask) for source in range(si...]
    ppermute x21 -> x7, waiting for transfers between devices: 10.5 us -> 2.59 us  [exchange_ordered(): lax.ppermute(lax.dynamic_index_in_dim(blocks, (here + shift) % size, keep...]
    gather x0 -> x4, local copies, waits for them, and re-layouts: none -> 2.28 us  [the longest x2 1.14 us: exchange_summed(): jnp.take(blocks, chips + 1 - core, axis=0)]
    unnamed x39 -> x25, local copies, waits for them, and re-layouts: 5.27 us -> 4.55 us
  transfers between devices with their start and end apart: 41 -> 35, of which waited for: 18 -> 18; matrix products, arithmetic and copies ran while one was open for 1% -> 2% of each run, Pallas kernels for 0% -> 0%
where the time goes in v15:
time: 119 us; the launch traced here: 118 us
  starting transfers between devices  41.4 us (35%)
  waiting for transfers between devices  28.8 us (24%)
  blocking collectives  17.3 us (15%)
  local copies, waits for them, and re-layouts  10.6 us (9%)
  matrix products  9.21 us (8%)
  other arithmetic  9.15 us (8%)
  between operations  2.08 us (2%)
    ppermute x20, starting transfers between devices, gather_ordered(): lax.ppermute(value, axis, shift_pairs(size, shift))  24.1 us
    all_gather x1, blocking collectives, gather_ordered(): return lax.all_gather(value, axis)  17.3 us
    ppermute x20, waiting for transfers between devices, gather_ordered(): lax.ppermute(value, axis, shift_pairs(size, shift))  15.2 us
    ppermute x6, waiting for transfers between devices, exchange_summed(): lax.ppermute(piece, axis, [(source, source ^ mask) for source in range(si...  9.95 us
    ppermute x6, starting transfers between devices, exchange_summed(): lax.ppermute(piece, axis, [(source, source ^ mask) for source in range(si...  9.17 us
    ppermute x7, starting transfers between devices, exchange_ordered(): lax.ppermute(lax.dynamic_index_in_dim(blocks, (here + shift) % size, keep...  7.66 us
    unnamed x25, local copies, waits for them, and re-layouts  4.55 us
    dot_general x1, matrix products, one_block(): return jnp.dot(d_logits, table, preferred_element_type=jnp.float32)  3.49 us
  transfers between devices with their start and end apart: 35, of which 18 were waited for; matrix products, arithmetic and copies ran while one was open for 2% of the time, Pallas kernels for 0%

profile of v15, /device:TPU:0, one launch (start us, length us, event | category | flops | bytes accessed | tf_op | source)
XLA Modules:
  0.0 118.5 jit_solution(16234511011260071247)
XLA Ops:
  7.2 17.3 %all-gather.1 = bf16[8,389,128]{2,1,0:T(8,128)(2,1)S(1)} all-gather(bf16[1,389,128]{2,1,0:T(8,128)(2,1)S(1)} %bitcast.186), channel_id=2, replica_groups=mesh['dp'=4,'fsdp'=8] {'fsdp'}, dimensions={0}, use_global_device_ids=true | all-gather | bytes 896256 | tf_op jit(solution)/shard_map/all_gather | solution.py:41
  24.5 1.8 %fusion.3 = bf16[1024,128]{1,0:T(8,128)(2,1)S(1)} fusion(bf16[1024,128]{1,0:T(8,128)(2,1)} %param.23, s32[1024]{0:T(1024)S(1)} %bitcast.220), kind=kOutput, calls=%fused_computation.15 | convolution fusion | flops 269615104 | bytes 528384 | tf_op jit(solution)/shard_map/dot_general | solution.py:218
  28.6 1.7 %collective-permute-start.1 = (bf16[128,128]{0,1:T(8,128)(2,1)S(1)}, bf16[128,128]{0,1:T(8,128)(2,1)S(1)}, u32[]{:S(2)}, u32[]{:S(2)}) collective-permute-start(bf16[128,128]{0,1:T(8,128)(2,1)S(1)} %bitcast.210), channel_id=1, source_target_pairs={{0,2},{1,3},{2,0},{3,1},{4,6},{5,7},{6,4},{7,5},{8,10},{9,11},{10,... | collective-permute-start | bytes 98312 | tf_op jit(solution)/shard_map/ppermute | solution.py:78
  30.4 2.6 %collective-permute-start.2 = (bf16[128,128]{0,1:T(8,128)(2,1)S(1)}, bf16[128,128]{0,1:T(8,128)(2,1)S(1)}, u32[]{:S(2)}, u32[]{:S(2)}) collective-permute-start(bf16[128,128]{0,1:T(8,128)(2,1)S(1)} %bitcast.211), channel_id=1, source_target_pairs={{0,4},{1,5},{2,6},{3,7},{4,0},{5,1},{6,2},{7,3},{8,12},{9,13},{10,... | collective-permute-start | bytes 98312 | tf_op jit(solution)/shard_map/ppermute | solution.py:78
  34.0 1.7 %collective-permute-done.2 = bf16[128,128]{0,1:T(8,128)(2,1)S(1)} collective-permute-done((bf16[128,128]{0,1:T(8,128)(2,1)S(1)}, bf16[128,128]{0,1:T(8,128)(2,1)S(1)}, u32[]{:S(2)}, u32[]{:S(2)}) %collective-permute-start.2) | collective-permute-done | bytes 32800 | tf_op jit(solution)/shard_map/ppermute | solution.py:78
  35.7 3.1 %collective-permute-done.3 = bf16[128,128]{0,1:T(8,128)(2,1)S(1)} collective-permute-done((bf16[128,128]{0,1:T(8,128)(2,1)S(1)}, bf16[128,128]{0,1:T(8,128)(2,1)S(1)}, u32[]{:S(2)}, u32[]{:S(2)}) %collective-permute-start.3) | collective-permute-done | bytes 32800 | tf_op jit(solution)/shard_map/ppermute | solution.py:78
  41.6 3.2 %collective-permute-start.7 = (bf16[128,256]{0,1:T(8,128)(2,1)S(1)}, bf16[128,256]{0,1:T(8,128)(2,1)S(1)}, u32[]{:S(2)}, u32[]{:S(2)}) collective-permute-start(bf16[128,256]{0,1:T(8,128)(2,1)S(1)} %pad_maximum_fusion.2), channel_id=1, source_target_pairs={{0,4},{1,5},{2,6},{3,7},{4,0},{5,1},{6,2},{7,3},{8,12},{9,13},{10,... | collective-permute-start | bytes 196616 | tf_op jit(solution)/shard_map/ppermute | solution.py:43
  44.9 1.5 %collective-permute-done.4 = bf16[128,256]{0,1:T(8,128)(2,1)S(1)} collective-permute-done((bf16[128,256]{0,1:T(8,128)(2,1)S(1)}, bf16[128,256]{0,1:T(8,128)(2,1)S(1)}, u32[]{:S(2)}, u32[]{:S(2)}) %collective-permute-start.4) | collective-permute-done | bytes 65568 | tf_op jit(solution)/shard_map/ppermute | solution.py:43
  47.7 4.8 %collective-permute-done.6 = bf16[128,256]{0,1:T(8,128)(2,1)S(1)} collective-permute-done((bf16[128,256]{0,1:T(8,128)(2,1)S(1)}, bf16[128,256]{0,1:T(8,128)(2,1)S(1)}, u32[]{:S(2)}, u32[]{:S(2)}) %collective-permute-start.6) | collective-permute-done | bytes 65568 | tf_op jit(solution)/shard_map/ppermute | solution.py:43
  54.8 2.0 %select_reduce_fusion = (f32[1024]{0:T(1024)S(1)}, f32[1024]{0:T(1024)S(1)}, f32[1024]{0:T(1024)S(1)}, f32[1024]{0:T(1024)S(1)}) fusion(f32[1024,1024]{0,1:T(8,128)S(1)} %get-tuple-element.74, s32[1024]{0:T(1024)S(1)} %bitcast.217, f32[1024]{0:T(1024)S(1)} %get-tuple-element.73, f32[1024,1024]{0,1:T(8,128)S(1)} %get-tuple-element.72, ...), kind=kLoop, calls=%fused_computation.6 | loop fusion | flops 9433088 | bytes 8417280 | tf_op jit(solution)/shard_map/reduce_sum | solution.py:109
  56.8 1.9 %collective-permute-start.11 = (f32[6,1024]{1,0:T(8,128)S(1)}, f32[6,1024]{1,0:T(8,128)S(1)}, u32[]{:S(2)}, u32[]{:S(2)}) collective-permute-start(f32[6,1024]{1,0:T(8,128)S(1)} %concatenate.39), channel_id=1, source_target_pairs={{0,1},{1,2},{2,3},{3,4},{4,5},{5,6},{6,7},{7,0},{8,9},{9,10},{10,1... | collective-permute-start | bytes 73736 | tf_op jit(solution)/shard_map/ppermute | solution.py:43
  58.7 2.6 %collective-permute-start.12 = (f32[6,1024]{1,0:T(8,128)S(1)}, f32[6,1024]{1,0:T(8,128)S(1)}, u32[]{:S(2)}, u32[]{:S(2)}) collective-permute-start(f32[6,1024]{1,0:T(8,128)S(1)} %concatenate.39), channel_id=1, source_target_pairs={{0,2},{1,3},{2,4},{3,5},{4,6},{5,7},{6,0},{7,1},{8,10},{9,11},{10,... | collective-permute-start | bytes 73736 | tf_op jit(solution)/shard_map/ppermute | solution.py:43
  61.5 2.7 %collective-permute-start.14 = (f32[6,1024]{1,0:T(8,128)S(1)}, f32[6,1024]{1,0:T(8,128)S(1)}, u32[]{:S(2)}, u32[]{:S(2)}) collective-permute-start(f32[6,1024]{1,0:T(8,128)S(1)} %concatenate.39), channel_id=1, source_target_pairs={{0,4},{1,5},{2,6},{3,7},{4,0},{5,1},{6,2},{7,3},{8,12},{9,13},{10,... | collective-permute-start | bytes 73736 | tf_op jit(solution)/shard_map/ppermute | solution.py:43
  64.2 2.1 %collective-permute-start.16 = (f32[6,1024]{1,0:T(8,128)S(1)}, f32[6,1024]{1,0:T(8,128)S(1)}, u32[]{:S(2)}, u32[]{:S(2)}) collective-permute-start(f32[6,1024]{1,0:T(8,128)S(1)} %concatenate.39), channel_id=1, source_target_pairs={{0,6},{1,7},{2,0},{3,1},{4,2},{5,3},{6,4},{7,5},{8,14},{9,15},{10,... | collective-permute-start | bytes 73736 | tf_op jit(solution)/shard_map/ppermute | solution.py:43
  70.2 1.5 %collective-permute-start.18 = (f32[2,22]{1,0:T(2,128)S(1)}, f32[2,22]{1,0:T(2,128)S(1)}, u32[]{:S(2)}, u32[]{:S(2)}) collective-permute-start(f32[2,22]{1,0:T(2,128)S(1)} %get-tuple-element.60), channel_id=1, source_target_pairs={{0,8},{8,16},{16,24},{24,0},{1,9},{9,17},{17,25},{25,1},{2,10},{10... | collective-permute-start | bytes 536 | tf_op jit(solution)/shard_map/ppermute | solution.py:43
  71.7 1.5 %collective-permute-start.19 = (f32[2,22]{1,0:T(2,128)S(1)}, f32[2,22]{1,0:T(2,128)S(1)}, u32[]{:S(2)}, u32[]{:S(2)}) collective-permute-start(f32[2,22]{1,0:T(2,128)S(1)} %get-tuple-element.60), channel_id=1, source_target_pairs={{0,16},{8,24},{16,0},{24,8},{1,17},{9,25},{17,1},{25,9},{2,18},{10... | collective-permute-start | bytes 536 | tf_op jit(solution)/shard_map/ppermute | solution.py:43
  73.2 1.4 %collective-permute-start.20 = (f32[2,22]{1,0:T(2,128)S(1)}, f32[2,22]{1,0:T(2,128)S(1)}, u32[]{:S(2)}, u32[]{:S(2)}) collective-permute-start(f32[2,22]{1,0:T(2,128)S(1)} %get-tuple-element.60), channel_id=1, source_target_pairs={{0,24},{8,0},{16,8},{24,16},{1,25},{9,1},{17,9},{25,17},{2,26},{10... | collective-permute-start | bytes 536 | tf_op jit(solution)/shard_map/ppermute | solution.py:43
  75.3 1.5 %collective-permute-done.20 = f32[2,22]{1,0:T(2,128)S(1)} collective-permute-done((f32[2,22]{1,0:T(2,128)S(1)}, f32[2,22]{1,0:T(2,128)S(1)}, u32[]{:S(2)}, u32[]{:S(2)}) %collective-permute-start.20) | collective-permute-done | bytes 208 | tf_op jit(solution)/shard_map/ppermute | solution.py:43
  78.7 1.8 %bitcast_divide_fusion = (f32[22]{0:T(128)S(1)}, f32[22]{0:T(128)}) fusion(f32[2,22]{1,0:T(2,128)S(1)} %fusion.50, f32[]{:T(128)} %fusion.59, f32[22]{0:T(128)S(1)} %get-tuple-element.23, f32[]{:T(128)} %get-tuple-element.22), kind=kLoop, calls=%fused_computation.173 | loop fusion | flops 132 | bytes 360 | tf_op jit(solution)/shard_map/div | solution.py:262
  81.3 3.5 %fusion.2 = f32[1024,128]{1,0:T(8,128)S(1)} fusion(bf16[1024,128]{1,0:T(8,128)(2,1)S(1)} %copy-done, f32[1024,1024]{0,1:T(8,128)} %copy-done.1, f32[1024]{0:T(1024)S(1)} %bitcast.221, f32[1024]{0:T(1024)S(1)} %broadcast_bitcast_fusion, s32[1024]{0:T(1024)S(1)} %bitcast.218), kind=kOutput, calls=%fused_computation.14 | convolution fusion | flops 274726912 | bytes 4993024 | tf_op jit(solution)/shard_map/dot_general | solution.py:131
  88.2 2.7 %collective-permute-start.23 = (f32[128,128]{0,1:T(8,128)S(1)}, f32[128,128]{0,1:T(8,128)S(1)}, u32[]{:S(2)}, u32[]{:S(2)}) collective-permute-start(f32[128,128]{0,1:T(8,128)S(1)} %bitcast.200), channel_id=1, source_target_pairs={{0,4},{1,5},{2,6},{3,7},{4,0},{5,1},{6,2},{7,3},{8,12},{9,13},{10,... | collective-permute-start | bytes 196616 | tf_op jit(solution)/shard_map/ppermute | solution.py:78
  92.1 3.8 %collective-permute-done.23 = f32[128,128]{0,1:T(8,128)S(1)} collective-permute-done((f32[128,128]{0,1:T(8,128)S(1)}, f32[128,128]{0,1:T(8,128)S(1)}, u32[]{:S(2)}, u32[]{:S(2)}) %collective-permute-start.23) | collective-permute-done | bytes 65568 | tf_op jit(solution)/shard_map/ppermute | solution.py:78
  95.9 1.3 %collective-permute-done.24 = f32[128,128]{0,1:T(8,128)S(1)} collective-permute-done((f32[128,128]{0,1:T(8,128)S(1)}, f32[128,128]{0,1:T(8,128)S(1)}, u32[]{:S(2)}, u32[]{:S(2)}) %collective-permute-start.24) | collective-permute-done | bytes 65568 | tf_op jit(solution)/shard_map/ppermute | solution.py:78
  99.4 1.4 %collective-permute-start.27 = (bf16[64,384]{1,0:T(8,128)(2,1)S(1)}, bf16[64,384]{1,0:T(8,128)(2,1)S(1)}, u32[]{:S(2)}, u32[]{:S(2)}) collective-permute-start(bf16[64,384]{1,0:T(8,128)(2,1)S(1)} %get-tuple-element.38), channel_id=1, source_target_pairs={{0,3},{1,4},{2,5},{3,6},{4,7},{5,0},{6,1},{7,2},{8,11},{9,12},{10,... | collective-permute-start | bytes 147464 | tf_op jit(solution)/shard_map/ppermute | solution.py:54
  100.8 2.3 %collective-permute-start.28 = (bf16[64,384]{1,0:T(8,128)(2,1)S(1)}, bf16[64,384]{1,0:T(8,128)(2,1)S(1)}, u32[]{:S(2)}, u32[]{:S(2)}) collective-permute-start(bf16[64,384]{1,0:T(8,128)(2,1)S(1)} %get-tuple-element.37), channel_id=1, source_target_pairs={{0,4},{1,5},{2,6},{3,7},{4,0},{5,1},{6,2},{7,3},{8,12},{9,13},{10,... | collective-permute-start | bytes 147464 | tf_op jit(solution)/shard_map/ppermute | solution.py:54
  103.9 1.5 %collective-permute-start.30 = (bf16[64,384]{1,0:T(8,128)(2,1)S(1)}, bf16[64,384]{1,0:T(8,128)(2,1)S(1)}, u32[]{:S(2)}, u32[]{:S(2)}) collective-permute-start(bf16[64,384]{1,0:T(8,128)(2,1)S(1)} %get-tuple-element.35), channel_id=1, source_target_pairs={{0,6},{1,7},{2,0},{3,1},{4,2},{5,3},{6,4},{7,5},{8,14},{9,15},{10,... | collective-permute-start | bytes 147464 | tf_op jit(solution)/shard_map/ppermute | solution.py:54
  105.4 1.5 %collective-permute-start.31 = (bf16[64,384]{1,0:T(8,128)(2,1)S(1)}, bf16[64,384]{1,0:T(8,128)(2,1)S(1)}, u32[]{:S(2)}, u32[]{:S(2)}) collective-permute-start(bf16[64,384]{1,0:T(8,128)(2,1)S(1)} %get-tuple-element.34), channel_id=1, source_target_pairs={{0,7},{1,0},{2,1},{3,2},{4,3},{5,4},{6,5},{7,6},{8,15},{9,8},{10,9... | collective-permute-start | bytes 147464 | tf_op jit(solution)/shard_map/ppermute | solution.py:54
  106.9 1.7 %collective-permute-done.27 = bf16[64,384]{1,0:T(8,128)(2,1)S(1)} collective-permute-done((bf16[64,384]{1,0:T(8,128)(2,1)S(1)}, bf16[64,384]{1,0:T(8,128)(2,1)S(1)}, u32[]{:S(2)}, u32[]{:S(2)}) %collective-permute-start.27) | collective-permute-done | bytes 49184 | tf_op jit(solution)/shard_map/ppermute | solution.py:54
  109.0 1.4 %collective-permute-start.32 = (f32[64,384]{1,0:T(8,128)S(1)}, f32[64,384]{1,0:T(8,128)S(1)}, u32[]{:S(2)}, u32[]{:S(2)}) collective-permute-start(f32[64,384]{1,0:T(8,128)S(1)} %convert_reduce_fusion), channel_id=1, source_target_pairs={{0,8},{8,16},{16,24},{24,0},{1,9},{9,17},{17,25},{25,1},{2,10},{10... | collective-permute-start | bytes 294920 | tf_op jit(solution)/shard_map/ppermute | solution.py:43
  110.4 1.5 %collective-permute-start.33 = (f32[64,384]{1,0:T(8,128)S(1)}, f32[64,384]{1,0:T(8,128)S(1)}, u32[]{:S(2)}, u32[]{:S(2)}) collective-permute-start(f32[64,384]{1,0:T(8,128)S(1)} %convert_reduce_fusion), channel_id=1, source_target_pairs={{0,16},{8,24},{16,0},{24,8},{1,17},{9,25},{17,1},{25,9},{2,18},{10... | collective-permute-start | bytes 294920 | tf_op jit(solution)/shard_map/ppermute | solution.py:43
  112.5 2.8 %collective-permute-done.32 = f32[64,384]{1,0:T(8,128)S(1)} collective-permute-done((f32[64,384]{1,0:T(8,128)S(1)}, f32[64,384]{1,0:T(8,128)S(1)}, u32[]{:S(2)}, u32[]{:S(2)}) %collective-permute-start.32) | collective-permute-done | bytes 98336 | tf_op jit(solution)/shard_map/ppermute | solution.py:43
  115.2 2.5 %collective-permute-done.33 = f32[64,384]{1,0:T(8,128)S(1)} collective-permute-done((f32[64,384]{1,0:T(8,128)S(1)}, f32[64,384]{1,0:T(8,128)S(1)}, u32[]{:S(2)}, u32[]{:S(2)}) %collective-permute-start.33) | collective-permute-done | bytes 98336 | tf_op jit(solution)/shard_map/ppermute | solution.py:43
  (169 shorter events, 31.7 us)
Async XLA Ops:
  28.6 5.4 %collective-permute-start.1 = (bf16[128,128]{0,1:T(8,128)(2,1)S(1)}, bf16[128,128]{0,1:T(8,128)(2,1)S(1)}, u32[]{:S(2)}, u32[]{:S(2)}) collective-permute-start(bf16[128,128]{0,1:T(8,128)(2,1)S(1)} %bitcast.210), channel_id=1, source_target_pairs={{0,2},{1,3},{2,0},{3,1},{4,6},{5,7},{6,4},{7,5},{8,10},{9,11},{10,... | collective-permute-start | bytes 98312 | tf_op jit(solution)/shard_map/ppermute | solution.py:78
  30.4 5.3 %collective-permute-start.2 = (bf16[128,128]{0,1:T(8,128)(2,1)S(1)}, bf16[128,128]{0,1:T(8,128)(2,1)S(1)}, u32[]{:S(2)}, u32[]{:S(2)}) collective-permute-start(bf16[128,128]{0,1:T(8,128)(2,1)S(1)} %bitcast.211), channel_id=1, source_target_pairs={{0,4},{1,5},{2,6},{3,7},{4,0},{5,1},{6,2},{7,3},{8,12},{9,13},{10,... | collective-permute-start | bytes 98312 | tf_op jit(solution)/shard_map/ppermute | solution.py:78
  33.1 5.8 %collective-permute-start.3 = (bf16[128,128]{0,1:T(8,128)(2,1)S(1)}, bf16[128,128]{0,1:T(8,128)(2,1)S(1)}, u32[]{:S(2)}, u32[]{:S(2)}) collective-permute-start(bf16[128,128]{0,1:T(8,128)(2,1)S(1)} %bitcast.212), channel_id=1, source_target_pairs={{0,6},{1,7},{2,4},{3,5},{4,2},{5,3},{6,0},{7,1},{8,14},{9,15},{10,... | collective-permute-start | bytes 98312 | tf_op jit(solution)/shard_map/ppermute | solution.py:78
  40.7 5.7 %collective-permute-start.4 = (bf16[128,256]{0,1:T(8,128)(2,1)S(1)}, bf16[128,256]{0,1:T(8,128)(2,1)S(1)}, u32[]{:S(2)}, u32[]{:S(2)}) collective-permute-start(bf16[128,256]{0,1:T(8,128)(2,1)S(1)} %pad_maximum_fusion.2), channel_id=1, source_target_pairs={{0,1},{1,2},{2,3},{3,4},{4,5},{5,6},{6,7},{7,0},{8,9},{9,10},{10,1... | collective-permute-start | bytes 196616 | tf_op jit(solution)/shard_map/ppermute | solution.py:43
  40.7 6.9 %collective-permute-start.5 = (bf16[128,256]{0,1:T(8,128)(2,1)S(1)}, bf16[128,256]{0,1:T(8,128)(2,1)S(1)}, u32[]{:S(2)}, u32[]{:S(2)}) collective-permute-start(bf16[128,256]{0,1:T(8,128)(2,1)S(1)} %pad_maximum_fusion.2), channel_id=1, source_target_pairs={{0,2},{1,3},{2,4},{3,5},{4,6},{5,7},{6,0},{7,1},{8,10},{9,11},{10,... | collective-permute-start | bytes 196616 | tf_op jit(solution)/shard_map/ppermute | solution.py:43
  40.8 11.8 %collective-permute-start.6 = (bf16[128,256]{0,1:T(8,128)(2,1)S(1)}, bf16[128,256]{0,1:T(8,128)(2,1)S(1)}, u32[]{:S(2)}, u32[]{:S(2)}) collective-permute-start(bf16[128,256]{0,1:T(8,128)(2,1)S(1)} %pad_maximum_fusion.2), channel_id=1, source_target_pairs={{0,3},{1,4},{2,5},{3,6},{4,7},{5,0},{6,1},{7,2},{8,11},{9,12},{10,... | collective-permute-start | bytes 196616 | tf_op jit(solution)/shard_map/ppermute | solution.py:43
  41.6 11.1 %collective-permute-start.7 = (bf16[128,256]{0,1:T(8,128)(2,1)S(1)}, bf16[128,256]{0,1:T(8,128)(2,1)S(1)}, u32[]{:S(2)}, u32[]{:S(2)}) collective-permute-start(bf16[128,256]{0,1:T(8,128)(2,1)S(1)} %pad_maximum_fusion.2), channel_id=1, source_target_pairs={{0,4},{1,5},{2,6},{3,7},{4,0},{5,1},{6,2},{7,3},{8,12},{9,13},{10,... | collective-permute-start | bytes 196616 | tf_op jit(solution)/shard_map/ppermute | solution.py:43
  44.9 7.8 %collective-permute-start.8 = (bf16[128,256]{0,1:T(8,128)(2,1)S(1)}, bf16[128,256]{0,1:T(8,128)(2,1)S(1)}, u32[]{:S(2)}, u32[]{:S(2)}) collective-permute-start(bf16[128,256]{0,1:T(8,128)(2,1)S(1)} %pad_maximum_fusion.2), channel_id=1, source_target_pairs={{0,5},{1,6},{2,7},{3,0},{4,1},{5,2},{6,3},{7,4},{8,13},{9,14},{10,... | collective-permute-start | bytes 196616 | tf_op jit(solution)/shard_map/ppermute | solution.py:43
  46.4 6.4 %collective-permute-start.9 = (bf16[128,256]{0,1:T(8,128)(2,1)S(1)}, bf16[128,256]{0,1:T(8,128)(2,1)S(1)}, u32[]{:S(2)}, u32[]{:S(2)}) collective-permute-start(bf16[128,256]{0,1:T(8,128)(2,1)S(1)} %pad_maximum_fusion.2), channel_id=1, source_target_pairs={{0,6},{1,7},{2,0},{3,1},{4,2},{5,3},{6,4},{7,5},{8,14},{9,15},{10,... | collective-permute-start | bytes 196616 | tf_op jit(solution)/shard_map/ppermute | solution.py:43
  47.6 5.2 %collective-permute-start.10 = (bf16[128,256]{0,1:T(8,128)(2,1)S(1)}, bf16[128,256]{0,1:T(8,128)(2,1)S(1)}, u32[]{:S(2)}, u32[]{:S(2)}) collective-permute-start(bf16[128,256]{0,1:T(8,128)(2,1)S(1)} %pad_maximum_fusion.2), channel_id=1, source_target_pairs={{0,7},{1,0},{2,1},{3,2},{4,3},{5,4},{6,5},{7,6},{8,15},{9,8},{10,9... | collective-permute-start | bytes 196616 | tf_op jit(solution)/shard_map/ppermute | solution.py:43
  56.8 7.4 %collective-permute-start.11 = (f32[6,1024]{1,0:T(8,128)S(1)}, f32[6,1024]{1,0:T(8,128)S(1)}, u32[]{:S(2)}, u32[]{:S(2)}) collective-permute-start(f32[6,1024]{1,0:T(8,128)S(1)} %concatenate.39), channel_id=1, source_target_pairs={{0,1},{1,2},{2,3},{3,4},{4,5},{5,6},{6,7},{7,0},{8,9},{9,10},{10,1... | collective-permute-start | bytes 73736 | tf_op jit(solution)/shard_map/ppermute | solution.py:43
  58.7 7.6 %collective-permute-start.12 = (f32[6,1024]{1,0:T(8,128)S(1)}, f32[6,1024]{1,0:T(8,128)S(1)}, u32[]{:S(2)}, u32[]{:S(2)}) collective-permute-start(f32[6,1024]{1,0:T(8,128)S(1)} %concatenate.39), channel_id=1, source_target_pairs={{0,2},{1,3},{2,4},{3,5},{4,6},{5,7},{6,0},{7,1},{8,10},{9,11},{10,... | collective-permute-start | bytes 73736 | tf_op jit(solution)/shard_map/ppermute | solution.py:43
  61.4 6.3 %collective-permute-start.13 = (f32[6,1024]{1,0:T(8,128)S(1)}, f32[6,1024]{1,0:T(8,128)S(1)}, u32[]{:S(2)}, u32[]{:S(2)}) collective-permute-start(f32[6,1024]{1,0:T(8,128)S(1)} %concatenate.39), channel_id=1, source_target_pairs={{0,3},{1,4},{2,5},{3,6},{4,7},{5,0},{6,1},{7,2},{8,11},{9,12},{10,... | collective-permute-start | bytes 73736 | tf_op jit(solution)/shard_map/ppermute | solution.py:43
  61.5 6.3 %collective-permute-start.14 = (f32[6,1024]{1,0:T(8,128)S(1)}, f32[6,1024]{1,0:T(8,128)S(1)}, u32[]{:S(2)}, u32[]{:S(2)}) collective-permute-start(f32[6,1024]{1,0:T(8,128)S(1)} %concatenate.39), channel_id=1, source_target_pairs={{0,4},{1,5},{2,6},{3,7},{4,0},{5,1},{6,2},{7,3},{8,12},{9,13},{10,... | collective-permute-start | bytes 73736 | tf_op jit(solution)/shard_map/ppermute | solution.py:43
  64.2 3.6 %collective-permute-start.15 = (f32[6,1024]{1,0:T(8,128)S(1)}, f32[6,1024]{1,0:T(8,128)S(1)}, u32[]{:S(2)}, u32[]{:S(2)}) collective-permute-start(f32[6,1024]{1,0:T(8,128)S(1)} %concatenate.39), channel_id=1, source_target_pairs={{0,5},{1,6},{2,7},{3,0},{4,1},{5,2},{6,3},{7,4},{8,13},{9,14},{10,... | collective-permute-start | bytes 73736 | tf_op jit(solution)/shard_map/ppermute | solution.py:43
  64.2 4.1 %collective-permute-start.16 = (f32[6,1024]{1,0:T(8,128)S(1)}, f32[6,1024]{1,0:T(8,128)S(1)}, u32[]{:S(2)}, u32[]{:S(2)}) collective-permute-start(f32[6,1024]{1,0:T(8,128)S(1)} %concatenate.39), channel_id=1, source_target_pairs={{0,6},{1,7},{2,0},{3,1},{4,2},{5,3},{6,4},{7,5},{8,14},{9,15},{10,... | collective-permute-start | bytes 73736 | tf_op jit(solution)/shard_map/ppermute | solution.py:43
  70.2 4.5 %collective-permute-start.18 = (f32[2,22]{1,0:T(2,128)S(1)}, f32[2,22]{1,0:T(2,128)S(1)}, u32[]{:S(2)}, u32[]{:S(2)}) collective-permute-start(f32[2,22]{1,0:T(2,128)S(1)} %get-tuple-element.60), channel_id=1, source_target_pairs={{0,8},{8,16},{16,24},{24,0},{1,9},{9,17},{17,25},{25,1},{2,10},{10... | collective-permute-start | bytes 536 | tf_op jit(solution)/shard_map/ppermute | solution.py:43
  71.7 3.6 %collective-permute-start.19 = (f32[2,22]{1,0:T(2,128)S(1)}, f32[2,22]{1,0:T(2,128)S(1)}, u32[]{:S(2)}, u32[]{:S(2)}) collective-permute-start(f32[2,22]{1,0:T(2,128)S(1)} %get-tuple-element.60), channel_id=1, source_target_pairs={{0,16},{8,24},{16,0},{24,8},{1,17},{9,25},{17,1},{25,9},{2,18},{10... | collective-permute-start | bytes 536 | tf_op jit(solution)/shard_map/ppermute | solution.py:43
  73.2 3.6 %collective-permute-start.20 = (f32[2,22]{1,0:T(2,128)S(1)}, f32[2,22]{1,0:T(2,128)S(1)}, u32[]{:S(2)}, u32[]{:S(2)}) collective-permute-start(f32[2,22]{1,0:T(2,128)S(1)} %get-tuple-element.60), channel_id=1, source_target_pairs={{0,24},{8,0},{16,8},{24,16},{1,25},{9,1},{17,9},{25,17},{2,26},{10... | collective-permute-start | bytes 536 | tf_op jit(solution)/shard_map/ppermute | solution.py:43
  87.3 4.9 %collective-permute-start.22 = (f32[128,128]{0,1:T(8,128)S(1)}, f32[128,128]{0,1:T(8,128)S(1)}, u32[]{:S(2)}, u32[]{:S(2)}) collective-permute-start(f32[128,128]{0,1:T(8,128)S(1)} %bitcast.199), channel_id=1, source_target_pairs={{0,2},{1,3},{2,0},{3,1},{4,6},{5,7},{6,4},{7,5},{8,10},{9,11},{10,... | collective-permute-start | bytes 196616 | tf_op jit(solution)/shard_map/ppermute | solution.py:78
  88.2 7.7 %collective-permute-start.23 = (f32[128,128]{0,1:T(8,128)S(1)}, f32[128,128]{0,1:T(8,128)S(1)}, u32[]{:S(2)}, u32[]{:S(2)}) collective-permute-start(f32[128,128]{0,1:T(8,128)S(1)} %bitcast.200), channel_id=1, source_target_pairs={{0,4},{1,5},{2,6},{3,7},{4,0},{5,1},{6,2},{7,3},{8,12},{9,13},{10,... | collective-permute-start | bytes 196616 | tf_op jit(solution)/shard_map/ppermute | solution.py:78
  91.0 6.2 %collective-permute-start.24 = (f32[128,128]{0,1:T(8,128)S(1)}, f32[128,128]{0,1:T(8,128)S(1)}, u32[]{:S(2)}, u32[]{:S(2)}) collective-permute-start(f32[128,128]{0,1:T(8,128)S(1)} %bitcast.201), channel_id=1, source_target_pairs={{0,6},{1,7},{2,4},{3,5},{4,2},{5,3},{6,0},{7,1},{8,14},{9,15},{10,... | collective-permute-start | bytes 196616 | tf_op jit(solution)/shard_map/ppermute | solution.py:78
  98.5 5.4 %collective-permute-start.25 = (bf16[64,384]{1,0:T(8,128)(2,1)S(1)}, bf16[64,384]{1,0:T(8,128)(2,1)S(1)}, u32[]{:S(2)}, u32[]{:S(2)}) collective-permute-start(bf16[64,384]{1,0:T(8,128)(2,1)S(1)} %get-tuple-element.40), channel_id=1, source_target_pairs={{0,1},{1,2},{2,3},{3,4},{4,5},{5,6},{6,7},{7,0},{8,9},{9,10},{10,1... | collective-permute-start | bytes 147464 | tf_op jit(solution)/shard_map/ppermute | solution.py:54
  98.6 6.8 %collective-permute-start.26 = (bf16[64,384]{1,0:T(8,128)(2,1)S(1)}, bf16[64,384]{1,0:T(8,128)(2,1)S(1)}, u32[]{:S(2)}, u32[]{:S(2)}) collective-permute-start(bf16[64,384]{1,0:T(8,128)(2,1)S(1)} %get-tuple-element.39), channel_id=1, source_target_pairs={{0,2},{1,3},{2,4},{3,5},{4,6},{5,7},{6,0},{7,1},{8,10},{9,11},{10,... | collective-permute-start | bytes 147464 | tf_op jit(solution)/shard_map/ppermute | solution.py:54
  99.4 9.3 %collective-permute-start.27 = (bf16[64,384]{1,0:T(8,128)(2,1)S(1)}, bf16[64,384]{1,0:T(8,128)(2,1)S(1)}, u32[]{:S(2)}, u32[]{:S(2)}) collective-permute-start(bf16[64,384]{1,0:T(8,128)(2,1)S(1)} %get-tuple-element.38), channel_id=1, source_target_pairs={{0,3},{1,4},{2,5},{3,6},{4,7},{5,0},{6,1},{7,2},{8,11},{9,12},{10,... | collective-permute-start | bytes 147464 | tf_op jit(solution)/shard_map/ppermute | solution.py:54
  100.8 8.0 %collective-permute-start.28 = (bf16[64,384]{1,0:T(8,128)(2,1)S(1)}, bf16[64,384]{1,0:T(8,128)(2,1)S(1)}, u32[]{:S(2)}, u32[]{:S(2)}) collective-permute-start(bf16[64,384]{1,0:T(8,128)(2,1)S(1)} %get-tuple-element.37), channel_id=1, source_target_pairs={{0,4},{1,5},{2,6},{3,7},{4,0},{5,1},{6,2},{7,3},{8,12},{9,13},{10,... | collective-permute-start | bytes 147464 | tf_op jit(solution)/shard_map/ppermute | solution.py:54
  103.1 5.7 %collective-permute-start.29 = (bf16[64,384]{1,0:T(8,128)(2,1)S(1)}, bf16[64,384]{1,0:T(8,128)(2,1)S(1)}, u32[]{:S(2)}, u32[]{:S(2)}) collective-permute-start(bf16[64,384]{1,0:T(8,128)(2,1)S(1)} %get-tuple-element.36), channel_id=1, source_target_pairs={{0,5},{1,6},{2,7},{3,0},{4,1},{5,2},{6,3},{7,4},{8,13},{9,14},{10,... | collective-permute-start | bytes 147464 | tf_op jit(solution)/shard_map/ppermute | solution.py:54
  103.9 5.0 %collective-permute-start.30 = (bf16[64,384]{1,0:T(8,128)(2,1)S(1)}, bf16[64,384]{1,0:T(8,128)(2,1)S(1)}, u32[]{:S(2)}, u32[]{:S(2)}) collective-permute-start(bf16[64,384]{1,0:T(8,128)(2,1)S(1)} %get-tuple-element.35), channel_id=1, source_target_pairs={{0,6},{1,7},{2,0},{3,1},{4,2},{5,3},{6,4},{7,5},{8,14},{9,15},{10,... | collective-permute-start | bytes 147464 | tf_op jit(solution)/shard_map/ppermute | solution.py:54
  105.4 3.5 %collective-permute-start.31 = (bf16[64,384]{1,0:T(8,128)(2,1)S(1)}, bf16[64,384]{1,0:T(8,128)(2,1)S(1)}, u32[]{:S(2)}, u32[]{:S(2)}) collective-permute-start(bf16[64,384]{1,0:T(8,128)(2,1)S(1)} %get-tuple-element.34), channel_id=1, source_target_pairs={{0,7},{1,0},{2,1},{3,2},{4,3},{5,4},{6,5},{7,6},{8,15},{9,8},{10,9... | collective-permute-start | bytes 147464 | tf_op jit(solution)/shard_map/ppermute | solution.py:54
  109.0 6.2 %collective-permute-start.32 = (f32[64,384]{1,0:T(8,128)S(1)}, f32[64,384]{1,0:T(8,128)S(1)}, u32[]{:S(2)}, u32[]{:S(2)}) collective-permute-start(f32[64,384]{1,0:T(8,128)S(1)} %convert_reduce_fusion), channel_id=1, source_target_pairs={{0,8},{8,16},{16,24},{24,0},{1,9},{9,17},{17,25},{25,1},{2,10},{10... | collective-permute-start | bytes 294920 | tf_op jit(solution)/shard_map/ppermute | solution.py:43
  110.4 7.3 %collective-permute-start.33 = (f32[64,384]{1,0:T(8,128)S(1)}, f32[64,384]{1,0:T(8,128)S(1)}, u32[]{:S(2)}, u32[]{:S(2)}) collective-permute-start(f32[64,384]{1,0:T(8,128)S(1)} %convert_reduce_fusion), channel_id=1, source_target_pairs={{0,16},{8,24},{16,0},{24,8},{1,17},{9,25},{17,1},{25,9},{2,18},{10... | collective-permute-start | bytes 294920 | tf_op jit(solution)/shard_map/ppermute | solution.py:43
  111.9 5.8 %collective-permute-start.34 = (f32[64,384]{1,0:T(8,128)S(1)}, f32[64,384]{1,0:T(8,128)S(1)}, u32[]{:S(2)}, u32[]{:S(2)}) collective-permute-start(f32[64,384]{1,0:T(8,128)S(1)} %convert_reduce_fusion), channel_id=1, source_target_pairs={{0,24},{8,0},{16,8},{24,16},{1,25},{9,1},{17,9},{25,17},{2,26},{10... | collective-permute-start | bytes 294920 | tf_op jit(solution)/shard_map/ppermute | solution.py:43
  (6 other events, 82.7 us)

commit v16 on v15

--- a/solution.py
+++ b/solution.py
@@ -61,17 +61,18 @@
     return jnp.stack(pieces)
 
 
-def exchange_summed(blocks, axis, native):
+def exchange_summed(blocks, axis, native, sum_type=None):
     size = lax.axis_size(axis)
+    sum_type = sum_type or blocks.dtype
     if native or size > FAN_OUT_MAX or size < 4 or size & (size - 1):
-        return jnp.sum(exchange_ordered(blocks, axis, native), axis=0)
+        return jnp.sum(exchange_ordered(blocks, axis, native).astype(sum_type), axis=0)
     here = lax.axis_index(axis)
     core = here % 2
     chips = jnp.arange(size // 2) * 2
     sent = lax.ppermute(
         jnp.take(blocks, chips + 1 - core, axis=0), axis, [(source, source ^ 1) for source in range(size)]
     )
-    combined = jnp.take(blocks, chips + core, axis=0) + sent
+    combined = jnp.take(blocks, chips + core, axis=0).astype(sum_type) + sent.astype(sum_type)
     total = lax.dynamic_index_in_dim(combined, here // 2, keepdims=False)
     for mask in range(2, size, 2):
         piece = lax.dynamic_index_in_dim(combined, (here ^ mask) // 2, keepdims=False)
@@ -289,10 +290,9 @@
         axis=1,
     ).astype(jnp.bfloat16)
 
-    arrived_grad = exchange_ordered(
-        partial_grad.reshape(fsdp_size, unit_rows, 3 * width), "fsdp", False
-    )
-    local_grad = jnp.sum(arrived_grad.astype(jnp.float32), axis=0)
+    local_grad = exchange_summed(
+        partial_grad.reshape(fsdp_size, unit_rows, 3 * width), "fsdp", False, jnp.float32
+    )
 
     grad_shard = jnp.sum(gather_ordered(local_grad, "dp", False), axis=0)
     return (

time: 119 us -> 121 us (1.017)
  waiting for transfers between devices: 28.8 us -> 32.9 us
  starting transfers between devices: 41.4 us -> 38.3 us
    ppermute x7 -> x0, starting transfers between devices: 7.66 us -> none  [exchange_ordered(): lax.ppermute(lax.dynamic_index_in_dim(blocks, (here + shift) % size, keep...]
    ppermute x6 -> x9, waiting for transfers between devices: 9.95 us -> 17 us  [exchange_summed(): lax.ppermute(piece, axis, [(source, source ^ mask) for source in range(si...]
    ppermute x6 -> x9, starting transfers between devices: 9.17 us -> 13.6 us  [exchange_summed(): lax.ppermute(piece, axis, [(source, source ^ mask) for source in range(si...]
    ppermute x7 -> x0, waiting for transfers between devices: 2.59 us -> none  [exchange_ordered(): lax.ppermute(lax.dynamic_index_in_dim(blocks, (here + shift) % size, keep...]
    unnamed x25 -> x19, local copies, waits for them, and re-layouts: 4.55 us -> 4.48 us
  transfers between devices with their start and end apart: 35 -> 32, of which waited for: 18 -> 19; matrix products, arithmetic and copies ran while one was open for 2% -> 3% of each run, Pallas kernels for 0% -> 0%
where the time goes in v16:
time: 121 us
  starting transfers between devices  38.3 us (32%)
  waiting for transfers between devices  32.9 us (27%)
  blocking collectives  17.3 us (14%)
  local copies, waits for them, and re-layouts  11.6 us (10%)
  other arithmetic  9.34 us (8%)
  matrix products  9.22 us (8%)
  between operations  2.05 us (2%)
    ppermute x20, starting transfers between devices, gather_ordered(): lax.ppermute(value, axis, shift_pairs(size, shift))  24.1 us
    all_gather x1, blocking collectives, gather_ordered(): return lax.all_gather(value, axis)  17.3 us
    ppermute x9, waiting for transfers between devices, exchange_summed(): lax.ppermute(piece, axis, [(source, source ^ mask) for source in range(si...  17 us
    ppermute x20, waiting for transfers between devices, gather_ordered(): lax.ppermute(value, axis, shift_pairs(size, shift))  14 us
    ppermute x9, starting transfers between devices, exchange_summed(): lax.ppermute(piece, axis, [(source, source ^ mask) for source in range(si...  13.6 us
    unnamed x19, local copies, waits for them, and re-layouts  4.48 us
    dot_general x1, matrix products, one_block(): return jnp.dot(d_logits, table, preferred_element_type=jnp.float32)  3.49 us
    dot_general x6, matrix products, contract_last(): lax.dot_general(left_side, right_side, (((1,), (1,)), ((), ())), preferre...  2.47 us
  transfers between devices with their start and end apart: 32, of which 19 were waited for; matrix products, arithmetic and copies ran while one was open for 3% of the time, Pallas kernels for 0%

profile of v16, /device:TPU:0, one launch (start us, length us, event | category | flops | bytes accessed | tf_op | source)
XLA Modules:
  0.0 120.7 jit_solution(9046139800259258849)
XLA Ops:
  7.2 17.3 %all-gather.1 = bf16[8,389,128]{2,1,0:T(8,128)(2,1)S(1)} all-gather(bf16[1,389,128]{2,1,0:T(8,128)(2,1)S(1)} %bitcast.170), channel_id=2, replica_groups=mesh['dp'=4,'fsdp'=8] {'fsdp'}, dimensions={0}, use_global_device_ids=true | all-gather | bytes 896256 | tf_op jit(solution)/shard_map/all_gather | solution.py:41
  24.5 1.8 %fusion.3 = bf16[1024,128]{1,0:T(8,128)(2,1)S(1)} fusion(bf16[1024,128]{1,0:T(8,128)(2,1)} %param.25, s32[1024]{0:T(1024)S(1)} %bitcast.204), kind=kOutput, calls=%fused_computation.17 | convolution fusion | flops 269615104 | bytes 528384 | tf_op jit(solution)/shard_map/dot_general | solution.py:219
  28.6 1.7 %collective-permute-start.1 = (bf16[128,128]{0,1:T(8,128)(2,1)S(1)}, bf16[128,128]{0,1:T(8,128)(2,1)S(1)}, u32[]{:S(2)}, u32[]{:S(2)}) collective-permute-start(bf16[128,128]{0,1:T(8,128)(2,1)S(1)} %bitcast.194), channel_id=1, source_target_pairs={{0,2},{1,3},{2,0},{3,1},{4,6},{5,7},{6,4},{7,5},{8,10},{9,11},{10,... | collective-permute-start | bytes 98312 | tf_op jit(solution)/shard_map/ppermute | solution.py:79
  30.4 2.6 %collective-permute-start.2 = (bf16[128,128]{0,1:T(8,128)(2,1)S(1)}, bf16[128,128]{0,1:T(8,128)(2,1)S(1)}, u32[]{:S(2)}, u32[]{:S(2)}) collective-permute-start(bf16[128,128]{0,1:T(8,128)(2,1)S(1)} %bitcast.195), channel_id=1, source_target_pairs={{0,4},{1,5},{2,6},{3,7},{4,0},{5,1},{6,2},{7,3},{8,12},{9,13},{10,... | collective-permute-start | bytes 98312 | tf_op jit(solution)/shard_map/ppermute | solution.py:79
  34.0 1.7 %collective-permute-done.2 = bf16[128,128]{0,1:T(8,128)(2,1)S(1)} collective-permute-done((bf16[128,128]{0,1:T(8,128)(2,1)S(1)}, bf16[128,128]{0,1:T(8,128)(2,1)S(1)}, u32[]{:S(2)}, u32[]{:S(2)}) %collective-permute-start.2) | collective-permute-done | bytes 32800 | tf_op jit(solution)/shard_map/ppermute | solution.py:79
  35.7 3.1 %collective-permute-done.3 = bf16[128,128]{0,1:T(8,128)(2,1)S(1)} collective-permute-done((bf16[128,128]{0,1:T(8,128)(2,1)S(1)}, bf16[128,128]{0,1:T(8,128)(2,1)S(1)}, u32[]{:S(2)}, u32[]{:S(2)}) %collective-permute-start.3) | collective-permute-done | bytes 32800 | tf_op jit(solution)/shard_map/ppermute | solution.py:79
  41.6 3.2 %collective-permute-start.7 = (bf16[128,256]{0,1:T(8,128)(2,1)S(1)}, bf16[128,256]{0,1:T(8,128)(2,1)S(1)}, u32[]{:S(2)}, u32[]{:S(2)}) collective-permute-start(bf16[128,256]{0,1:T(8,128)(2,1)S(1)} %pad_maximum_fusion.2), channel_id=1, source_target_pairs={{0,4},{1,5},{2,6},{3,7},{4,0},{5,1},{6,2},{7,3},{8,12},{9,13},{10,... | collective-permute-start | bytes 196616 | tf_op jit(solution)/shard_map/ppermute | solution.py:43
  44.9 1.5 %collective-permute-done.4 = bf16[128,256]{0,1:T(8,128)(2,1)S(1)} collective-permute-done((bf16[128,256]{0,1:T(8,128)(2,1)S(1)}, bf16[128,256]{0,1:T(8,128)(2,1)S(1)}, u32[]{:S(2)}, u32[]{:S(2)}) %collective-permute-start.4) | collective-permute-done | bytes 65568 | tf_op jit(solution)/shard_map/ppermute | solution.py:43
  47.7 4.8 %collective-permute-done.6 = bf16[128,256]{0,1:T(8,128)(2,1)S(1)} collective-permute-done((bf16[128,256]{0,1:T(8,128)(2,1)S(1)}, bf16[128,256]{0,1:T(8,128)(2,1)S(1)}, u32[]{:S(2)}, u32[]{:S(2)}) %collective-permute-start.6) | collective-permute-done | bytes 65568 | tf_op jit(solution)/shard_map/ppermute | solution.py:43
  54.8 2.0 %select_reduce_fusion = (f32[1024]{0:T(1024)S(1)}, f32[1024]{0:T(1024)S(1)}, f32[1024]{0:T(1024)S(1)}, f32[1024]{0:T(1024)S(1)}) fusion(f32[1024,1024]{0,1:T(8,128)S(1)} %get-tuple-element.70, s32[1024]{0:T(1024)S(1)} %bitcast.201, f32[1024]{0:T(1024)S(1)} %get-tuple-element.69, f32[1024,1024]{0,1:T(8,128)S(1)} %get-tuple-element.68, ...), kind=kLoop, calls=%fused_computation.8 | loop fusion | flops 9433088 | bytes 8417280 | tf_op jit(solution)/shard_map/reduce_sum | solution.py:110
  56.8 1.9 %collective-permute-start.11 = (f32[6,1024]{1,0:T(8,128)S(1)}, f32[6,1024]{1,0:T(8,128)S(1)}, u32[]{:S(2)}, u32[]{:S(2)}) collective-permute-start(f32[6,1024]{1,0:T(8,128)S(1)} %concatenate.39), channel_id=1, source_target_pairs={{0,1},{1,2},{2,3},{3,4},{4,5},{5,6},{6,7},{7,0},{8,9},{9,10},{10,1... | collective-permute-start | bytes 73736 | tf_op jit(solution)/shard_map/ppermute | solution.py:43
  58.7 2.6 %collective-permute-start.12 = (f32[6,1024]{1,0:T(8,128)S(1)}, f32[6,1024]{1,0:T(8,128)S(1)}, u32[]{:S(2)}, u32[]{:S(2)}) collective-permute-start(f32[6,1024]{1,0:T(8,128)S(1)} %concatenate.39), channel_id=1, source_target_pairs={{0,2},{1,3},{2,4},{3,5},{4,6},{5,7},{6,0},{7,1},{8,10},{9,11},{10,... | collective-permute-start | bytes 73736 | tf_op jit(solution)/shard_map/ppermute | solution.py:43
  61.5 2.7 %collective-permute-start.14 = (f32[6,1024]{1,0:T(8,128)S(1)}, f32[6,1024]{1,0:T(8,128)S(1)}, u32[]{:S(2)}, u32[]{:S(2)}) collective-permute-start(f32[6,1024]{1,0:T(8,128)S(1)} %concatenate.39), channel_id=1, source_target_pairs={{0,4},{1,5},{2,6},{3,7},{4,0},{5,1},{6,2},{7,3},{8,12},{9,13},{10,... | collective-permute-start | bytes 73736 | tf_op jit(solution)/shard_map/ppermute | solution.py:43
  64.2 2.1 %collective-permute-start.16 = (f32[6,1024]{1,0:T(8,128)S(1)}, f32[6,1024]{1,0:T(8,128)S(1)}, u32[]{:S(2)}, u32[]{:S(2)}) collective-permute-start(f32[6,1024]{1,0:T(8,128)S(1)} %concatenate.39), channel_id=1, source_target_pairs={{0,6},{1,7},{2,0},{3,1},{4,2},{5,3},{6,4},{7,5},{8,14},{9,15},{10,... | collective-permute-start | bytes 73736 | tf_op jit(solution)/shard_map/ppermute | solution.py:43
  66.3 1.3 %collective-permute-start.17 = (f32[6,1024]{1,0:T(8,128)S(1)}, f32[6,1024]{1,0:T(8,128)S(1)}, u32[]{:S(2)}, u32[]{:S(2)}) collective-permute-start(f32[6,1024]{1,0:T(8,128)S(1)} %concatenate.39), channel_id=1, source_target_pairs={{0,7},{1,0},{2,1},{3,2},{4,3},{5,4},{6,5},{7,6},{8,15},{9,8},{10,9... | collective-permute-start | bytes 73736 | tf_op jit(solution)/shard_map/ppermute | solution.py:43
  70.2 1.5 %collective-permute-start.18 = (f32[2,22]{1,0:T(2,128)S(1)}, f32[2,22]{1,0:T(2,128)S(1)}, u32[]{:S(2)}, u32[]{:S(2)}) collective-permute-start(f32[2,22]{1,0:T(2,128)S(1)} %get-tuple-element.56), channel_id=1, source_target_pairs={{0,8},{8,16},{16,24},{24,0},{1,9},{9,17},{17,25},{25,1},{2,10},{10... | collective-permute-start | bytes 536 | tf_op jit(solution)/shard_map/ppermute | solution.py:43
  71.7 1.5 %collective-permute-start.19 = (f32[2,22]{1,0:T(2,128)S(1)}, f32[2,22]{1,0:T(2,128)S(1)}, u32[]{:S(2)}, u32[]{:S(2)}) collective-permute-start(f32[2,22]{1,0:T(2,128)S(1)} %get-tuple-element.56), channel_id=1, source_target_pairs={{0,16},{8,24},{16,0},{24,8},{1,17},{9,25},{17,1},{25,9},{2,18},{10... | collective-permute-start | bytes 536 | tf_op jit(solution)/shard_map/ppermute | solution.py:43
  73.2 1.4 %collective-permute-start.20 = (f32[2,22]{1,0:T(2,128)S(1)}, f32[2,22]{1,0:T(2,128)S(1)}, u32[]{:S(2)}, u32[]{:S(2)}) collective-permute-start(f32[2,22]{1,0:T(2,128)S(1)} %get-tuple-element.56), channel_id=1, source_target_pairs={{0,24},{8,0},{16,8},{24,16},{1,25},{9,1},{17,9},{25,17},{2,26},{10... | collective-permute-start | bytes 536 | tf_op jit(solution)/shard_map/ppermute | solution.py:43
  75.3 1.5 %collective-permute-done.20 = f32[2,22]{1,0:T(2,128)S(1)} collective-permute-done((f32[2,22]{1,0:T(2,128)S(1)}, f32[2,22]{1,0:T(2,128)S(1)}, u32[]{:S(2)}, u32[]{:S(2)}) %collective-permute-start.20) | collective-permute-done | bytes 208 | tf_op jit(solution)/shard_map/ppermute | solution.py:43
  77.5 1.2 %fusion.61 = f32[]{:T(128)} fusion(f32[22]{0:T(128)S(1)} %get-tuple-element.24, f32[]{:T(128)} %get-tuple-element.23), kind=kLoop, calls=%fused_computation.186 | loop fusion | flops 43 | bytes 96 | tf_op jit(solution)/shard_map/reduce_sum | solution.py:260
  78.7 1.8 %bitcast_divide_fusion = (f32[22]{0:T(128)S(1)}, f32[22]{0:T(128)}) fusion(f32[2,22]{1,0:T(2,128)S(1)} %fusion.52, f32[]{:T(128)} %fusion.61, f32[22]{0:T(128)S(1)} %get-tuple-element.24, f32[]{:T(128)} %get-tuple-element.23), kind=kLoop, calls=%fused_computation.167 | loop fusion | flops 132 | bytes 360 | tf_op jit(solution)/shard_map/div | solution.py:263
  81.3 3.5 %fusion.2 = f32[1024,128]{1,0:T(8,128)S(1)} fusion(bf16[1024,128]{1,0:T(8,128)(2,1)S(1)} %copy-done, f32[1024,1024]{0,1:T(8,128)} %copy-done.1, f32[1024]{0:T(1024)S(1)} %bitcast.205, f32[1024]{0:T(1024)S(1)} %broadcast_bitcast_fusion, s32[1024]{0:T(1024)S(1)} %bitcast.202), kind=kOutput, calls=%fused_computation.16 | convolution fusion | flops 274726912 | bytes 4993024 | tf_op jit(solution)/shard_map/dot_general | solution.py:132
  88.2 2.7 %collective-permute-start.23 = (f32[128,128]{0,1:T(8,128)S(1)}, f32[128,128]{0,1:T(8,128)S(1)}, u32[]{:S(2)}, u32[]{:S(2)}) collective-permute-start(f32[128,128]{0,1:T(8,128)S(1)} %bitcast.184), channel_id=1, source_target_pairs={{0,4},{1,5},{2,6},{3,7},{4,0},{5,1},{6,2},{7,3},{8,12},{9,13},{10,... | collective-permute-start | bytes 196616 | tf_op jit(solution)/shard_map/ppermute | solution.py:79
  92.1 3.8 %collective-permute-done.23 = f32[128,128]{0,1:T(8,128)S(1)} collective-permute-done((f32[128,128]{0,1:T(8,128)S(1)}, f32[128,128]{0,1:T(8,128)S(1)}, u32[]{:S(2)}, u32[]{:S(2)}) %collective-permute-start.23) | collective-permute-done | bytes 65568 | tf_op jit(solution)/shard_map/ppermute | solution.py:79
  95.9 1.3 %collective-permute-done.24 = f32[128,128]{0,1:T(8,128)S(1)} collective-permute-done((f32[128,128]{0,1:T(8,128)S(1)}, f32[128,128]{0,1:T(8,128)S(1)}, u32[]{:S(2)}, u32[]{:S(2)}) %collective-permute-start.24) | collective-permute-done | bytes 65568 | tf_op jit(solution)/shard_map/ppermute | solution.py:79
  101.6 1.5 %collective-permute-start.27 = (f32[64,384]{1,0:T(8,128)S(1)}, f32[64,384]{1,0:T(8,128)S(1)}, u32[]{:S(2)}, u32[]{:S(2)}) collective-permute-start(f32[64,384]{1,0:T(8,128)S(1)} %get-tuple-element.37), channel_id=1, source_target_pairs={{0,4},{1,5},{2,6},{3,7},{4,0},{5,1},{6,2},{7,3},{8,12},{9,13},{10,... | collective-permute-start | bytes 294920 | tf_op jit(solution)/shard_map/ppermute | solution.py:79
  103.1 2.2 %collective-permute-start.28 = (f32[64,384]{1,0:T(8,128)S(1)}, f32[64,384]{1,0:T(8,128)S(1)}, u32[]{:S(2)}, u32[]{:S(2)}) collective-permute-start(f32[64,384]{1,0:T(8,128)S(1)} %get-tuple-element.36), channel_id=1, source_target_pairs={{0,6},{1,7},{2,4},{3,5},{4,2},{5,3},{6,0},{7,1},{8,14},{9,15},{10,... | collective-permute-start | bytes 294920 | tf_op jit(solution)/shard_map/ppermute | solution.py:79
  105.3 1.7 %collective-permute-done.26 = f32[64,384]{1,0:T(8,128)S(1)} collective-permute-done((f32[64,384]{1,0:T(8,128)S(1)}, f32[64,384]{1,0:T(8,128)S(1)}, u32[]{:S(2)}, u32[]{:S(2)}) %collective-permute-start.26) | collective-permute-done | bytes 98336 | tf_op jit(solution)/shard_map/ppermute | solution.py:79
  107.0 5.3 %collective-permute-done.27 = f32[64,384]{1,0:T(8,128)S(1)} collective-permute-done((f32[64,384]{1,0:T(8,128)S(1)}, f32[64,384]{1,0:T(8,128)S(1)}, u32[]{:S(2)}, u32[]{:S(2)}) %collective-permute-start.27) | collective-permute-done | bytes 98336 | tf_op jit(solution)/shard_map/ppermute | solution.py:79
  112.3 1.4 %collective-permute-start.29 = (f32[64,384]{1,0:T(8,128)S(1)}, f32[64,384]{1,0:T(8,128)S(1)}, u32[]{:S(2)}, u32[]{:S(2)}) collective-permute-start(f32[64,384]{1,0:T(8,128)S(1)} %fusion.22), channel_id=1, source_target_pairs={{0,8},{8,16},{16,24},{24,0},{1,9},{9,17},{17,25},{25,1},{2,10},{10... | collective-permute-start | bytes 294920 | tf_op jit(solution)/shard_map/ppermute | solution.py:43
  113.7 1.5 %collective-permute-start.30 = (f32[64,384]{1,0:T(8,128)S(1)}, f32[64,384]{1,0:T(8,128)S(1)}, u32[]{:S(2)}, u32[]{:S(2)}) collective-permute-start(f32[64,384]{1,0:T(8,128)S(1)} %fusion.22), channel_id=1, source_target_pairs={{0,16},{8,24},{16,0},{24,8},{1,17},{9,25},{17,1},{25,9},{2,18},{10... | collective-permute-start | bytes 294920 | tf_op jit(solution)/shard_map/ppermute | solution.py:43
  115.8 2.1 %collective-permute-done.29 = f32[64,384]{1,0:T(8,128)S(1)} collective-permute-done((f32[64,384]{1,0:T(8,128)S(1)}, f32[64,384]{1,0:T(8,128)S(1)}, u32[]{:S(2)}, u32[]{:S(2)}) %collective-permute-start.29) | collective-permute-done | bytes 98336 | tf_op jit(solution)/shard_map/ppermute | solution.py:43
  (160 shorter events, 32.2 us)
Async XLA Ops:
  27.0 1.4 %collective-permute-start = (bf16[4,128,128]{2,1,0:T(8,128)(2,1)S(1)}, bf16[4,128,128]{2,1,0:T(8,128)(2,1)S(1)}, u32[]{:S(2)}, u32[]{:S(2)}) collective-permute-start(bf16[4,128,128]{2,1,0:T(8,128)(2,1)S(1)} %broadcast_select_fusion.2), channel_id=1, source_target_pairs={{0,1},{1,0},{2,3},{3,2},{4,5},{5,4},{6,7},{7,6},{8,9},{9,8},{10,11... | collective-permute-start | bytes 393224 | tf_op jit(solution)/shard_map/ppermute | solution.py:72
  28.6 5.4 %collective-permute-start.1 = (bf16[128,128]{0,1:T(8,128)(2,1)S(1)}, bf16[128,128]{0,1:T(8,128)(2,1)S(1)}, u32[]{:S(2)}, u32[]{:S(2)}) collective-permute-start(bf16[128,128]{0,1:T(8,128)(2,1)S(1)} %bitcast.194), channel_id=1, source_target_pairs={{0,2},{1,3},{2,0},{3,1},{4,6},{5,7},{6,4},{7,5},{8,10},{9,11},{10,... | collective-permute-start | bytes 98312 | tf_op jit(solution)/shard_map/ppermute | solution.py:79
  30.4 5.3 %collective-permute-start.2 = (bf16[128,128]{0,1:T(8,128)(2,1)S(1)}, bf16[128,128]{0,1:T(8,128)(2,1)S(1)}, u32[]{:S(2)}, u32[]{:S(2)}) collective-permute-start(bf16[128,128]{0,1:T(8,128)(2,1)S(1)} %bitcast.195), channel_id=1, source_target_pairs={{0,4},{1,5},{2,6},{3,7},{4,0},{5,1},{6,2},{7,3},{8,12},{9,13},{10,... | collective-permute-start | bytes 98312 | tf_op jit(solution)/shard_map/ppermute | solution.py:79
  33.1 5.8 %collective-permute-start.3 = (bf16[128,128]{0,1:T(8,128)(2,1)S(1)}, bf16[128,128]{0,1:T(8,128)(2,1)S(1)}, u32[]{:S(2)}, u32[]{:S(2)}) collective-permute-start(bf16[128,128]{0,1:T(8,128)(2,1)S(1)} %bitcast.196), channel_id=1, source_target_pairs={{0,6},{1,7},{2,4},{3,5},{4,2},{5,3},{6,0},{7,1},{8,14},{9,15},{10,... | collective-permute-start | bytes 98312 | tf_op jit(solution)/shard_map/ppermute | solution.py:79
  40.7 5.7 %collective-permute-start.4 = (bf16[128,256]{0,1:T(8,128)(2,1)S(1)}, bf16[128,256]{0,1:T(8,128)(2,1)S(1)}, u32[]{:S(2)}, u32[]{:S(2)}) collective-permute-start(bf16[128,256]{0,1:T(8,128)(2,1)S(1)} %pad_maximum_fusion.2), channel_id=1, source_target_pairs={{0,1},{1,2},{2,3},{3,4},{4,5},{5,6},{6,7},{7,0},{8,9},{9,10},{10,1... | collective-permute-start | bytes 196616 | tf_op jit(solution)/shard_map/ppermute | solution.py:43
  40.7 6.9 %collective-permute-start.5 = (bf16[128,256]{0,1:T(8,128)(2,1)S(1)}, bf16[128,256]{0,1:T(8,128)(2,1)S(1)}, u32[]{:S(2)}, u32[]{:S(2)}) collective-permute-start(bf16[128,256]{0,1:T(8,128)(2,1)S(1)} %pad_maximum_fusion.2), channel_id=1, source_target_pairs={{0,2},{1,3},{2,4},{3,5},{4,6},{5,7},{6,0},{7,1},{8,10},{9,11},{10,... | collective-permute-start | bytes 196616 | tf_op jit(solution)/shard_map/ppermute | solution.py:43
  40.8 11.8 %collective-permute-start.6 = (bf16[128,256]{0,1:T(8,128)(2,1)S(1)}, bf16[128,256]{0,1:T(8,128)(2,1)S(1)}, u32[]{:S(2)}, u32[]{:S(2)}) collective-permute-start(bf16[128,256]{0,1:T(8,128)(2,1)S(1)} %pad_maximum_fusion.2), channel_id=1, source_target_pairs={{0,3},{1,4},{2,5},{3,6},{4,7},{5,0},{6,1},{7,2},{8,11},{9,12},{10,... | collective-permute-start | bytes 196616 | tf_op jit(solution)/shard_map/ppermute | solution.py:43
  41.6 11.1 %collective-permute-start.7 = (bf16[128,256]{0,1:T(8,128)(2,1)S(1)}, bf16[128,256]{0,1:T(8,128)(2,1)S(1)}, u32[]{:S(2)}, u32[]{:S(2)}) collective-permute-start(bf16[128,256]{0,1:T(8,128)(2,1)S(1)} %pad_maximum_fusion.2), channel_id=1, source_target_pairs={{0,4},{1,5},{2,6},{3,7},{4,0},{5,1},{6,2},{7,3},{8,12},{9,13},{10,... | collective-permute-start | bytes 196616 | tf_op jit(solution)/shard_map/ppermute | solution.py:43
  44.9 7.8 %collective-permute-start.8 = (bf16[128,256]{0,1:T(8,128)(2,1)S(1)}, bf16[128,256]{0,1:T(8,128)(2,1)S(1)}, u32[]{:S(2)}, u32[]{:S(2)}) collective-permute-start(bf16[128,256]{0,1:T(8,128)(2,1)S(1)} %pad_maximum_fusion.2), channel_id=1, source_target_pairs={{0,5},{1,6},{2,7},{3,0},{4,1},{5,2},{6,3},{7,4},{8,13},{9,14},{10,... | collective-permute-start | bytes 196616 | tf_op jit(solution)/shard_map/ppermute | solution.py:43
  46.4 6.4 %collective-permute-start.9 = (bf16[128,256]{0,1:T(8,128)(2,1)S(1)}, bf16[128,256]{0,1:T(8,128)(2,1)S(1)}, u32[]{:S(2)}, u32[]{:S(2)}) collective-permute-start(bf16[128,256]{0,1:T(8,128)(2,1)S(1)} %pad_maximum_fusion.2), channel_id=1, source_target_pairs={{0,6},{1,7},{2,0},{3,1},{4,2},{5,3},{6,4},{7,5},{8,14},{9,15},{10,... | collective-permute-start | bytes 196616 | tf_op jit(solution)/shard_map/ppermute | solution.py:43
  47.6 5.2 %collective-permute-start.10 = (bf16[128,256]{0,1:T(8,128)(2,1)S(1)}, bf16[128,256]{0,1:T(8,128)(2,1)S(1)}, u32[]{:S(2)}, u32[]{:S(2)}) collective-permute-start(bf16[128,256]{0,1:T(8,128)(2,1)S(1)} %pad_maximum_fusion.2), channel_id=1, source_target_pairs={{0,7},{1,0},{2,1},{3,2},{4,3},{5,4},{6,5},{7,6},{8,15},{9,8},{10,9... | collective-permute-start | bytes 196616 | tf_op jit(solution)/shard_map/ppermute | solution.py:43
  56.8 7.4 %collective-permute-start.11 = (f32[6,1024]{1,0:T(8,128)S(1)}, f32[6,1024]{1,0:T(8,128)S(1)}, u32[]{:S(2)}, u32[]{:S(2)}) collective-permute-start(f32[6,1024]{1,0:T(8,128)S(1)} %concatenate.39), channel_id=1, source_target_pairs={{0,1},{1,2},{2,3},{3,4},{4,5},{5,6},{6,7},{7,0},{8,9},{9,10},{10,1... | collective-permute-start | bytes 73736 | tf_op jit(solution)/shard_map/ppermute | solution.py:43
  58.7 7.6 %collective-permute-start.12 = (f32[6,1024]{1,0:T(8,128)S(1)}, f32[6,1024]{1,0:T(8,128)S(1)}, u32[]{:S(2)}, u32[]{:S(2)}) collective-permute-start(f32[6,1024]{1,0:T(8,128)S(1)} %concatenate.39), channel_id=1, source_target_pairs={{0,2},{1,3},{2,4},{3,5},{4,6},{5,7},{6,0},{7,1},{8,10},{9,11},{10,... | collective-permute-start | bytes 73736 | tf_op jit(solution)/shard_map/ppermute | solution.py:43
  61.4 6.3 %collective-permute-start.13 = (f32[6,1024]{1,0:T(8,128)S(1)}, f32[6,1024]{1,0:T(8,128)S(1)}, u32[]{:S(2)}, u32[]{:S(2)}) collective-permute-start(f32[6,1024]{1,0:T(8,128)S(1)} %concatenate.39), channel_id=1, source_target_pairs={{0,3},{1,4},{2,5},{3,6},{4,7},{5,0},{6,1},{7,2},{8,11},{9,12},{10,... | collective-permute-start | bytes 73736 | tf_op jit(solution)/shard_map/ppermute | solution.py:43
  61.5 6.3 %collective-permute-start.14 = (f32[6,1024]{1,0:T(8,128)S(1)}, f32[6,1024]{1,0:T(8,128)S(1)}, u32[]{:S(2)}, u32[]{:S(2)}) collective-permute-start(f32[6,1024]{1,0:T(8,128)S(1)} %concatenate.39), channel_id=1, source_target_pairs={{0,4},{1,5},{2,6},{3,7},{4,0},{5,1},{6,2},{7,3},{8,12},{9,13},{10,... | collective-permute-start | bytes 73736 | tf_op jit(solution)/shard_map/ppermute | solution.py:43
  64.2 3.6 %collective-permute-start.15 = (f32[6,1024]{1,0:T(8,128)S(1)}, f32[6,1024]{1,0:T(8,128)S(1)}, u32[]{:S(2)}, u32[]{:S(2)}) collective-permute-start(f32[6,1024]{1,0:T(8,128)S(1)} %concatenate.39), channel_id=1, source_target_pairs={{0,5},{1,6},{2,7},{3,0},{4,1},{5,2},{6,3},{7,4},{8,13},{9,14},{10,... | collective-permute-start | bytes 73736 | tf_op jit(solution)/shard_map/ppermute | solution.py:43
  64.2 4.1 %collective-permute-start.16 = (f32[6,1024]{1,0:T(8,128)S(1)}, f32[6,1024]{1,0:T(8,128)S(1)}, u32[]{:S(2)}, u32[]{:S(2)}) collective-permute-start(f32[6,1024]{1,0:T(8,128)S(1)} %concatenate.39), channel_id=1, source_target_pairs={{0,6},{1,7},{2,0},{3,1},{4,2},{5,3},{6,4},{7,5},{8,14},{9,15},{10,... | collective-permute-start | bytes 73736 | tf_op jit(solution)/shard_map/ppermute | solution.py:43
  66.3 2.9 %collective-permute-start.17 = (f32[6,1024]{1,0:T(8,128)S(1)}, f32[6,1024]{1,0:T(8,128)S(1)}, u32[]{:S(2)}, u32[]{:S(2)}) collective-permute-start(f32[6,1024]{1,0:T(8,128)S(1)} %concatenate.39), channel_id=1, source_target_pairs={{0,7},{1,0},{2,1},{3,2},{4,3},{5,4},{6,5},{7,6},{8,15},{9,8},{10,9... | collective-permute-start | bytes 73736 | tf_op jit(solution)/shard_map/ppermute | solution.py:43
  70.2 4.5 %collective-permute-start.18 = (f32[2,22]{1,0:T(2,128)S(1)}, f32[2,22]{1,0:T(2,128)S(1)}, u32[]{:S(2)}, u32[]{:S(2)}) collective-permute-start(f32[2,22]{1,0:T(2,128)S(1)} %get-tuple-element.56), channel_id=1, source_target_pairs={{0,8},{8,16},{16,24},{24,0},{1,9},{9,17},{17,25},{25,1},{2,10},{10... | collective-permute-start | bytes 536 | tf_op jit(solution)/shard_map/ppermute | solution.py:43
  71.7 3.6 %collective-permute-start.19 = (f32[2,22]{1,0:T(2,128)S(1)}, f32[2,22]{1,0:T(2,128)S(1)}, u32[]{:S(2)}, u32[]{:S(2)}) collective-permute-start(f32[2,22]{1,0:T(2,128)S(1)} %get-tuple-element.56), channel_id=1, source_target_pairs={{0,16},{8,24},{16,0},{24,8},{1,17},{9,25},{17,1},{25,9},{2,18},{10... | collective-permute-start | bytes 536 | tf_op jit(solution)/shard_map/ppermute | solution.py:43
  73.2 3.6 %collective-permute-start.20 = (f32[2,22]{1,0:T(2,128)S(1)}, f32[2,22]{1,0:T(2,128)S(1)}, u32[]{:S(2)}, u32[]{:S(2)}) collective-permute-start(f32[2,22]{1,0:T(2,128)S(1)} %get-tuple-element.56), channel_id=1, source_target_pairs={{0,24},{8,0},{16,8},{24,16},{1,25},{9,1},{17,9},{25,17},{2,26},{10... | collective-permute-start | bytes 536 | tf_op jit(solution)/shard_map/ppermute | solution.py:43
  85.4 1.6 %collective-permute-start.21 = (f32[4,128,128]{2,1,0:T(8,128)S(1)}, f32[4,128,128]{2,1,0:T(8,128)S(1)}, u32[]{:S(2)}, u32[]{:S(2)}) collective-permute-start(f32[4,128,128]{2,1,0:T(8,128)S(1)} %broadcast_select_fusion.1), channel_id=1, source_target_pairs={{0,1},{1,0},{2,3},{3,2},{4,5},{5,4},{6,7},{7,6},{8,9},{9,8},{10,11... | collective-permute-start | bytes 786440 | tf_op jit(solution)/shard_map/ppermute | solution.py:72
  87.3 4.9 %collective-permute-start.22 = (f32[128,128]{0,1:T(8,128)S(1)}, f32[128,128]{0,1:T(8,128)S(1)}, u32[]{:S(2)}, u32[]{:S(2)}) collective-permute-start(f32[128,128]{0,1:T(8,128)S(1)} %bitcast.183), channel_id=1, source_target_pairs={{0,2},{1,3},{2,0},{3,1},{4,6},{5,7},{6,4},{7,5},{8,10},{9,11},{10,... | collective-permute-start | bytes 196616 | tf_op jit(solution)/shard_map/ppermute | solution.py:79
  88.2 7.7 %collective-permute-start.23 = (f32[128,128]{0,1:T(8,128)S(1)}, f32[128,128]{0,1:T(8,128)S(1)}, u32[]{:S(2)}, u32[]{:S(2)}) collective-permute-start(f32[128,128]{0,1:T(8,128)S(1)} %bitcast.184), channel_id=1, source_target_pairs={{0,4},{1,5},{2,6},{3,7},{4,0},{5,1},{6,2},{7,3},{8,12},{9,13},{10,... | collective-permute-start | bytes 196616 | tf_op jit(solution)/shard_map/ppermute | solution.py:79
  91.0 6.2 %collective-permute-start.24 = (f32[128,128]{0,1:T(8,128)S(1)}, f32[128,128]{0,1:T(8,128)S(1)}, u32[]{:S(2)}, u32[]{:S(2)}) collective-permute-start(f32[128,128]{0,1:T(8,128)S(1)} %bitcast.185), channel_id=1, source_target_pairs={{0,6},{1,7},{2,4},{3,5},{4,2},{5,3},{6,0},{7,1},{8,14},{9,15},{10,... | collective-permute-start | bytes 196616 | tf_op jit(solution)/shard_map/ppermute | solution.py:79
  99.1 1.5 %collective-permute-start.25 = (bf16[4,64,384]{2,1,0:T(8,128)(2,1)S(1)}, bf16[4,64,384]{2,1,0:T(8,128)(2,1)S(1)}, u32[]{:S(2)}, u32[]{:S(2)}) collective-permute-start(bf16[4,64,384]{2,1,0:T(8,128)(2,1)S(1)} %broadcast_select_fusion), channel_id=1, source_target_pairs={{0,1},{1,0},{2,3},{3,2},{4,5},{5,4},{6,7},{7,6},{8,9},{9,8},{10,11... | collective-permute-start | bytes 589832 | tf_op jit(solution)/shard_map/ppermute | solution.py:72
  100.8 6.2 %collective-permute-start.26 = (f32[64,384]{1,0:T(8,128)S(1)}, f32[64,384]{1,0:T(8,128)S(1)}, u32[]{:S(2)}, u32[]{:S(2)}) collective-permute-start(f32[64,384]{1,0:T(8,128)S(1)} %get-tuple-element.35), channel_id=1, source_target_pairs={{0,2},{1,3},{2,0},{3,1},{4,6},{5,7},{6,4},{7,5},{8,10},{9,11},{10,... | collective-permute-start | bytes 294920 | tf_op jit(solution)/shard_map/ppermute | solution.py:79
  101.6 10.7 %collective-permute-start.27 = (f32[64,384]{1,0:T(8,128)S(1)}, f32[64,384]{1,0:T(8,128)S(1)}, u32[]{:S(2)}, u32[]{:S(2)}) collective-permute-start(f32[64,384]{1,0:T(8,128)S(1)} %get-tuple-element.37), channel_id=1, source_target_pairs={{0,4},{1,5},{2,6},{3,7},{4,0},{5,1},{6,2},{7,3},{8,12},{9,13},{10,... | collective-permute-start | bytes 294920 | tf_op jit(solution)/shard_map/ppermute | solution.py:79
  103.1 9.2 %collective-permute-start.28 = (f32[64,384]{1,0:T(8,128)S(1)}, f32[64,384]{1,0:T(8,128)S(1)}, u32[]{:S(2)}, u32[]{:S(2)}) collective-permute-start(f32[64,384]{1,0:T(8,128)S(1)} %get-tuple-element.36), channel_id=1, source_target_pairs={{0,6},{1,7},{2,4},{3,5},{4,2},{5,3},{6,0},{7,1},{8,14},{9,15},{10,... | collective-permute-start | bytes 294920 | tf_op jit(solution)/shard_map/ppermute | solution.py:79
  112.3 5.6 %collective-permute-start.29 = (f32[64,384]{1,0:T(8,128)S(1)}, f32[64,384]{1,0:T(8,128)S(1)}, u32[]{:S(2)}, u32[]{:S(2)}) collective-permute-start(f32[64,384]{1,0:T(8,128)S(1)} %fusion.22), channel_id=1, source_target_pairs={{0,8},{8,16},{16,24},{24,0},{1,9},{9,17},{17,25},{25,1},{2,10},{10... | collective-permute-start | bytes 294920 | tf_op jit(solution)/shard_map/ppermute | solution.py:43
  113.7 5.2 %collective-permute-start.30 = (f32[64,384]{1,0:T(8,128)S(1)}, f32[64,384]{1,0:T(8,128)S(1)}, u32[]{:S(2)}, u32[]{:S(2)}) collective-permute-start(f32[64,384]{1,0:T(8,128)S(1)} %fusion.22), channel_id=1, source_target_pairs={{0,16},{8,24},{16,0},{24,8},{1,17},{9,25},{17,1},{25,9},{2,18},{10... | collective-permute-start | bytes 294920 | tf_op jit(solution)/shard_map/ppermute | solution.py:43
  115.3 4.6 %collective-permute-start.31 = (f32[64,384]{1,0:T(8,128)S(1)}, f32[64,384]{1,0:T(8,128)S(1)}, u32[]{:S(2)}, u32[]{:S(2)}) collective-permute-start(f32[64,384]{1,0:T(8,128)S(1)} %fusion.22), channel_id=1, source_target_pairs={{0,24},{8,0},{16,8},{24,16},{1,25},{9,1},{17,9},{25,17},{2,26},{10... | collective-permute-start | bytes 294920 | tf_op jit(solution)/shard_map/ppermute | solution.py:43
  (3 other events, 76.8 us)
